TPU v7x, 32 devices: a whole 2x2x4 slice. The times are simulated.
32 devices in a mesh: seq: 8 (over z, y), head: 4 (over x, core).
Axes of the slice: x: 2, y: 2, z: 4, core: 2. Of those that a mesh axis runs over, the one named last changes fastest.
Arguments:
- queries: bfloat16 [2048, 4096], P(('seq', 'head')), may hold values from -120 to 120
- key_rows: bfloat16 [2048, 4096], P(('seq', 'head')), may hold values from -24 to 24
- value_rows: bfloat16 [2048, 4096], P(('seq', 'head')), may hold values from -6 to 6
- out_grad: bfloat16 [2048, 4096], P(('seq', 'head')), may hold values from -6 to 6
- summary_columns: int32 [16, 8], P('seq'), may hold values from 0 to 127, as said below
Outputs:
- attended: bfloat16 [2048, 4096], P(('seq', 'head'))
- query_grad: bfloat16 [2048, 4096], P(('seq', 'head'))
- key_grad: bfloat16 [2048, 4096], P(('seq', 'head'))
- value_grad: bfloat16 [2048, 4096], P(('seq', 'head'))
Inputs may be any that keep to these rules, and one draw needn't show every extreme that they name: `summary_columns`: in each block the 8 columns are distinct and increasing, and the last one is always 128 - 1.
All inputs are finite; a program needn't handle non-finite values.
Results may differ from a plain program's by a relative error of at most 0.025.
Values may be sent and summed in bfloat16 or wider, within the bound.
No kernel may reach another device: no remote copies, remote signals or barrier semaphores. Data moves between devices by JAX's collectives and lax.ppermute only.
A program may use at most 128 MiB of HBM per device.

v0:
```python
import math

import jax
import jax.numpy as jnp
from jax import lax
from jax.sharding import PartitionSpec as P

HEAD_DIM = 128
BLOCK = 128
SUMMARY = 8


MASKED_SCORE = -1e30


def take_rows(source, row_offset, count):
    return lax.dynamic_slice_in_dim(source, row_offset, count, 0)


def put_rows(target, update, row_offset):
    return lax.dynamic_update_slice_in_dim(target, update, row_offset, 0)


def pair_sweep(row_block, key_block, row_size, key_size, visit_fn, initial):
    row_tiles = row_block.shape[0] // row_size
    key_tiles = key_block.shape[0] // key_size

    def visit_pair(pair_index, current):
        row_start = pair_index // key_tiles * row_size
        key_start = pair_index % key_tiles * key_size
        newest = jnp.max(take_rows(row_block, row_start, row_size))
        oldest = take_rows(key_block, key_start, 1)[0]
        return lax.cond(
            oldest < newest,
            lambda held_state: visit_fn(held_state, row_start, key_start),
            lambda held_state: held_state,
            current,
        )

    return lax.fori_loop(0, row_tiles * key_tiles, visit_pair, initial)


def tile_mask(row_block, key_block, row_start, key_start, row_size, key_size):
    row_part = take_rows(row_block, row_start, row_size)
    key_part = take_rows(key_block, key_start, key_size)
    return (key_part[None, :] < row_part[:, None])[:, None, :]


def tile_scores(query_heads, sum_keys, row_start, key_start, row_size, key_size, score_scale):
    query_tile = take_rows(query_heads, row_start, row_size)
    key_tile = take_rows(sum_keys, key_start, key_size)
    return (
        jnp.einsum("rhd,khd->rhk", query_tile, key_tile, preferred_element_type=jnp.float32)
        * score_scale
    )


def joint_norm(first_max, first_total, second_max, second_total):
    highest = jnp.maximum(first_max, second_max)
    return highest + jnp.log(
        first_total * jnp.exp(first_max - highest) + second_total * jnp.exp(second_max - highest)
    )


def summary_stats(query_heads, row_block, sum_keys, key_block, row_size, key_size, score_scale):
    row_count, head_count = (query_heads.shape[0], query_heads.shape[1])

    def stats_visit(running, row_start, key_start):
        run_max, run_total = running
        allowed = tile_mask(row_block, key_block, row_start, key_start, row_size, key_size)
        scores = jnp.where(
            allowed,
            tile_scores(
                query_heads, sum_keys, row_start, key_start, row_size, key_size, score_scale
            ),
            MASKED_SCORE,
        )
        old_max = take_rows(run_max, row_start, row_size)
        new_max = jnp.maximum(old_max, jnp.max(scores, axis=2))
        weights = jnp.where(allowed, jnp.exp(scores - new_max[:, :, None]), 0.0)
        new_total = take_rows(run_total, row_start, row_size) * jnp.exp(
            old_max - new_max
        ) + jnp.sum(weights, axis=2)
        return (put_rows(run_max, new_max, row_start), put_rows(run_total, new_total, row_start))

    start_max = jnp.full((row_count, head_count), MASKED_SCORE, jnp.float32)
    start_total = jnp.zeros((row_count, head_count), jnp.float32)
    return pair_sweep(
        row_block, key_block, row_size, key_size, stats_visit, (start_max, start_total)
    )


def summary_output(
    query_heads,
    row_block,
    sum_keys,
    sum_values,
    key_block,
    log_norm,
    row_size,
    key_size,
    score_scale,
):

    def output_visit(totals, row_start, key_start):
        allowed = tile_mask(row_block, key_block, row_start, key_start, row_size, key_size)
        scores = tile_scores(
            query_heads, sum_keys, row_start, key_start, row_size, key_size, score_scale
        )
        norm_part = take_rows(log_norm, row_start, row_size)
        weights_low = jnp.where(allowed, jnp.exp(scores - norm_part[:, :, None]), 0.0).astype(
            jnp.bfloat16
        )
        added = jnp.einsum(
            "rhk,khd->rhd",
            weights_low,
            take_rows(sum_values, key_start, key_size),
            preferred_element_type=jnp.float32,
        )
        return put_rows(totals, take_rows(totals, row_start, row_size) + added, row_start)

    return pair_sweep(
        row_block,
        key_block,
        row_size,
        key_size,
        output_visit,
        jnp.zeros(query_heads.shape, jnp.float32),
    )


def summary_backward(
    query_heads,
    grad_heads,
    row_block,
    sum_keys,
    sum_values,
    key_block,
    log_norm,
    grad_dot,
    row_size,
    key_size,
    score_scale,
):

    def backward_visit(running, row_start, key_start):
        query_acc, key_acc, value_acc = running
        allowed = tile_mask(row_block, key_block, row_start, key_start, row_size, key_size)
        scores = tile_scores(
            query_heads, sum_keys, row_start, key_start, row_size, key_size, score_scale
        )
        weights_full = jnp.where(
            allowed, jnp.exp(scores - take_rows(log_norm, row_start, row_size)[:, :, None]), 0.0
        )
        query_tile = take_rows(query_heads, row_start, row_size)
        grad_tile = take_rows(grad_heads, row_start, row_size)
        key_tile = take_rows(sum_keys, key_start, key_size)
        value_tile = take_rows(sum_values, key_start, key_size)
        grad_weights = jnp.einsum(
            "rhd,khd->rhk", grad_tile, value_tile, preferred_element_type=jnp.float32
        )
        grad_scores = (
            weights_full * (grad_weights - take_rows(grad_dot, row_start, row_size)[:, :, None])
        ).astype(jnp.bfloat16)
        query_add = (
            jnp.einsum("rhk,khd->rhd", grad_scores, key_tile, preferred_element_type=jnp.float32)
            * score_scale
        )
        key_add = (
            jnp.einsum("rhk,rhd->khd", grad_scores, query_tile, preferred_element_type=jnp.float32)
            * score_scale
        )
        value_add = jnp.einsum(
            "rhk,rhd->khd",
            weights_full.astype(jnp.bfloat16),
            grad_tile,
            preferred_element_type=jnp.float32,
        )
        query_acc = put_rows(
            query_acc, take_rows(query_acc, row_start, row_size) + query_add, row_start
        )
        key_acc = put_rows(key_acc, take_rows(key_acc, key_start, key_size) + key_add, key_start)
        value_acc = put_rows(
            value_acc, take_rows(value_acc, key_start, key_size) + value_add, key_start
        )
        return (query_acc, key_acc, value_acc)

    initial = (
        jnp.zeros(query_heads.shape, jnp.float32),
        jnp.zeros(sum_keys.shape, jnp.float32),
        jnp.zeros(sum_keys.shape, jnp.float32),
    )
    return pair_sweep(row_block, key_block, row_size, key_size, backward_visit, initial)


def body(queries, key_rows, value_rows, out_grad, summary_columns):
    local_query, local_key, local_value, local_grad = (
        lax.all_to_all(queries, "head", split_axis=1, concat_axis=0, tiled=True),
        lax.all_to_all(key_rows, "head", split_axis=1, concat_axis=0, tiled=True),
        lax.all_to_all(value_rows, "head", split_axis=1, concat_axis=0, tiled=True),
        lax.all_to_all(out_grad, "head", split_axis=1, concat_axis=0, tiled=True),
    )
    row_count, feature_count = local_query.shape
    head_count = feature_count // HEAD_DIM
    block_count = row_count // BLOCK
    score_scale = 1.0 / math.sqrt(HEAD_DIM)
    shard_index = lax.axis_index("seq")
    local_rows = jnp.arange(row_count, dtype=jnp.int32)
    positions = (
        jnp.arange(block_count, dtype=jnp.int32)[:, None] * BLOCK + summary_columns
    ).reshape(-1)
    own_keys = jnp.take(local_key, positions, axis=0)
    own_values = jnp.take(local_value, positions, axis=0)
    all_keys, all_values = (
        lax.all_gather(own_keys, "seq", axis=0, tiled=True),
        lax.all_gather(own_values, "seq", axis=0, tiled=True),
    )
    sum_total = all_keys.shape[0]
    sum_keys = all_keys.reshape(sum_total, head_count, HEAD_DIM)
    sum_values = all_values.reshape(sum_total, head_count, HEAD_DIM)
    key_block = jnp.arange(sum_total, dtype=jnp.int32) // SUMMARY
    row_size = math.gcd(row_count, 64)
    key_size = math.gcd(sum_total, 256)
    query_heads = local_query.reshape(row_count, head_count, HEAD_DIM)
    grad_heads = local_grad.reshape(row_count, head_count, HEAD_DIM)
    query_blocks = local_query.reshape(block_count, BLOCK, head_count, HEAD_DIM)
    key_blocks = local_key.reshape(block_count, BLOCK, head_count, HEAD_DIM)
    value_blocks = local_value.reshape(block_count, BLOCK, head_count, HEAD_DIM)
    grad_blocks = local_grad.reshape(block_count, BLOCK, head_count, HEAD_DIM)
    span_index = jnp.arange(BLOCK, dtype=jnp.int32)
    causal = (span_index[:, None] >= span_index[None, :])[None, :, None, :]
    window_raw = (
        jnp.einsum("bihd,bjhd->bihj", query_blocks, key_blocks, preferred_element_type=jnp.float32)
        * score_scale
    )
    window_scores = jnp.where(causal, window_raw, MASKED_SCORE)
    window_max = jnp.max(window_scores, axis=3)
    window_total = jnp.sum(
        jnp.where(causal, jnp.exp(window_scores - window_max[..., None]), 0.0), axis=3
    )
    window_max = window_max.reshape(row_count, head_count)
    window_total = window_total.reshape(row_count, head_count)
    row_block = (shard_index * row_count + local_rows) // BLOCK
    sum_max, sum_totals = summary_stats(
        query_heads, row_block, sum_keys, key_block, row_size, key_size, score_scale
    )
    owner_norm = joint_norm(window_max, window_total, sum_max, sum_totals)
    summary_part = summary_output(
        query_heads,
        row_block,
        sum_keys,
        sum_values,
        key_block,
        owner_norm,
        row_size,
        key_size,
        score_scale,
    )
    norm_blocks = owner_norm.reshape(block_count, BLOCK, head_count)
    window_full = jnp.where(causal, jnp.exp(window_scores - norm_blocks[..., None]), 0.0)
    window_low = window_full.astype(jnp.bfloat16)
    window_out = jnp.einsum(
        "bihj,bjhd->bihd", window_low, value_blocks, preferred_element_type=jnp.float32
    ).reshape(row_count, head_count, HEAD_DIM)
    attended = (window_out + summary_part).astype(jnp.bfloat16)
    grad_dot = jnp.sum(grad_heads.astype(jnp.float32) * attended.astype(jnp.float32), axis=2)
    back_query, back_grad, back_norm, back_dot = (query_heads, grad_heads, owner_norm, grad_dot)
    summary_query, key_part, value_part = summary_backward(
        back_query,
        back_grad,
        row_block,
        sum_keys,
        sum_values,
        key_block,
        back_norm,
        back_dot,
        row_size,
        key_size,
        score_scale,
    )
    dot_blocks = grad_dot.reshape(block_count, BLOCK, head_count)
    grad_window = jnp.einsum(
        "bihd,bjhd->bihj", grad_blocks, value_blocks, preferred_element_type=jnp.float32
    )
    window_dscore = (window_full * (grad_window - dot_blocks[..., None])).astype(jnp.bfloat16)
    window_query = (
        jnp.einsum("bihj,bjhd->bihd", window_dscore, key_blocks, preferred_element_type=jnp.float32)
        * score_scale
    )
    window_key = (
        jnp.einsum(
            "bihj,bihd->bjhd", window_dscore, query_blocks, preferred_element_type=jnp.float32
        )
        * score_scale
    )
    window_value = jnp.einsum(
        "bihj,bihd->bjhd", window_low, grad_blocks, preferred_element_type=jnp.float32
    )
    key_sums, value_sums = (
        lax.psum_scatter(key_part, "seq", scatter_dimension=0, tiled=True),
        lax.psum_scatter(value_part, "seq", scatter_dimension=0, tiled=True),
    )
    selector = (local_rows[:, None] == positions[None, :]).astype(jnp.float32)
    key_grad = window_key.reshape(row_count, feature_count) + jnp.dot(
        selector, key_sums.reshape(-1, feature_count), precision=lax.Precision.HIGHEST
    )
    value_grad = window_value.reshape(row_count, feature_count) + jnp.dot(
        selector, value_sums.reshape(-1, feature_count), precision=lax.Precision.HIGHEST
    )
    query_grad = (
        window_query.reshape(row_count, feature_count)
        + summary_query.reshape(row_count, feature_count)
    ).astype(jnp.bfloat16)
    return (
        lax.all_to_all(
            attended.reshape(row_count, feature_count),
            "head",
            split_axis=0,
            concat_axis=1,
            tiled=True,
        ),
        lax.all_to_all(query_grad, "head", split_axis=0, concat_axis=1, tiled=True),
        lax.all_to_all(
            key_grad.astype(jnp.bfloat16), "head", split_axis=0, concat_axis=1, tiled=True
        ),
        lax.all_to_all(
            value_grad.astype(jnp.bfloat16), "head", split_axis=0, concat_axis=1, tiled=True
        ),
    )


def solution(mesh):
    return jax.shard_map(
        body,
        mesh=mesh,
        in_specs=(
            P(("seq", "head"), None),
            P(("seq", "head"), None),
            P(("seq", "head"), None),
            P(("seq", "head"), None),
            P("seq", None),
        ),
        out_specs=(
            P(("seq", "head"), None),
            P(("seq", "head"), None),
            P(("seq", "head"), None),
            P(("seq", "head"), None),
        ),
        check_vma=False,
    )
```

profile of v0, /device:TPU:1, one launch (start us, length us, event | category | flops | bytes accessed | tf_op | source)
XLA Modules:
  0.0 307.0 jit_solution(10793082260249974392)
XLA Ops:
  9.0 4.4 %all-to-all-start = ((bf16[64,4,1024]{2,0,1:T(8,128)(2,1)}), bf16[64,4,1024]{2,0,1:T(8,128)(2,1)S(1)}, u32[]{:S(2)}, u32[]{:S(2)}) async-start(bf16[64,4,1024]{2,0,1:T(8,128)(2,1)} %bitcast.201), calls=%async_computation | async-start | bytes 1048576 | tf_op jit(solution)/shard_map/all_to_all | solution.py:199
  17.2 4.1 %all-to-all-done = bf16[64,4,1024]{2,0,1:T(8,128)(2,1)S(1)} async-done(((bf16[64,4,1024]{2,0,1:T(8,128)(2,1)}), bf16[64,4,1024]{2,0,1:T(8,128)(2,1)S(1)}, u32[]{:S(2)}, u32[]{:S(2)}) %all-to-all-start) | async-done | bytes 524320 | tf_op jit(solution)/shard_map/all_to_all | solution.py:199
  21.2 4.5 %all-to-all-start.1 = ((bf16[64,4,1024]{2,0,1:T(8,128)(2,1)}), bf16[64,4,1024]{2,0,1:T(8,128)(2,1)S(1)}, u32[]{:S(2)}, u32[]{:S(2)}) async-start(bf16[64,4,1024]{2,0,1:T(8,128)(2,1)} %bitcast.200), calls=%async_computation.1 | async-start | bytes 1048576 | tf_op jit(solution)/shard_map/all_to_all | solution.py:198
  25.8 7.9 %all-to-all-done.1 = bf16[64,4,1024]{2,0,1:T(8,128)(2,1)S(1)} async-done(((bf16[64,4,1024]{2,0,1:T(8,128)(2,1)}), bf16[64,4,1024]{2,0,1:T(8,128)(2,1)S(1)}, u32[]{:S(2)}, u32[]{:S(2)}) %all-to-all-start.1) | async-done | bytes 524320 | tf_op jit(solution)/shard_map/all_to_all | solution.py:198
  33.7 4.3 %all-to-all-start.2 = ((bf16[64,4,1024]{2,0,1:T(8,128)(2,1)}), bf16[64,4,1024]{2,0,1:T(8,128)(2,1)S(1)}, u32[]{:S(2)}, u32[]{:S(2)}) async-start(bf16[64,4,1024]{2,0,1:T(8,128)(2,1)} %bitcast.199), calls=%async_computation.2 | async-start | bytes 1048576 | tf_op jit(solution)/shard_map/all_to_all | solution.py:200
  38.9 7.1 %all-to-all-done.2 = bf16[64,4,1024]{2,0,1:T(8,128)(2,1)S(1)} async-done(((bf16[64,4,1024]{2,0,1:T(8,128)(2,1)}), bf16[64,4,1024]{2,0,1:T(8,128)(2,1)S(1)}, u32[]{:S(2)}, u32[]{:S(2)}) %all-to-all-start.2) | async-done | bytes 524320 | tf_op jit(solution)/shard_map/all_to_all | solution.py:200
  46.0 5.0 %all-to-all-start.4 = ((bf16[64,4,1024]{2,0,1:T(8,128)(2,1)}), bf16[64,4,1024]{2,0,1:T(8,128)(2,1)}, u32[]{:S(2)}, u32[]{:S(2)}) async-start(bf16[64,4,1024]{2,0,1:T(8,128)(2,1)} %bitcast.198), calls=%async_computation.4 | async-start | bytes 1048576 | tf_op jit(solution)/shard_map/all_to_all | solution.py:201
  51.6 25.4 %all_gather.6 = bf16[128,1024]{1,0:T(8,128)(2,1)S(1)} all-gather(bf16[16,1024]{1,0:T(8,128)(2,1)S(1)} %get-tuple-element.1206), channel_id=1, replica_groups=mesh['seq'=8,'head'=4] {'seq'}, dimensions={0}, use_global_device_ids=true | all-gather | bytes 294912 | tf_op jit(solution)/shard_map/all_gather | solution.py:215
  77.2 8.6 %while.60 = (s32[]{:T(128)}, f32[256,8]{0,1:T(8,128)S(1)}, f32[256,8]{0,1:T(8,128)S(1)}, s32[128]{0:T(128)S(1)}, s32[256]{0:T(256)S(1)}, /*index=5*/bf16[256,8,1...) while((s32[]{:T(128)}, f32[256,8]{0,1:T(8,128)S(1)}, ...), condition=%wide.region_7.9_spmd.clone, body=%wide.region_1.8_spmd.clone.sunk | while | flops 17179724 | bytes 974667 | solution.py:40
  88.0 28.1 %all_gather.7 = bf16[128,1024]{1,0:T(8,128)(2,1)S(1)} all-gather(bf16[16,1024]{1,0:T(8,128)(2,1)S(1)} %get-tuple-element.1205), channel_id=1, replica_groups=mesh['seq'=8,'head'=4] {'seq'}, dimensions={0}, use_global_device_ids=true | all-gather | bytes 294912 | tf_op jit(solution)/shard_map/all_gather | solution.py:216
  116.2 7.1 %while.61 = (s32[]{:T(128)}, f32[256,8,128]{2,0,1:T(8,128)S(1)}, s32[128]{0:T(128)S(1)}, s32[256]{0:T(256)S(1)}, bf16[256,8,128]{2,0,1:T(8,128)(2,1)S(1)}, /*ind...) while((s32[]{:T(128)}, f32[256,8,128]{2,0,1:T(8,128)S(1)}, ...), condition=%wide.region_13.15_spmd.clone, body=%wide.region_9.14_spmd.clone.sunk | while | flops 33890376 | bytes 1207083 | solution.py:40
  127.4 10.4 %while.62 = (s32[]{:T(128)}, f32[256,8,128]{2,0,1:T(8,128)S(1)}, f32[128,8,128]{0,2,1:T(8,128)S(1)}, f32[128,8,128]{0,2,1:T(8,128)S(1)}, s32[128]{0:T(128)S(1)},...) while((s32[]{:T(128)}, f32[256,8,128]{2,0,1:T(8,128)S(1)}, ...), condition=%wide.region_19.21_spmd.clone, body=%wide.region_15.20_spmd.clone.sunk | while | flops 84877384 | bytes 7243723 | solution.py:40
  135.6 2.2 conditional.11
  146.2 2.3 reshape.207
  150.7 15.1 %all-to-all-start.5 = ((bf16[4,64,1024]{2,1,0:T(8,128)(2,1)}), bf16[4,64,1024]{2,1,0:T(8,128)(2,1)S(1)}, u32[]{:S(2)}, u32[]{:S(2)}) async-start(bf16[4,64,1024]{2,1,0:T(8,128)(2,1)} %add_convert_fusion), calls=%async_computation.5 | async-start | bytes 1048576 | tf_op jit(solution)/shard_map/all_to_all | solution.py:322
  168.9 4.9 %all-to-all-done.5 = bf16[4,64,1024]{2,1,0:T(8,128)(2,1)S(1)} async-done(((bf16[4,64,1024]{2,1,0:T(8,128)(2,1)}), bf16[4,64,1024]{2,1,0:T(8,128)(2,1)S(1)}, u32[]{:S(2)}, u32[]{:S(2)}) %all-to-all-start.5) | async-done | bytes 524320 | tf_op jit(solution)/shard_map/all_to_all | solution.py:322
  173.8 4.3 %all-to-all-start.3 = ((bf16[4,64,1024]{2,1,0:T(8,128)(2,1)}), bf16[4,64,1024]{2,1,0:T(8,128)(2,1)S(1)}, u32[]{:S(2)}, u32[]{:S(2)}) async-start(bf16[4,64,1024]{2,1,0:T(8,128)(2,1)} %all_to_all.117), calls=%async_computation.3 | async-start | bytes 1048576 | tf_op jit(solution)/shard_map/all_to_all | solution.py:315
  179.0 38.7 %reduce-scatter.5.cloned.1.call-done = f32[16,8,128]{2,1,0:T(8,128)} async-done(((f32[128,8,128]{2,1,0:T(8,128)}), f32[16,8,128]{2,1,0:T(8,128)}) %reduce-scatter.5.cloned.1.call-update) | async-done | bytes 65552 | tf_op jit(solution)/shard_map/reduce_scatter | solution.py:301
  217.8 2.3 fusion.51
  220.1 6.1 %all-to-all-start.7 = ((bf16[4,64,1024]{2,1,0:T(8,128)(2,1)}), bf16[4,64,1024]{2,1,0:T(8,128)(2,1)S(1)}, u32[]{:S(2)}, u32[]{:S(2)}) async-start(bf16[4,64,1024]{2,1,0:T(8,128)(2,1)} %bitcast.29), calls=%async_computation.9 | async-start | bytes 1048576 | tf_op jit(solution)/shard_map/all_to_all | solution.py:326
  227.1 55.9 %reduce-scatter.3.cloned.1.call-done = f32[16,8,128]{2,1,0:T(8,128)} async-done(((f32[128,8,128]{2,1,0:T(8,128)}), f32[16,8,128]{2,1,0:T(8,128)}) %reduce-scatter.3.cloned.1.call-update) | async-done | bytes 65552 | tf_op jit(solution)/shard_map/reduce_scatter | solution.py:300
  283.1 2.3 fusion.50
  285.3 6.0 %all-to-all-start.6 = ((bf16[4,64,1024]{2,1,0:T(8,128)(2,1)}), bf16[4,64,1024]{2,1,0:T(8,128)(2,1)S(1)}, u32[]{:S(2)}, u32[]{:S(2)}) async-start(bf16[4,64,1024]{2,1,0:T(8,128)(2,1)} %bitcast.26), calls=%async_computation.7 | async-start | bytes 1048576 | tf_op jit(solution)/shard_map/all_to_all | solution.py:323
  293.8 5.5 %all-to-all-done.6 = bf16[4,64,1024]{2,1,0:T(8,128)(2,1)S(1)} async-done(((bf16[4,64,1024]{2,1,0:T(8,128)(2,1)}), bf16[4,64,1024]{2,1,0:T(8,128)(2,1)S(1)}, u32[]{:S(2)}, u32[]{:S(2)}) %all-to-all-start.6) | async-done | bytes 524320 | tf_op jit(solution)/shard_map/all_to_all | solution.py:323
  (164 shorter events, 55.9 us)
Async XLA Ops:
  9.0 4.4 %copy-start.14 = (bf16[64,4096]{1,0:T(8,128)(2,1)S(1)}, bf16[64,4096]{1,0:T(8,128)(2,1)}, u32[]{:S(2)}) copy-start(bf16[64,4096]{1,0:T(8,128)(2,1)} %param.19) | copy-start | bytes 1572868
  9.0 12.2 %all-to-all-start = ((bf16[64,4,1024]{2,0,1:T(8,128)(2,1)}), bf16[64,4,1024]{2,0,1:T(8,128)(2,1)S(1)}, u32[]{:S(2)}, u32[]{:S(2)}) async-start(bf16[64,4,1024]{2,0,1:T(8,128)(2,1)} %bitcast.201), calls=%async_computation | async-start | bytes 1048576 | tf_op jit(solution)/shard_map/all_to_all | solution.py:199
  13.4 1.7 copy-start.15
  15.1 1.2 copy-start.16
  21.2 12.5 %all-to-all-start.1 = ((bf16[64,4,1024]{2,0,1:T(8,128)(2,1)}), bf16[64,4,1024]{2,0,1:T(8,128)(2,1)S(1)}, u32[]{:S(2)}, u32[]{:S(2)}) async-start(bf16[64,4,1024]{2,0,1:T(8,128)(2,1)} %bitcast.200), calls=%async_computation.1 | async-start | bytes 1048576 | tf_op jit(solution)/shard_map/all_to_all | solution.py:198
  33.7 12.3 %all-to-all-start.2 = ((bf16[64,4,1024]{2,0,1:T(8,128)(2,1)}), bf16[64,4,1024]{2,0,1:T(8,128)(2,1)S(1)}, u32[]{:S(2)}, u32[]{:S(2)}) async-start(bf16[64,4,1024]{2,0,1:T(8,128)(2,1)} %bitcast.199), calls=%async_computation.2 | async-start | bytes 1048576 | tf_op jit(solution)/shard_map/all_to_all | solution.py:200
  38.2 47.7 %copy-start.10 = (bf16[32,8,8,128]{3,2,1,0:T(8,128)(2,1)}, bf16[32,8,8,128]{3,2,1,0:T(8,128)(2,1)S(1)}, u32[]{:S(2)}) copy-start(bf16[32,8,8,128]{3,2,1,0:T(8,128)(2,1)S(1)} %copy.131) | copy-start | bytes 1572868
  38.3 47.6 %copy-start.7 = (bf16[32,8,8,128]{3,2,1,0:T(8,128)(2,1)}, bf16[32,8,8,128]{3,2,1,0:T(8,128)(2,1)S(1)}, u32[]{:S(2)}) copy-start(bf16[32,8,8,128]{3,2,1,0:T(8,128)(2,1)S(1)} %copy.132) | copy-start | bytes 1572868
  46.0 77.3 %all-to-all-start.4 = ((bf16[64,4,1024]{2,0,1:T(8,128)(2,1)}), bf16[64,4,1024]{2,0,1:T(8,128)(2,1)}, u32[]{:S(2)}, u32[]{:S(2)}) async-start(bf16[64,4,1024]{2,0,1:T(8,128)(2,1)} %bitcast.198), calls=%async_computation.4 | async-start | bytes 1048576 | tf_op jit(solution)/shard_map/all_to_all | solution.py:201
  51.0 166.8 %reduce-scatter.5.cloned.1.call-start = ((), (), s32[]{:S(2)}) async-start(), calls=%async_computation.11 | async-start | bytes 589824 | tf_op jit(solution)/shard_map/reduce_scatter | solution.py:301
  124.4 1.6 copy-start.2
  131.9 1.0 copy-start.4
  135.6 1.0 copy-start.4
  140.5 1.5 copy-start.1
  140.5 1.7 copy-start.3
  142.2 1.6 copy-start.11
  150.7 23.1 %all-to-all-start.5 = ((bf16[4,64,1024]{2,1,0:T(8,128)(2,1)}), bf16[4,64,1024]{2,1,0:T(8,128)(2,1)S(1)}, u32[]{:S(2)}, u32[]{:S(2)}) async-start(bf16[4,64,1024]{2,1,0:T(8,128)(2,1)} %add_convert_fusion), calls=%async_computation.5 | async-start | bytes 1048576 | tf_op jit(solution)/shard_map/all_to_all | solution.py:322
  165.8 117.3 %reduce-scatter.3.cloned.1.call-start = ((), (), s32[]{:S(2)}) async-start(), calls=%async_computation.10 | async-start | bytes 589824 | tf_op jit(solution)/shard_map/reduce_scatter | solution.py:300
  166.8 1.0 copy-start.6
  173.8 46.3 %all-to-all-start.3 = ((bf16[4,64,1024]{2,1,0:T(8,128)(2,1)}), bf16[4,64,1024]{2,1,0:T(8,128)(2,1)S(1)}, u32[]{:S(2)}, u32[]{:S(2)}) async-start(bf16[4,64,1024]{2,1,0:T(8,128)(2,1)} %all_to_all.117), calls=%async_computation.3 | async-start | bytes 1048576 | tf_op jit(solution)/shard_map/all_to_all | solution.py:315
  220.0 6.1 %copy-start.8 = (bf16[32,8,8,128]{3,2,1,0:T(8,128)(2,1)S(1)}, bf16[32,8,8,128]{3,2,1,0:T(8,128)(2,1)}, u32[]{:S(2)}) copy-start(bf16[32,8,8,128]{3,2,1,0:T(8,128)(2,1)} %copy-done.7) | copy-start | bytes 1572868
  220.1 6.1 %copy-start.13 = (bf16[2,128,8,128]{1,3,2,0:T(8,128)(2,1)S(1)}, bf16[2,128,8,128]{1,3,2,0:T(8,128)(2,1)}, u32[]{:S(2)}) copy-start(bf16[2,128,8,128]{1,3,2,0:T(8,128)(2,1)} %copy-done.12) | copy-start | bytes 1572868
  220.1 65.3 %all-to-all-start.7 = ((bf16[4,64,1024]{2,1,0:T(8,128)(2,1)}), bf16[4,64,1024]{2,1,0:T(8,128)(2,1)S(1)}, u32[]{:S(2)}, u32[]{:S(2)}) async-start(bf16[4,64,1024]{2,1,0:T(8,128)(2,1)} %bitcast.29), calls=%async_computation.9 | async-start | bytes 1048576 | tf_op jit(solution)/shard_map/all_to_all | solution.py:326
  285.3 13.9 %all-to-all-start.6 = ((bf16[4,64,1024]{2,1,0:T(8,128)(2,1)}), bf16[4,64,1024]{2,1,0:T(8,128)(2,1)S(1)}, u32[]{:S(2)}, u32[]{:S(2)}) async-start(bf16[4,64,1024]{2,1,0:T(8,128)(2,1)} %bitcast.26), calls=%async_computation.7 | async-start | bytes 1048576 | tf_op jit(solution)/shard_map/all_to_all | solution.py:323
  (5 other events, 4.1 us)
Sparse Core Ops, SparseCore 0:
  139.0 78.7 reduce-scatter.4
  222.0 60.9 reduce-scatter.2
where the time goes:
time: 309 us; the launch traced here: 307 us
  waiting for transfers between devices  124 us (40%)
  blocking collectives  53.5 us (17%)
  starting transfers between devices  49.7 us (16%)
  local copies, waits for them, and re-layouts  30.2 us (10%)
  between operations  14.4 us (5%)
  other arithmetic  13.6 us (4%)
  matrix products  12.5 us (4%)
  loops' own time  8.93 us (3%)
    reduce_scatter x1, waiting for transfers between devices, body(): lax.psum_scatter(key_part, 'seq', scatter_dimension=0, tiled=True)  55.9 us
    reduce_scatter x1, waiting for transfers between devices, body(): lax.psum_scatter(value_part, 'seq', scatter_dimension=0, tiled=True)  38.7 us
    all_gather x1, blocking collectives, body(): lax.all_gather(own_values, 'seq', axis=0, tiled=True)  28.1 us
    all_gather x1, blocking collectives, body(): lax.all_gather(own_keys, 'seq', axis=0, tiled=True)  25.4 us
    all_to_all x1, starting transfers between devices, body(): lax.all_to_all(query_grad, 'head', split_axis=0, concat_axis=1, tiled=True)  15.1 us
    reduce_max x12, other arithmetic, visit_pair(): newest = jnp.max(take_rows(row_block, row_start, row_size))  8.74 us
    another operation x3, loops' own time, pair_sweep(): return lax.fori_loop(0, row_tiles * key_tiles, visit_pair, initial)  8.56 us
    all_to_all x1, waiting for transfers between devices, body(): lax.all_to_all(queries, 'head', split_axis=1, concat_axis=0, tiled=True)  7.94 us
  transfers between devices with their start and end apart: 10, of which 7 were waited for; matrix products, arithmetic and copies ran while one was open for 12% of the time, Pallas kernels for 0%

commit v1 on v0

v1 whole, which is shorter than its diff:
```python
import math

import jax
import jax.numpy as jnp
from jax import lax
from jax.sharding import Mesh
from jax.sharding import PartitionSpec as P

HEAD_DIM = 128
BLOCK = 128
SUMMARY = 8

MASKED_SCORE = -1e30
GROUP = ("seq", "hx")


def swap_with_partner(x):
    return lax.ppermute(x, "hc", [(0, 1), (1, 0)])


def to_block_layout(arrays, core):
    rows, feats = arrays[0].shape
    half = feats // 2
    mine = [lax.dynamic_slice_in_dim(a, core * half, half, 1) for a in arrays]
    theirs = [lax.dynamic_slice_in_dim(a, (1 - core) * half, half, 1) for a in arrays]
    got = swap_with_partner(jnp.concatenate(theirs, axis=1))
    out = []
    for i, m in enumerate(mine):
        r = got[:, i * half:(i + 1) * half]
        out.append(jnp.where(core == 0, jnp.concatenate([m, r], 0), jnp.concatenate([r, m], 0)))
    return out


def to_token_layout(arrays, core):
    rows2, half = arrays[0].shape
    rows = rows2 // 2
    mine = [lax.dynamic_slice_in_dim(a, core * rows, rows, 0) for a in arrays]
    theirs = [lax.dynamic_slice_in_dim(a, (1 - core) * rows, rows, 0) for a in arrays]
    got = swap_with_partner(jnp.concatenate(theirs, axis=1))
    out = []
    for i, m in enumerate(mine):
        r = got[:, i * half:(i + 1) * half]
        out.append(jnp.where(core == 0, jnp.concatenate([m, r], 1), jnp.concatenate([r, m], 1)))
    return out


def body(queries, key_rows, value_rows, out_grad, summary_columns):
    core = lax.axis_index("hc")
    hx = lax.axis_index("hx")
    shard = lax.axis_index("seq")
    score_scale = 1.0 / math.sqrt(HEAD_DIM)
    f32 = jnp.float32

    qb, kb, vb, gb = to_block_layout([queries, key_rows, value_rows, out_grad], core)
    rows, half = qb.shape
    heads = half // HEAD_DIM
    nb = rows // BLOCK
    pair_count = summary_columns.shape[0] // nb
    first_block = (shard * pair_count + hx) * nb
    cols = lax.dynamic_slice_in_dim(summary_columns, hx * nb, nb, 0)
    positions = (jnp.arange(nb, dtype=jnp.int32)[:, None] * BLOCK + cols).reshape(-1)

    own_sum = jnp.concatenate([jnp.take(kb, positions, axis=0), jnp.take(vb, positions, axis=0)], axis=1)
    all_sum = lax.all_gather(own_sum, GROUP, axis=0, tiled=True)
    sum_count = all_sum.shape[0]
    sk = all_sum[:, :half].reshape(sum_count, heads, HEAD_DIM)
    sv = all_sum[:, half:].reshape(sum_count, heads, HEAD_DIM)

    q = qb.reshape(nb, BLOCK, heads, HEAD_DIM)
    k = kb.reshape(nb, BLOCK, heads, HEAD_DIM)
    v = vb.reshape(nb, BLOCK, heads, HEAD_DIM)
    g = gb.reshape(nb, BLOCK, heads, HEAD_DIM)

    span = jnp.arange(BLOCK, dtype=jnp.int32)
    causal = (span[:, None] >= span[None, :])[None, None]
    key_block = jnp.arange(sum_count, dtype=jnp.int32) // SUMMARY
    query_block = first_block + jnp.arange(nb, dtype=jnp.int32)
    allowed = (key_block[None, :] < query_block[:, None])[:, None, None, :]

    sw = jnp.einsum("bqhd,bkhd->bhqk", q, k, preferred_element_type=f32) * score_scale
    ss = jnp.einsum("bqhd,khd->bhqk", q, sk, preferred_element_type=f32) * score_scale
    sw = jnp.where(causal, sw, MASKED_SCORE)
    ss = jnp.where(allowed, ss, MASKED_SCORE)
    top = jnp.maximum(jnp.max(sw, axis=3), jnp.max(ss, axis=3))
    ew = jnp.where(causal, jnp.exp(sw - top[..., None]), 0.0)
    es = jnp.where(allowed, jnp.exp(ss - top[..., None]), 0.0)
    log_norm = top + jnp.log(jnp.sum(ew, axis=3) + jnp.sum(es, axis=3))
    pw = jnp.where(causal, jnp.exp(sw - log_norm[..., None]), 0.0)
    ps = jnp.where(allowed, jnp.exp(ss - log_norm[..., None]), 0.0)
    pw_low = pw.astype(jnp.bfloat16)
    ps_low = ps.astype(jnp.bfloat16)
    att = jnp.einsum("bhqk,bkhd->bqhd", pw_low, v, preferred_element_type=f32) + jnp.einsum(
        "bhqk,khd->bqhd", ps_low, sv, preferred_element_type=f32
    )
    attended = att.astype(jnp.bfloat16)
    delta = jnp.einsum("bqhd,bqhd->bhq", g.astype(f32), attended.astype(f32), precision=lax.Precision.HIGHEST)

    dpw = jnp.einsum("bqhd,bkhd->bhqk", g, v, preferred_element_type=f32)
    dps = jnp.einsum("bqhd,khd->bhqk", g, sv, preferred_element_type=f32)
    dsw = (pw * (dpw - delta[..., None])).astype(jnp.bfloat16)
    dss = (ps * (dps - delta[..., None])).astype(jnp.bfloat16)
    dq = (
        jnp.einsum("bhqk,bkhd->bqhd", dsw, k, preferred_element_type=f32)
        + jnp.einsum("bhqk,khd->bqhd", dss, sk, preferred_element_type=f32)
    ) * score_scale
    dkw = jnp.einsum("bhqk,bqhd->bkhd", dsw, q, preferred_element_type=f32) * score_scale
    dvw = jnp.einsum("bhqk,bqhd->bkhd", pw_low, g, preferred_element_type=f32)
    dks = jnp.einsum("bhqk,bqhd->khd", dss, q, preferred_element_type=f32) * score_scale
    dvs = jnp.einsum("bhqk,bqhd->khd", ps_low, g, preferred_element_type=f32)

    att_tok, dq_tok = to_token_layout(
        [attended.reshape(rows, half), dq.astype(jnp.bfloat16).reshape(rows, half)], core
    )

    parts = jnp.concatenate([dks.reshape(sum_count, half), dvs.reshape(sum_count, half)], axis=1)
    own_grad = lax.psum_scatter(parts, GROUP, scatter_dimension=0, tiled=True)
    dk = dkw.reshape(rows, half).at[positions].add(own_grad[:, :half])
    dv = dvw.reshape(rows, half).at[positions].add(own_grad[:, half:])
    dk_tok, dv_tok = to_token_layout([dk.astype(jnp.bfloat16), dv.astype(jnp.bfloat16)], core)
    return att_tok, dq_tok, dk_tok, dv_tok


def solution(mesh):
    seq_size, head_size = mesh.devices.shape
    split = Mesh(mesh.devices.reshape(seq_size, head_size // 2, 2), ("seq", "hx", "hc"))
    tok = P(("seq", "hx", "hc"), None)
    return jax.shard_map(
        body,
        mesh=split,
        in_specs=(tok, tok, tok, tok, P("seq", None)),
        out_specs=(tok, tok, tok, tok),
        check_vma=False,
    )
```

time: 309 us -> 190 us (0.61)
  blocking collectives: 53.5 us -> 0 us
  starting transfers between devices: 49.7 us -> 13.8 us
  waiting for transfers between devices: 124 us -> 101 us
  loops' own time: 8.93 us -> 0 us
  local copies, waits for them, and re-layouts: 30.2 us -> 33.4 us
    reduce_scatter x2 -> x0, waiting for transfers between devices: 94.7 us -> none  [the longest x1 55.9 us: body(): lax.psum_scatter(key_part, 'seq', scatter_dimension=0, tiled=True)]
    all_gather x2 -> x0, blocking collectives: 53.5 us -> none  [the longest x1 28.1 us: body(): lax.all_gather(own_values, 'seq', axis=0, tiled=True)]
    unnamed x2 -> x3, waiting for transfers between devices: 0.03 us -> 51.2 us
    all_to_all x8 -> x0, starting transfers between devices: 49.7 us -> none  [the longest x1 15.1 us: body(): lax.all_to_all(query_grad, 'head', split_axis=0, concat_axis=1, tiled=True)]
    all_gather x0 -> x1, waiting for transfers between devices: none -> 48 us  [body(): all_sum = lax.all_gather(own_sum, GROUP, axis=0, tiled=True)]
    all_to_all x8 -> x0, waiting for transfers between devices: 29.5 us -> none  [the longest x1 7.94 us: body(): lax.all_to_all(queries, 'head', split_axis=1, concat_axis=0, tiled=True)]
    ppermute x0 -> x3, starting transfers between devices: none -> 13.7 us  [swap_with_partner(): return lax.ppermute(x, 'hc', [(0, 1), (1, 0)])]
    unnamed x43 -> x52, local copies, waits for them, and re-layouts: 6.46 us -> 15.7 us
  transfers between devices with their start and end apart: 10 -> 5, of which waited for: 7 -> 3; matrix products, arithmetic and copies ran while one was open for 12% -> 14% of each run, Pallas kernels for 0% -> 0%
where the time goes in v1:
time: 190 us; the launch traced here: 188 us
  waiting for transfers between devices  101 us (53%)
  local copies, waits for them, and re-layouts  33.4 us (18%)
  other arithmetic  15.2 us (8%)
  between operations  14.6 us (8%)
  starting transfers between devices  13.8 us (7%)
  matrix products  9.94 us (5%)
    unnamed x3, waiting for transfers between devices  51.2 us
    all_gather x1, waiting for transfers between devices, body(): all_sum = lax.all_gather(own_sum, GROUP, axis=0, tiled=True)  48 us
    unnamed x52, local copies, waits for them, and re-layouts  15.7 us
    ppermute x3, starting transfers between devices, swap_with_partner(): return lax.ppermute(x, 'hc', [(0, 1), (1, 0)])  13.7 us
    slice x2, local copies, waits for them, and re-layouts, body(): sv = all_sum[:, half:].reshape(sum_count, heads, HEAD_DIM)  4.32 us
  transfers between devices with their start and end apart: 5, of which 3 were waited for; matrix products, arithmetic and copies ran while one was open for 14% of the time, Pallas kernels for 0%

profile of v1, /device:TPU:1, one launch (start us, length us, event | category | flops | bytes accessed | tf_op | source)
XLA Modules:
  0.0 188.2 jit_solution(12393249305650952725)
XLA Ops:
  7.2 2.2 %dynamic-slice_bitcast_fusion = (bf16[8,8,16,128]{3,1,2,0:T(8,128)(2,1)}, bf16[64,2048]{1,0:T(8,128)(2,1)S(1)}, bf16[64,2048]{1,0:T(8,128)(2,1)S(1)}, bf16[8,8,16,128]{3,1,2,0:T(8,128)(2,1)}) fusion(bf16[64,4096]{1,0:T(8,128)(2,1)} %param.10, s32[]{:T(128)S(6)} %select_n.146, s32[]{:T(128)S(6)} %select_n.147, bf16[64,4096]{1,0:T(8,128)(2,1)} %param.7), kind=kLoop, calls=%fused_computation.59 | loop fusion | bytes 2097160
  10.1 2.2 %collective-permute-done = bf16[64,8192]{1,0:T(8,128)(2,1)S(1)} collective-permute-done((bf16[64,8192]{1,0:T(8,128)(2,1)S(1)}, bf16[64,8192]{1,0:T(8,128)(2,1)S(1)}, u32[]{:S(2)}, u32[]{:S(2)}) %collective-permute-start) | collective-permute-done | bytes 1048608 | tf_op jit(solution)/shard_map/ppermute | solution.py:18
  19.4 1.4 copy.120
  23.0 48.0 %all-gather.2.cloned.1.call-done = bf16[128,4096]{1,0:T(8,128)(2,1)} async-done(((bf16[8,4096]{1,0:T(8,128)(2,1)}), bf16[128,4096]{1,0:T(8,128)(2,1)}) %all-gather.2.cloned.1.call-update) | async-done | bytes 1048592 | tf_op jit(solution)/shard_map/all_gather | solution.py:64
  71.0 2.3 %fusion.39 = (bf16[128,2048]{1,0:T(8,128)(2,1)}, bf16[128,2048]{1,0:T(8,128)(2,1)}) fusion(bf16[128,4096]{1,0:T(8,128)(2,1)} %all-gather.2.cloned.1.call-done), kind=kLoop, calls=%fused_computation.103 | loop fusion | bytes 2097152 | tf_op jit(solution)/shard_map/slice | solution.py:67
  73.2 1.3 copy.78
  74.6 2.0 %copy.84 = bf16[128,2048]{0,1:T(8,128)(2,1)} copy(bf16[128,2048]{1,0:T(8,128)(2,1)} %get-tuple-element.15) | data formatting | bytes 1048576 | tf_op jit(solution)/shard_map/slice | solution.py:67
  78.6 1.5 fusion.23
  80.2 1.3 multiply_reduce_fusion
  83.2 1.5 fusion.2
  84.7 2.5 %copy.103 = f32[128,16,128]{0,2,1:T(8,128)} copy(f32[128,16,128]{2,0,1:T(8,128)} %fusion.2) | data formatting | bytes 2097152 | tf_op jit(solution)/shard_map/mul | solution.py:108
  87.2 3.0 %pad_maximum_fusion = f32[128,4096]{0,1:T(8,128)} fusion(f32[128,2048]{0,1:T(8,128)} %bitcast.142, f32[128,2048]{0,1:T(8,128)} %bitcast.143), kind=kLoop, calls=%fused_computation.4 | loop fusion | flops 524288 | bytes 4194304 | tf_op jit(solution)/shard_map/concatenate | solution.py:115
  90.2 2.9 %copy.128 = f32[128,4096]{1,0:T(8,128)} copy(f32[128,4096]{0,1:T(8,128)} %pad_maximum_fusion) | data formatting | bytes 4194304
  93.2 1.6 convolution_bitcast_fusion.1
  96.7 1.2 copy.132
  97.9 1.3 constant_dynamic-slice_fusion.7
  99.2 2.0 %copy.131 = bf16[64,2048]{1,0:T(8,128)(2,1)} copy(bf16[64,2048]{0,1:T(8,128)(2,1)} %get-tuple-element.28) | data formatting | bytes 524288
  101.2 1.8 pad_maximum_fusion.2
  103.0 2.0 %collective-permute-start.1 = (bf16[64,4096]{1,0:T(8,128)(2,1)}, bf16[64,4096]{1,0:T(8,128)(2,1)}, u32[]{:S(2)}, u32[]{:S(2)}) collective-permute-start(bf16[64,4096]{1,0:T(8,128)(2,1)} %pad_maximum_fusion.2), channel_id=1, source_target_pairs={{0,1},{1,0},{2,3},{3,2},{4,5},{5,4},{6,7},{7,6},{8,9},{9,8},{10,11... | collective-permute-start | bytes 1572872 | tf_op jit(solution)/shard_map/ppermute | solution.py:18
  108.1 1.3 copy.100
  109.4 1.6 copy.105
  112.1 51.1 %reduce-scatter.4.cloned.1.call-done = f32[8,4096]{1,0:T(8,128)} async-done(((f32[128,4096]{1,0:T(8,128)}), f32[8,4096]{1,0:T(8,128)}) %reduce-scatter.4.cloned.1.call-update) | async-done | bytes 131088
  163.2 1.4 scatter_custom_fusion.1
  166.0 11.6 %collective-permute-start.2 = (bf16[64,4096]{1,0:T(8,128)(2,1)S(1)}, bf16[64,4096]{1,0:T(8,128)(2,1)S(1)}, u32[]{:S(2)}, u32[]{:S(2)}) collective-permute-start(bf16[64,4096]{1,0:T(8,128)(2,1)S(1)} %pad_maximum_fusion.3), channel_id=1, source_target_pairs={{0,1},{1,0},{2,3},{3,2},{4,5},{5,4},{6,7},{7,6},{8,9},{9,8},{10,11... | collective-permute-start | bytes 1572872 | tf_op jit(solution)/shard_map/ppermute | solution.py:18
  (100 shorter events, 24.7 us)
Async XLA Ops:
  7.2 2.2 %copy-start.14 = (bf16[64,4096]{1,0:T(8,128)(2,1)S(1)}, bf16[64,4096]{1,0:T(8,128)(2,1)}, u32[]{:S(2)}) copy-start(bf16[64,4096]{1,0:T(8,128)(2,1)} %param.8) | copy-start | bytes 1572868
  7.2 2.2 %copy-start.15 = (bf16[64,4096]{1,0:T(8,128)(2,1)S(1)}, bf16[64,4096]{1,0:T(8,128)(2,1)}, u32[]{:S(2)}) copy-start(bf16[64,4096]{1,0:T(8,128)(2,1)} %param.9) | copy-start | bytes 1572868
  7.2 63.8 %all-gather.2.cloned.1.call-start = ((), (), s32[]{:S(2)}) async-start(), calls=%async_computation.1 | async-start | bytes 1114112 | tf_op jit(solution)/shard_map/all_gather | solution.py:64
  9.4 0.7 copy-start.17
  9.6 2.7 %collective-permute-start = (bf16[64,8192]{1,0:T(8,128)(2,1)S(1)}, bf16[64,8192]{1,0:T(8,128)(2,1)S(1)}, u32[]{:S(2)}, u32[]{:S(2)}) collective-permute-start(bf16[64,8192]{1,0:T(8,128)(2,1)S(1)} %pad_maximum_fusion.1), channel_id=1, source_target_pairs={{0,1},{1,0},{2,3},{3,2},{4,5},{5,4},{6,7},{7,6},{8,9},{9,8},{10,11... | collective-permute-start | bytes 3145736 | tf_op jit(solution)/shard_map/ppermute | solution.py:18
  12.6 2.2 %copy-start.13 = (bf16[8,8,16,128]{3,1,2,0:T(8,128)(2,1)S(1)}, bf16[8,8,16,128]{3,1,2,0:T(8,128)(2,1)}, u32[]{:S(2)}) copy-start(bf16[8,8,16,128]{3,1,2,0:T(8,128)(2,1)} %get-tuple-element.31) | copy-start | bytes 786436
  12.6 2.2 %copy-start.12 = (bf16[8,8,16,128]{3,1,2,0:T(8,128)(2,1)S(1)}, bf16[8,8,16,128]{3,1,2,0:T(8,128)(2,1)}, u32[]{:S(2)}) copy-start(bf16[8,8,16,128]{3,1,2,0:T(8,128)(2,1)} %get-tuple-element.46) | copy-start | bytes 786436
  14.7 148.4 %reduce-scatter.4.cloned.1.call-start = ((), (), s32[]{:S(2)}) async-start(), calls=%async_computation.2 | async-start | bytes 2228224
  18.9 1.9 %copy-start.11 = (bf16[8,8,16,128]{3,2,1,0:T(8,128)(2,1)S(1)}, bf16[8,8,16,128]{3,2,1,0:T(8,128)(2,1)}, u32[]{:S(2)}) copy-start(bf16[8,8,16,128]{3,2,1,0:T(8,128)(2,1)} %copy.140) | copy-start | bytes 786436
  20.8 0.9 copy-start.10
  76.6 1.4 copy-start
  78.1 2.1 %copy-start.3 = (f32[16,128,128]{1,2,0:T(8,128)S(1)}, f32[16,128,128]{1,2,0:T(8,128)}, u32[]{:S(2)}) copy-start(f32[16,128,128]{1,2,0:T(8,128)} %copy.120) | copy-start | bytes 3145732
  78.1 2.1 %copy-start.7 = (bf16[128,16,128]{2,1,0:T(8,128)(2,1)S(1)}, bf16[128,16,128]{2,1,0:T(8,128)(2,1)}, u32[]{:S(2)}) copy-start(bf16[128,16,128]{2,1,0:T(8,128)(2,1)} %maximum_select_fusion) | copy-start | bytes 1572868
  82.4 0.8 copy-start.1
  93.2 1.6 copy-start.8
  95.2 1.5 copy-start.4
  95.5 2.4 %copy-start.2 = (bf16[1,128,16,128]{1,3,2,0:T(8,128)(2,1)S(1)}, bf16[1,128,16,128]{1,3,2,0:T(8,128)(2,1)}, u32[]{:S(2)}) copy-start(bf16[1,128,16,128]{1,3,2,0:T(8,128)(2,1)} %get-tuple-element.44) | copy-start | bytes 1572868
  99.2 5.8 %copy-start.6 = (bf16[64,2048]{0,1:T(8,128)(2,1)S(1)}, bf16[64,2048]{0,1:T(8,128)(2,1)}, u32[]{:S(2)}) copy-start(bf16[64,2048]{0,1:T(8,128)(2,1)} %get-tuple-element.27) | copy-start | bytes 786436
  103.0 8.0 %collective-permute-start.1 = (bf16[64,4096]{1,0:T(8,128)(2,1)}, bf16[64,4096]{1,0:T(8,128)(2,1)}, u32[]{:S(2)}, u32[]{:S(2)}) collective-permute-start(bf16[64,4096]{1,0:T(8,128)(2,1)} %pad_maximum_fusion.2), channel_id=1, source_target_pairs={{0,1},{1,0},{2,3},{3,2},{4,5},{5,4},{6,7},{7,6},{8,9},{9,8},{10,11... | collective-permute-start | bytes 1572872 | tf_op jit(solution)/shard_map/ppermute | solution.py:18
  106.6 1.0 copy-start.5
  163.2 1.5 copy-start.16
  165.8 11.8 %copy-start.9 = (bf16[64,2048]{1,0:T(8,128)(2,1)S(1)}, bf16[64,2048]{1,0:T(8,128)(2,1)}, u32[]{:S(2)}) copy-start(bf16[64,2048]{1,0:T(8,128)(2,1)} %copy.130) | copy-start | bytes 786436
  166.0 13.5 %collective-permute-start.2 = (bf16[64,4096]{1,0:T(8,128)(2,1)S(1)}, bf16[64,4096]{1,0:T(8,128)(2,1)S(1)}, u32[]{:S(2)}, u32[]{:S(2)}) collective-permute-start(bf16[64,4096]{1,0:T(8,128)(2,1)S(1)} %pad_maximum_fusion.3), channel_id=1, source_target_pairs={{0,1},{1,0},{2,3},{3,2},{4,5},{5,4},{6,7},{7,6},{8,9},{9,8},{10,11... | collective-permute-start | bytes 1572872 | tf_op jit(solution)/shard_map/ppermute | solution.py:18
Sparse Core Ops, SparseCore 0:
  14.9 56.0 all-gather.1
  93.3 69.8 reduce-scatter.3

commit v2 on v1

--- a/solution.py
+++ b/solution.py
@@ -12,6 +12,46 @@
 
 MASKED_SCORE = -1e30
 GROUP = ("seq", "hx")
+
+
+def group_size():
+    return lax.axis_size("seq") * lax.axis_size("hx")
+
+
+def group_bits():
+    size = group_size()
+    bits = size.bit_length() - 1
+    assert 1 << bits == size
+    return bits
+
+
+def exchange(x, mask):
+    size = group_size()
+    return lax.ppermute(x, GROUP, [(i, i ^ mask) for i in range(size)])
+
+
+def gather_blocks(x):
+    me = lax.axis_index("seq") * lax.axis_size("hx") + lax.axis_index("hx")
+    held = x[None]
+    for bit in reversed(range(group_bits())):
+        got = exchange(held, 1 << bit)
+        low = ((me >> bit) & 1) == 0
+        held = jnp.where(low, jnp.stack([held, got], 1), jnp.stack([got, held], 1))
+        held = held.reshape((-1,) + x.shape)
+    return held.reshape((-1,) + x.shape[1:])
+
+
+def reduce_blocks(x):
+    me = lax.axis_index("seq") * lax.axis_size("hx") + lax.axis_index("hx")
+    size = group_size()
+    held = x.reshape((size, -1) + x.shape[1:])
+    for bit in range(group_bits()):
+        pairs = held.reshape((held.shape[0] // 2, 2) + held.shape[1:])
+        mine = (me >> bit) & 1
+        keep = jnp.where(mine == 0, pairs[:, 0], pairs[:, 1])
+        send = jnp.where(mine == 0, pairs[:, 1], pairs[:, 0])
+        held = keep + exchange(send, 1 << bit)
+    return held.reshape(x.shape[0] // size, *x.shape[1:])
 
 
 def swap_with_partner(x):
@@ -61,7 +101,7 @@
     positions = (jnp.arange(nb, dtype=jnp.int32)[:, None] * BLOCK + cols).reshape(-1)
 
     own_sum = jnp.concatenate([jnp.take(kb, positions, axis=0), jnp.take(vb, positions, axis=0)], axis=1)
-    all_sum = lax.all_gather(own_sum, GROUP, axis=0, tiled=True)
+    all_sum = gather_blocks(own_sum)
     sum_count = all_sum.shape[0]
     sk = all_sum[:, :half].reshape(sum_count, heads, HEAD_DIM)
     sv = all_sum[:, half:].reshape(sum_count, heads, HEAD_DIM)
@@ -113,7 +153,7 @@
     )
 
     parts = jnp.concatenate([dks.reshape(sum_count, half), dvs.reshape(sum_count, half)], axis=1)
-    own_grad = lax.psum_scatter(parts, GROUP, scatter_dimension=0, tiled=True)
+    own_grad = reduce_blocks(parts)
     dk = dkw.reshape(rows, half).at[positions].add(own_grad[:, :half])
     dv = dvw.reshape(rows, half).at[positions].add(own_grad[:, half:])
     dk_tok, dv_tok = to_token_layout([dk.astype(jnp.bfloat16), dv.astype(jnp.bfloat16)], core)

time: 190 us -> 130 us (0.68)
  waiting for transfers between devices: 101 us -> 38.1 us
  starting transfers between devices: 13.8 us -> 27.6 us
  between operations: 14.6 us -> 1.32 us
  other arithmetic: 15.2 us -> 18.2 us
    unnamed x3 -> x0, waiting for transfers between devices: 51.2 us -> none
    all_gather x1 -> x0, waiting for transfers between devices: 48 us -> none  [body(): all_sum = lax.all_gather(own_sum, GROUP, axis=0, tiled=True)]
    ppermute x0 -> x8, waiting for transfers between devices: none -> 37.8 us  [exchange(): return lax.ppermute(x, GROUP, [(i, i ^ mask) for i in range(size)])]
    ppermute x0 -> x8, starting transfers between devices: none -> 21.4 us  [exchange(): return lax.ppermute(x, GROUP, [(i, i ^ mask) for i in range(size)])]
    ppermute x3, starting transfers between devices: 13.7 us -> 6.19 us  [swap_with_partner(): return lax.ppermute(x, 'hc', [(0, 1), (1, 0)])]
    select_n x0 -> x9, other arithmetic: none -> 5.41 us  [the longest x5 2.73 us: gather_blocks(): held = jnp.where(low, jnp.stack([held, got], 1), jnp.stack([got, held], 1))]
    concatenate x0 -> x3, local copies, waits for them, and re-layouts: none -> 4.78 us  [body(): jnp.concatenate([dks.reshape(sum_count, half), dvs.reshape(sum_count, hal...]
    unnamed x52 -> x68, local copies, waits for them, and re-layouts: 15.7 us -> 11.9 us
  transfers between devices with their start and end apart: 5 -> 11, of which waited for: 3 -> 8; matrix products, arithmetic and copies ran while one was open for 14% -> 20% of each run, Pallas kernels for 0% -> 0%
where the time goes in v2:
time: 130 us; the launch traced here: 129 us
  waiting for transfers between devices  38.1 us (29%)
  local copies, waits for them, and re-layouts  33.7 us (26%)
  starting transfers between devices  27.6 us (21%)
  other arithmetic  18.2 us (14%)
  matrix products  10.2 us (8%)
  between operations  1.32 us (1%)
    ppermute x8, waiting for transfers between devices, exchange(): return lax.ppermute(x, GROUP, [(i, i ^ mask) for i in range(size)])  37.8 us
    ppermute x8, starting transfers between devices, exchange(): return lax.ppermute(x, GROUP, [(i, i ^ mask) for i in range(size)])  21.4 us
    unnamed x68, local copies, waits for them, and re-layouts  11.9 us
    ppermute x3, starting transfers between devices, swap_with_partner(): return lax.ppermute(x, 'hc', [(0, 1), (1, 0)])  6.19 us
    concatenate x3, local copies, waits for them, and re-layouts, body(): jnp.concatenate([dks.reshape(sum_count, half), dvs.reshape(sum_count, hal...  4.78 us
    select_n x4, other arithmetic, to_token_layout(): jnp.where(core == 0, jnp.concatenate([m, r], 1), jnp.concatenate([r, m], 1))  3.66 us
    select_n x5, other arithmetic, gather_blocks(): held = jnp.where(low, jnp.stack([held, got], 1), jnp.stack([got, held], 1))  2.73 us
    select_n x4, other arithmetic, reduce_blocks(): send = jnp.where(mine == 0, pairs[:, 1], pairs[:, 0])  2.68 us
  transfers between devices with their start and end apart: 11, of which 8 were waited for; matrix products, arithmetic and copies ran while one was open for 20% of the time, Pallas kernels for 0%

profile of v2, /device:TPU:1, one launch (start us, length us, event | category | flops | bytes accessed | tf_op | source)
XLA Modules:
  0.0 129.1 jit_solution(18436730392141651289)
XLA Ops:
  6.8 3.6 %collective-permute-start.1 = (bf16[1,8,4096]{2,1,0:T(8,128)(2,1)S(1)}, bf16[1,8,4096]{2,1,0:T(8,128)(2,1)S(1)}, u32[]{:S(2)}, u32[]{:S(2)}) collective-permute-start(bf16[1,8,4096]{2,1,0:T(8,128)(2,1)S(1)} %get-tuple-element.38), channel_id=1, source_target_pairs={{0,16},{2,18},{4,20},{6,22},{8,24},{10,26},{12,28},{14,30},{16,0},... | collective-permute-start | bytes 196616 | tf_op jit(solution)/shard_map/ppermute | solution.py:30
  10.4 2.2 %collective-permute-done.1 = bf16[1,8,4096]{2,1,0:T(8,128)(2,1)S(1)} collective-permute-done((bf16[1,8,4096]{2,1,0:T(8,128)(2,1)S(1)}, bf16[1,8,4096]{2,1,0:T(8,128)(2,1)S(1)}, u32[]{:S(2)}, u32[]{:S(2)}) %collective-permute-start.1) | collective-permute-done | bytes 65568 | tf_op jit(solution)/shard_map/ppermute | solution.py:30
  12.6 2.3 %collective-permute-start.2 = (bf16[2,8,4096]{2,1,0:T(8,128)(2,1)S(1)}, bf16[2,8,4096]{2,1,0:T(8,128)(2,1)S(1)}, u32[]{:S(2)}, u32[]{:S(2)}) collective-permute-start(bf16[2,8,4096]{2,1,0:T(8,128)(2,1)S(1)} %maximum_select_fusion.14), channel_id=1, source_target_pairs={{0,8},{2,10},{4,12},{6,14},{8,0},{10,2},{12,4},{14,6},{16,24},{18,... | collective-permute-start | bytes 393224 | tf_op jit(solution)/shard_map/ppermute | solution.py:30
  14.9 2.4 %collective-permute-done.2 = bf16[2,8,4096]{2,1,0:T(8,128)(2,1)S(1)} collective-permute-done((bf16[2,8,4096]{2,1,0:T(8,128)(2,1)S(1)}, bf16[2,8,4096]{2,1,0:T(8,128)(2,1)S(1)}, u32[]{:S(2)}, u32[]{:S(2)}) %collective-permute-start.2) | collective-permute-done | bytes 131104 | tf_op jit(solution)/shard_map/ppermute | solution.py:30
  20.5 1.4 %copy.153 = f32[16,128,128]{1,2,0:T(8,128)} copy(f32[16,128,128]{2,0,1:T(8,128)S(1)} %get-tuple-element.5) | data formatting | bytes 2097152
  21.9 1.6 %collective-permute-done.3 = bf16[4,8,4096]{2,1,0:T(8,128)(2,1)} collective-permute-done((bf16[4,8,4096]{2,1,0:T(8,128)(2,1)}, bf16[4,8,4096]{2,1,0:T(8,128)(2,1)}, u32[]{:S(2)}, u32[]{:S(2)}) %collective-permute-start.3) | collective-permute-done | bytes 262176 | tf_op jit(solution)/shard_map/ppermute | solution.py:30
  28.1 6.6 %collective-permute-done.4 = bf16[8,8,4096]{2,1,0:T(8,128)(2,1)} collective-permute-done((bf16[8,8,4096]{2,1,0:T(8,128)(2,1)S(1)}, bf16[8,8,4096]{2,1,0:T(8,128)(2,1)}, u32[]{:S(2)}, u32[]{:S(2)}) %collective-permute-start.4) | collective-permute-done | bytes 524320 | tf_op jit(solution)/shard_map/ppermute | solution.py:30
  34.7 1.4 %maximum_select_fusion = bf16[8,2,8,4096]{3,2,0,1:T(8,128)(2,1)S(1)} fusion(bf16[8,1,8,4096]{3,2,0,1:T(8,128)(2,1)} %bitcast.12, bf16[8,1,8,4096]{3,2,0,1:T(8,128)(2,1)S(1)} %bitcast.228, pred[]{:T(512)S(6)} %eq.11), kind=kLoop, calls=%fused_computation.34 | loop fusion | flops 1572864 | bytes 2097153 | tf_op jit(solution)/shard_map/jit(_where)/select_n | solution.py:39
  37.4 1.5 %copy.108 = bf16[128,2048]{0,1:T(8,128)(2,1)S(1)} copy(bf16[128,2048]{1,0:T(8,128)(2,1)} %get-tuple-element.15) | data formatting | bytes 1048576 | tf_op jit(solution)/shard_map/slice | solution.py:107
  40.9 1.5 %convolution_bitcast_fusion.1 = f32[128,16,128]{0,2,1:T(8,128)} fusion(bf16[128,16,128]{0,2,1:T(8,128)(2,1)S(1)} %copy.128, f32[1,16,128,128]{3,2,1,0:T(8,128)S(1)} %get-tuple-element.44, f32[16,128]{1,0:T(8,128)S(1)} %log_add_fusion, pred[128]{0:T(512)(128)(4,1)S(1)} %fusion.40), kind=kOutput, calls=%fused_computation.9 | convolution fusion | flops 67895296 | bytes 2629760 | tf_op jit(solution)/shard_map/bhqk,bqhd->khd/dot_general | solution.py:149
  48.5 2.6 %copy.129 = f32[128,16,128]{2,1,0:T(8,128)} copy(f32[128,16,128]{0,2,1:T(8,128)} %convolution_bitcast_fusion.1) | data formatting | bytes 2097152 | tf_op jit(solution)/shard_map/bhqk,bqhd->khd/transpose | solution.py:149
  51.1 2.4 %concatenate.174 = f32[8,2,8,2048]{3,2,1,0:T(8,128)} reshape(f32[128,16,128]{2,1,0:T(8,128)} %copy.129) | data formatting | bytes 2097152 | tf_op jit(solution)/shard_map/concatenate | solution.py:155
  57.0 1.8 %convolution_bitcast_fusion.2 = f32[1,128,16,128]{1,3,2,0:T(8,128)S(1)} fusion(bf16[128,16,128]{0,2,1:T(8,128)(2,1)} %bitcast.217, bf16[16,128,128]{2,1,0:T(8,128)(2,1)} %copy-done.10), kind=kOutput, calls=%fused_computation.14 | convolution fusion | flops 67108864 | bytes 2097152 | tf_op jit(solution)/shard_map/bhqk,khd->bqhd/dot_general | solution.py:144
  60.9 15.3 %collective-permute-done.6 = f32[8,8,4096]{2,1,0:T(8,128)} collective-permute-done((f32[8,8,4096]{2,1,0:T(8,128)}, f32[8,8,4096]{2,1,0:T(8,128)}, u32[]{:S(2)}, u32[]{:S(2)}) %collective-permute-start.6) | collective-permute-done | bytes 1048608 | tf_op jit(solution)/shard_map/ppermute | solution.py:30
  76.2 1.4 %fusion.19 = f32[8,8,4096]{2,1,0:T(8,128)S(1)} fusion(f32[8,8,4096]{2,1,0:T(8,128)} %collective-permute-done.6, f32[8,2,8,4096]{3,2,1,0:T(8,128)S(1)} %constant_dynamic-update-slice_fusion, pred[]{:T(512)S(6)} %eq.11), kind=kLoop, calls=%fused_computation.37 | loop fusion | flops 524288 | bytes 4194305 | tf_op jit(solution)/shard_map/add | solution.py:53
  82.8 4.9 %collective-permute-done.7 = f32[4,8,4096]{2,1,0:T(8,128)} collective-permute-done((f32[4,8,4096]{2,1,0:T(8,128)}, f32[4,8,4096]{2,1,0:T(8,128)}, u32[]{:S(2)}, u32[]{:S(2)}) %collective-permute-start.7) | collective-permute-done | bytes 524320 | tf_op jit(solution)/shard_map/ppermute | solution.py:30
  89.6 7.8 %collective-permute-start.8 = (f32[2,8,4096]{2,1,0:T(8,128)}, f32[2,8,4096]{2,1,0:T(8,128)}, u32[]{:S(2)}, u32[]{:S(2)}) collective-permute-start(f32[2,8,4096]{2,1,0:T(8,128)} %select_bitcast_fusion.2), channel_id=1, source_target_pairs={{0,8},{2,10},{4,12},{6,14},{8,0},{10,2},{12,4},{14,6},{16,24},{18,... | collective-permute-start | bytes 786440 | tf_op jit(solution)/shard_map/ppermute | solution.py:30
  97.9 5.4 %collective-permute-start.5 = (bf16[64,4096]{1,0:T(8,128)(2,1)}, bf16[64,4096]{1,0:T(8,128)(2,1)}, u32[]{:S(2)}, u32[]{:S(2)}) collective-permute-start(bf16[64,4096]{1,0:T(8,128)(2,1)} %pad_maximum_fusion.1), channel_id=1, source_target_pairs={{0,1},{1,0},{2,3},{3,2},{4,5},{5,4},{6,7},{7,6},{8,9},{9,8},{10,11... | collective-permute-start | bytes 1572872 | tf_op jit(solution)/shard_map/ppermute | solution.py:58
  103.2 1.9 %copy.161 = bf16[64,2048]{1,0:T(8,128)(2,1)} copy(bf16[64,2048]{0,1:T(8,128)(2,1)} %get-tuple-element.27) | data formatting | bytes 524288
  106.7 1.5 %fusion.3 = f32[1,128,16,128]{3,1,2,0:T(8,128)S(1)} fusion(bf16[128,16,128]{0,2,1:T(8,128)(2,1)S(1)} %copy-done.1, bf16[16,128,128]{1,2,0:T(8,128)(2,1)} %copy-done.13), kind=kOutput, calls=%fused_computation.13 | convolution fusion | flops 67371008 | bytes 2097152 | tf_op jit(solution)/shard_map/bhqk,bqhd->bkhd/dot_general | solution.py:146
  109.6 1.6 %copy.140 = f32[128,2048]{1,0:T(8,128)S(1)} copy(f32[128,2048]{0,1:T(8,128)} %bitcast.224) | data formatting | bytes 2097152 | tf_op jit(solution)/shard_map/reshape | solution.py:157
  112.2 3.2 %collective-permute-start.9 = (f32[1,8,4096]{2,1,0:T(8,128)S(1)}, f32[1,8,4096]{2,1,0:T(8,128)S(1)}, u32[]{:S(2)}, u32[]{:S(2)}) collective-permute-start(f32[1,8,4096]{2,1,0:T(8,128)S(1)} %select_bitcast_fusion.3), channel_id=1, source_target_pairs={{0,16},{2,18},{4,20},{6,22},{8,24},{10,26},{12,28},{14,30},{16,0},... | collective-permute-start | bytes 393224 | tf_op jit(solution)/shard_map/ppermute | solution.py:30
  115.4 1.9 %fusion.48 = (bf16[64,2048]{1,0:T(8,128)(2,1)}, bf16[64,2048]{1,0:T(8,128)(2,1)}) fusion(bf16[64,4096]{1,0:T(8,128)(2,1)} %collective-permute-done.5), kind=kLoop, calls=%fused_computation.129 | loop fusion | bytes 1048576 | tf_op jit(solution)/shard_map/slice | solution.py:82
  117.2 4.8 %collective-permute-done.9 = f32[1,8,4096]{2,1,0:T(8,128)S(1)} collective-permute-done((f32[1,8,4096]{2,1,0:T(8,128)S(1)}, f32[1,8,4096]{2,1,0:T(8,128)S(1)}, u32[]{:S(2)}, u32[]{:S(2)}) %collective-permute-start.9) | collective-permute-done | bytes 131104 | tf_op jit(solution)/shard_map/ppermute | solution.py:30
  (145 shorter events, 47.0 us)
Async XLA Ops:
  2.3 2.5 %copy-start.25 = (s32[2,8]{1,0:T(2,128)S(1)}, s32[2,8]{1,0:T(2,128)}, u32[]{:S(2)}) copy-start(s32[2,8]{1,0:T(2,128)} %param.11) | copy-start | bytes 196
  2.3 2.7 %collective-permute-start = (bf16[64,8192]{1,0:T(8,128)(2,1)S(1)}, bf16[64,8192]{1,0:T(8,128)(2,1)S(1)}, u32[]{:S(2)}, u32[]{:S(2)}) collective-permute-start(bf16[64,8192]{1,0:T(8,128)(2,1)S(1)} %pad_maximum_fusion), channel_id=1, source_target_pairs={{0,1},{1,0},{2,3},{3,2},{4,5},{5,4},{6,7},{7,6},{8,9},{9,8},{10,11... | collective-permute-start | bytes 3145736 | tf_op jit(solution)/shard_map/ppermute | solution.py:58
  6.8 5.8 %collective-permute-start.1 = (bf16[1,8,4096]{2,1,0:T(8,128)(2,1)S(1)}, bf16[1,8,4096]{2,1,0:T(8,128)(2,1)S(1)}, u32[]{:S(2)}, u32[]{:S(2)}) collective-permute-start(bf16[1,8,4096]{2,1,0:T(8,128)(2,1)S(1)} %get-tuple-element.38), channel_id=1, source_target_pairs={{0,16},{2,18},{4,20},{6,22},{8,24},{10,26},{12,28},{14,30},{16,0},... | collective-permute-start | bytes 196616 | tf_op jit(solution)/shard_map/ppermute | solution.py:30
  12.6 4.6 %collective-permute-start.2 = (bf16[2,8,4096]{2,1,0:T(8,128)(2,1)S(1)}, bf16[2,8,4096]{2,1,0:T(8,128)(2,1)S(1)}, u32[]{:S(2)}, u32[]{:S(2)}) collective-permute-start(bf16[2,8,4096]{2,1,0:T(8,128)(2,1)S(1)} %maximum_select_fusion.14), channel_id=1, source_target_pairs={{0,8},{2,10},{4,12},{6,14},{8,0},{10,2},{12,4},{14,6},{16,24},{18,... | collective-permute-start | bytes 393224 | tf_op jit(solution)/shard_map/ppermute | solution.py:30
  18.0 5.5 %collective-permute-start.3 = (bf16[4,8,4096]{2,1,0:T(8,128)(2,1)}, bf16[4,8,4096]{2,1,0:T(8,128)(2,1)}, u32[]{:S(2)}, u32[]{:S(2)}) collective-permute-start(bf16[4,8,4096]{2,1,0:T(8,128)(2,1)} %bitcast.8), channel_id=1, source_target_pairs={{0,4},{2,6},{4,0},{6,2},{8,12},{10,14},{12,8},{14,10},{16,20},{18,... | collective-permute-start | bytes 786440 | tf_op jit(solution)/shard_map/ppermute | solution.py:30
  19.8 23.9 %copy-start.4 = (bf16[128,16,128]{0,2,1:T(8,128)(2,1)}, bf16[128,16,128]{0,2,1:T(8,128)(2,1)S(1)}, u32[]{:S(2)}) copy-start(bf16[128,16,128]{0,2,1:T(8,128)(2,1)S(1)} %copy.128) | copy-start | bytes 1572868
  20.5 24.2 %copy-start = (bf16[128,16,128]{0,2,1:T(8,128)(2,1)}, bf16[128,16,128]{0,2,1:T(8,128)(2,1)S(1)}, u32[]{:S(2)}) copy-start(bf16[128,16,128]{0,2,1:T(8,128)(2,1)S(1)} %copy.121) | copy-start | bytes 1572868
  21.9 4.3 %copy-start.19 = (bf16[8,8,16,128]{3,2,1,0:T(8,128)(2,1)S(1)}, bf16[8,8,16,128]{3,2,1,0:T(8,128)(2,1)}, u32[]{:S(2)}) copy-start(bf16[8,8,16,128]{3,2,1,0:T(8,128)(2,1)} %copy.173) | copy-start | bytes 786436
  24.9 9.8 %collective-permute-start.4 = (bf16[8,8,4096]{2,1,0:T(8,128)(2,1)S(1)}, bf16[8,8,4096]{2,1,0:T(8,128)(2,1)}, u32[]{:S(2)}, u32[]{:S(2)}) collective-permute-start(bf16[8,8,4096]{2,1,0:T(8,128)(2,1)S(1)} %bitcast.227), channel_id=1, source_target_pairs={{0,2},{2,0},{4,6},{6,4},{8,10},{10,8},{12,14},{14,12},{16,18},{18,... | collective-permute-start | bytes 1572872 | tf_op jit(solution)/shard_map/ppermute | solution.py:30
  26.7 9.4 %copy-start.7 = (bf16[128,16,128]{0,2,1:T(8,128)(2,1)}, bf16[128,16,128]{0,2,1:T(8,128)(2,1)S(1)}, u32[]{:S(2)}) copy-start(bf16[128,16,128]{0,2,1:T(8,128)(2,1)S(1)} %copy.114) | copy-start | bytes 1572868
  37.4 2.3 %copy-start.9 = (bf16[128,2048]{0,1:T(8,128)(2,1)}, bf16[128,2048]{0,1:T(8,128)(2,1)S(1)}, u32[]{:S(2)}) copy-start(bf16[128,2048]{0,1:T(8,128)(2,1)S(1)} %copy.102) | copy-start | bytes 1572868
  40.3 2.1 %copy-start.12 = (f32[16,128,128]{1,2,0:T(8,128)S(1)}, f32[16,128,128]{1,2,0:T(8,128)}, u32[]{:S(2)}) copy-start(f32[16,128,128]{1,2,0:T(8,128)} %copy.153) | copy-start | bytes 3145732
  55.9 20.3 %collective-permute-start.6 = (f32[8,8,4096]{2,1,0:T(8,128)}, f32[8,8,4096]{2,1,0:T(8,128)}, u32[]{:S(2)}, u32[]{:S(2)}) collective-permute-start(f32[8,8,4096]{2,1,0:T(8,128)} %select_bitcast_fusion), channel_id=1, source_target_pairs={{0,2},{2,0},{4,6},{6,4},{8,10},{10,8},{12,14},{14,12},{16,18},{18,... | collective-permute-start | bytes 3145736 | tf_op jit(solution)/shard_map/ppermute | solution.py:30
  57.0 2.2 %copy-start.8 = (bf16[128,16,128]{0,2,1:T(8,128)(2,1)S(1)}, bf16[128,16,128]{0,2,1:T(8,128)(2,1)}, u32[]{:S(2)}) copy-start(bf16[128,16,128]{0,2,1:T(8,128)(2,1)} %copy-done.7) | copy-start | bytes 1572868
  60.9 19.5 %copy-start.11 = (bf16[1,128,16,128]{1,3,2,0:T(8,128)(2,1)S(1)}, bf16[1,128,16,128]{1,3,2,0:T(8,128)(2,1)}, u32[]{:S(2)}) copy-start(bf16[1,128,16,128]{1,3,2,0:T(8,128)(2,1)} %get-tuple-element.46) | copy-start | bytes 1572868
  77.5 4.0 %copy-start.14 = (bf16[64,2048]{0,1:T(8,128)(2,1)S(1)}, bf16[64,2048]{0,1:T(8,128)(2,1)}, u32[]{:S(2)}) copy-start(bf16[64,2048]{0,1:T(8,128)(2,1)} %get-tuple-element.24) | copy-start | bytes 786436
  79.4 8.3 %collective-permute-start.7 = (f32[4,8,4096]{2,1,0:T(8,128)}, f32[4,8,4096]{2,1,0:T(8,128)}, u32[]{:S(2)}, u32[]{:S(2)}) collective-permute-start(f32[4,8,4096]{2,1,0:T(8,128)} %select_bitcast_fusion.1), channel_id=1, source_target_pairs={{0,4},{2,6},{4,0},{6,2},{8,12},{10,14},{12,8},{14,10},{16,20},{18,... | collective-permute-start | bytes 1572872 | tf_op jit(solution)/shard_map/ppermute | solution.py:30
  80.4 7.3 %copy-start.3 = (f32[8,8,4096]{2,1,0:T(8,128)S(1)}, f32[8,8,4096]{2,1,0:T(8,128)}, u32[]{:S(2)}) copy-start(f32[8,8,4096]{2,1,0:T(8,128)} %copy-done.2) | copy-start | bytes 3145732
  81.9 15.4 %copy-start.6 = (bf16[128,16,128]{0,2,1:T(8,128)(2,1)S(1)}, bf16[128,16,128]{0,2,1:T(8,128)(2,1)}, u32[]{:S(2)}) copy-start(bf16[128,16,128]{0,2,1:T(8,128)(2,1)} %copy-done.4) | copy-start | bytes 1572868
  89.6 21.6 %collective-permute-start.8 = (f32[2,8,4096]{2,1,0:T(8,128)}, f32[2,8,4096]{2,1,0:T(8,128)}, u32[]{:S(2)}, u32[]{:S(2)}) collective-permute-start(f32[2,8,4096]{2,1,0:T(8,128)} %select_bitcast_fusion.2), channel_id=1, source_target_pairs={{0,8},{2,10},{4,12},{6,14},{8,0},{10,2},{12,4},{14,6},{16,24},{18,... | collective-permute-start | bytes 786440 | tf_op jit(solution)/shard_map/ppermute | solution.py:30
  97.8 8.9 %copy-start.1 = (bf16[128,16,128]{0,2,1:T(8,128)(2,1)S(1)}, bf16[128,16,128]{0,2,1:T(8,128)(2,1)}, u32[]{:S(2)}) copy-start(bf16[128,16,128]{0,2,1:T(8,128)(2,1)} %copy-done) | copy-start | bytes 1572868
  97.9 17.5 %collective-permute-start.5 = (bf16[64,4096]{1,0:T(8,128)(2,1)}, bf16[64,4096]{1,0:T(8,128)(2,1)}, u32[]{:S(2)}, u32[]{:S(2)}) collective-permute-start(bf16[64,4096]{1,0:T(8,128)(2,1)} %pad_maximum_fusion.1), channel_id=1, source_target_pairs={{0,1},{1,0},{2,3},{3,2},{4,5},{5,4},{6,7},{7,6},{8,9},{9,8},{10,11... | collective-permute-start | bytes 1572872 | tf_op jit(solution)/shard_map/ppermute | solution.py:58
  112.2 9.8 %collective-permute-start.9 = (f32[1,8,4096]{2,1,0:T(8,128)S(1)}, f32[1,8,4096]{2,1,0:T(8,128)S(1)}, u32[]{:S(2)}, u32[]{:S(2)}) collective-permute-start(f32[1,8,4096]{2,1,0:T(8,128)S(1)} %select_bitcast_fusion.3), channel_id=1, source_target_pairs={{0,16},{2,18},{4,20},{6,22},{8,24},{10,26},{12,28},{14,30},{16,0},... | collective-permute-start | bytes 393224 | tf_op jit(solution)/shard_map/ppermute | solution.py:30
  124.6 2.7 %collective-permute-start.10 = (bf16[64,4096]{1,0:T(8,128)(2,1)S(1)}, bf16[64,4096]{1,0:T(8,128)(2,1)S(1)}, u32[]{:S(2)}, u32[]{:S(2)}) collective-permute-start(bf16[64,4096]{1,0:T(8,128)(2,1)S(1)} %pad_maximum_fusion.2), channel_id=1, source_target_pairs={{0,1},{1,0},{2,3},{3,2},{4,5},{5,4},{6,7},{7,6},{8,9},{9,8},{10,11... | collective-permute-start | bytes 1572872 | tf_op jit(solution)/shard_map/ppermute | solution.py:58
  (13 other events, 19.8 us)

commit v3 on v1

--- a/solution.py
+++ b/solution.py
@@ -12,6 +12,26 @@
 
 MASKED_SCORE = -1e30
 GROUP = ("seq", "hx")
+
+
+def group_size():
+    return lax.axis_size("seq") * lax.axis_size("hx")
+
+
+def send_forward(x):
+    size = group_size()
+    got = [x]
+    for d in range(1, size):
+        got.append(lax.ppermute(x, GROUP, [(i, i + d) for i in range(size - d)]))
+    return jnp.stack(got)
+
+
+def send_back(parts):
+    size = group_size()
+    total = parts[0]
+    for d in range(1, size):
+        total = total + lax.ppermute(parts[d], GROUP, [(i, i - d) for i in range(d, size)])
+    return total
 
 
 def swap_with_partner(x):
@@ -61,7 +81,10 @@
     positions = (jnp.arange(nb, dtype=jnp.int32)[:, None] * BLOCK + cols).reshape(-1)
 
     own_sum = jnp.concatenate([jnp.take(kb, positions, axis=0), jnp.take(vb, positions, axis=0)], axis=1)
-    all_sum = lax.all_gather(own_sum, GROUP, axis=0, tiled=True)
+    me = shard * pair_count + hx
+    all_sum = send_forward(own_sum)
+    size = all_sum.shape[0]
+    all_sum = all_sum.reshape(-1, all_sum.shape[-1])
     sum_count = all_sum.shape[0]
     sk = all_sum[:, :half].reshape(sum_count, heads, HEAD_DIM)
     sv = all_sum[:, half:].reshape(sum_count, heads, HEAD_DIM)
@@ -73,9 +96,11 @@
 
     span = jnp.arange(BLOCK, dtype=jnp.int32)
     causal = (span[:, None] >= span[None, :])[None, None]
-    key_block = jnp.arange(sum_count, dtype=jnp.int32) // SUMMARY
+    slot = jnp.arange(sum_count, dtype=jnp.int32) // SUMMARY
+    key_block = (me - slot // nb) * nb + slot % nb
     query_block = first_block + jnp.arange(nb, dtype=jnp.int32)
-    allowed = (key_block[None, :] < query_block[:, None])[:, None, None, :]
+    present = key_block >= 0
+    allowed = (present[None, :] & (key_block[None, :] < query_block[:, None]))[:, None, None, :]
 
     sw = jnp.einsum("bqhd,bkhd->bhqk", q, k, preferred_element_type=f32) * score_scale
     ss = jnp.einsum("bqhd,khd->bhqk", q, sk, preferred_element_type=f32) * score_scale
@@ -113,7 +138,7 @@
     )
 
     parts = jnp.concatenate([dks.reshape(sum_count, half), dvs.reshape(sum_count, half)], axis=1)
-    own_grad = lax.psum_scatter(parts, GROUP, scatter_dimension=0, tiled=True)
+    own_grad = send_back(parts.reshape(size, -1, parts.shape[-1]))
     dk = dkw.reshape(rows, half).at[positions].add(own_grad[:, :half])
     dv = dvw.reshape(rows, half).at[positions].add(own_grad[:, half:])
     dk_tok, dv_tok = to_token_layout([dk.astype(jnp.bfloat16), dv.astype(jnp.bfloat16)], core)

time: 190 us -> 159 us (0.84)
  the two profiles are of different devices: /device:TPU:1 before, /device:TPU:31 now
where the time goes in v3:
time: 159 us; the launch traced here: 157 us
  starting transfers between devices  69.5 us (44%)
  local copies, waits for them, and re-layouts  38.5 us (24%)
  waiting for transfers between devices  20.5 us (13%)
  other arithmetic  15.8 us (10%)
  matrix products  11.6 us (7%)
    ppermute x15, starting transfers between devices, send_back(): lax.ppermute(parts[d], GROUP, [(i, i - d) for i in range(d, size)])  46.9 us
    ppermute x15, waiting for transfers between devices, send_forward(): got.append(lax.ppermute(x, GROUP, [(i, i + d) for i in range(size - d)]))  20.4 us
    unnamed x89, local copies, waits for them, and re-layouts  20 us
    ppermute x15, starting transfers between devices, send_forward(): got.append(lax.ppermute(x, GROUP, [(i, i + d) for i in range(size - d)]))  19.4 us
    dynamic_slice x4, local copies, waits for them, and re-layouts, to_token_layout(): mine = [lax.dynamic_slice_in_dim(a, core * rows, rows, 0) for a in arrays]  3.96 us
    select_n x4, other arithmetic, to_token_layout(): jnp.where(core == 0, jnp.concatenate([m, r], 1), jnp.concatenate([r, m], 1))  3.66 us
  transfers between devices with their start and end apart: 33, of which 7 were waited for; matrix products, arithmetic and copies ran while one was open for 20% of the time, Pallas kernels for 0%

profile of v3, /device:TPU:31, one launch (start us, length us, event | category | flops | bytes accessed | tf_op | source)
XLA Modules:
  0.0 157.3 jit_solution(15476533050269688597)
XLA Ops:
  32.9 2.3 %collective-permute-done.7 = bf16[8,4096]{1,0:T(8,128)(2,1)S(1)} collective-permute-done((bf16[8,4096]{1,0:T(8,128)(2,1)S(1)}, bf16[8,4096]{1,0:T(8,128)(2,1)S(1)}, u32[]{:S(2)}, u32[]{:S(2)}) %collective-permute-start.7) | collective-permute-done | bytes 65568 | tf_op jit(solution)/shard_map/ppermute | solution.py:25
  36.5 2.6 %collective-permute-done.8 = bf16[8,4096]{1,0:T(8,128)(2,1)S(1)} collective-permute-done((bf16[8,4096]{1,0:T(8,128)(2,1)S(1)}, bf16[8,4096]{1,0:T(8,128)(2,1)S(1)}, u32[]{:S(2)}, u32[]{:S(2)}) %collective-permute-start.8) | collective-permute-done | bytes 65568 | tf_op jit(solution)/shard_map/ppermute | solution.py:25
  40.5 3.7 %collective-permute-done.9 = bf16[8,4096]{1,0:T(8,128)(2,1)S(1)} collective-permute-done((bf16[8,4096]{1,0:T(8,128)(2,1)S(1)}, bf16[8,4096]{1,0:T(8,128)(2,1)S(1)}, u32[]{:S(2)}, u32[]{:S(2)}) %collective-permute-start.9) | collective-permute-done | bytes 65568 | tf_op jit(solution)/shard_map/ppermute | solution.py:25
  45.5 4.1 %collective-permute-done.10 = bf16[8,4096]{1,0:T(8,128)(2,1)S(1)} collective-permute-done((bf16[8,4096]{1,0:T(8,128)(2,1)S(1)}, bf16[8,4096]{1,0:T(8,128)(2,1)S(1)}, u32[]{:S(2)}, u32[]{:S(2)}) %collective-permute-start.10) | collective-permute-done | bytes 65568 | tf_op jit(solution)/shard_map/ppermute | solution.py:25
  51.0 1.6 collective-permute-done.11
  52.7 5.5 %collective-permute-done.15 = bf16[8,4096]{1,0:T(8,128)(2,1)S(1)} collective-permute-done((bf16[8,4096]{1,0:T(8,128)(2,1)S(1)}, bf16[8,4096]{1,0:T(8,128)(2,1)S(1)}, u32[]{:S(2)}, u32[]{:S(2)}) %collective-permute-start.15) | collective-permute-done | bytes 65568 | tf_op jit(solution)/shard_map/ppermute | solution.py:25
  80.6 2.5 %constant_dynamic-slice_fusion.7 = (bf16[64,2048]{0,1:T(8,128)(2,1)}, bf16[64,2048]{0,1:T(8,128)(2,1)}) fusion(bf16[128,2048]{0,1:T(8,128)(2,1)} %bitcast.171, s32[]{:T(128)S(6)} %select_n.177, s32[]{:T(128)S(6)} %select_n.178), kind=kLoop, calls=%fused_computation.142 | loop fusion | bytes 1048584 | tf_op jit(solution)/shard_map/dynamic_slice | solution.py:57
  83.1 1.9 %copy.185 = bf16[64,2048]{1,0:T(8,128)(2,1)} copy(bf16[64,2048]{0,1:T(8,128)(2,1)} %get-tuple-element.43) | data formatting | bytes 524288
  85.1 1.7 %collective-permute-start.31 = (f32[8,4096]{1,0:T(8,128)}, f32[8,4096]{1,0:T(8,128)S(1)}, u32[]{:S(2)}, u32[]{:S(2)}) collective-permute-start(f32[8,4096]{1,0:T(8,128)} %get-tuple-element.22), channel_id=1, source_target_pairs={{30,0},{31,1}} | collective-permute-start | bytes 393224 | tf_op jit(solution)/shard_map/ppermute | solution.py:33
  92.0 1.8 %pad_maximum_fusion.1 = bf16[64,4096]{1,0:T(8,128)(2,1)} fusion(bf16[64,2048]{1,0:T(8,128)(2,1)S(1)} %copy.186, bf16[64,2048]{1,0:T(8,128)(2,1)} %copy.185), kind=kLoop, calls=%fused_computation.77 | loop fusion | flops 1048576 | bytes 1048576 | tf_op jit(solution)/shard_map/concatenate | solution.py:59
  93.8 1.9 %collective-permute-start.26 = (f32[8,4096]{1,0:T(8,128)}, f32[8,4096]{1,0:T(8,128)}, u32[]{:S(2)}, u32[]{:S(2)}) collective-permute-start(f32[8,4096]{1,0:T(8,128)} %get-tuple-element.18), channel_id=1, source_target_pairs={{20,0},{22,2},{24,4},{26,6},{28,8},{30,10},{21,1},{23,3},{25,5},{2... | collective-permute-start | bytes 393224 | tf_op jit(solution)/shard_map/ppermute | solution.py:33
  95.7 1.9 %collective-permute-start.25 = (f32[8,4096]{1,0:T(8,128)}, f32[8,4096]{1,0:T(8,128)}, u32[]{:S(2)}, u32[]{:S(2)}) collective-permute-start(f32[8,4096]{1,0:T(8,128)} %get-tuple-element.17), channel_id=1, source_target_pairs={{18,0},{20,2},{22,4},{24,6},{26,8},{28,10},{30,12},{19,1},{21,3},{... | collective-permute-start | bytes 393224 | tf_op jit(solution)/shard_map/ppermute | solution.py:33
  97.7 1.9 %collective-permute-start.24 = (f32[8,4096]{1,0:T(8,128)}, f32[8,4096]{1,0:T(8,128)}, u32[]{:S(2)}, u32[]{:S(2)}) collective-permute-start(f32[8,4096]{1,0:T(8,128)} %get-tuple-element.16), channel_id=1, source_target_pairs={{16,0},{18,2},{20,4},{22,6},{24,8},{26,10},{28,12},{30,14},{17,1},... | collective-permute-start | bytes 393224 | tf_op jit(solution)/shard_map/ppermute | solution.py:33
  99.6 3.8 %collective-permute-start.23 = (f32[8,4096]{1,0:T(8,128)}, f32[8,4096]{1,0:T(8,128)}, u32[]{:S(2)}, u32[]{:S(2)}) collective-permute-start(f32[8,4096]{1,0:T(8,128)} %get-tuple-element.15), channel_id=1, source_target_pairs={{14,0},{16,2},{18,4},{20,6},{22,8},{24,10},{26,12},{28,14},{30,16}... | collective-permute-start | bytes 393224 | tf_op jit(solution)/shard_map/ppermute | solution.py:33
  103.4 2.6 %collective-permute-start.22 = (f32[8,4096]{1,0:T(8,128)}, f32[8,4096]{1,0:T(8,128)}, u32[]{:S(2)}, u32[]{:S(2)}) collective-permute-start(f32[8,4096]{1,0:T(8,128)} %get-tuple-element.14), channel_id=1, source_target_pairs={{12,0},{14,2},{16,4},{18,6},{20,8},{22,10},{24,12},{26,14},{28,16}... | collective-permute-start | bytes 393224 | tf_op jit(solution)/shard_map/ppermute | solution.py:33
  107.5 2.0 %copy.184 = bf16[64,2048]{1,0:T(8,128)(2,1)} copy(bf16[64,2048]{0,1:T(8,128)(2,1)} %get-tuple-element.42) | data formatting | bytes 524288
  109.7 2.6 %copy.163 = f32[128,2048]{1,0:T(8,128)} copy(f32[128,2048]{0,1:T(8,128)} %bitcast.172) | data formatting | bytes 2097152 | tf_op jit(solution)/shard_map/reshape | solution.py:143
  112.4 5.7 %collective-permute-start.21 = (f32[8,4096]{1,0:T(8,128)}, f32[8,4096]{1,0:T(8,128)}, u32[]{:S(2)}, u32[]{:S(2)}) collective-permute-start(f32[8,4096]{1,0:T(8,128)} %get-tuple-element.13), channel_id=1, source_target_pairs={{10,0},{12,2},{14,4},{16,6},{18,8},{20,10},{22,12},{24,14},{26,16}... | collective-permute-start | bytes 393224 | tf_op jit(solution)/shard_map/ppermute | solution.py:33
  118.1 14.5 %collective-permute-start.20 = (f32[8,4096]{1,0:T(8,128)}, f32[8,4096]{1,0:T(8,128)}, u32[]{:S(2)}, u32[]{:S(2)}) collective-permute-start(f32[8,4096]{1,0:T(8,128)} %get-tuple-element.12), channel_id=1, source_target_pairs={{8,0},{10,2},{12,4},{14,6},{16,8},{18,10},{20,12},{22,14},{24,16},... | collective-permute-start | bytes 393224 | tf_op jit(solution)/shard_map/ppermute | solution.py:33
  132.6 1.9 %collective-permute-start.19 = (f32[8,4096]{1,0:T(8,128)}, f32[8,4096]{1,0:T(8,128)}, u32[]{:S(2)}, u32[]{:S(2)}) collective-permute-start(f32[8,4096]{1,0:T(8,128)} %get-tuple-element.11), channel_id=1, source_target_pairs={{6,0},{8,2},{10,4},{12,6},{14,8},{16,10},{18,12},{20,14},{22,16},{... | collective-permute-start | bytes 393224 | tf_op jit(solution)/shard_map/ppermute | solution.py:33
  134.6 3.1 %collective-permute-start.18 = (f32[8,4096]{1,0:T(8,128)}, f32[8,4096]{1,0:T(8,128)}, u32[]{:S(2)}, u32[]{:S(2)}) collective-permute-start(f32[8,4096]{1,0:T(8,128)} %get-tuple-element.10), channel_id=1, source_target_pairs={{4,0},{6,2},{8,4},{10,6},{12,8},{14,10},{16,12},{18,14},{20,16},{2... | collective-permute-start | bytes 393224 | tf_op jit(solution)/shard_map/ppermute | solution.py:33
  137.7 2.6 %collective-permute-start.17 = (f32[8,4096]{1,0:T(8,128)S(1)}, f32[8,4096]{1,0:T(8,128)}, u32[]{:S(2)}, u32[]{:S(2)}) collective-permute-start(f32[8,4096]{1,0:T(8,128)S(1)} %copy-done.21), channel_id=1, source_target_pairs={{2,0},{4,2},{6,4},{8,6},{10,8},{12,10},{14,12},{16,14},{18,16},{20... | collective-permute-start | bytes 393224 | tf_op jit(solution)/shard_map/ppermute | solution.py:33
  144.6 2.1 %collective-permute-start.16 = (bf16[64,4096]{1,0:T(8,128)(2,1)}, bf16[64,4096]{1,0:T(8,128)(2,1)}, u32[]{:S(2)}, u32[]{:S(2)}) collective-permute-start(bf16[64,4096]{1,0:T(8,128)(2,1)} %pad_maximum_fusion.1), channel_id=1, source_target_pairs={{0,1},{1,0},{2,3},{3,2},{4,5},{5,4},{6,7},{7,6},{8,9},{9,8},{10,11... | collective-permute-start | bytes 1572872 | tf_op jit(solution)/shard_map/ppermute | solution.py:38
  146.7 1.7 %add_add_fusion = f32[8,4096]{1,0:T(8,128)S(1)} fusion(f32[8,4096]{1,0:T(8,128)} %copy-done.22, f32[8,4096]{1,0:T(8,128)} %copy-done.23, f32[8,4096]{1,0:T(8,128)} %copy-done.24, f32[8,4096]{1,0:T(8,128)} %copy-done.25, f32[8,4096]{1,0:T(8,128)} %copy-done.26, f32[8,4096]{1,0:T(8,128)} %collective-permute-done.26, f32[8,4096]{1,0:T(8,128)} %collective-permute-done.25, ...), kind=kLoop, calls=%fused_computation.107 | loop fusion | flops 524288 | bytes 4194304 | tf_op jit(solution)/shard_map/add | solution.py:33
  (195 shorter events, 79.6 us)
Async XLA Ops:
  8.8 12.3 %collective-permute-start.1 = (bf16[8,4096]{1,0:T(8,128)(2,1)S(1)}, bf16[8,4096]{1,0:T(8,128)(2,1)}, u32[]{:S(2)}, u32[]{:S(2)}) collective-permute-start(bf16[8,4096]{1,0:T(8,128)(2,1)S(1)} %pad_maximum_fusion.4), channel_id=1, source_target_pairs={{0,2},{2,4},{4,6},{6,8},{8,10},{10,12},{12,14},{14,16},{16,18},{18... | collective-permute-start | bytes 196616 | tf_op jit(solution)/shard_map/ppermute | solution.py:25
  10.1 13.1 %collective-permute-start.2 = (bf16[8,4096]{1,0:T(8,128)(2,1)S(1)}, bf16[8,4096]{1,0:T(8,128)(2,1)}, u32[]{:S(2)}, u32[]{:S(2)}) collective-permute-start(bf16[8,4096]{1,0:T(8,128)(2,1)S(1)} %pad_maximum_fusion.4), channel_id=1, source_target_pairs={{0,4},{2,6},{4,8},{6,10},{8,12},{10,14},{12,16},{14,18},{16,20},{1... | collective-permute-start | bytes 196616 | tf_op jit(solution)/shard_map/ppermute | solution.py:25
  11.4 14.0 %collective-permute-start.3 = (bf16[8,4096]{1,0:T(8,128)(2,1)S(1)}, bf16[8,4096]{1,0:T(8,128)(2,1)}, u32[]{:S(2)}, u32[]{:S(2)}) collective-permute-start(bf16[8,4096]{1,0:T(8,128)(2,1)S(1)} %pad_maximum_fusion.4), channel_id=1, source_target_pairs={{0,6},{2,8},{4,10},{6,12},{8,14},{10,16},{12,18},{14,20},{16,22},{... | collective-permute-start | bytes 196616 | tf_op jit(solution)/shard_map/ppermute | solution.py:25
  12.7 14.8 %collective-permute-start.4 = (bf16[8,4096]{1,0:T(8,128)(2,1)S(1)}, bf16[8,4096]{1,0:T(8,128)(2,1)}, u32[]{:S(2)}, u32[]{:S(2)}) collective-permute-start(bf16[8,4096]{1,0:T(8,128)(2,1)S(1)} %pad_maximum_fusion.4), channel_id=1, source_target_pairs={{0,8},{2,10},{4,12},{6,14},{8,16},{10,18},{12,20},{14,22},{16,24},... | collective-permute-start | bytes 196616 | tf_op jit(solution)/shard_map/ppermute | solution.py:25
  14.0 15.6 %collective-permute-start.5 = (bf16[8,4096]{1,0:T(8,128)(2,1)S(1)}, bf16[8,4096]{1,0:T(8,128)(2,1)S(1)}, u32[]{:S(2)}, u32[]{:S(2)}) collective-permute-start(bf16[8,4096]{1,0:T(8,128)(2,1)S(1)} %pad_maximum_fusion.4), channel_id=1, source_target_pairs={{0,10},{2,12},{4,14},{6,16},{8,18},{10,20},{12,22},{14,24},{16,26}... | collective-permute-start | bytes 196616 | tf_op jit(solution)/shard_map/ppermute | solution.py:25
  21.1 10.5 %collective-permute-start.6 = (bf16[8,4096]{1,0:T(8,128)(2,1)S(1)}, bf16[8,4096]{1,0:T(8,128)(2,1)S(1)}, u32[]{:S(2)}, u32[]{:S(2)}) collective-permute-start(bf16[8,4096]{1,0:T(8,128)(2,1)S(1)} %pad_maximum_fusion.4), channel_id=1, source_target_pairs={{0,12},{2,14},{4,16},{6,18},{8,20},{10,22},{12,24},{14,26},{16,28}... | collective-permute-start | bytes 196616 | tf_op jit(solution)/shard_map/ppermute | solution.py:25
  23.2 12.0 %collective-permute-start.7 = (bf16[8,4096]{1,0:T(8,128)(2,1)S(1)}, bf16[8,4096]{1,0:T(8,128)(2,1)S(1)}, u32[]{:S(2)}, u32[]{:S(2)}) collective-permute-start(bf16[8,4096]{1,0:T(8,128)(2,1)S(1)} %pad_maximum_fusion.4), channel_id=1, source_target_pairs={{0,14},{2,16},{4,18},{6,20},{8,22},{10,24},{12,26},{14,28},{16,30}... | collective-permute-start | bytes 196616 | tf_op jit(solution)/shard_map/ppermute | solution.py:25
  25.4 13.8 %collective-permute-start.8 = (bf16[8,4096]{1,0:T(8,128)(2,1)S(1)}, bf16[8,4096]{1,0:T(8,128)(2,1)S(1)}, u32[]{:S(2)}, u32[]{:S(2)}) collective-permute-start(bf16[8,4096]{1,0:T(8,128)(2,1)S(1)} %pad_maximum_fusion.4), channel_id=1, source_target_pairs={{0,16},{2,18},{4,20},{6,22},{8,24},{10,26},{12,28},{14,30},{1,17},... | collective-permute-start | bytes 196616 | tf_op jit(solution)/shard_map/ppermute | solution.py:25
  27.5 16.7 %collective-permute-start.9 = (bf16[8,4096]{1,0:T(8,128)(2,1)S(1)}, bf16[8,4096]{1,0:T(8,128)(2,1)S(1)}, u32[]{:S(2)}, u32[]{:S(2)}) collective-permute-start(bf16[8,4096]{1,0:T(8,128)(2,1)S(1)} %pad_maximum_fusion.4), channel_id=1, source_target_pairs={{0,18},{2,20},{4,22},{6,24},{8,26},{10,28},{12,30},{1,19},{3,21},{... | collective-permute-start | bytes 196616 | tf_op jit(solution)/shard_map/ppermute | solution.py:25
  29.6 19.9 %collective-permute-start.10 = (bf16[8,4096]{1,0:T(8,128)(2,1)S(1)}, bf16[8,4096]{1,0:T(8,128)(2,1)S(1)}, u32[]{:S(2)}, u32[]{:S(2)}) collective-permute-start(bf16[8,4096]{1,0:T(8,128)(2,1)S(1)} %pad_maximum_fusion.4), channel_id=1, source_target_pairs={{0,20},{2,22},{4,24},{6,26},{8,28},{10,30},{1,21},{3,23},{5,25},{7... | collective-permute-start | bytes 196616 | tf_op jit(solution)/shard_map/ppermute | solution.py:25
  31.6 21.0 %collective-permute-start.11 = (bf16[8,4096]{1,0:T(8,128)(2,1)S(1)}, bf16[8,4096]{1,0:T(8,128)(2,1)S(1)}, u32[]{:S(2)}, u32[]{:S(2)}) collective-permute-start(bf16[8,4096]{1,0:T(8,128)(2,1)S(1)} %pad_maximum_fusion.4), channel_id=1, source_target_pairs={{0,22},{2,24},{4,26},{6,28},{8,30},{1,23},{3,25},{5,27},{7,29},{9,... | collective-permute-start | bytes 196616 | tf_op jit(solution)/shard_map/ppermute | solution.py:25
  35.2 17.4 %collective-permute-start.12 = (bf16[8,4096]{1,0:T(8,128)(2,1)S(1)}, bf16[8,4096]{1,0:T(8,128)(2,1)S(1)}, u32[]{:S(2)}, u32[]{:S(2)}) collective-permute-start(bf16[8,4096]{1,0:T(8,128)(2,1)S(1)} %pad_maximum_fusion.4), channel_id=1, source_target_pairs={{0,24},{2,26},{4,28},{6,30},{1,25},{3,27},{5,29},{7,31}} | collective-permute-start | bytes 196616 | tf_op jit(solution)/shard_map/ppermute | solution.py:25
  39.2 13.5 %collective-permute-start.13 = (bf16[8,4096]{1,0:T(8,128)(2,1)S(1)}, bf16[8,4096]{1,0:T(8,128)(2,1)S(1)}, u32[]{:S(2)}, u32[]{:S(2)}) collective-permute-start(bf16[8,4096]{1,0:T(8,128)(2,1)S(1)} %pad_maximum_fusion.4), channel_id=1, source_target_pairs={{0,26},{2,28},{4,30},{1,27},{3,29},{5,31}} | collective-permute-start | bytes 196616 | tf_op jit(solution)/shard_map/ppermute | solution.py:25
  89.4 10.2 %collective-permute-start.28 = (f32[8,4096]{1,0:T(8,128)}, f32[8,4096]{1,0:T(8,128)S(1)}, u32[]{:S(2)}, u32[]{:S(2)}) collective-permute-start(f32[8,4096]{1,0:T(8,128)} %get-tuple-element.20), channel_id=1, source_target_pairs={{24,0},{26,2},{28,4},{30,6},{25,1},{27,3},{29,5},{31,7}} | collective-permute-start | bytes 393224 | tf_op jit(solution)/shard_map/ppermute | solution.py:33
  90.7 12.7 %collective-permute-start.27 = (f32[8,4096]{1,0:T(8,128)}, f32[8,4096]{1,0:T(8,128)S(1)}, u32[]{:S(2)}, u32[]{:S(2)}) collective-permute-start(f32[8,4096]{1,0:T(8,128)} %get-tuple-element.19), channel_id=1, source_target_pairs={{22,0},{24,2},{26,4},{28,6},{30,8},{23,1},{25,3},{27,5},{29,7},{31... | collective-permute-start | bytes 393224 | tf_op jit(solution)/shard_map/ppermute | solution.py:33
  93.8 18.6 %collective-permute-start.26 = (f32[8,4096]{1,0:T(8,128)}, f32[8,4096]{1,0:T(8,128)}, u32[]{:S(2)}, u32[]{:S(2)}) collective-permute-start(f32[8,4096]{1,0:T(8,128)} %get-tuple-element.18), channel_id=1, source_target_pairs={{20,0},{22,2},{24,4},{26,6},{28,8},{30,10},{21,1},{23,3},{25,5},{2... | collective-permute-start | bytes 393224 | tf_op jit(solution)/shard_map/ppermute | solution.py:33
  95.7 22.4 %collective-permute-start.25 = (f32[8,4096]{1,0:T(8,128)}, f32[8,4096]{1,0:T(8,128)}, u32[]{:S(2)}, u32[]{:S(2)}) collective-permute-start(f32[8,4096]{1,0:T(8,128)} %get-tuple-element.17), channel_id=1, source_target_pairs={{18,0},{20,2},{22,4},{24,6},{26,8},{28,10},{30,12},{19,1},{21,3},{... | collective-permute-start | bytes 393224 | tf_op jit(solution)/shard_map/ppermute | solution.py:33
  97.7 34.9 %collective-permute-start.24 = (f32[8,4096]{1,0:T(8,128)}, f32[8,4096]{1,0:T(8,128)}, u32[]{:S(2)}, u32[]{:S(2)}) collective-permute-start(f32[8,4096]{1,0:T(8,128)} %get-tuple-element.16), channel_id=1, source_target_pairs={{16,0},{18,2},{20,4},{22,6},{24,8},{26,10},{28,12},{30,14},{17,1},... | collective-permute-start | bytes 393224 | tf_op jit(solution)/shard_map/ppermute | solution.py:33
  99.6 35.0 %collective-permute-start.23 = (f32[8,4096]{1,0:T(8,128)}, f32[8,4096]{1,0:T(8,128)}, u32[]{:S(2)}, u32[]{:S(2)}) collective-permute-start(f32[8,4096]{1,0:T(8,128)} %get-tuple-element.15), channel_id=1, source_target_pairs={{14,0},{16,2},{18,4},{20,6},{22,8},{24,10},{26,12},{28,14},{30,16}... | collective-permute-start | bytes 393224 | tf_op jit(solution)/shard_map/ppermute | solution.py:33
  103.4 34.2 %collective-permute-start.22 = (f32[8,4096]{1,0:T(8,128)}, f32[8,4096]{1,0:T(8,128)}, u32[]{:S(2)}, u32[]{:S(2)}) collective-permute-start(f32[8,4096]{1,0:T(8,128)} %get-tuple-element.14), channel_id=1, source_target_pairs={{12,0},{14,2},{16,4},{18,6},{20,8},{22,10},{24,12},{26,14},{28,16}... | collective-permute-start | bytes 393224 | tf_op jit(solution)/shard_map/ppermute | solution.py:33
  112.4 32.2 %collective-permute-start.21 = (f32[8,4096]{1,0:T(8,128)}, f32[8,4096]{1,0:T(8,128)}, u32[]{:S(2)}, u32[]{:S(2)}) collective-permute-start(f32[8,4096]{1,0:T(8,128)} %get-tuple-element.13), channel_id=1, source_target_pairs={{10,0},{12,2},{14,4},{16,6},{18,8},{20,10},{22,12},{24,14},{26,16}... | collective-permute-start | bytes 393224 | tf_op jit(solution)/shard_map/ppermute | solution.py:33
  118.1 28.5 %collective-permute-start.20 = (f32[8,4096]{1,0:T(8,128)}, f32[8,4096]{1,0:T(8,128)}, u32[]{:S(2)}, u32[]{:S(2)}) collective-permute-start(f32[8,4096]{1,0:T(8,128)} %get-tuple-element.12), channel_id=1, source_target_pairs={{8,0},{10,2},{12,4},{14,6},{16,8},{18,10},{20,12},{22,14},{24,16},... | collective-permute-start | bytes 393224 | tf_op jit(solution)/shard_map/ppermute | solution.py:33
  132.6 14.1 %collective-permute-start.19 = (f32[8,4096]{1,0:T(8,128)}, f32[8,4096]{1,0:T(8,128)}, u32[]{:S(2)}, u32[]{:S(2)}) collective-permute-start(f32[8,4096]{1,0:T(8,128)} %get-tuple-element.11), channel_id=1, source_target_pairs={{6,0},{8,2},{10,4},{12,6},{14,8},{16,10},{18,12},{20,14},{22,16},{... | collective-permute-start | bytes 393224 | tf_op jit(solution)/shard_map/ppermute | solution.py:33
  134.6 12.1 %collective-permute-start.18 = (f32[8,4096]{1,0:T(8,128)}, f32[8,4096]{1,0:T(8,128)}, u32[]{:S(2)}, u32[]{:S(2)}) collective-permute-start(f32[8,4096]{1,0:T(8,128)} %get-tuple-element.10), channel_id=1, source_target_pairs={{4,0},{6,2},{8,4},{10,6},{12,8},{14,10},{16,12},{18,14},{20,16},{2... | collective-permute-start | bytes 393224 | tf_op jit(solution)/shard_map/ppermute | solution.py:33
  (38 other events, 360.1 us)

commit v4 on v2

--- a/solution.py
+++ b/solution.py
@@ -25,32 +25,58 @@
     return bits
 
 
-def exchange(x, mask):
-    size = group_size()
-    return lax.ppermute(x, GROUP, [(i, i ^ mask) for i in range(size)])
+def physical_bit(core, bit):
+    if core == 1 and group_bits() >= 2 and bit < 2:
+        return 1 - bit
+    return bit
 
 
-def gather_blocks(x):
-    me = lax.axis_index("seq") * lax.axis_size("hx") + lax.axis_index("hx")
+def exchange(x, bit):
+    size = group_size()
+    pairs = [
+        (g * 2 + c, (g ^ (1 << physical_bit(c, bit))) * 2 + c) for g in range(size) for c in range(2)
+    ]
+    return lax.ppermute(x, ("seq", "hx", "hc"), pairs)
+
+
+def swap_low_bits(x, core):
+    if group_bits() < 2:
+        return x
+    size = x.shape[0]
+    swapped = jnp.swapaxes(x.reshape((size // 4, 2, 2) + x.shape[1:]), 1, 2).reshape(x.shape)
+    return jnp.where(core == 1, swapped, x)
+
+
+def virtual_index(core):
+    g = lax.axis_index("seq") * lax.axis_size("hx") + lax.axis_index("hx")
+    if group_bits() < 2:
+        return g
+    swapped = (g & ~3) | ((g & 1) << 1) | ((g >> 1) & 1)
+    return jnp.where(core == 1, swapped, g)
+
+
+def gather_blocks(x, core):
+    me = virtual_index(core)
     held = x[None]
     for bit in reversed(range(group_bits())):
-        got = exchange(held, 1 << bit)
+        got = exchange(held, bit)
         low = ((me >> bit) & 1) == 0
         held = jnp.where(low, jnp.stack([held, got], 1), jnp.stack([got, held], 1))
         held = held.reshape((-1,) + x.shape)
+    held = swap_low_bits(held, core)
     return held.reshape((-1,) + x.shape[1:])
 
 
-def reduce_blocks(x):
-    me = lax.axis_index("seq") * lax.axis_size("hx") + lax.axis_index("hx")
+def reduce_blocks(x, core):
+    me = virtual_index(core)
     size = group_size()
-    held = x.reshape((size, -1) + x.shape[1:])
+    held = swap_low_bits(x.reshape((size, -1) + x.shape[1:]), core)
     for bit in range(group_bits()):
         pairs = held.reshape((held.shape[0] // 2, 2) + held.shape[1:])
         mine = (me >> bit) & 1
         keep = jnp.where(mine == 0, pairs[:, 0], pairs[:, 1])
         send = jnp.where(mine == 0, pairs[:, 1], pairs[:, 0])
-        held = keep + exchange(send, 1 << bit)
+        held = keep + exchange(send.astype(jnp.bfloat16), bit).astype(jnp.float32)
     return held.reshape(x.shape[0] // size, *x.shape[1:])
 
 
@@ -101,7 +127,7 @@
     positions = (jnp.arange(nb, dtype=jnp.int32)[:, None] * BLOCK + cols).reshape(-1)
 
     own_sum = jnp.concatenate([jnp.take(kb, positions, axis=0), jnp.take(vb, positions, axis=0)], axis=1)
-    all_sum = gather_blocks(own_sum)
+    all_sum = gather_blocks(own_sum, core)
     sum_count = all_sum.shape[0]
     sk = all_sum[:, :half].reshape(sum_count, heads, HEAD_DIM)
     sv = all_sum[:, half:].reshape(sum_count, heads, HEAD_DIM)
@@ -153,7 +179,7 @@
     )
 
     parts = jnp.concatenate([dks.reshape(sum_count, half), dvs.reshape(sum_count, half)], axis=1)
-    own_grad = reduce_blocks(parts)
+    own_grad = reduce_blocks(parts, core)
     dk = dkw.reshape(rows, half).at[positions].add(own_grad[:, :half])
     dv = dvw.reshape(rows, half).at[positions].add(own_grad[:, half:])
     dk_tok, dv_tok = to_token_layout([dk.astype(jnp.bfloat16), dv.astype(jnp.bfloat16)], core)

time: 130 us -> 102 us (0.78)
  waiting for transfers between devices: 38.1 us -> 16.4 us
  starting transfers between devices: 27.6 us -> 17.1 us
  other arithmetic: 18.2 us -> 19.8 us
  matrix products: 10.2 us -> 11.6 us
    ppermute x8, waiting for transfers between devices: 37.8 us -> 16.4 us  [exchange(): return lax.ppermute(x, ('seq', 'hx', 'hc'), pairs)]
    ppermute x8, starting transfers between devices: 21.4 us -> 11 us  [exchange(): return lax.ppermute(x, ('seq', 'hx', 'hc'), pairs)]
    select_n x4 -> x2, other arithmetic: 2.68 us -> 0.47 us  [swap_low_bits(): return jnp.where(core == 1, swapped, x)]
    transpose x1, local copies, waits for them, and re-layouts: 2.6 us -> 0.51 us  [body(): dvs = jnp.einsum('bhqk,bqhd->khd', ps_low, g, preferred_element_type=f32)]
    unnamed x68 -> x73, local copies, waits for them, and re-layouts: 11.9 us -> 13.9 us
    convert_element_type x0 -> x4, other arithmetic: none -> 1.63 us  [reduce_blocks(): held = keep + exchange(send.astype(jnp.bfloat16), bit).astype(jnp.float32)]
    transpose x0 -> x2, other arithmetic: none -> 1.57 us  [swap_low_bits(): jnp.swapaxes(x.reshape((size // 4, 2, 2) + x.shape[1:]), 1, 2)]
    reshape x1, local copies, waits for them, and re-layouts: 0.33 us -> 1.67 us  [body(): dv = dvw.reshape(rows, half).at[positions].add(own_grad[:, half:])]
  transfers between devices with their start and end apart: 11 -> 11, of which waited for: 8 -> 5; matrix products, arithmetic and copies ran while one was open for 20% -> 33% of each run, Pallas kernels for 0% -> 0%
where the time goes in v4:
time: 102 us; the launch traced here: 100 us
  local copies, waits for them, and re-layouts  34.3 us (34%)
  other arithmetic  19.8 us (19%)
  starting transfers between devices  17.1 us (17%)
  waiting for transfers between devices  16.4 us (16%)
  matrix products  11.6 us (11%)
  between operations  1.34 us (1%)
    ppermute x8, waiting for transfers between devices, exchange(): return lax.ppermute(x, ('seq', 'hx', 'hc'), pairs)  16.4 us
    unnamed x73, local copies, waits for them, and re-layouts  13.9 us
    ppermute x8, starting transfers between devices, exchange(): return lax.ppermute(x, ('seq', 'hx', 'hc'), pairs)  11 us
    ppermute x3, starting transfers between devices, swap_with_partner(): return lax.ppermute(x, 'hc', [(0, 1), (1, 0)])  6.09 us
    concatenate x4, local copies, waits for them, and re-layouts, body(): jnp.concatenate([dks.reshape(sum_count, half), dvs.reshape(sum_count, hal...  4.58 us
    select_n x4, other arithmetic, to_token_layout(): jnp.where(core == 0, jnp.concatenate([m, r], 1), jnp.concatenate([r, m], 1))  3.66 us
    dynamic_slice x4, local copies, waits for them, and re-layouts, to_token_layout(): mine = [lax.dynamic_slice_in_dim(a, core * rows, rows, 0) for a in arrays]  2.74 us
    add x2, other arithmetic, reduce_blocks(): held = keep + exchange(send.astype(jnp.bfloat16), bit).astype(jnp.float32)  2.25 us
  transfers between devices with their start and end apart: 11, of which 5 were waited for; matrix products, arithmetic and copies ran while one was open for 33% of the time, Pallas kernels for 0%

profile of v4, /device:TPU:1, one launch (start us, length us, event | category | flops | bytes accessed | tf_op | source)
XLA Modules:
  0.0 100.4 jit_solution(5644219701212025504)
XLA Ops:
  0.7 1.3 %dynamic-slice_bitcast_fusion = (bf16[8,8,16,128]{3,1,2,0:T(8,128)(2,1)S(1)}, bf16[64,2048]{1,0:T(8,128)(2,1)S(1)}, bf16[64,2048]{1,0:T(8,128)(2,1)S(1)}, bf16[8,8,16,128]{3,1,2,0:T(8,128)(2,1)S(1)}) fusion(bf16[64,4096]{1,0:T(8,128)(2,1)} %param.10, s32[]{:T(128)S(6)} %select_n.345, s32[]{:T(128)S(6)} %select_n.346, bf16[64,4096]{1,0:T(8,128)(2,1)} %param.7), kind=kLoop, calls=%fused_computation.81 | loop fusion | bytes 2097160
  7.7 3.8 %collective-permute-start.1 = (bf16[1,8,4096]{2,1,0:T(8,128)(2,1)S(1)}, bf16[1,8,4096]{2,1,0:T(8,128)(2,1)}, u32[]{:S(2)}, u32[]{:S(2)}) collective-permute-start(bf16[1,8,4096]{2,1,0:T(8,128)(2,1)S(1)} %get-tuple-element.38), channel_id=1, source_target_pairs={{0,16},{1,17},{2,18},{3,19},{4,20},{5,21},{6,22},{7,23},{8,24},{9,... | collective-permute-start | bytes 196616 | tf_op jit(solution)/shard_map/ppermute | solution.py:39
  13.0 1.4 %copy.161 = f32[16,128,128]{1,2,0:T(8,128)} copy(f32[16,128,128]{2,0,1:T(8,128)S(1)} %get-tuple-element.5) | data formatting | bytes 2097152
  18.4 2.4 %collective-permute-done.2 = bf16[2,8,4096]{2,1,0:T(8,128)(2,1)S(1)} collective-permute-done((bf16[2,8,4096]{2,1,0:T(8,128)(2,1)S(1)}, bf16[2,8,4096]{2,1,0:T(8,128)(2,1)S(1)}, u32[]{:S(2)}, u32[]{:S(2)}) %collective-permute-start.2) | collective-permute-done | bytes 131104 | tf_op jit(solution)/shard_map/ppermute | solution.py:39
  21.8 4.7 %collective-permute-done.3 = bf16[4,8,4096]{2,1,0:T(8,128)(2,1)S(1)} collective-permute-done((bf16[4,8,4096]{2,1,0:T(8,128)(2,1)S(1)}, bf16[4,8,4096]{2,1,0:T(8,128)(2,1)S(1)}, u32[]{:S(2)}, u32[]{:S(2)}) %collective-permute-start.3) | collective-permute-done | bytes 262176 | tf_op jit(solution)/shard_map/ppermute | solution.py:39
  28.1 6.9 %collective-permute-done.4 = bf16[8,8,4096]{2,1,0:T(8,128)(2,1)S(1)} collective-permute-done((bf16[8,8,4096]{2,1,0:T(8,128)(2,1)S(1)}, bf16[8,8,4096]{2,1,0:T(8,128)(2,1)S(1)}, u32[]{:S(2)}, u32[]{:S(2)}) %collective-permute-start.4) | collective-permute-done | bytes 524320 | tf_op jit(solution)/shard_map/ppermute | solution.py:39
  43.9 1.5 %convolution_bitcast_fusion.1 = f32[128,16,128]{0,2,1:T(8,128)} fusion(bf16[128,16,128]{0,2,1:T(8,128)(2,1)S(1)} %copy.137, f32[1,16,128,128]{3,2,1,0:T(8,128)S(1)} %get-tuple-element.44, f32[16,128]{1,0:T(8,128)S(1)} %log_add_fusion, pred[128]{0:T(512)(128)(4,1)S(1)} %copy-done.27), kind=kOutput, calls=%fused_computation.11 | convolution fusion | flops 67895296 | bytes 2629760 | tf_op jit(solution)/shard_map/bhqk,bqhd->khd/dot_general | solution.py:175
  45.4 1.5 %convolution_bitcast_fusion.2 = f32[1,128,16,128]{1,3,2,0:T(8,128)} fusion(bf16[128,16,128]{0,2,1:T(8,128)(2,1)S(1)} %bitcast.219, bf16[16,128,128]{2,1,0:T(8,128)(2,1)S(1)} %fusion.17), kind=kOutput, calls=%fused_computation.16 | convolution fusion | flops 67108864 | bytes 2097152 | tf_op jit(solution)/shard_map/bhqk,khd->bqhd/dot_general | solution.py:170
  46.8 1.5 %fusion.2 = f32[128,16,128]{2,0,1:T(8,128)} fusion(bf16[128,16,128]{0,2,1:T(8,128)(2,1)S(1)} %copy.130, bf16[16,128,128]{2,1,0:T(8,128)(2,1)S(1)} %fusion.17), kind=kOutput, calls=%fused_computation.13 | convolution fusion | flops 67371008 | bytes 2097152 | tf_op jit(solution)/shard_map/bhqk,bqhd->khd/dot_general | solution.py:174
  54.1 1.4 %maximum_bitcast_fusion = f32[4,2,2,8,4096]{4,3,1,2,0:T(8,128)S(1)} fusion(f32[4,2,2,8,2048]{4,3,2,1,0:T(8,128)S(1)} %copy-done.15, f32[4,2,2,8,2048]{4,3,2,1,0:T(8,128)} %concatenate.189), kind=kLoop, calls=%fused_computation.4 | loop fusion | flops 524288 | bytes 4194304 | tf_op jit(solution)/shard_map/transpose | solution.py:46
  59.1 1.3 %constant_dynamic-slice_fusion.4 = (bf16[64,2048]{0,1:T(8,128)(2,1)}, bf16[64,2048]{0,1:T(8,128)(2,1)}) fusion(bf16[128,2048]{0,1:T(8,128)(2,1)S(1)} %bitcast.220, s32[]{:T(128)S(6)} %select_n.384, s32[]{:T(128)S(6)} %select_n.385), kind=kLoop, calls=%fused_computation.106 | loop fusion | bytes 1048584 | tf_op jit(solution)/shard_map/dynamic_slice | solution.py:103
  60.4 1.3 %constant_dynamic-slice_fusion.7 = (bf16[64,2048]{0,1:T(8,128)(2,1)}, bf16[64,2048]{0,1:T(8,128)(2,1)}) fusion(bf16[128,2048]{0,1:T(8,128)(2,1)S(1)} %bitcast.223, s32[]{:T(128)S(6)} %select_n.384, s32[]{:T(128)S(6)} %select_n.385), kind=kLoop, calls=%fused_computation.109 | loop fusion | bytes 1048584 | tf_op jit(solution)/shard_map/dynamic_slice | solution.py:103
  63.0 1.9 %copy.170 = bf16[64,2048]{1,0:T(8,128)(2,1)} copy(bf16[64,2048]{0,1:T(8,128)(2,1)} %get-tuple-element.28) | data formatting | bytes 524288
  64.9 1.8 %pad_maximum_fusion.1 = bf16[64,4096]{1,0:T(8,128)(2,1)} fusion(bf16[64,2048]{1,0:T(8,128)(2,1)S(1)} %copy.171, bf16[64,2048]{1,0:T(8,128)(2,1)} %copy.170), kind=kLoop, calls=%fused_computation.61 | loop fusion | flops 1048576 | bytes 1048576 | tf_op jit(solution)/shard_map/concatenate | solution.py:105
  66.7 3.8 %collective-permute-start.5 = (bf16[64,4096]{1,0:T(8,128)(2,1)}, bf16[64,4096]{1,0:T(8,128)(2,1)}, u32[]{:S(2)}, u32[]{:S(2)}) collective-permute-start(bf16[64,4096]{1,0:T(8,128)(2,1)} %pad_maximum_fusion.1), channel_id=1, source_target_pairs={{0,1},{1,0},{2,3},{3,2},{4,5},{5,4},{6,7},{7,6},{8,9},{9,8},{10,11... | collective-permute-start | bytes 1572872 | tf_op jit(solution)/shard_map/ppermute | solution.py:84
  70.5 1.9 %copy.169 = bf16[64,2048]{1,0:T(8,128)(2,1)} copy(bf16[64,2048]{0,1:T(8,128)(2,1)} %get-tuple-element.27) | data formatting | bytes 524288
  75.6 1.5 %fusion.38 = f32[16,128,128]{2,1,0:T(8,128)} fusion(bf16[128,16,128]{0,2,1:T(8,128)(2,1)S(1)} %copy-done.3, f32[16,128,128]{1,2,0:T(8,128)S(1)} %get-tuple-element.42, f32[16,128]{1,0:T(8,128)S(1)} %log_add_fusion, pred[128,128]{0,1:T(8,128)(4,1)S(1)} %iota_compare_fusion), kind=kOutput, calls=%fused_computation.96 | convolution fusion | flops 67895296 | bytes 2646016 | tf_op jit(solution)/shard_map/bhqk,bqhd->bkhd/dot_general | solution.py:173
  77.0 1.7 %copy.151 = f32[128,2048]{1,0:T(8,128)S(1)} copy(f32[128,2048]{0,1:T(8,128)} %bitcast.224) | data formatting | bytes 2097152 | tf_op jit(solution)/shard_map/reshape | solution.py:184
  78.7 2.0 %collective-permute-done.7 = bf16[4,8,4096]{2,1,0:T(8,128)(2,1)} collective-permute-done((bf16[4,8,4096]{2,1,0:T(8,128)(2,1)S(1)}, bf16[4,8,4096]{2,1,0:T(8,128)(2,1)}, u32[]{:S(2)}, u32[]{:S(2)}) %collective-permute-start.7) | collective-permute-done | bytes 262176 | tf_op jit(solution)/shard_map/ppermute | solution.py:39
  84.2 1.3 %copy.133 = f32[1,128,16,128]{1,3,2,0:T(8,128)} copy(f32[1,128,16,128]{3,1,2,0:T(8,128)S(1)} %fusion.3) | data formatting | bytes 2097152 | tf_op jit(solution)/shard_map/mul | solution.py:172
  85.5 1.6 %copy.148 = f32[128,2048]{1,0:T(8,128)S(1)} copy(f32[128,2048]{0,1:T(8,128)} %bitcast.225) | data formatting | bytes 2097152 | tf_op jit(solution)/shard_map/reshape | solution.py:183
  87.2 2.7 %collective-permute-start.9 = (bf16[1,8,4096]{2,1,0:T(8,128)(2,1)S(1)}, bf16[1,8,4096]{2,1,0:T(8,128)(2,1)S(1)}, u32[]{:S(2)}, u32[]{:S(2)}) collective-permute-start(bf16[1,8,4096]{2,1,0:T(8,128)(2,1)S(1)} %fusion.33), channel_id=1, source_target_pairs={{0,16},{1,17},{2,18},{3,19},{4,20},{5,21},{6,22},{7,23},{8,24},{9,... | collective-permute-start | bytes 196616 | tf_op jit(solution)/shard_map/ppermute | solution.py:39
  89.9 1.9 %fusion.51 = (bf16[64,2048]{1,0:T(8,128)(2,1)}, bf16[64,2048]{1,0:T(8,128)(2,1)}) fusion(bf16[64,4096]{1,0:T(8,128)(2,1)} %collective-permute-done.5), kind=kLoop, calls=%fused_computation.135 | loop fusion | bytes 1048576 | tf_op jit(solution)/shard_map/slice | solution.py:108
  94.6 2.1 %collective-permute-start.10 = (bf16[64,4096]{1,0:T(8,128)(2,1)S(1)}, bf16[64,4096]{1,0:T(8,128)(2,1)S(1)}, u32[]{:S(2)}, u32[]{:S(2)}) collective-permute-start(bf16[64,4096]{1,0:T(8,128)(2,1)S(1)} %pad_maximum_fusion.2), channel_id=1, source_target_pairs={{0,1},{1,0},{2,3},{3,2},{4,5},{5,4},{6,7},{7,6},{8,9},{9,8},{10,11... | collective-permute-start | bytes 1572872 | tf_op jit(solution)/shard_map/ppermute | solution.py:84
  (158 shorter events, 45.8 us)
Async XLA Ops:
  2.3 3.1 %copy-start.28 = (s32[2,8]{1,0:T(2,128)S(1)}, s32[2,8]{1,0:T(2,128)}, u32[]{:S(2)}) copy-start(s32[2,8]{1,0:T(2,128)} %param.11) | copy-start | bytes 196
  2.3 3.6 %collective-permute-start = (bf16[64,8192]{1,0:T(8,128)(2,1)S(1)}, bf16[64,8192]{1,0:T(8,128)(2,1)S(1)}, u32[]{:S(2)}, u32[]{:S(2)}) collective-permute-start(bf16[64,8192]{1,0:T(8,128)(2,1)S(1)} %pad_maximum_fusion), channel_id=1, source_target_pairs={{0,1},{1,0},{2,3},{3,2},{4,5},{5,4},{6,7},{7,6},{8,9},{9,8},{10,11... | collective-permute-start | bytes 3145736 | tf_op jit(solution)/shard_map/ppermute | solution.py:84
  7.7 7.7 %collective-permute-start.1 = (bf16[1,8,4096]{2,1,0:T(8,128)(2,1)S(1)}, bf16[1,8,4096]{2,1,0:T(8,128)(2,1)}, u32[]{:S(2)}, u32[]{:S(2)}) collective-permute-start(bf16[1,8,4096]{2,1,0:T(8,128)(2,1)S(1)} %get-tuple-element.38), channel_id=1, source_target_pairs={{0,16},{1,17},{2,18},{3,19},{4,20},{5,21},{6,22},{7,23},{8,24},{9,... | collective-permute-start | bytes 196616 | tf_op jit(solution)/shard_map/ppermute | solution.py:39
  12.1 31.7 %copy-start.2 = (bf16[128,16,128]{0,2,1:T(8,128)(2,1)}, bf16[128,16,128]{0,2,1:T(8,128)(2,1)S(1)}, u32[]{:S(2)}) copy-start(bf16[128,16,128]{0,2,1:T(8,128)(2,1)S(1)} %copy.137) | copy-start | bytes 1572868
  13.0 33.8 %copy-start = (bf16[128,16,128]{0,2,1:T(8,128)(2,1)}, bf16[128,16,128]{0,2,1:T(8,128)(2,1)S(1)}, u32[]{:S(2)}) copy-start(bf16[128,16,128]{0,2,1:T(8,128)(2,1)S(1)} %copy.130) | copy-start | bytes 1572868
  15.0 6.7 %copy-start.6 = (bf16[128,16,128]{0,2,1:T(8,128)(2,1)}, bf16[128,16,128]{0,2,1:T(8,128)(2,1)S(1)}, u32[]{:S(2)}) copy-start(bf16[128,16,128]{0,2,1:T(8,128)(2,1)S(1)} %copy.123) | copy-start | bytes 1572868
  16.4 4.5 %collective-permute-start.2 = (bf16[2,8,4096]{2,1,0:T(8,128)(2,1)S(1)}, bf16[2,8,4096]{2,1,0:T(8,128)(2,1)S(1)}, u32[]{:S(2)}, u32[]{:S(2)}) collective-permute-start(bf16[2,8,4096]{2,1,0:T(8,128)(2,1)S(1)} %maximum_select_fusion.17), channel_id=1, source_target_pairs={{0,8},{1,9},{2,10},{3,11},{4,12},{5,13},{6,14},{7,15},{8,0},{9,1},... | collective-permute-start | bytes 393224 | tf_op jit(solution)/shard_map/ppermute | solution.py:39
  20.9 6.2 %copy-start.20 = (bf16[8,8,16,128]{3,2,1,0:T(8,128)(2,1)S(1)}, bf16[8,8,16,128]{3,2,1,0:T(8,128)(2,1)}, u32[]{:S(2)}) copy-start(bf16[8,8,16,128]{3,2,1,0:T(8,128)(2,1)} %copy.176) | copy-start | bytes 786436
  20.9 5.6 %collective-permute-start.3 = (bf16[4,8,4096]{2,1,0:T(8,128)(2,1)S(1)}, bf16[4,8,4096]{2,1,0:T(8,128)(2,1)S(1)}, u32[]{:S(2)}, u32[]{:S(2)}) collective-permute-start(bf16[4,8,4096]{2,1,0:T(8,128)(2,1)S(1)} %bitcast.228), channel_id=1, source_target_pairs={{0,4},{1,3},{2,6},{3,1},{4,0},{5,7},{6,2},{7,5},{8,12},{9,11},{10,... | collective-permute-start | bytes 786440 | tf_op jit(solution)/shard_map/ppermute | solution.py:39
  26.6 8.4 %collective-permute-start.4 = (bf16[8,8,4096]{2,1,0:T(8,128)(2,1)S(1)}, bf16[8,8,4096]{2,1,0:T(8,128)(2,1)S(1)}, u32[]{:S(2)}, u32[]{:S(2)}) collective-permute-start(bf16[8,8,4096]{2,1,0:T(8,128)(2,1)S(1)} %bitcast.235), channel_id=1, source_target_pairs={{0,2},{1,5},{2,0},{3,7},{4,6},{5,1},{6,4},{7,3},{8,10},{9,13},{10,... | collective-permute-start | bytes 1572872 | tf_op jit(solution)/shard_map/ppermute | solution.py:39
  35.8 2.5 %copy-start.27 = (pred[128]{0:T(512)(128)(4,1)S(1)}, pred[128]{0:T(512)(128)(4,1)}, u32[]{:S(2)}) copy-start(pred[128]{0:T(512)(128)(4,1)} %fusion.43) | copy-start | bytes 388
  51.7 2.3 %copy-start.15 = (f32[4,2,2,8,2048]{4,3,2,1,0:T(8,128)S(1)}, f32[4,2,2,8,2048]{4,3,2,1,0:T(8,128)}, u32[]{:S(2)}) copy-start(f32[4,2,2,8,2048]{4,3,2,1,0:T(8,128)} %concatenate.190) | copy-start | bytes 3145732
  58.1 15.6 %collective-permute-start.6 = (bf16[8,8,4096]{2,1,0:T(8,128)(2,1)}, bf16[8,8,4096]{2,1,0:T(8,128)(2,1)}, u32[]{:S(2)}, u32[]{:S(2)}) collective-permute-start(bf16[8,8,4096]{2,1,0:T(8,128)(2,1)} %fusion.22), channel_id=1, source_target_pairs={{0,2},{1,5},{2,0},{3,7},{4,6},{5,1},{6,4},{7,3},{8,10},{9,13},{10,... | collective-permute-start | bytes 1572872 | tf_op jit(solution)/shard_map/ppermute | solution.py:39
  66.7 23.2 %collective-permute-start.5 = (bf16[64,4096]{1,0:T(8,128)(2,1)}, bf16[64,4096]{1,0:T(8,128)(2,1)}, u32[]{:S(2)}, u32[]{:S(2)}) collective-permute-start(bf16[64,4096]{1,0:T(8,128)(2,1)} %pad_maximum_fusion.1), channel_id=1, source_target_pairs={{0,1},{1,0},{2,3},{3,2},{4,5},{5,4},{6,7},{7,6},{8,9},{9,8},{10,11... | collective-permute-start | bytes 1572872 | tf_op jit(solution)/shard_map/ppermute | solution.py:84
  75.0 5.7 %collective-permute-start.7 = (bf16[4,8,4096]{2,1,0:T(8,128)(2,1)S(1)}, bf16[4,8,4096]{2,1,0:T(8,128)(2,1)}, u32[]{:S(2)}, u32[]{:S(2)}) collective-permute-start(bf16[4,8,4096]{2,1,0:T(8,128)(2,1)S(1)} %fusion.25), channel_id=1, source_target_pairs={{0,4},{1,3},{2,6},{3,1},{4,0},{5,7},{6,2},{7,5},{8,12},{9,11},{10,... | collective-permute-start | bytes 786440 | tf_op jit(solution)/shard_map/ppermute | solution.py:39
  77.0 3.7 %copy-start.5 = (f32[8,8,4096]{2,1,0:T(8,128)S(1)}, f32[8,8,4096]{2,1,0:T(8,128)}, u32[]{:S(2)}) copy-start(f32[8,8,4096]{2,1,0:T(8,128)} %copy-done.4) | copy-start | bytes 3145732
  77.0 6.7 %copy-start.1 = (bf16[128,16,128]{0,2,1:T(8,128)(2,1)S(1)}, bf16[128,16,128]{0,2,1:T(8,128)(2,1)}, u32[]{:S(2)}) copy-start(bf16[128,16,128]{0,2,1:T(8,128)(2,1)} %copy-done) | copy-start | bytes 1572868
  78.7 5.0 %copy-start.17 = (bf16[16,128,128]{1,2,0:T(8,128)(2,1)S(1)}, bf16[16,128,128]{1,2,0:T(8,128)(2,1)}, u32[]{:S(2)}) copy-start(bf16[16,128,128]{1,2,0:T(8,128)(2,1)} %fusion.13) | copy-start | bytes 1572868
  82.4 4.7 %collective-permute-start.8 = (bf16[2,8,4096]{2,1,0:T(8,128)(2,1)}, bf16[2,8,4096]{2,1,0:T(8,128)(2,1)S(1)}, u32[]{:S(2)}, u32[]{:S(2)}) collective-permute-start(bf16[2,8,4096]{2,1,0:T(8,128)(2,1)} %fusion.29), channel_id=1, source_target_pairs={{0,8},{1,9},{2,10},{3,11},{4,12},{5,13},{6,14},{7,15},{8,0},{9,1},... | collective-permute-start | bytes 393224 | tf_op jit(solution)/shard_map/ppermute | solution.py:39
  87.2 4.6 %collective-permute-start.9 = (bf16[1,8,4096]{2,1,0:T(8,128)(2,1)S(1)}, bf16[1,8,4096]{2,1,0:T(8,128)(2,1)S(1)}, u32[]{:S(2)}, u32[]{:S(2)}) collective-permute-start(bf16[1,8,4096]{2,1,0:T(8,128)(2,1)S(1)} %fusion.33), channel_id=1, source_target_pairs={{0,16},{1,17},{2,18},{3,19},{4,20},{5,21},{6,22},{7,23},{8,24},{9,... | collective-permute-start | bytes 196616 | tf_op jit(solution)/shard_map/ppermute | solution.py:39
  94.4 2.4 %copy-start.19 = (bf16[64,2048]{1,0:T(8,128)(2,1)S(1)}, bf16[64,2048]{1,0:T(8,128)(2,1)}, u32[]{:S(2)}) copy-start(bf16[64,2048]{1,0:T(8,128)(2,1)} %copy.169) | copy-start | bytes 786436
  94.4 2.3 %copy-start.24 = (bf16[64,2048]{1,0:T(8,128)(2,1)S(1)}, bf16[64,2048]{1,0:T(8,128)(2,1)}, u32[]{:S(2)}) copy-start(bf16[64,2048]{1,0:T(8,128)(2,1)} %get-tuple-element.26) | copy-start | bytes 786436
  94.4 3.3 %copy-start.23 = (bf16[64,2048]{1,0:T(8,128)(2,1)S(1)}, bf16[64,2048]{1,0:T(8,128)(2,1)}, u32[]{:S(2)}) copy-start(bf16[64,2048]{1,0:T(8,128)(2,1)} %get-tuple-element.25) | copy-start | bytes 786436
  94.6 4.0 %collective-permute-start.10 = (bf16[64,4096]{1,0:T(8,128)(2,1)S(1)}, bf16[64,4096]{1,0:T(8,128)(2,1)S(1)}, u32[]{:S(2)}, u32[]{:S(2)}) collective-permute-start(bf16[64,4096]{1,0:T(8,128)(2,1)S(1)} %pad_maximum_fusion.2), channel_id=1, source_target_pairs={{0,1},{1,0},{2,3},{3,2},{4,5},{5,4},{6,7},{7,6},{8,9},{9,8},{10,11... | collective-permute-start | bytes 1572872 | tf_op jit(solution)/shard_map/ppermute | solution.py:84
  (16 other events, 25.9 us)

commit v5 on v4

--- a/solution.py
+++ b/solution.py
@@ -3,6 +3,8 @@
 import jax
 import jax.numpy as jnp
 from jax import lax
+from jax.experimental import pallas as pl
+from jax.experimental.pallas import tpu as pltpu
 from jax.sharding import Mesh
 from jax.sharding import PartitionSpec as P
 
@@ -110,6 +112,91 @@
     return out
 
 
+def mm(a, b, trans_a=False, trans_b=False):
+    dims = (((0 if trans_a else 1,), (1 if trans_b else 0,)), ((), ()))
+    return lax.dot_general(a, b, dims, preferred_element_type=jnp.float32)
+
+
+def attention_kernel(
+    q_ref, k_ref, v_ref, g_ref, s_ref, mask_ref, att_ref, dq_ref, dkw_ref, dvw_ref, ds_ref
+):
+    j = pl.program_id(1)
+    scale = 1.0 / math.sqrt(HEAD_DIM)
+    f32 = jnp.float32
+    bf16 = jnp.bfloat16
+    q = q_ref[...]
+    k = k_ref[...]
+    v = v_ref[...]
+    g = g_ref[...]
+    sk = s_ref[:, :HEAD_DIM]
+    sv = s_ref[:, HEAD_DIM:]
+    allowed = mask_ref[0:1, :] > 0
+    row = lax.broadcasted_iota(jnp.int32, (BLOCK, BLOCK), 0)
+    col = lax.broadcasted_iota(jnp.int32, (BLOCK, BLOCK), 1)
+    causal = row >= col
+
+    sw = jnp.where(causal, mm(q, k, trans_b=True) * scale, MASKED_SCORE)
+    ss = jnp.where(allowed, mm(q, sk, trans_b=True) * scale, MASKED_SCORE)
+    top = jnp.maximum(jnp.max(sw, axis=1, keepdims=True), jnp.max(ss, axis=1, keepdims=True))
+    total = jnp.sum(jnp.exp(sw - top), axis=1, keepdims=True) + jnp.sum(
+        jnp.exp(ss - top), axis=1, keepdims=True
+    )
+    log_norm = top + jnp.log(total)
+    pw = jnp.where(causal, jnp.exp(sw - log_norm), 0.0)
+    ps = jnp.where(allowed, jnp.exp(ss - log_norm), 0.0)
+    pw_low = pw.astype(bf16)
+    ps_low = ps.astype(bf16)
+    att = (mm(pw_low, v) + mm(ps_low, sv)).astype(bf16)
+    att_ref[...] = att
+    delta = jnp.sum(g.astype(f32) * att.astype(f32), axis=1, keepdims=True)
+    dsw = (pw * (mm(g, v, trans_b=True) - delta)).astype(bf16)
+    dss = (ps * (mm(g, sv, trans_b=True) - delta)).astype(bf16)
+    dq_ref[...] = ((mm(dsw, k) + mm(dss, sk)) * scale).astype(bf16)
+    dkw_ref[...] = mm(dsw, q, trans_a=True) * scale
+    dvw_ref[...] = mm(pw_low, g, trans_a=True)
+    dks = mm(dss, q, trans_a=True) * scale
+    dvs = mm(ps_low, g, trans_a=True)
+
+    @pl.when(j == 0)
+    def _():
+        ds_ref[:, :HEAD_DIM] = dks
+        ds_ref[:, HEAD_DIM:] = dvs
+
+    @pl.when(j > 0)
+    def _():
+        ds_ref[:, :HEAD_DIM] += dks
+        ds_ref[:, HEAD_DIM:] += dvs
+
+
+def attention(q, k, v, g, summary, mask):
+    rows, half = q.shape
+    heads = half // HEAD_DIM
+    nb = rows // BLOCK
+    count = summary.shape[0]
+    tile = pl.BlockSpec((BLOCK, HEAD_DIM), lambda h, j: (j, h))
+    pair = pl.BlockSpec((count, 2 * HEAD_DIM), lambda h, j: (0, h))
+    bf16 = jnp.bfloat16
+    f32 = jnp.float32
+    flops = 2 * rows * heads * HEAD_DIM * (BLOCK + count) * 6
+    return pl.pallas_call(
+        attention_kernel,
+        grid=(heads, nb),
+        in_specs=[tile, tile, tile, tile, pair, pl.BlockSpec((8, count), lambda h, j: (j, 0))],
+        out_specs=[tile, tile, tile, tile, pair],
+        out_shape=[
+            jax.ShapeDtypeStruct((rows, half), bf16),
+            jax.ShapeDtypeStruct((rows, half), bf16),
+            jax.ShapeDtypeStruct((rows, half), f32),
+            jax.ShapeDtypeStruct((rows, half), f32),
+            jax.ShapeDtypeStruct((count, 2 * half), f32),
+        ],
+        cost_estimate=pl.CostEstimate(
+            flops=flops, transcendentals=rows * heads * (BLOCK + count) * 2,
+            bytes_accessed=rows * half * 2 * 8 + count * half * 2 * 6,
+        ),
+    )(q, k, v, g, summary, mask)
+
+
 def body(queries, key_rows, value_rows, out_grad, summary_columns):
     core = lax.axis_index("hc")
     hx = lax.axis_index("hx")
@@ -126,62 +213,26 @@
     cols = lax.dynamic_slice_in_dim(summary_columns, hx * nb, nb, 0)
     positions = (jnp.arange(nb, dtype=jnp.int32)[:, None] * BLOCK + cols).reshape(-1)
 
-    own_sum = jnp.concatenate([jnp.take(kb, positions, axis=0), jnp.take(vb, positions, axis=0)], axis=1)
+    own_sum = jnp.stack(
+        [
+            jnp.take(kb, positions, axis=0).reshape(-1, heads, HEAD_DIM),
+            jnp.take(vb, positions, axis=0).reshape(-1, heads, HEAD_DIM),
+        ],
+        axis=2,
+    ).reshape(-1, 2 * half)
     all_sum = gather_blocks(own_sum, core)
     sum_count = all_sum.shape[0]
-    sk = all_sum[:, :half].reshape(sum_count, heads, HEAD_DIM)
-    sv = all_sum[:, half:].reshape(sum_count, heads, HEAD_DIM)
-
-    q = qb.reshape(nb, BLOCK, heads, HEAD_DIM)
-    k = kb.reshape(nb, BLOCK, heads, HEAD_DIM)
-    v = vb.reshape(nb, BLOCK, heads, HEAD_DIM)
-    g = gb.reshape(nb, BLOCK, heads, HEAD_DIM)
-
-    span = jnp.arange(BLOCK, dtype=jnp.int32)
-    causal = (span[:, None] >= span[None, :])[None, None]
     key_block = jnp.arange(sum_count, dtype=jnp.int32) // SUMMARY
     query_block = first_block + jnp.arange(nb, dtype=jnp.int32)
-    allowed = (key_block[None, :] < query_block[:, None])[:, None, None, :]
-
-    sw = jnp.einsum("bqhd,bkhd->bhqk", q, k, preferred_element_type=f32) * score_scale
-    ss = jnp.einsum("bqhd,khd->bhqk", q, sk, preferred_element_type=f32) * score_scale
-    sw = jnp.where(causal, sw, MASKED_SCORE)
-    ss = jnp.where(allowed, ss, MASKED_SCORE)
-    top = jnp.maximum(jnp.max(sw, axis=3), jnp.max(ss, axis=3))
-    ew = jnp.where(causal, jnp.exp(sw - top[..., None]), 0.0)
-    es = jnp.where(allowed, jnp.exp(ss - top[..., None]), 0.0)
-    log_norm = top + jnp.log(jnp.sum(ew, axis=3) + jnp.sum(es, axis=3))
-    pw = jnp.where(causal, jnp.exp(sw - log_norm[..., None]), 0.0)
-    ps = jnp.where(allowed, jnp.exp(ss - log_norm[..., None]), 0.0)
-    pw_low = pw.astype(jnp.bfloat16)
-    ps_low = ps.astype(jnp.bfloat16)
-    att = jnp.einsum("bhqk,bkhd->bqhd", pw_low, v, preferred_element_type=f32) + jnp.einsum(
-        "bhqk,khd->bqhd", ps_low, sv, preferred_element_type=f32
-    )
-    attended = att.astype(jnp.bfloat16)
-    delta = jnp.einsum("bqhd,bqhd->bhq", g.astype(f32), attended.astype(f32), precision=lax.Precision.HIGHEST)
-
-    dpw = jnp.einsum("bqhd,bkhd->bhqk", g, v, preferred_element_type=f32)
-    dps = jnp.einsum("bqhd,khd->bhqk", g, sv, preferred_element_type=f32)
-    dsw = (pw * (dpw - delta[..., None])).astype(jnp.bfloat16)
-    dss = (ps * (dps - delta[..., None])).astype(jnp.bfloat16)
-    dq = (
-        jnp.einsum("bhqk,bkhd->bqhd", dsw, k, preferred_element_type=f32)
-        + jnp.einsum("bhqk,khd->bqhd", dss, sk, preferred_element_type=f32)
-    ) * score_scale
-    dkw = jnp.einsum("bhqk,bqhd->bkhd", dsw, q, preferred_element_type=f32) * score_scale
-    dvw = jnp.einsum("bhqk,bqhd->bkhd", pw_low, g, preferred_element_type=f32)
-    dks = jnp.einsum("bhqk,bqhd->khd", dss, q, preferred_element_type=f32) * score_scale
-    dvs = jnp.einsum("bhqk,bqhd->khd", ps_low, g, preferred_element_type=f32)
-
-    att_tok, dq_tok = to_token_layout(
-        [attended.reshape(rows, half), dq.astype(jnp.bfloat16).reshape(rows, half)], core
-    )
-
-    parts = jnp.concatenate([dks.reshape(sum_count, half), dvs.reshape(sum_count, half)], axis=1)
-    own_grad = reduce_blocks(parts, core)
-    dk = dkw.reshape(rows, half).at[positions].add(own_grad[:, :half])
-    dv = dvw.reshape(rows, half).at[positions].add(own_grad[:, half:])
+    mask = (key_block[None, :] < query_block[:, None]).astype(jnp.int32)
+    mask = jnp.repeat(mask, 8, axis=0)
+
+    attended, dq, dkw, dvw, parts = attention(qb, kb, vb, gb, all_sum, mask)
+    att_tok, dq_tok = to_token_layout([attended, dq], core)
+
+    own_grad = reduce_blocks(parts, core).reshape(-1, heads, 2, HEAD_DIM)
+    dk = dkw.at[positions].add(own_grad[:, :, 0].reshape(-1, half))
+    dv = dvw.at[positions].add(own_grad[:, :, 1].reshape(-1, half))
     dk_tok, dv_tok = to_token_layout([dk.astype(jnp.bfloat16), dv.astype(jnp.bfloat16)], core)
     return att_tok, dq_tok, dk_tok, dv_tok
 

time: 102 us -> 94.7 us (0.928)
  local copies, waits for them, and re-layouts: 34.3 us -> 7.66 us
  Pallas kernels: 0 us -> 15.7 us
  waiting for transfers between devices: 16.4 us -> 29.2 us
  matrix products: 11.6 us -> 0 us
  starting transfers between devices: 17.1 us -> 27.6 us
  other arithmetic: 19.8 us -> 11.8 us
    pallas_call x0 -> x1, Pallas kernels: none -> 15.7 us  [attention(): pl.pallas_call(attention_kernel, grid=(heads, nb), in_specs=[tile, tile,...]
    unnamed x73 -> x22, local copies, waits for them, and re-layouts: 13.9 us -> 0.85 us
    dot_general x12 -> x0, matrix products: 11.6 us -> none  [the longest x1 1.51 us: body(): dvs = jnp.einsum('bhqk,bqhd->khd', ps_low, g, preferred_element_type=f32)]
    ppermute x8, waiting for transfers between devices: 16.4 us -> 26.9 us  [exchange(): return lax.ppermute(x, ('seq', 'hx', 'hc'), pairs)]
    ppermute x3, starting transfers between devices: 6.09 us -> 12.4 us  [swap_with_partner(): return lax.ppermute(x, 'hc', [(0, 1), (1, 0)])]
    concatenate x4 -> x0, local copies, waits for them, and re-layouts: 4.58 us -> none  [body(): jnp.concatenate([dks.reshape(sum_count, half), dvs.reshape(sum_count, hal...]
    ppermute x8, starting transfers between devices: 11 us -> 15.2 us  [exchange(): return lax.ppermute(x, ('seq', 'hx', 'hc'), pairs)]
    reshape x2 -> x1, local copies, waits for them, and re-layouts: 3.23 us -> 0.59 us  [body(): mask = jnp.repeat(mask, 8, axis=0)]
  transfers between devices with their start and end apart: 11 -> 11, of which waited for: 5 -> 8; matrix products, arithmetic and copies ran while one was open for 33% -> 5% of each run, Pallas kernels for 0% -> 0%
where the time goes in v5:
time: 94.7 us; the launch traced here: 92.9 us
  waiting for transfers between devices  29.2 us (31%)
  starting transfers between devices  27.6 us (29%)
  Pallas kernels  15.7 us (17%)
  other arithmetic  11.8 us (12%)
  local copies, waits for them, and re-layouts  7.66 us (8%)
  between operations  1.04 us (1%)
    ppermute x8, waiting for transfers between devices, exchange(): return lax.ppermute(x, ('seq', 'hx', 'hc'), pairs)  26.9 us
    pallas_call x1, Pallas kernels, attention(): pl.pallas_call(attention_kernel, grid=(heads, nb), in_specs=[tile, tile,...  15.7 us
    ppermute x8, starting transfers between devices, exchange(): return lax.ppermute(x, ('seq', 'hx', 'hc'), pairs)  15.2 us
    ppermute x3, starting transfers between devices, swap_with_partner(): return lax.ppermute(x, 'hc', [(0, 1), (1, 0)])  12.4 us
    select_n x4, other arithmetic, to_token_layout(): jnp.where(core == 0, jnp.concatenate([m, r], 1), jnp.concatenate([r, m], 1))  3.66 us
    ppermute x3, waiting for transfers between devices, swap_with_partner(): return lax.ppermute(x, 'hc', [(0, 1), (1, 0)])  2.22 us
    select_n x4, other arithmetic, to_block_layout(): jnp.where(core == 0, jnp.concatenate([m, r], 0), jnp.concatenate([r, m], 0))  2.01 us
    transpose x1, local copies, waits for them, and re-layouts, swap_low_bits(): jnp.swapaxes(x.reshape((size // 4, 2, 2) + x.shape[1:]), 1, 2)  1.89 us
  transfers between devices with their start and end apart: 11, of which 8 were waited for; matrix products, arithmetic and copies ran while one was open for 5% of the time, Pallas kernels for 0%

profile of v5, /device:TPU:1, one launch (start us, length us, event | category | flops | bytes accessed | tf_op | source)
XLA Modules:
  0.0 92.9 jit_solution(7875832094310851325)
XLA Ops:
  0.7 1.3 %constant_dynamic-slice_fusion.11 = (bf16[64,2048]{1,0:T(8,128)(2,1)S(1)}, bf16[64,2048]{1,0:T(8,128)(2,1)S(1)}, bf16[64,2048]{1,0:T(8,128)(2,1)S(1)}, bf16[64,2048]{1,0:T(8,128)(2,1)S(1)}) fusion(bf16[64,4096]{1,0:T(8,128)(2,1)} %param.8, s32[]{:T(128)S(6)} %select_n.293, s32[]{:T(128)S(6)} %select_n.294, bf16[64,4096]{1,0:T(8,128)(2,1)} %param.7), kind=kLoop, calls=%fused_computation.63 | loop fusion | bytes 2097160 | tf_op jit(solution)/shard_map/dynamic_slice | solution.py:92
  2.9 2.2 %collective-permute-done = bf16[64,8192]{1,0:T(8,128)(2,1)S(1)} collective-permute-done((bf16[64,8192]{1,0:T(8,128)(2,1)S(1)}, bf16[64,8192]{1,0:T(8,128)(2,1)S(1)}, u32[]{:S(2)}, u32[]{:S(2)}) %collective-permute-start) | collective-permute-done | bytes 1048608 | tf_op jit(solution)/shard_map/ppermute | solution.py:86
  7.0 3.5 %collective-permute-start.1 = (bf16[1,8,4096]{2,1,0:T(8,128)(2,1)S(1)}, bf16[1,8,4096]{2,1,0:T(8,128)(2,1)S(1)}, u32[]{:S(2)}, u32[]{:S(2)}) collective-permute-start(bf16[1,8,4096]{2,1,0:T(8,128)(2,1)S(1)} %broadcast_in_dim_reshape.3), channel_id=1, source_target_pairs={{0,16},{1,17},{2,18},{3,19},{4,20},{5,21},{6,22},{7,23},{8,24},{9,... | collective-permute-start | bytes 196616 | tf_op jit(solution)/shard_map/ppermute | solution.py:41
  10.5 2.1 %collective-permute-done.1 = bf16[1,8,4096]{2,1,0:T(8,128)(2,1)S(1)} collective-permute-done((bf16[1,8,4096]{2,1,0:T(8,128)(2,1)S(1)}, bf16[1,8,4096]{2,1,0:T(8,128)(2,1)S(1)}, u32[]{:S(2)}, u32[]{:S(2)}) %collective-permute-start.1) | collective-permute-done | bytes 65568 | tf_op jit(solution)/shard_map/ppermute | solution.py:41
  12.7 2.3 %collective-permute-start.2 = (bf16[2,8,4096]{2,1,0:T(8,128)(2,1)S(1)}, bf16[2,8,4096]{2,1,0:T(8,128)(2,1)S(1)}, u32[]{:S(2)}, u32[]{:S(2)}) collective-permute-start(bf16[2,8,4096]{2,1,0:T(8,128)(2,1)S(1)} %maximum_select_fusion.14), channel_id=1, source_target_pairs={{0,8},{1,9},{2,10},{3,11},{4,12},{5,13},{6,14},{7,15},{8,0},{9,1},... | collective-permute-start | bytes 393224 | tf_op jit(solution)/shard_map/ppermute | solution.py:41
  15.0 2.3 %collective-permute-done.2 = bf16[2,8,4096]{2,1,0:T(8,128)(2,1)S(1)} collective-permute-done((bf16[2,8,4096]{2,1,0:T(8,128)(2,1)S(1)}, bf16[2,8,4096]{2,1,0:T(8,128)(2,1)S(1)}, u32[]{:S(2)}, u32[]{:S(2)}) %collective-permute-start.2) | collective-permute-done | bytes 131104 | tf_op jit(solution)/shard_map/ppermute | solution.py:41
  17.3 1.3 %collective-permute-start.3 = (bf16[4,8,4096]{2,1,0:T(8,128)(2,1)S(1)}, bf16[4,8,4096]{2,1,0:T(8,128)(2,1)S(1)}, u32[]{:S(2)}, u32[]{:S(2)}) collective-permute-start(bf16[4,8,4096]{2,1,0:T(8,128)(2,1)S(1)} %bitcast.108), channel_id=1, source_target_pairs={{0,4},{1,3},{2,6},{3,1},{4,0},{5,7},{6,2},{7,5},{8,12},{9,11},{10,... | collective-permute-start | bytes 786440 | tf_op jit(solution)/shard_map/ppermute | solution.py:41
  19.5 3.1 %collective-permute-done.3 = bf16[4,8,4096]{2,1,0:T(8,128)(2,1)S(1)} collective-permute-done((bf16[4,8,4096]{2,1,0:T(8,128)(2,1)S(1)}, bf16[4,8,4096]{2,1,0:T(8,128)(2,1)S(1)}, u32[]{:S(2)}, u32[]{:S(2)}) %collective-permute-start.3) | collective-permute-done | bytes 262176 | tf_op jit(solution)/shard_map/ppermute | solution.py:41
  22.7 1.3 %collective-permute-start.4 = (bf16[8,8,4096]{2,1,0:T(8,128)(2,1)S(1)}, bf16[8,8,4096]{2,1,0:T(8,128)(2,1)S(1)}, u32[]{:S(2)}, u32[]{:S(2)}) collective-permute-start(bf16[8,8,4096]{2,1,0:T(8,128)(2,1)S(1)} %bitcast.113), channel_id=1, source_target_pairs={{0,2},{1,5},{2,0},{3,7},{4,6},{5,1},{6,4},{7,3},{8,10},{9,13},{10,... | collective-permute-start | bytes 1572872 | tf_op jit(solution)/shard_map/ppermute | solution.py:41
  25.0 6.7 %collective-permute-done.4 = bf16[8,8,4096]{2,1,0:T(8,128)(2,1)S(1)} collective-permute-done((bf16[8,8,4096]{2,1,0:T(8,128)(2,1)S(1)}, bf16[8,8,4096]{2,1,0:T(8,128)(2,1)S(1)}, u32[]{:S(2)}, u32[]{:S(2)}) %collective-permute-start.4) | collective-permute-done | bytes 524320 | tf_op jit(solution)/shard_map/ppermute | solution.py:41
  31.9 1.2 %bitcast_select_fusion.s_ref = bf16[128,4096]{1,0:T(8,128)(2,1)} fusion(bf16[4,2,2,8,4096]{4,3,1,2,0:T(8,128)(2,1)S(1)} %maximum_select_fusion, bf16[8,2,8,4096]{3,2,1,0:T(8,128)(2,1)S(1)} %maximum_select_fusion.1, pred[]{:T(512)S(6)} %eq.13), kind=kLoop, calls=%fused_computation.8 | loop fusion | flops 524288 | bytes 3145729 | tf_op jit(solution)/shard_map/jit(_where)/select_n | solution.py:49
  33.7 15.7 %shard_map.84 = (bf16[128,2048]{1,0:T(8,128)(2,1)}, bf16[128,2048]{1,0:T(8,128)(2,1)}, f32[128,2048]{1,0:T(8,128)}, f32[128,2048]{1,0:T(8,128)}, f32[128,4096]{1,0:T(8,128)}) custom-call(bf16[128,2048]{1,0:T(8,128)(2,1)} %maximum_select_fusion.2.q_ref, bf16[128,2048]{1,0:T(8,128)(2,1)} %copy-done.2, bf16[128,2048]{1,0:T(8,128)(2,1)} %copy-done.1, ...), custom_call_target="tpu_custom_call" | custom-call | flops 805306368 | bytes 7340032 | tf_op jit(solution)/shard_map/pallas_call | solution.py:181
  49.4 1.9 %copy.68 = f32[4,2,2,8,4096]{4,3,1,0,2:T(8,128)S(1)} copy(f32[4,2,2,8,4096]{4,3,1,2,0:T(8,128)} %bitcast.101) | data formatting | bytes 4194304 | tf_op jit(solution)/shard_map/transpose | solution.py:48
  52.0 1.5 %collective-permute-start.6 = (bf16[8,8,4096]{2,1,0:T(8,128)(2,1)S(1)}, bf16[8,8,4096]{2,1,0:T(8,128)(2,1)}, u32[]{:S(2)}, u32[]{:S(2)}) collective-permute-start(bf16[8,8,4096]{2,1,0:T(8,128)(2,1)S(1)} %fusion), channel_id=1, source_target_pairs={{0,2},{1,5},{2,0},{3,7},{4,6},{5,1},{6,4},{7,3},{8,10},{9,13},{10,... | collective-permute-start | bytes 1572872 | tf_op jit(solution)/shard_map/ppermute | solution.py:41
  53.5 7.0 %collective-permute-done.6 = bf16[8,8,4096]{2,1,0:T(8,128)(2,1)} collective-permute-done((bf16[8,8,4096]{2,1,0:T(8,128)(2,1)S(1)}, bf16[8,8,4096]{2,1,0:T(8,128)(2,1)}, u32[]{:S(2)}, u32[]{:S(2)}) %collective-permute-start.6) | collective-permute-done | bytes 524320 | tf_op jit(solution)/shard_map/ppermute | solution.py:41
  60.5 1.2 %bitcast_add_fusion = f32[8,8,4096]{2,1,0:T(8,128)S(1)} fusion(bf16[8,8,4096]{2,1,0:T(8,128)(2,1)} %collective-permute-done.6, f32[8,2,8,4096]{3,2,0,1:T(8,128)S(1)} %copy_select_fusion, pred[]{:T(512)S(6)} %eq.14), kind=kLoop, calls=%fused_computation.9 | loop fusion | flops 786432 | bytes 3670017 | tf_op jit(solution)/shard_map/add | solution.py:81
  61.7 1.5 %collective-permute-start.7 = (bf16[4,8,4096]{2,1,0:T(8,128)(2,1)S(1)}, bf16[4,8,4096]{2,1,0:T(8,128)(2,1)S(1)}, u32[]{:S(2)}, u32[]{:S(2)}) collective-permute-start(bf16[4,8,4096]{2,1,0:T(8,128)(2,1)S(1)} %fusion.3), channel_id=1, source_target_pairs={{0,4},{1,3},{2,6},{3,1},{4,0},{5,7},{6,2},{7,5},{8,12},{9,11},{10,... | collective-permute-start | bytes 786440 | tf_op jit(solution)/shard_map/ppermute | solution.py:41
  63.3 4.7 %collective-permute-done.7 = bf16[4,8,4096]{2,1,0:T(8,128)(2,1)S(1)} collective-permute-done((bf16[4,8,4096]{2,1,0:T(8,128)(2,1)S(1)}, bf16[4,8,4096]{2,1,0:T(8,128)(2,1)S(1)}, u32[]{:S(2)}, u32[]{:S(2)}) %collective-permute-start.7) | collective-permute-done | bytes 262176 | tf_op jit(solution)/shard_map/ppermute | solution.py:41
  68.1 1.0 %collective-permute-start.8 = (bf16[2,8,4096]{2,1,0:T(8,128)(2,1)S(1)}, bf16[2,8,4096]{2,1,0:T(8,128)(2,1)S(1)}, u32[]{:S(2)}, u32[]{:S(2)}) collective-permute-start(bf16[2,8,4096]{2,1,0:T(8,128)(2,1)S(1)} %fusion.7), channel_id=1, source_target_pairs={{0,8},{1,9},{2,10},{3,11},{4,12},{5,13},{6,14},{7,15},{8,0},{9,1},... | collective-permute-start | bytes 393224 | tf_op jit(solution)/shard_map/ppermute | solution.py:41
  69.1 5.7 %collective-permute-start.5 = (bf16[64,4096]{1,0:T(8,128)(2,1)S(1)}, bf16[64,4096]{1,0:T(8,128)(2,1)S(1)}, u32[]{:S(2)}, u32[]{:S(2)}) collective-permute-start(bf16[64,4096]{1,0:T(8,128)(2,1)S(1)} %pad_maximum_fusion.1), channel_id=1, source_target_pairs={{0,1},{1,0},{2,3},{3,2},{4,5},{5,4},{6,7},{7,6},{8,9},{9,8},{10,11... | collective-permute-start | bytes 1572872 | tf_op jit(solution)/shard_map/ppermute | solution.py:86
  74.9 2.9 %collective-permute-start.9 = (bf16[1,8,4096]{2,1,0:T(8,128)(2,1)S(1)}, bf16[1,8,4096]{2,1,0:T(8,128)(2,1)S(1)}, u32[]{:S(2)}, u32[]{:S(2)}) collective-permute-start(bf16[1,8,4096]{2,1,0:T(8,128)(2,1)S(1)} %fusion.8), channel_id=1, source_target_pairs={{0,16},{1,17},{2,18},{3,19},{4,20},{5,21},{6,22},{7,23},{8,24},{9,... | collective-permute-start | bytes 196616 | tf_op jit(solution)/shard_map/ppermute | solution.py:41
  80.1 1.1 %scatter_custom_fusion = f32[128,2048]{1,0:T(8,128)S(1)} fusion(f32[128,2048]{1,0:T(8,128)S(1)} %copy-done.4, s32[8]{0:T(128)S(1)} %fusion.15, f32[1,8,16,128]{3,2,1,0:T(8,128)S(1)} %bitcast.118), kind=kCustom, calls=%fused_computation.44 | custom fusion | flops 16384 | bytes 1114112 | tf_op jit(solution)/shard_map/scatter-add | solution.py:234
  81.3 1.1 %scatter_custom_fusion.1 = f32[128,2048]{1,0:T(8,128)S(1)} fusion(f32[128,2048]{1,0:T(8,128)S(1)} %copy-done.3, s32[8]{0:T(128)S(1)} %fusion.15, f32[1,8,16,128]{3,2,1,0:T(8,128)S(1)} %bitcast.117), kind=kCustom, calls=%fused_computation.41 | custom fusion | flops 16384 | bytes 1114112 | tf_op jit(solution)/shard_map/scatter-add | solution.py:235
  82.7 6.5 %collective-permute-start.10 = (bf16[64,4096]{1,0:T(8,128)(2,1)S(1)}, bf16[64,4096]{1,0:T(8,128)(2,1)S(1)}, u32[]{:S(2)}, u32[]{:S(2)}) collective-permute-start(bf16[64,4096]{1,0:T(8,128)(2,1)S(1)} %pad_maximum_fusion.2), channel_id=1, source_target_pairs={{0,1},{1,0},{2,3},{3,2},{4,5},{5,4},{6,7},{7,6},{8,9},{9,8},{10,11... | collective-permute-start | bytes 1572872 | tf_op jit(solution)/shard_map/ppermute | solution.py:86
  (79 shorter events, 12.7 us)
Async XLA Ops:
  0.6 1.4 %copy-start.8 = (bf16[64,4096]{1,0:T(8,128)(2,1)S(1)}, bf16[64,4096]{1,0:T(8,128)(2,1)}, u32[]{:S(2)}) copy-start(bf16[64,4096]{1,0:T(8,128)(2,1)} %param.10) | copy-start | bytes 1572868
  0.6 1.5 %copy-start.9 = (bf16[64,4096]{1,0:T(8,128)(2,1)S(1)}, bf16[64,4096]{1,0:T(8,128)(2,1)}, u32[]{:S(2)}) copy-start(bf16[64,4096]{1,0:T(8,128)(2,1)} %param.9) | copy-start | bytes 1572868
  2.1 0.7 copy-start.10
  2.3 2.7 %collective-permute-start = (bf16[64,8192]{1,0:T(8,128)(2,1)S(1)}, bf16[64,8192]{1,0:T(8,128)(2,1)S(1)}, u32[]{:S(2)}, u32[]{:S(2)}) collective-permute-start(bf16[64,8192]{1,0:T(8,128)(2,1)S(1)} %pad_maximum_fusion), channel_id=1, source_target_pairs={{0,1},{1,0},{2,3},{3,2},{4,5},{5,4},{6,7},{7,6},{8,9},{9,8},{10,11... | collective-permute-start | bytes 3145736 | tf_op jit(solution)/shard_map/ppermute | solution.py:86
  5.3 14.2 %copy-start.1 = (bf16[128,2048]{1,0:T(8,128)(2,1)}, bf16[128,2048]{1,0:T(8,128)(2,1)S(1)}, u32[]{:S(2)}) copy-start(bf16[128,2048]{1,0:T(8,128)(2,1)S(1)} %maximum_select_fusion.4.v_ref) | copy-start | bytes 1572868
  6.0 16.7 %copy-start.2 = (bf16[128,2048]{1,0:T(8,128)(2,1)}, bf16[128,2048]{1,0:T(8,128)(2,1)S(1)}, u32[]{:S(2)}) copy-start(bf16[128,2048]{1,0:T(8,128)(2,1)S(1)} %maximum_select_fusion.3.k_ref) | copy-start | bytes 1572868
  7.0 5.7 %collective-permute-start.1 = (bf16[1,8,4096]{2,1,0:T(8,128)(2,1)S(1)}, bf16[1,8,4096]{2,1,0:T(8,128)(2,1)S(1)}, u32[]{:S(2)}, u32[]{:S(2)}) collective-permute-start(bf16[1,8,4096]{2,1,0:T(8,128)(2,1)S(1)} %broadcast_in_dim_reshape.3), channel_id=1, source_target_pairs={{0,16},{1,17},{2,18},{3,19},{4,20},{5,21},{6,22},{7,23},{8,24},{9,... | collective-permute-start | bytes 196616 | tf_op jit(solution)/shard_map/ppermute | solution.py:41
  12.7 4.6 %collective-permute-start.2 = (bf16[2,8,4096]{2,1,0:T(8,128)(2,1)S(1)}, bf16[2,8,4096]{2,1,0:T(8,128)(2,1)S(1)}, u32[]{:S(2)}, u32[]{:S(2)}) collective-permute-start(bf16[2,8,4096]{2,1,0:T(8,128)(2,1)S(1)} %maximum_select_fusion.14), channel_id=1, source_target_pairs={{0,8},{1,9},{2,10},{3,11},{4,12},{5,13},{6,14},{7,15},{8,0},{9,1},... | collective-permute-start | bytes 393224 | tf_op jit(solution)/shard_map/ppermute | solution.py:41
  17.3 5.3 %collective-permute-start.3 = (bf16[4,8,4096]{2,1,0:T(8,128)(2,1)S(1)}, bf16[4,8,4096]{2,1,0:T(8,128)(2,1)S(1)}, u32[]{:S(2)}, u32[]{:S(2)}) collective-permute-start(bf16[4,8,4096]{2,1,0:T(8,128)(2,1)S(1)} %bitcast.108), channel_id=1, source_target_pairs={{0,4},{1,3},{2,6},{3,1},{4,0},{5,7},{6,2},{7,5},{8,12},{9,11},{10,... | collective-permute-start | bytes 786440 | tf_op jit(solution)/shard_map/ppermute | solution.py:41
  22.7 8.9 %collective-permute-start.4 = (bf16[8,8,4096]{2,1,0:T(8,128)(2,1)S(1)}, bf16[8,8,4096]{2,1,0:T(8,128)(2,1)S(1)}, u32[]{:S(2)}, u32[]{:S(2)}) collective-permute-start(bf16[8,8,4096]{2,1,0:T(8,128)(2,1)S(1)} %bitcast.113), channel_id=1, source_target_pairs={{0,2},{1,5},{2,0},{3,7},{4,6},{5,1},{6,4},{7,3},{8,10},{9,13},{10,... | collective-permute-start | bytes 1572872 | tf_op jit(solution)/shard_map/ppermute | solution.py:41
  49.4 2.2 %copy-start = (f32[128,4096]{1,0:T(8,128)S(1)}, f32[128,4096]{1,0:T(8,128)}, u32[]{:S(2)}) copy-start(f32[128,4096]{1,0:T(8,128)} %get-tuple-element.13) | copy-start | bytes 6291460
  52.0 8.5 %collective-permute-start.6 = (bf16[8,8,4096]{2,1,0:T(8,128)(2,1)S(1)}, bf16[8,8,4096]{2,1,0:T(8,128)(2,1)}, u32[]{:S(2)}, u32[]{:S(2)}) collective-permute-start(bf16[8,8,4096]{2,1,0:T(8,128)(2,1)S(1)} %fusion), channel_id=1, source_target_pairs={{0,2},{1,5},{2,0},{3,7},{4,6},{5,1},{6,4},{7,3},{8,10},{9,13},{10,... | collective-permute-start | bytes 1572872 | tf_op jit(solution)/shard_map/ppermute | solution.py:41
  53.5 9.7 %copy-start.7 = (bf16[128,2048]{1,0:T(8,128)(2,1)S(1)}, bf16[128,2048]{1,0:T(8,128)(2,1)}, u32[]{:S(2)}) copy-start(bf16[128,2048]{1,0:T(8,128)(2,1)} %get-tuple-element.10) | copy-start | bytes 1572868
  53.5 9.7 %copy-start.6 = (bf16[128,2048]{1,0:T(8,128)(2,1)S(1)}, bf16[128,2048]{1,0:T(8,128)(2,1)}, u32[]{:S(2)}) copy-start(bf16[128,2048]{1,0:T(8,128)(2,1)} %get-tuple-element.11) | copy-start | bytes 1572868
  61.7 6.3 %collective-permute-start.7 = (bf16[4,8,4096]{2,1,0:T(8,128)(2,1)S(1)}, bf16[4,8,4096]{2,1,0:T(8,128)(2,1)S(1)}, u32[]{:S(2)}, u32[]{:S(2)}) collective-permute-start(bf16[4,8,4096]{2,1,0:T(8,128)(2,1)S(1)} %fusion.3), channel_id=1, source_target_pairs={{0,4},{1,3},{2,6},{3,1},{4,0},{5,7},{6,2},{7,5},{8,12},{9,11},{10,... | collective-permute-start | bytes 786440 | tf_op jit(solution)/shard_map/ppermute | solution.py:41
  68.1 6.8 %collective-permute-start.8 = (bf16[2,8,4096]{2,1,0:T(8,128)(2,1)S(1)}, bf16[2,8,4096]{2,1,0:T(8,128)(2,1)S(1)}, u32[]{:S(2)}, u32[]{:S(2)}) collective-permute-start(bf16[2,8,4096]{2,1,0:T(8,128)(2,1)S(1)} %fusion.7), channel_id=1, source_target_pairs={{0,8},{1,9},{2,10},{3,11},{4,12},{5,13},{6,14},{7,15},{8,0},{9,1},... | collective-permute-start | bytes 393224 | tf_op jit(solution)/shard_map/ppermute | solution.py:41
  69.1 11.0 %copy-start.4 = (f32[128,2048]{1,0:T(8,128)S(1)}, f32[128,2048]{1,0:T(8,128)}, u32[]{:S(2)}) copy-start(f32[128,2048]{1,0:T(8,128)} %get-tuple-element.12) | copy-start | bytes 3145732
  69.1 8.7 %collective-permute-start.5 = (bf16[64,4096]{1,0:T(8,128)(2,1)S(1)}, bf16[64,4096]{1,0:T(8,128)(2,1)S(1)}, u32[]{:S(2)}, u32[]{:S(2)}) collective-permute-start(bf16[64,4096]{1,0:T(8,128)(2,1)S(1)} %pad_maximum_fusion.1), channel_id=1, source_target_pairs={{0,1},{1,0},{2,3},{3,2},{4,5},{5,4},{6,7},{7,6},{8,9},{9,8},{10,11... | collective-permute-start | bytes 1572872 | tf_op jit(solution)/shard_map/ppermute | solution.py:86
  74.9 4.6 %collective-permute-start.9 = (bf16[1,8,4096]{2,1,0:T(8,128)(2,1)S(1)}, bf16[1,8,4096]{2,1,0:T(8,128)(2,1)S(1)}, u32[]{:S(2)}, u32[]{:S(2)}) collective-permute-start(bf16[1,8,4096]{2,1,0:T(8,128)(2,1)S(1)} %fusion.8), channel_id=1, source_target_pairs={{0,16},{1,17},{2,18},{3,19},{4,20},{5,21},{6,22},{7,23},{8,24},{9,... | collective-permute-start | bytes 196616 | tf_op jit(solution)/shard_map/ppermute | solution.py:41
  78.6 2.7 %copy-start.3 = (f32[128,2048]{1,0:T(8,128)S(1)}, f32[128,2048]{1,0:T(8,128)}, u32[]{:S(2)}) copy-start(f32[128,2048]{1,0:T(8,128)} %get-tuple-element.14) | copy-start | bytes 3145732
  82.4 6.8 %copy-start.5 = (bf16[64,2048]{1,0:T(8,128)(2,1)S(1)}, bf16[64,2048]{1,0:T(8,128)(2,1)}, u32[]{:S(2)}) copy-start(bf16[64,2048]{1,0:T(8,128)(2,1)} %get-tuple-element.31) | copy-start | bytes 786436
  82.7 8.4 %collective-permute-start.10 = (bf16[64,4096]{1,0:T(8,128)(2,1)S(1)}, bf16[64,4096]{1,0:T(8,128)(2,1)S(1)}, u32[]{:S(2)}, u32[]{:S(2)}) collective-permute-start(bf16[64,4096]{1,0:T(8,128)(2,1)S(1)} %pad_maximum_fusion.2), channel_id=1, source_target_pairs={{0,1},{1,0},{2,3},{3,2},{4,5},{5,4},{6,7},{7,6},{8,9},{9,8},{10,11... | collective-permute-start | bytes 1572872 | tf_op jit(solution)/shard_map/ppermute | solution.py:86

commit v6 on v5

--- a/solution.py
+++ b/solution.py
@@ -117,9 +117,7 @@
     return lax.dot_general(a, b, dims, preferred_element_type=jnp.float32)
 
 
-def attention_kernel(
-    q_ref, k_ref, v_ref, g_ref, s_ref, mask_ref, att_ref, dq_ref, dkw_ref, dvw_ref, ds_ref
-):
+def forward_kernel(q_ref, k_ref, v_ref, g_ref, s_ref, mask_ref, att_ref, stats_ref, dqs_ref, ds_ref):
     j = pl.program_id(1)
     scale = 1.0 / math.sqrt(HEAD_DIM)
     f32 = jnp.float32
@@ -144,16 +142,14 @@
     log_norm = top + jnp.log(total)
     pw = jnp.where(causal, jnp.exp(sw - log_norm), 0.0)
     ps = jnp.where(allowed, jnp.exp(ss - log_norm), 0.0)
-    pw_low = pw.astype(bf16)
     ps_low = ps.astype(bf16)
-    att = (mm(pw_low, v) + mm(ps_low, sv)).astype(bf16)
+    att = (mm(pw.astype(bf16), v) + mm(ps_low, sv)).astype(bf16)
     att_ref[...] = att
     delta = jnp.sum(g.astype(f32) * att.astype(f32), axis=1, keepdims=True)
-    dsw = (pw * (mm(g, v, trans_b=True) - delta)).astype(bf16)
+    stats_ref[:, :HEAD_DIM] = jnp.broadcast_to(log_norm, (BLOCK, HEAD_DIM))
+    stats_ref[:, HEAD_DIM:] = jnp.broadcast_to(delta, (BLOCK, HEAD_DIM))
     dss = (ps * (mm(g, sv, trans_b=True) - delta)).astype(bf16)
-    dq_ref[...] = ((mm(dsw, k) + mm(dss, sk)) * scale).astype(bf16)
-    dkw_ref[...] = mm(dsw, q, trans_a=True) * scale
-    dvw_ref[...] = mm(pw_low, g, trans_a=True)
+    dqs_ref[...] = mm(dss, sk) * scale
     dks = mm(dss, q, trans_a=True) * scale
     dvs = mm(ps_low, g, trans_a=True)
 
@@ -168,33 +164,77 @@
         ds_ref[:, HEAD_DIM:] += dvs
 
 
-def attention(q, k, v, g, summary, mask):
+def window_kernel(q_ref, k_ref, v_ref, g_ref, stats_ref, dqs_ref, dq_ref, dkw_ref, dvw_ref):
+    scale = 1.0 / math.sqrt(HEAD_DIM)
+    bf16 = jnp.bfloat16
+    q = q_ref[...]
+    k = k_ref[...]
+    v = v_ref[...]
+    g = g_ref[...]
+    log_norm = stats_ref[:, 0:1]
+    delta = stats_ref[:, HEAD_DIM:HEAD_DIM + 1]
+    row = lax.broadcasted_iota(jnp.int32, (BLOCK, BLOCK), 0)
+    col = lax.broadcasted_iota(jnp.int32, (BLOCK, BLOCK), 1)
+    causal = row >= col
+    sw = mm(q, k, trans_b=True) * scale
+    pw = jnp.where(causal, jnp.exp(jnp.where(causal, sw, MASKED_SCORE) - log_norm), 0.0)
+    dsw = (pw * (mm(g, v, trans_b=True) - delta)).astype(bf16)
+    dq_ref[...] = (mm(dsw, k) * scale + dqs_ref[...]).astype(bf16)
+    dkw_ref[...] = mm(dsw, q, trans_a=True) * scale
+    dvw_ref[...] = mm(pw.astype(bf16), g, trans_a=True)
+
+
+def attention_forward(q, k, v, g, summary, mask):
     rows, half = q.shape
     heads = half // HEAD_DIM
     nb = rows // BLOCK
     count = summary.shape[0]
     tile = pl.BlockSpec((BLOCK, HEAD_DIM), lambda h, j: (j, h))
+    wide = pl.BlockSpec((BLOCK, 2 * HEAD_DIM), lambda h, j: (j, h))
     pair = pl.BlockSpec((count, 2 * HEAD_DIM), lambda h, j: (0, h))
-    bf16 = jnp.bfloat16
-    f32 = jnp.float32
-    flops = 2 * rows * heads * HEAD_DIM * (BLOCK + count) * 6
+    f32 = jnp.float32
     return pl.pallas_call(
-        attention_kernel,
+        forward_kernel,
         grid=(heads, nb),
         in_specs=[tile, tile, tile, tile, pair, pl.BlockSpec((8, count), lambda h, j: (j, 0))],
-        out_specs=[tile, tile, tile, tile, pair],
+        out_specs=[tile, wide, tile, pair],
         out_shape=[
-            jax.ShapeDtypeStruct((rows, half), bf16),
-            jax.ShapeDtypeStruct((rows, half), bf16),
-            jax.ShapeDtypeStruct((rows, half), f32),
+            jax.ShapeDtypeStruct((rows, half), jnp.bfloat16),
+            jax.ShapeDtypeStruct((rows, 2 * half), f32),
             jax.ShapeDtypeStruct((rows, half), f32),
             jax.ShapeDtypeStruct((count, 2 * half), f32),
         ],
         cost_estimate=pl.CostEstimate(
-            flops=flops, transcendentals=rows * heads * (BLOCK + count) * 2,
-            bytes_accessed=rows * half * 2 * 8 + count * half * 2 * 6,
+            flops=2 * rows * half * (BLOCK * 2 + count * 5),
+            transcendentals=rows * heads * (BLOCK + count) * 2,
+            bytes_accessed=rows * half * 2 * 10 + count * half * 2 * 6,
         ),
     )(q, k, v, g, summary, mask)
+
+
+def attention_window(q, k, v, g, stats, dq_summary):
+    rows, half = q.shape
+    heads = half // HEAD_DIM
+    nb = rows // BLOCK
+    tile = pl.BlockSpec((BLOCK, HEAD_DIM), lambda h, j: (j, h))
+    wide = pl.BlockSpec((BLOCK, 2 * HEAD_DIM), lambda h, j: (j, h))
+    f32 = jnp.float32
+    return pl.pallas_call(
+        window_kernel,
+        grid=(heads, nb),
+        in_specs=[tile, tile, tile, tile, wide, tile],
+        out_specs=[tile, tile, tile],
+        out_shape=[
+            jax.ShapeDtypeStruct((rows, half), jnp.bfloat16),
+            jax.ShapeDtypeStruct((rows, half), f32),
+            jax.ShapeDtypeStruct((rows, half), f32),
+        ],
+        cost_estimate=pl.CostEstimate(
+            flops=2 * rows * half * BLOCK * 5,
+            transcendentals=rows * heads * BLOCK,
+            bytes_accessed=rows * half * 2 * 14,
+        ),
+    )(q, k, v, g, stats, dq_summary)
 
 
 def body(queries, key_rows, value_rows, out_grad, summary_columns):
@@ -227,10 +267,11 @@
     mask = (key_block[None, :] < query_block[:, None]).astype(jnp.int32)
     mask = jnp.repeat(mask, 8, axis=0)
 
-    attended, dq, dkw, dvw, parts = attention(qb, kb, vb, gb, all_sum, mask)
+    attended, stats, dq_summary, parts = attention_forward(qb, kb, vb, gb, all_sum, mask)
+    own_grad = reduce_blocks(parts, core).reshape(-1, heads, 2, HEAD_DIM)
+    dq, dkw, dvw = attention_window(qb, kb, vb, gb, stats, dq_summary)
     att_tok, dq_tok = to_token_layout([attended, dq], core)
 
-    own_grad = reduce_blocks(parts, core).reshape(-1, heads, 2, HEAD_DIM)
     dk = dkw.at[positions].add(own_grad[:, :, 0].reshape(-1, half))
     dv = dvw.at[positions].add(own_grad[:, :, 1].reshape(-1, half))
     dk_tok, dv_tok = to_token_layout([dk.astype(jnp.bfloat16), dv.astype(jnp.bfloat16)], core)

time: 94.7 us -> 105 us (1.11)
  Pallas kernels: 15.7 us -> 28.2 us
  waiting for transfers between devices: 29.2 us -> 24.5 us
  local copies, waits for them, and re-layouts: 7.66 us -> 9.44 us
    pallas_call x1 -> x2, Pallas kernels: 15.7 us -> 28.2 us  [the longest x1 15.4 us: attention_forward(): pl.pallas_call(forward_kernel, grid=(heads, nb), in_specs=[tile, tile, ti...]
    ppermute x8, waiting for transfers between devices: 26.9 us -> 22.3 us  [exchange(): return lax.ppermute(x, ('seq', 'hx', 'hc'), pairs)]
    dynamic_slice x4, local copies, waits for them, and re-layouts: 0.18 us -> 2.67 us  [to_token_layout(): mine = [lax.dynamic_slice_in_dim(a, core * rows, rows, 0) for a in arrays]]
  transfers between devices with their start and end apart: 11 -> 11, of which waited for: 8 -> 7; matrix products, arithmetic and copies ran while one was open for 5% -> 6% of each run, Pallas kernels for 0% -> 12%
where the time goes in v6:
time: 105 us; the launch traced here: 103 us
  Pallas kernels  28.2 us (27%)
  starting transfers between devices  27.6 us (26%)
  waiting for transfers between devices  24.5 us (23%)
  other arithmetic  11.8 us (11%)
  local copies, waits for them, and re-layouts  9.44 us (9%)
    ppermute x8, waiting for transfers between devices, exchange(): return lax.ppermute(x, ('seq', 'hx', 'hc'), pairs)  22.3 us
    ppermute x8, starting transfers between devices, exchange(): return lax.ppermute(x, ('seq', 'hx', 'hc'), pairs)  15.4 us
    pallas_call x1, Pallas kernels, attention_forward(): pl.pallas_call(forward_kernel, grid=(heads, nb), in_specs=[tile, tile, ti...  15.4 us
    pallas_call x1, Pallas kernels, attention_window(): pl.pallas_call(window_kernel, grid=(heads, nb), in_specs=[tile, tile, til...  12.8 us
    ppermute x3, starting transfers between devices, swap_with_partner(): return lax.ppermute(x, 'hc', [(0, 1), (1, 0)])  12.2 us
    select_n x4, other arithmetic, to_token_layout(): jnp.where(core == 0, jnp.concatenate([m, r], 1), jnp.concatenate([r, m], 1))  3.66 us
    dynamic_slice x4, local copies, waits for them, and re-layouts, to_token_layout(): mine = [lax.dynamic_slice_in_dim(a, core * rows, rows, 0) for a in arrays]  2.67 us
    ppermute x3, waiting for transfers between devices, swap_with_partner(): return lax.ppermute(x, 'hc', [(0, 1), (1, 0)])  2.22 us
  transfers between devices with their start and end apart: 11, of which 7 were waited for; matrix products, arithmetic and copies ran while one was open for 6% of the time, Pallas kernels for 12%

profile of v6, /device:TPU:1, one launch (start us, length us, event | category | flops | bytes accessed | tf_op | source)
XLA Modules:
  0.0 102.6 jit_solution(11217217461476914078)
XLA Ops:
  0.7 1.3 %constant_dynamic-slice_fusion.11 = (bf16[64,2048]{1,0:T(8,128)(2,1)S(1)}, bf16[64,2048]{1,0:T(8,128)(2,1)S(1)}, bf16[64,2048]{1,0:T(8,128)(2,1)S(1)}, bf16[64,2048]{1,0:T(8,128)(2,1)S(1)}) fusion(bf16[64,4096]{1,0:T(8,128)(2,1)} %param.8, s32[]{:T(128)S(6)} %select_n.293, s32[]{:T(128)S(6)} %select_n.294, bf16[64,4096]{1,0:T(8,128)(2,1)} %param.7), kind=kLoop, calls=%fused_computation.63 | loop fusion | bytes 2097160 | tf_op jit(solution)/shard_map/dynamic_slice | solution.py:92
  2.9 2.2 %collective-permute-done = bf16[64,8192]{1,0:T(8,128)(2,1)S(1)} collective-permute-done((bf16[64,8192]{1,0:T(8,128)(2,1)S(1)}, bf16[64,8192]{1,0:T(8,128)(2,1)S(1)}, u32[]{:S(2)}, u32[]{:S(2)}) %collective-permute-start) | collective-permute-done | bytes 1048608 | tf_op jit(solution)/shard_map/ppermute | solution.py:86
  7.0 3.5 %collective-permute-start.1 = (bf16[1,8,4096]{2,1,0:T(8,128)(2,1)S(1)}, bf16[1,8,4096]{2,1,0:T(8,128)(2,1)S(1)}, u32[]{:S(2)}, u32[]{:S(2)}) collective-permute-start(bf16[1,8,4096]{2,1,0:T(8,128)(2,1)S(1)} %broadcast_in_dim_reshape.3), channel_id=1, source_target_pairs={{0,16},{1,17},{2,18},{3,19},{4,20},{5,21},{6,22},{7,23},{8,24},{9,... | collective-permute-start | bytes 196616 | tf_op jit(solution)/shard_map/ppermute | solution.py:41
  10.5 2.1 %collective-permute-done.1 = bf16[1,8,4096]{2,1,0:T(8,128)(2,1)S(1)} collective-permute-done((bf16[1,8,4096]{2,1,0:T(8,128)(2,1)S(1)}, bf16[1,8,4096]{2,1,0:T(8,128)(2,1)S(1)}, u32[]{:S(2)}, u32[]{:S(2)}) %collective-permute-start.1) | collective-permute-done | bytes 65568 | tf_op jit(solution)/shard_map/ppermute | solution.py:41
  12.7 2.3 %collective-permute-start.2 = (bf16[2,8,4096]{2,1,0:T(8,128)(2,1)S(1)}, bf16[2,8,4096]{2,1,0:T(8,128)(2,1)S(1)}, u32[]{:S(2)}, u32[]{:S(2)}) collective-permute-start(bf16[2,8,4096]{2,1,0:T(8,128)(2,1)S(1)} %maximum_select_fusion.14), channel_id=1, source_target_pairs={{0,8},{1,9},{2,10},{3,11},{4,12},{5,13},{6,14},{7,15},{8,0},{9,1},... | collective-permute-start | bytes 393224 | tf_op jit(solution)/shard_map/ppermute | solution.py:41
  15.0 2.3 %collective-permute-done.2 = bf16[2,8,4096]{2,1,0:T(8,128)(2,1)S(1)} collective-permute-done((bf16[2,8,4096]{2,1,0:T(8,128)(2,1)S(1)}, bf16[2,8,4096]{2,1,0:T(8,128)(2,1)S(1)}, u32[]{:S(2)}, u32[]{:S(2)}) %collective-permute-start.2) | collective-permute-done | bytes 131104 | tf_op jit(solution)/shard_map/ppermute | solution.py:41
  17.3 1.3 %collective-permute-start.3 = (bf16[4,8,4096]{2,1,0:T(8,128)(2,1)S(1)}, bf16[4,8,4096]{2,1,0:T(8,128)(2,1)S(1)}, u32[]{:S(2)}, u32[]{:S(2)}) collective-permute-start(bf16[4,8,4096]{2,1,0:T(8,128)(2,1)S(1)} %bitcast.108), channel_id=1, source_target_pairs={{0,4},{1,3},{2,6},{3,1},{4,0},{5,7},{6,2},{7,5},{8,12},{9,11},{10,... | collective-permute-start | bytes 786440 | tf_op jit(solution)/shard_map/ppermute | solution.py:41
  19.5 3.1 %collective-permute-done.3 = bf16[4,8,4096]{2,1,0:T(8,128)(2,1)S(1)} collective-permute-done((bf16[4,8,4096]{2,1,0:T(8,128)(2,1)S(1)}, bf16[4,8,4096]{2,1,0:T(8,128)(2,1)S(1)}, u32[]{:S(2)}, u32[]{:S(2)}) %collective-permute-start.3) | collective-permute-done | bytes 262176 | tf_op jit(solution)/shard_map/ppermute | solution.py:41
  22.7 1.3 %collective-permute-start.4 = (bf16[8,8,4096]{2,1,0:T(8,128)(2,1)S(1)}, bf16[8,8,4096]{2,1,0:T(8,128)(2,1)S(1)}, u32[]{:S(2)}, u32[]{:S(2)}) collective-permute-start(bf16[8,8,4096]{2,1,0:T(8,128)(2,1)S(1)} %bitcast.113), channel_id=1, source_target_pairs={{0,2},{1,5},{2,0},{3,7},{4,6},{5,1},{6,4},{7,3},{8,10},{9,13},{10,... | collective-permute-start | bytes 1572872 | tf_op jit(solution)/shard_map/ppermute | solution.py:41
  25.0 6.7 %collective-permute-done.4 = bf16[8,8,4096]{2,1,0:T(8,128)(2,1)S(1)} collective-permute-done((bf16[8,8,4096]{2,1,0:T(8,128)(2,1)S(1)}, bf16[8,8,4096]{2,1,0:T(8,128)(2,1)S(1)}, u32[]{:S(2)}, u32[]{:S(2)}) %collective-permute-start.4) | collective-permute-done | bytes 524320 | tf_op jit(solution)/shard_map/ppermute | solution.py:41
  31.9 1.2 %bitcast_select_fusion.s_ref = bf16[128,4096]{1,0:T(8,128)(2,1)} fusion(bf16[4,2,2,8,4096]{4,3,1,2,0:T(8,128)(2,1)S(1)} %maximum_select_fusion, bf16[8,2,8,4096]{3,2,1,0:T(8,128)(2,1)S(1)} %maximum_select_fusion.1, pred[]{:T(512)S(6)} %eq.13), kind=kLoop, calls=%fused_computation.8 | loop fusion | flops 524288 | bytes 3145729 | tf_op jit(solution)/shard_map/jit(_where)/select_n | solution.py:49
  33.7 15.4 %shard_map.84 = (bf16[128,2048]{1,0:T(8,128)(2,1)}, f32[128,4096]{1,0:T(8,128)}, f32[128,2048]{1,0:T(8,128)}, f32[128,4096]{1,0:T(8,128)}) custom-call(bf16[128,2048]{1,0:T(8,128)(2,1)} %maximum_select_fusion.2.q_ref, bf16[128,2048]{1,0:T(8,128)(2,1)} %copy-done.2, bf16[128,2048]{1,0:T(8,128)(2,1)} %copy-done.1, ...), custom_call_target="tpu_custom_call" | custom-call | flops 469762048 | bytes 8388608 | tf_op jit(solution)/shard_map/pallas_call | solution.py:196
  49.2 1.9 %copy.68 = f32[4,2,2,8,4096]{4,3,1,0,2:T(8,128)S(1)} copy(f32[4,2,2,8,4096]{4,3,1,2,0:T(8,128)} %bitcast.101) | data formatting | bytes 4194304 | tf_op jit(solution)/shard_map/transpose | solution.py:48
  51.7 1.5 %collective-permute-start.6 = (bf16[8,8,4096]{2,1,0:T(8,128)(2,1)S(1)}, bf16[8,8,4096]{2,1,0:T(8,128)(2,1)}, u32[]{:S(2)}, u32[]{:S(2)}) collective-permute-start(bf16[8,8,4096]{2,1,0:T(8,128)(2,1)S(1)} %fusion), channel_id=1, source_target_pairs={{0,2},{1,5},{2,0},{3,7},{4,6},{5,1},{6,4},{7,3},{8,10},{9,13},{10,... | collective-permute-start | bytes 1572872 | tf_op jit(solution)/shard_map/ppermute | solution.py:41
  54.0 6.3 %collective-permute-done.6 = bf16[8,8,4096]{2,1,0:T(8,128)(2,1)} collective-permute-done((bf16[8,8,4096]{2,1,0:T(8,128)(2,1)S(1)}, bf16[8,8,4096]{2,1,0:T(8,128)(2,1)}, u32[]{:S(2)}, u32[]{:S(2)}) %collective-permute-start.6) | collective-permute-done | bytes 524320 | tf_op jit(solution)/shard_map/ppermute | solution.py:41
  60.2 1.2 %bitcast_add_fusion = f32[8,8,4096]{2,1,0:T(8,128)S(1)} fusion(bf16[8,8,4096]{2,1,0:T(8,128)(2,1)} %collective-permute-done.6, f32[8,2,8,4096]{3,2,0,1:T(8,128)S(1)} %copy_select_fusion, pred[]{:T(512)S(6)} %eq.14), kind=kLoop, calls=%fused_computation.9 | loop fusion | flops 786432 | bytes 3670017 | tf_op jit(solution)/shard_map/add | solution.py:81
  61.4 1.5 %collective-permute-start.7 = (bf16[4,8,4096]{2,1,0:T(8,128)(2,1)S(1)}, bf16[4,8,4096]{2,1,0:T(8,128)(2,1)S(1)}, u32[]{:S(2)}, u32[]{:S(2)}) collective-permute-start(bf16[4,8,4096]{2,1,0:T(8,128)(2,1)S(1)} %fusion.3), channel_id=1, source_target_pairs={{0,4},{1,3},{2,6},{3,1},{4,0},{5,7},{6,2},{7,5},{8,12},{9,11},{10,... | collective-permute-start | bytes 786440 | tf_op jit(solution)/shard_map/ppermute | solution.py:41
  62.9 12.8 %shard_map.85 = (bf16[128,2048]{1,0:T(8,128)(2,1)}, f32[128,2048]{1,0:T(8,128)}, f32[128,2048]{1,0:T(8,128)}) custom-call(bf16[128,2048]{1,0:T(8,128)(2,1)} %maximum_select_fusion.2.q_ref, bf16[128,2048]{1,0:T(8,128)(2,1)} %copy-done.2, bf16[128,2048]{1,0:T(8,128)(2,1)} %copy-done.1, bf16[128,2048]{1,0:T(8,128)(2,1)} %maximum_select_fusion.5.g_ref, ...), custom_call_target="tpu_custom_call" | custom-call | flops 335544320 | bytes 7340032 | tf_op jit(solution)/shard_map/pallas_call | solution.py:222
  75.7 1.8 %constant_dynamic-slice_fusion.4 = (bf16[64,2048]{1,0:T(8,128)(2,1)}, bf16[64,2048]{1,0:T(8,128)(2,1)S(1)}) fusion(bf16[128,2048]{1,0:T(8,128)(2,1)} %get-tuple-element.15, s32[]{:T(128)S(6)} %select_n.323, s32[]{:T(128)S(6)} %select_n.324), kind=kLoop, calls=%fused_computation.56 | loop fusion | bytes 1048584 | tf_op jit(solution)/shard_map/dynamic_slice | solution.py:105
  77.6 1.8 %collective-permute-start.8 = (bf16[2,8,4096]{2,1,0:T(8,128)(2,1)S(1)}, bf16[2,8,4096]{2,1,0:T(8,128)(2,1)S(1)}, u32[]{:S(2)}, u32[]{:S(2)}) collective-permute-start(bf16[2,8,4096]{2,1,0:T(8,128)(2,1)S(1)} %fusion.7), channel_id=1, source_target_pairs={{0,8},{1,9},{2,10},{3,11},{4,12},{5,13},{6,14},{7,15},{8,0},{9,1},... | collective-permute-start | bytes 393224 | tf_op jit(solution)/shard_map/ppermute | solution.py:41
  79.5 5.4 %collective-permute-start.5 = (bf16[64,4096]{1,0:T(8,128)(2,1)S(1)}, bf16[64,4096]{1,0:T(8,128)(2,1)S(1)}, u32[]{:S(2)}, u32[]{:S(2)}) collective-permute-start(bf16[64,4096]{1,0:T(8,128)(2,1)S(1)} %pad_maximum_fusion.1), channel_id=1, source_target_pairs={{0,1},{1,0},{2,3},{3,2},{4,5},{5,4},{6,7},{7,6},{8,9},{9,8},{10,11... | collective-permute-start | bytes 1572872 | tf_op jit(solution)/shard_map/ppermute | solution.py:86
  85.0 2.3 %collective-permute-start.9 = (bf16[1,8,4096]{2,1,0:T(8,128)(2,1)S(1)}, bf16[1,8,4096]{2,1,0:T(8,128)(2,1)S(1)}, u32[]{:S(2)}, u32[]{:S(2)}) collective-permute-start(bf16[1,8,4096]{2,1,0:T(8,128)(2,1)S(1)} %fusion.8), channel_id=1, source_target_pairs={{0,16},{1,17},{2,18},{3,19},{4,20},{5,21},{6,22},{7,23},{8,24},{9,... | collective-permute-start | bytes 196616 | tf_op jit(solution)/shard_map/ppermute | solution.py:41
  87.4 1.8 %collective-permute-done.9 = bf16[1,8,4096]{2,1,0:T(8,128)(2,1)S(1)} collective-permute-done((bf16[1,8,4096]{2,1,0:T(8,128)(2,1)S(1)}, bf16[1,8,4096]{2,1,0:T(8,128)(2,1)S(1)}, u32[]{:S(2)}, u32[]{:S(2)}) %collective-permute-start.9) | collective-permute-done | bytes 65568 | tf_op jit(solution)/shard_map/ppermute | solution.py:41
  92.2 6.6 %collective-permute-start.10 = (bf16[64,4096]{1,0:T(8,128)(2,1)S(1)}, bf16[64,4096]{1,0:T(8,128)(2,1)S(1)}, u32[]{:S(2)}, u32[]{:S(2)}) collective-permute-start(bf16[64,4096]{1,0:T(8,128)(2,1)S(1)} %pad_maximum_fusion.2), channel_id=1, source_target_pairs={{0,1},{1,0},{2,3},{3,2},{4,5},{5,4},{6,7},{7,6},{8,9},{9,8},{10,11... | collective-permute-start | bytes 1572872 | tf_op jit(solution)/shard_map/ppermute | solution.py:86
  (80 shorter events, 13.9 us)
Async XLA Ops:
  0.6 1.4 %copy-start.8 = (bf16[64,4096]{1,0:T(8,128)(2,1)S(1)}, bf16[64,4096]{1,0:T(8,128)(2,1)}, u32[]{:S(2)}) copy-start(bf16[64,4096]{1,0:T(8,128)(2,1)} %param.10) | copy-start | bytes 1572868
  0.6 1.5 %copy-start.9 = (bf16[64,4096]{1,0:T(8,128)(2,1)S(1)}, bf16[64,4096]{1,0:T(8,128)(2,1)}, u32[]{:S(2)}) copy-start(bf16[64,4096]{1,0:T(8,128)(2,1)} %param.9) | copy-start | bytes 1572868
  2.1 0.7 copy-start.10
  2.3 2.7 %collective-permute-start = (bf16[64,8192]{1,0:T(8,128)(2,1)S(1)}, bf16[64,8192]{1,0:T(8,128)(2,1)S(1)}, u32[]{:S(2)}, u32[]{:S(2)}) collective-permute-start(bf16[64,8192]{1,0:T(8,128)(2,1)S(1)} %pad_maximum_fusion), channel_id=1, source_target_pairs={{0,1},{1,0},{2,3},{3,2},{4,5},{5,4},{6,7},{7,6},{8,9},{9,8},{10,11... | collective-permute-start | bytes 3145736 | tf_op jit(solution)/shard_map/ppermute | solution.py:86
  5.3 14.2 %copy-start.1 = (bf16[128,2048]{1,0:T(8,128)(2,1)}, bf16[128,2048]{1,0:T(8,128)(2,1)S(1)}, u32[]{:S(2)}) copy-start(bf16[128,2048]{1,0:T(8,128)(2,1)S(1)} %maximum_select_fusion.4.v_ref) | copy-start | bytes 1572868
  6.0 16.7 %copy-start.2 = (bf16[128,2048]{1,0:T(8,128)(2,1)}, bf16[128,2048]{1,0:T(8,128)(2,1)S(1)}, u32[]{:S(2)}) copy-start(bf16[128,2048]{1,0:T(8,128)(2,1)S(1)} %maximum_select_fusion.3.k_ref) | copy-start | bytes 1572868
  7.0 5.7 %collective-permute-start.1 = (bf16[1,8,4096]{2,1,0:T(8,128)(2,1)S(1)}, bf16[1,8,4096]{2,1,0:T(8,128)(2,1)S(1)}, u32[]{:S(2)}, u32[]{:S(2)}) collective-permute-start(bf16[1,8,4096]{2,1,0:T(8,128)(2,1)S(1)} %broadcast_in_dim_reshape.3), channel_id=1, source_target_pairs={{0,16},{1,17},{2,18},{3,19},{4,20},{5,21},{6,22},{7,23},{8,24},{9,... | collective-permute-start | bytes 196616 | tf_op jit(solution)/shard_map/ppermute | solution.py:41
  12.7 4.6 %collective-permute-start.2 = (bf16[2,8,4096]{2,1,0:T(8,128)(2,1)S(1)}, bf16[2,8,4096]{2,1,0:T(8,128)(2,1)S(1)}, u32[]{:S(2)}, u32[]{:S(2)}) collective-permute-start(bf16[2,8,4096]{2,1,0:T(8,128)(2,1)S(1)} %maximum_select_fusion.14), channel_id=1, source_target_pairs={{0,8},{1,9},{2,10},{3,11},{4,12},{5,13},{6,14},{7,15},{8,0},{9,1},... | collective-permute-start | bytes 393224 | tf_op jit(solution)/shard_map/ppermute | solution.py:41
  17.3 5.3 %collective-permute-start.3 = (bf16[4,8,4096]{2,1,0:T(8,128)(2,1)S(1)}, bf16[4,8,4096]{2,1,0:T(8,128)(2,1)S(1)}, u32[]{:S(2)}, u32[]{:S(2)}) collective-permute-start(bf16[4,8,4096]{2,1,0:T(8,128)(2,1)S(1)} %bitcast.108), channel_id=1, source_target_pairs={{0,4},{1,3},{2,6},{3,1},{4,0},{5,7},{6,2},{7,5},{8,12},{9,11},{10,... | collective-permute-start | bytes 786440 | tf_op jit(solution)/shard_map/ppermute | solution.py:41
  22.7 8.9 %collective-permute-start.4 = (bf16[8,8,4096]{2,1,0:T(8,128)(2,1)S(1)}, bf16[8,8,4096]{2,1,0:T(8,128)(2,1)S(1)}, u32[]{:S(2)}, u32[]{:S(2)}) collective-permute-start(bf16[8,8,4096]{2,1,0:T(8,128)(2,1)S(1)} %bitcast.113), channel_id=1, source_target_pairs={{0,2},{1,5},{2,0},{3,7},{4,6},{5,1},{6,4},{7,3},{8,10},{9,13},{10,... | collective-permute-start | bytes 1572872 | tf_op jit(solution)/shard_map/ppermute | solution.py:41
  49.1 2.2 %copy-start = (f32[128,4096]{1,0:T(8,128)S(1)}, f32[128,4096]{1,0:T(8,128)}, u32[]{:S(2)}) copy-start(f32[128,4096]{1,0:T(8,128)} %get-tuple-element.17) | copy-start | bytes 6291460
  51.4 1.8 %copy-start.7 = (bf16[128,2048]{1,0:T(8,128)(2,1)S(1)}, bf16[128,2048]{1,0:T(8,128)(2,1)}, u32[]{:S(2)}) copy-start(bf16[128,2048]{1,0:T(8,128)(2,1)} %get-tuple-element.12) | copy-start | bytes 1572868
  51.7 8.5 %collective-permute-start.6 = (bf16[8,8,4096]{2,1,0:T(8,128)(2,1)S(1)}, bf16[8,8,4096]{2,1,0:T(8,128)(2,1)}, u32[]{:S(2)}, u32[]{:S(2)}) collective-permute-start(bf16[8,8,4096]{2,1,0:T(8,128)(2,1)S(1)} %fusion), channel_id=1, source_target_pairs={{0,2},{1,5},{2,0},{3,7},{4,6},{5,1},{6,4},{7,3},{8,10},{9,13},{10,... | collective-permute-start | bytes 1572872 | tf_op jit(solution)/shard_map/ppermute | solution.py:41
  61.4 16.1 %collective-permute-start.7 = (bf16[4,8,4096]{2,1,0:T(8,128)(2,1)S(1)}, bf16[4,8,4096]{2,1,0:T(8,128)(2,1)S(1)}, u32[]{:S(2)}, u32[]{:S(2)}) collective-permute-start(bf16[4,8,4096]{2,1,0:T(8,128)(2,1)S(1)} %fusion.3), channel_id=1, source_target_pairs={{0,4},{1,3},{2,6},{3,1},{4,0},{5,7},{6,2},{7,5},{8,12},{9,11},{10,... | collective-permute-start | bytes 786440 | tf_op jit(solution)/shard_map/ppermute | solution.py:41
  75.7 3.7 %copy-start.6 = (bf16[64,2048]{1,0:T(8,128)(2,1)S(1)}, bf16[64,2048]{1,0:T(8,128)(2,1)}, u32[]{:S(2)}) copy-start(bf16[64,2048]{1,0:T(8,128)(2,1)} %get-tuple-element.38) | copy-start | bytes 786436
  77.6 7.3 %collective-permute-start.8 = (bf16[2,8,4096]{2,1,0:T(8,128)(2,1)S(1)}, bf16[2,8,4096]{2,1,0:T(8,128)(2,1)S(1)}, u32[]{:S(2)}, u32[]{:S(2)}) collective-permute-start(bf16[2,8,4096]{2,1,0:T(8,128)(2,1)S(1)} %fusion.7), channel_id=1, source_target_pairs={{0,8},{1,9},{2,10},{3,11},{4,12},{5,13},{6,14},{7,15},{8,0},{9,1},... | collective-permute-start | bytes 393224 | tf_op jit(solution)/shard_map/ppermute | solution.py:41
  79.5 10.2 %copy-start.4 = (f32[128,2048]{1,0:T(8,128)S(1)}, f32[128,2048]{1,0:T(8,128)}, u32[]{:S(2)}) copy-start(f32[128,2048]{1,0:T(8,128)} %get-tuple-element.16) | copy-start | bytes 3145732
  79.5 7.8 %collective-permute-start.5 = (bf16[64,4096]{1,0:T(8,128)(2,1)S(1)}, bf16[64,4096]{1,0:T(8,128)(2,1)S(1)}, u32[]{:S(2)}, u32[]{:S(2)}) collective-permute-start(bf16[64,4096]{1,0:T(8,128)(2,1)S(1)} %pad_maximum_fusion.1), channel_id=1, source_target_pairs={{0,1},{1,0},{2,3},{3,2},{4,5},{5,4},{6,7},{7,6},{8,9},{9,8},{10,11... | collective-permute-start | bytes 1572872 | tf_op jit(solution)/shard_map/ppermute | solution.py:86
  85.0 4.2 %collective-permute-start.9 = (bf16[1,8,4096]{2,1,0:T(8,128)(2,1)S(1)}, bf16[1,8,4096]{2,1,0:T(8,128)(2,1)S(1)}, u32[]{:S(2)}, u32[]{:S(2)}) collective-permute-start(bf16[1,8,4096]{2,1,0:T(8,128)(2,1)S(1)} %fusion.8), channel_id=1, source_target_pairs={{0,16},{1,17},{2,18},{3,19},{4,20},{5,21},{6,22},{7,23},{8,24},{9,... | collective-permute-start | bytes 196616 | tf_op jit(solution)/shard_map/ppermute | solution.py:41
  87.4 3.5 %copy-start.3 = (f32[128,2048]{1,0:T(8,128)S(1)}, f32[128,2048]{1,0:T(8,128)}, u32[]{:S(2)}) copy-start(f32[128,2048]{1,0:T(8,128)} %get-tuple-element.18) | copy-start | bytes 3145732
  92.0 6.9 %copy-start.5 = (bf16[64,2048]{1,0:T(8,128)(2,1)S(1)}, bf16[64,2048]{1,0:T(8,128)(2,1)}, u32[]{:S(2)}) copy-start(bf16[64,2048]{1,0:T(8,128)(2,1)} %get-tuple-element.33) | copy-start | bytes 786436
  92.2 8.5 %collective-permute-start.10 = (bf16[64,4096]{1,0:T(8,128)(2,1)S(1)}, bf16[64,4096]{1,0:T(8,128)(2,1)S(1)}, u32[]{:S(2)}, u32[]{:S(2)}) collective-permute-start(bf16[64,4096]{1,0:T(8,128)(2,1)S(1)} %pad_maximum_fusion.2), channel_id=1, source_target_pairs={{0,1},{1,0},{2,3},{3,2},{4,5},{5,4},{6,7},{7,6},{8,9},{9,8},{10,11... | collective-permute-start | bytes 1572872 | tf_op jit(solution)/shard_map/ppermute | solution.py:86

commit v7 on v5

--- a/solution.py
+++ b/solution.py
@@ -14,6 +14,7 @@
 
 MASKED_SCORE = -1e30
 GROUP = ("seq", "hx")
+HEADS_PER_STEP = 4
 
 
 def group_size():
@@ -118,54 +119,58 @@
 
 
 def attention_kernel(
-    q_ref, k_ref, v_ref, g_ref, s_ref, mask_ref, att_ref, dq_ref, dkw_ref, dvw_ref, ds_ref
+    q_all, k_all, v_all, g_all, s_all, mask_ref, att_all, dq_all, dkw_all, dvw_all, ds_all
 ):
     j = pl.program_id(1)
     scale = 1.0 / math.sqrt(HEAD_DIM)
     f32 = jnp.float32
     bf16 = jnp.bfloat16
-    q = q_ref[...]
-    k = k_ref[...]
-    v = v_ref[...]
-    g = g_ref[...]
-    sk = s_ref[:, :HEAD_DIM]
-    sv = s_ref[:, HEAD_DIM:]
     allowed = mask_ref[0:1, :] > 0
     row = lax.broadcasted_iota(jnp.int32, (BLOCK, BLOCK), 0)
     col = lax.broadcasted_iota(jnp.int32, (BLOCK, BLOCK), 1)
     causal = row >= col
-
-    sw = jnp.where(causal, mm(q, k, trans_b=True) * scale, MASKED_SCORE)
-    ss = jnp.where(allowed, mm(q, sk, trans_b=True) * scale, MASKED_SCORE)
-    top = jnp.maximum(jnp.max(sw, axis=1, keepdims=True), jnp.max(ss, axis=1, keepdims=True))
-    total = jnp.sum(jnp.exp(sw - top), axis=1, keepdims=True) + jnp.sum(
-        jnp.exp(ss - top), axis=1, keepdims=True
-    )
-    log_norm = top + jnp.log(total)
-    pw = jnp.where(causal, jnp.exp(sw - log_norm), 0.0)
-    ps = jnp.where(allowed, jnp.exp(ss - log_norm), 0.0)
-    pw_low = pw.astype(bf16)
-    ps_low = ps.astype(bf16)
-    att = (mm(pw_low, v) + mm(ps_low, sv)).astype(bf16)
-    att_ref[...] = att
-    delta = jnp.sum(g.astype(f32) * att.astype(f32), axis=1, keepdims=True)
-    dsw = (pw * (mm(g, v, trans_b=True) - delta)).astype(bf16)
-    dss = (ps * (mm(g, sv, trans_b=True) - delta)).astype(bf16)
-    dq_ref[...] = ((mm(dsw, k) + mm(dss, sk)) * scale).astype(bf16)
-    dkw_ref[...] = mm(dsw, q, trans_a=True) * scale
-    dvw_ref[...] = mm(pw_low, g, trans_a=True)
-    dks = mm(dss, q, trans_a=True) * scale
-    dvs = mm(ps_low, g, trans_a=True)
-
-    @pl.when(j == 0)
-    def _():
-        ds_ref[:, :HEAD_DIM] = dks
-        ds_ref[:, HEAD_DIM:] = dvs
-
-    @pl.when(j > 0)
-    def _():
-        ds_ref[:, :HEAD_DIM] += dks
-        ds_ref[:, HEAD_DIM:] += dvs
+    for hh in range(q_all.shape[1] // HEAD_DIM):
+        cols = pl.ds(hh * HEAD_DIM, HEAD_DIM)
+        q = q_all[:, cols]
+        k = k_all[:, cols]
+        v = v_all[:, cols]
+        g = g_all[:, cols]
+        sk = s_all[:, pl.ds(2 * hh * HEAD_DIM, HEAD_DIM)]
+        sv = s_all[:, pl.ds((2 * hh + 1) * HEAD_DIM, HEAD_DIM)]
+
+        sw = jnp.where(causal, mm(q, k, trans_b=True) * scale, MASKED_SCORE)
+        ss = jnp.where(allowed, mm(q, sk, trans_b=True) * scale, MASKED_SCORE)
+        top = jnp.maximum(jnp.max(sw, axis=1, keepdims=True), jnp.max(ss, axis=1, keepdims=True))
+        total = jnp.sum(jnp.exp(sw - top), axis=1, keepdims=True) + jnp.sum(
+            jnp.exp(ss - top), axis=1, keepdims=True
+        )
+        log_norm = top + jnp.log(total)
+        pw = jnp.where(causal, jnp.exp(sw - log_norm), 0.0)
+        ps = jnp.where(allowed, jnp.exp(ss - log_norm), 0.0)
+        pw_low = pw.astype(bf16)
+        ps_low = ps.astype(bf16)
+        att = (mm(pw_low, v) + mm(ps_low, sv)).astype(bf16)
+        att_all[:, cols] = att
+        delta = jnp.sum(g.astype(f32) * att.astype(f32), axis=1, keepdims=True)
+        dsw = (pw * (mm(g, v, trans_b=True) - delta)).astype(bf16)
+        dss = (ps * (mm(g, sv, trans_b=True) - delta)).astype(bf16)
+        dq_all[:, cols] = ((mm(dsw, k) + mm(dss, sk)) * scale).astype(bf16)
+        dkw_all[:, cols] = mm(dsw, q, trans_a=True) * scale
+        dvw_all[:, cols] = mm(pw_low, g, trans_a=True)
+        dks = mm(dss, q, trans_a=True) * scale
+        dvs = mm(ps_low, g, trans_a=True)
+        kcols = pl.ds(2 * hh * HEAD_DIM, HEAD_DIM)
+        vcols = pl.ds((2 * hh + 1) * HEAD_DIM, HEAD_DIM)
+
+        @pl.when(j == 0)
+        def _():
+            ds_all[:, kcols] = dks
+            ds_all[:, vcols] = dvs
+
+        @pl.when(j > 0)
+        def _():
+            ds_all[:, kcols] += dks
+            ds_all[:, vcols] += dvs
 
 
 def attention(q, k, v, g, summary, mask):
@@ -173,14 +178,15 @@
     heads = half // HEAD_DIM
     nb = rows // BLOCK
     count = summary.shape[0]
-    tile = pl.BlockSpec((BLOCK, HEAD_DIM), lambda h, j: (j, h))
-    pair = pl.BlockSpec((count, 2 * HEAD_DIM), lambda h, j: (0, h))
+    per_step = math.gcd(heads, HEADS_PER_STEP)
+    tile = pl.BlockSpec((BLOCK, per_step * HEAD_DIM), lambda h, j: (j, h))
+    pair = pl.BlockSpec((count, 2 * per_step * HEAD_DIM), lambda h, j: (0, h))
     bf16 = jnp.bfloat16
     f32 = jnp.float32
     flops = 2 * rows * heads * HEAD_DIM * (BLOCK + count) * 6
     return pl.pallas_call(
         attention_kernel,
-        grid=(heads, nb),
+        grid=(heads // per_step, nb),
         in_specs=[tile, tile, tile, tile, pair, pl.BlockSpec((8, count), lambda h, j: (j, 0))],
         out_specs=[tile, tile, tile, tile, pair],
         out_shape=[

time: 94.7 us -> 91.4 us (0.965)
  Pallas kernels: 15.7 us -> 13.3 us
    pallas_call x1, Pallas kernels: 15.7 us -> 13.3 us  [attention(): pl.pallas_call(attention_kernel, grid=(heads // per_step, nb), in_specs=[...]
where the time goes in v7:
time: 91.4 us; the launch traced here: 90.5 us
  waiting for transfers between devices  29.2 us (32%)
  starting transfers between devices  27.6 us (30%)
  Pallas kernels  13.3 us (15%)
  other arithmetic  11.8 us (13%)
  local copies, waits for them, and re-layouts  7.66 us (8%)
  between operations  1.04 us (1%)
    ppermute x8, waiting for transfers between devices, exchange(): return lax.ppermute(x, ('seq', 'hx', 'hc'), pairs)  27 us
    ppermute x8, starting transfers between devices, exchange(): return lax.ppermute(x, ('seq', 'hx', 'hc'), pairs)  15.2 us
    pallas_call x1, Pallas kernels, attention(): pl.pallas_call(attention_kernel, grid=(heads // per_step, nb), in_specs=[...  13.3 us
    ppermute x3, starting transfers between devices, swap_with_partner(): return lax.ppermute(x, 'hc', [(0, 1), (1, 0)])  12.4 us
    select_n x4, other arithmetic, to_token_layout(): jnp.where(core == 0, jnp.concatenate([m, r], 1), jnp.concatenate([r, m], 1))  3.66 us
    ppermute x3, waiting for transfers between devices, swap_with_partner(): return lax.ppermute(x, 'hc', [(0, 1), (1, 0)])  2.22 us
    select_n x4, other arithmetic, to_block_layout(): jnp.where(core == 0, jnp.concatenate([m, r], 0), jnp.concatenate([r, m], 0))  2.01 us
    transpose x1, local copies, waits for them, and re-layouts, swap_low_bits(): jnp.swapaxes(x.reshape((size // 4, 2, 2) + x.shape[1:]), 1, 2)  1.89 us
  transfers between devices with their start and end apart: 11, of which 8 were waited for; matrix products, arithmetic and copies ran while one was open for 5% of the time, Pallas kernels for 0%

profile of v7, /device:TPU:1, one launch (start us, length us, event | category | flops | bytes accessed | tf_op | source)
XLA Modules:
  0.0 90.5 jit_solution(13106946138172467646)
XLA Ops:
  0.7 1.3 %constant_dynamic-slice_fusion.11 = (bf16[64,2048]{1,0:T(8,128)(2,1)S(1)}, bf16[64,2048]{1,0:T(8,128)(2,1)S(1)}, bf16[64,2048]{1,0:T(8,128)(2,1)S(1)}, bf16[64,2048]{1,0:T(8,128)(2,1)S(1)}) fusion(bf16[64,4096]{1,0:T(8,128)(2,1)} %param.8, s32[]{:T(128)S(6)} %select_n.293, s32[]{:T(128)S(6)} %select_n.294, bf16[64,4096]{1,0:T(8,128)(2,1)} %param.7), kind=kLoop, calls=%fused_computation.63 | loop fusion | bytes 2097160 | tf_op jit(solution)/shard_map/dynamic_slice | solution.py:93
  2.9 2.2 %collective-permute-done = bf16[64,8192]{1,0:T(8,128)(2,1)S(1)} collective-permute-done((bf16[64,8192]{1,0:T(8,128)(2,1)S(1)}, bf16[64,8192]{1,0:T(8,128)(2,1)S(1)}, u32[]{:S(2)}, u32[]{:S(2)}) %collective-permute-start) | collective-permute-done | bytes 1048608 | tf_op jit(solution)/shard_map/ppermute | solution.py:87
  7.0 3.5 %collective-permute-start.1 = (bf16[1,8,4096]{2,1,0:T(8,128)(2,1)S(1)}, bf16[1,8,4096]{2,1,0:T(8,128)(2,1)S(1)}, u32[]{:S(2)}, u32[]{:S(2)}) collective-permute-start(bf16[1,8,4096]{2,1,0:T(8,128)(2,1)S(1)} %broadcast_in_dim_reshape.3), channel_id=1, source_target_pairs={{0,16},{1,17},{2,18},{3,19},{4,20},{5,21},{6,22},{7,23},{8,24},{9,... | collective-permute-start | bytes 196616 | tf_op jit(solution)/shard_map/ppermute | solution.py:42
  10.5 2.1 %collective-permute-done.1 = bf16[1,8,4096]{2,1,0:T(8,128)(2,1)S(1)} collective-permute-done((bf16[1,8,4096]{2,1,0:T(8,128)(2,1)S(1)}, bf16[1,8,4096]{2,1,0:T(8,128)(2,1)S(1)}, u32[]{:S(2)}, u32[]{:S(2)}) %collective-permute-start.1) | collective-permute-done | bytes 65568 | tf_op jit(solution)/shard_map/ppermute | solution.py:42
  12.7 2.3 %collective-permute-start.2 = (bf16[2,8,4096]{2,1,0:T(8,128)(2,1)S(1)}, bf16[2,8,4096]{2,1,0:T(8,128)(2,1)S(1)}, u32[]{:S(2)}, u32[]{:S(2)}) collective-permute-start(bf16[2,8,4096]{2,1,0:T(8,128)(2,1)S(1)} %maximum_select_fusion.14), channel_id=1, source_target_pairs={{0,8},{1,9},{2,10},{3,11},{4,12},{5,13},{6,14},{7,15},{8,0},{9,1},... | collective-permute-start | bytes 393224 | tf_op jit(solution)/shard_map/ppermute | solution.py:42
  15.0 2.3 %collective-permute-done.2 = bf16[2,8,4096]{2,1,0:T(8,128)(2,1)S(1)} collective-permute-done((bf16[2,8,4096]{2,1,0:T(8,128)(2,1)S(1)}, bf16[2,8,4096]{2,1,0:T(8,128)(2,1)S(1)}, u32[]{:S(2)}, u32[]{:S(2)}) %collective-permute-start.2) | collective-permute-done | bytes 131104 | tf_op jit(solution)/shard_map/ppermute | solution.py:42
  17.3 1.3 %collective-permute-start.3 = (bf16[4,8,4096]{2,1,0:T(8,128)(2,1)S(1)}, bf16[4,8,4096]{2,1,0:T(8,128)(2,1)S(1)}, u32[]{:S(2)}, u32[]{:S(2)}) collective-permute-start(bf16[4,8,4096]{2,1,0:T(8,128)(2,1)S(1)} %bitcast.108), channel_id=1, source_target_pairs={{0,4},{1,3},{2,6},{3,1},{4,0},{5,7},{6,2},{7,5},{8,12},{9,11},{10,... | collective-permute-start | bytes 786440 | tf_op jit(solution)/shard_map/ppermute | solution.py:42
  19.5 3.1 %collective-permute-done.3 = bf16[4,8,4096]{2,1,0:T(8,128)(2,1)S(1)} collective-permute-done((bf16[4,8,4096]{2,1,0:T(8,128)(2,1)S(1)}, bf16[4,8,4096]{2,1,0:T(8,128)(2,1)S(1)}, u32[]{:S(2)}, u32[]{:S(2)}) %collective-permute-start.3) | collective-permute-done | bytes 262176 | tf_op jit(solution)/shard_map/ppermute | solution.py:42
  22.7 1.3 %collective-permute-start.4 = (bf16[8,8,4096]{2,1,0:T(8,128)(2,1)S(1)}, bf16[8,8,4096]{2,1,0:T(8,128)(2,1)S(1)}, u32[]{:S(2)}, u32[]{:S(2)}) collective-permute-start(bf16[8,8,4096]{2,1,0:T(8,128)(2,1)S(1)} %bitcast.113), channel_id=1, source_target_pairs={{0,2},{1,5},{2,0},{3,7},{4,6},{5,1},{6,4},{7,3},{8,10},{9,13},{10,... | collective-permute-start | bytes 1572872 | tf_op jit(solution)/shard_map/ppermute | solution.py:42
  25.0 6.7 %collective-permute-done.4 = bf16[8,8,4096]{2,1,0:T(8,128)(2,1)S(1)} collective-permute-done((bf16[8,8,4096]{2,1,0:T(8,128)(2,1)S(1)}, bf16[8,8,4096]{2,1,0:T(8,128)(2,1)S(1)}, u32[]{:S(2)}, u32[]{:S(2)}) %collective-permute-start.4) | collective-permute-done | bytes 524320 | tf_op jit(solution)/shard_map/ppermute | solution.py:42
  31.9 1.2 %bitcast_select_fusion.s_all = bf16[128,4096]{1,0:T(8,128)(2,1)} fusion(bf16[4,2,2,8,4096]{4,3,1,2,0:T(8,128)(2,1)S(1)} %maximum_select_fusion, bf16[8,2,8,4096]{3,2,1,0:T(8,128)(2,1)S(1)} %maximum_select_fusion.1, pred[]{:T(512)S(6)} %eq.13), kind=kLoop, calls=%fused_computation.8 | loop fusion | flops 524288 | bytes 3145729 | tf_op jit(solution)/shard_map/jit(_where)/select_n | solution.py:50
  33.7 13.3 %shard_map.84 = (bf16[128,2048]{1,0:T(8,128)(2,1)}, bf16[128,2048]{1,0:T(8,128)(2,1)}, f32[128,2048]{1,0:T(8,128)}, f32[128,2048]{1,0:T(8,128)}, f32[128,4096]{1,0:T(8,128)}) custom-call(bf16[128,2048]{1,0:T(8,128)(2,1)} %maximum_select_fusion.2.q_all, bf16[128,2048]{1,0:T(8,128)(2,1)} %copy-done.2, bf16[128,2048]{1,0:T(8,128)(2,1)} %copy-done.1, ...), custom_call_target="tpu_custom_call" | custom-call | flops 805306368 | bytes 7340032 | tf_op jit(solution)/shard_map/pallas_call | solution.py:187
  47.1 1.9 %copy.68 = f32[4,2,2,8,4096]{4,3,1,0,2:T(8,128)S(1)} copy(f32[4,2,2,8,4096]{4,3,1,2,0:T(8,128)} %bitcast.101) | data formatting | bytes 4194304 | tf_op jit(solution)/shard_map/transpose | solution.py:49
  49.6 1.5 %collective-permute-start.6 = (bf16[8,8,4096]{2,1,0:T(8,128)(2,1)S(1)}, bf16[8,8,4096]{2,1,0:T(8,128)(2,1)}, u32[]{:S(2)}, u32[]{:S(2)}) collective-permute-start(bf16[8,8,4096]{2,1,0:T(8,128)(2,1)S(1)} %fusion), channel_id=1, source_target_pairs={{0,2},{1,5},{2,0},{3,7},{4,6},{5,1},{6,4},{7,3},{8,10},{9,13},{10,... | collective-permute-start | bytes 1572872 | tf_op jit(solution)/shard_map/ppermute | solution.py:42
  51.1 7.0 %collective-permute-done.6 = bf16[8,8,4096]{2,1,0:T(8,128)(2,1)} collective-permute-done((bf16[8,8,4096]{2,1,0:T(8,128)(2,1)S(1)}, bf16[8,8,4096]{2,1,0:T(8,128)(2,1)}, u32[]{:S(2)}, u32[]{:S(2)}) %collective-permute-start.6) | collective-permute-done | bytes 524320 | tf_op jit(solution)/shard_map/ppermute | solution.py:42
  58.1 1.2 %bitcast_add_fusion = f32[8,8,4096]{2,1,0:T(8,128)S(1)} fusion(bf16[8,8,4096]{2,1,0:T(8,128)(2,1)} %collective-permute-done.6, f32[8,2,8,4096]{3,2,0,1:T(8,128)S(1)} %copy_select_fusion, pred[]{:T(512)S(6)} %eq.14), kind=kLoop, calls=%fused_computation.9 | loop fusion | flops 786432 | bytes 3670017 | tf_op jit(solution)/shard_map/add | solution.py:82
  59.3 1.5 %collective-permute-start.7 = (bf16[4,8,4096]{2,1,0:T(8,128)(2,1)S(1)}, bf16[4,8,4096]{2,1,0:T(8,128)(2,1)S(1)}, u32[]{:S(2)}, u32[]{:S(2)}) collective-permute-start(bf16[4,8,4096]{2,1,0:T(8,128)(2,1)S(1)} %fusion.3), channel_id=1, source_target_pairs={{0,4},{1,3},{2,6},{3,1},{4,0},{5,7},{6,2},{7,5},{8,12},{9,11},{10,... | collective-permute-start | bytes 786440 | tf_op jit(solution)/shard_map/ppermute | solution.py:42
  60.9 4.7 %collective-permute-done.7 = bf16[4,8,4096]{2,1,0:T(8,128)(2,1)S(1)} collective-permute-done((bf16[4,8,4096]{2,1,0:T(8,128)(2,1)S(1)}, bf16[4,8,4096]{2,1,0:T(8,128)(2,1)S(1)}, u32[]{:S(2)}, u32[]{:S(2)}) %collective-permute-start.7) | collective-permute-done | bytes 262176 | tf_op jit(solution)/shard_map/ppermute | solution.py:42
  65.7 1.0 %collective-permute-start.8 = (bf16[2,8,4096]{2,1,0:T(8,128)(2,1)S(1)}, bf16[2,8,4096]{2,1,0:T(8,128)(2,1)S(1)}, u32[]{:S(2)}, u32[]{:S(2)}) collective-permute-start(bf16[2,8,4096]{2,1,0:T(8,128)(2,1)S(1)} %fusion.7), channel_id=1, source_target_pairs={{0,8},{1,9},{2,10},{3,11},{4,12},{5,13},{6,14},{7,15},{8,0},{9,1},... | collective-permute-start | bytes 393224 | tf_op jit(solution)/shard_map/ppermute | solution.py:42
  66.8 5.8 %collective-permute-start.5 = (bf16[64,4096]{1,0:T(8,128)(2,1)S(1)}, bf16[64,4096]{1,0:T(8,128)(2,1)S(1)}, u32[]{:S(2)}, u32[]{:S(2)}) collective-permute-start(bf16[64,4096]{1,0:T(8,128)(2,1)S(1)} %pad_maximum_fusion.1), channel_id=1, source_target_pairs={{0,1},{1,0},{2,3},{3,2},{4,5},{5,4},{6,7},{7,6},{8,9},{9,8},{10,11... | collective-permute-start | bytes 1572872 | tf_op jit(solution)/shard_map/ppermute | solution.py:87
  72.6 2.8 %collective-permute-start.9 = (bf16[1,8,4096]{2,1,0:T(8,128)(2,1)S(1)}, bf16[1,8,4096]{2,1,0:T(8,128)(2,1)S(1)}, u32[]{:S(2)}, u32[]{:S(2)}) collective-permute-start(bf16[1,8,4096]{2,1,0:T(8,128)(2,1)S(1)} %fusion.8), channel_id=1, source_target_pairs={{0,16},{1,17},{2,18},{3,19},{4,20},{5,21},{6,22},{7,23},{8,24},{9,... | collective-permute-start | bytes 196616 | tf_op jit(solution)/shard_map/ppermute | solution.py:42
  77.7 1.1 %scatter_custom_fusion = f32[128,2048]{1,0:T(8,128)S(1)} fusion(f32[128,2048]{1,0:T(8,128)S(1)} %copy-done.4, s32[8]{0:T(128)S(1)} %fusion.15, f32[1,8,16,128]{3,2,1,0:T(8,128)S(1)} %bitcast.118), kind=kCustom, calls=%fused_computation.44 | custom fusion | flops 16384 | bytes 1114112 | tf_op jit(solution)/shard_map/scatter-add | solution.py:240
  78.9 1.1 %scatter_custom_fusion.1 = f32[128,2048]{1,0:T(8,128)S(1)} fusion(f32[128,2048]{1,0:T(8,128)S(1)} %copy-done.3, s32[8]{0:T(128)S(1)} %fusion.15, f32[1,8,16,128]{3,2,1,0:T(8,128)S(1)} %bitcast.117), kind=kCustom, calls=%fused_computation.41 | custom fusion | flops 16384 | bytes 1114112 | tf_op jit(solution)/shard_map/scatter-add | solution.py:241
  80.3 6.5 %collective-permute-start.10 = (bf16[64,4096]{1,0:T(8,128)(2,1)S(1)}, bf16[64,4096]{1,0:T(8,128)(2,1)S(1)}, u32[]{:S(2)}, u32[]{:S(2)}) collective-permute-start(bf16[64,4096]{1,0:T(8,128)(2,1)S(1)} %pad_maximum_fusion.2), channel_id=1, source_target_pairs={{0,1},{1,0},{2,3},{3,2},{4,5},{5,4},{6,7},{7,6},{8,9},{9,8},{10,11... | collective-permute-start | bytes 1572872 | tf_op jit(solution)/shard_map/ppermute | solution.py:87
  (79 shorter events, 12.7 us)
Async XLA Ops:
  0.6 1.4 %copy-start.8 = (bf16[64,4096]{1,0:T(8,128)(2,1)S(1)}, bf16[64,4096]{1,0:T(8,128)(2,1)}, u32[]{:S(2)}) copy-start(bf16[64,4096]{1,0:T(8,128)(2,1)} %param.10) | copy-start | bytes 1572868
  0.6 1.5 %copy-start.9 = (bf16[64,4096]{1,0:T(8,128)(2,1)S(1)}, bf16[64,4096]{1,0:T(8,128)(2,1)}, u32[]{:S(2)}) copy-start(bf16[64,4096]{1,0:T(8,128)(2,1)} %param.9) | copy-start | bytes 1572868
  2.1 0.7 copy-start.10
  2.3 2.7 %collective-permute-start = (bf16[64,8192]{1,0:T(8,128)(2,1)S(1)}, bf16[64,8192]{1,0:T(8,128)(2,1)S(1)}, u32[]{:S(2)}, u32[]{:S(2)}) collective-permute-start(bf16[64,8192]{1,0:T(8,128)(2,1)S(1)} %pad_maximum_fusion), channel_id=1, source_target_pairs={{0,1},{1,0},{2,3},{3,2},{4,5},{5,4},{6,7},{7,6},{8,9},{9,8},{10,11... | collective-permute-start | bytes 3145736 | tf_op jit(solution)/shard_map/ppermute | solution.py:87
  5.3 14.2 %copy-start.1 = (bf16[128,2048]{1,0:T(8,128)(2,1)}, bf16[128,2048]{1,0:T(8,128)(2,1)S(1)}, u32[]{:S(2)}) copy-start(bf16[128,2048]{1,0:T(8,128)(2,1)S(1)} %maximum_select_fusion.4.v_all) | copy-start | bytes 1572868
  6.0 16.7 %copy-start.2 = (bf16[128,2048]{1,0:T(8,128)(2,1)}, bf16[128,2048]{1,0:T(8,128)(2,1)S(1)}, u32[]{:S(2)}) copy-start(bf16[128,2048]{1,0:T(8,128)(2,1)S(1)} %maximum_select_fusion.3.k_all) | copy-start | bytes 1572868
  7.0 5.7 %collective-permute-start.1 = (bf16[1,8,4096]{2,1,0:T(8,128)(2,1)S(1)}, bf16[1,8,4096]{2,1,0:T(8,128)(2,1)S(1)}, u32[]{:S(2)}, u32[]{:S(2)}) collective-permute-start(bf16[1,8,4096]{2,1,0:T(8,128)(2,1)S(1)} %broadcast_in_dim_reshape.3), channel_id=1, source_target_pairs={{0,16},{1,17},{2,18},{3,19},{4,20},{5,21},{6,22},{7,23},{8,24},{9,... | collective-permute-start | bytes 196616 | tf_op jit(solution)/shard_map/ppermute | solution.py:42
  12.7 4.6 %collective-permute-start.2 = (bf16[2,8,4096]{2,1,0:T(8,128)(2,1)S(1)}, bf16[2,8,4096]{2,1,0:T(8,128)(2,1)S(1)}, u32[]{:S(2)}, u32[]{:S(2)}) collective-permute-start(bf16[2,8,4096]{2,1,0:T(8,128)(2,1)S(1)} %maximum_select_fusion.14), channel_id=1, source_target_pairs={{0,8},{1,9},{2,10},{3,11},{4,12},{5,13},{6,14},{7,15},{8,0},{9,1},... | collective-permute-start | bytes 393224 | tf_op jit(solution)/shard_map/ppermute | solution.py:42
  17.3 5.3 %collective-permute-start.3 = (bf16[4,8,4096]{2,1,0:T(8,128)(2,1)S(1)}, bf16[4,8,4096]{2,1,0:T(8,128)(2,1)S(1)}, u32[]{:S(2)}, u32[]{:S(2)}) collective-permute-start(bf16[4,8,4096]{2,1,0:T(8,128)(2,1)S(1)} %bitcast.108), channel_id=1, source_target_pairs={{0,4},{1,3},{2,6},{3,1},{4,0},{5,7},{6,2},{7,5},{8,12},{9,11},{10,... | collective-permute-start | bytes 786440 | tf_op jit(solution)/shard_map/ppermute | solution.py:42
  22.7 8.9 %collective-permute-start.4 = (bf16[8,8,4096]{2,1,0:T(8,128)(2,1)S(1)}, bf16[8,8,4096]{2,1,0:T(8,128)(2,1)S(1)}, u32[]{:S(2)}, u32[]{:S(2)}) collective-permute-start(bf16[8,8,4096]{2,1,0:T(8,128)(2,1)S(1)} %bitcast.113), channel_id=1, source_target_pairs={{0,2},{1,5},{2,0},{3,7},{4,6},{5,1},{6,4},{7,3},{8,10},{9,13},{10,... | collective-permute-start | bytes 1572872 | tf_op jit(solution)/shard_map/ppermute | solution.py:42
  47.0 2.2 %copy-start = (f32[128,4096]{1,0:T(8,128)S(1)}, f32[128,4096]{1,0:T(8,128)}, u32[]{:S(2)}) copy-start(f32[128,4096]{1,0:T(8,128)} %get-tuple-element.13) | copy-start | bytes 6291460
  49.6 8.5 %collective-permute-start.6 = (bf16[8,8,4096]{2,1,0:T(8,128)(2,1)S(1)}, bf16[8,8,4096]{2,1,0:T(8,128)(2,1)}, u32[]{:S(2)}, u32[]{:S(2)}) collective-permute-start(bf16[8,8,4096]{2,1,0:T(8,128)(2,1)S(1)} %fusion), channel_id=1, source_target_pairs={{0,2},{1,5},{2,0},{3,7},{4,6},{5,1},{6,4},{7,3},{8,10},{9,13},{10,... | collective-permute-start | bytes 1572872 | tf_op jit(solution)/shard_map/ppermute | solution.py:42
  51.1 9.7 %copy-start.7 = (bf16[128,2048]{1,0:T(8,128)(2,1)S(1)}, bf16[128,2048]{1,0:T(8,128)(2,1)}, u32[]{:S(2)}) copy-start(bf16[128,2048]{1,0:T(8,128)(2,1)} %get-tuple-element.10) | copy-start | bytes 1572868
  51.1 9.7 %copy-start.6 = (bf16[128,2048]{1,0:T(8,128)(2,1)S(1)}, bf16[128,2048]{1,0:T(8,128)(2,1)}, u32[]{:S(2)}) copy-start(bf16[128,2048]{1,0:T(8,128)(2,1)} %get-tuple-element.11) | copy-start | bytes 1572868
  59.3 6.3 %collective-permute-start.7 = (bf16[4,8,4096]{2,1,0:T(8,128)(2,1)S(1)}, bf16[4,8,4096]{2,1,0:T(8,128)(2,1)S(1)}, u32[]{:S(2)}, u32[]{:S(2)}) collective-permute-start(bf16[4,8,4096]{2,1,0:T(8,128)(2,1)S(1)} %fusion.3), channel_id=1, source_target_pairs={{0,4},{1,3},{2,6},{3,1},{4,0},{5,7},{6,2},{7,5},{8,12},{9,11},{10,... | collective-permute-start | bytes 786440 | tf_op jit(solution)/shard_map/ppermute | solution.py:42
  65.7 6.8 %collective-permute-start.8 = (bf16[2,8,4096]{2,1,0:T(8,128)(2,1)S(1)}, bf16[2,8,4096]{2,1,0:T(8,128)(2,1)S(1)}, u32[]{:S(2)}, u32[]{:S(2)}) collective-permute-start(bf16[2,8,4096]{2,1,0:T(8,128)(2,1)S(1)} %fusion.7), channel_id=1, source_target_pairs={{0,8},{1,9},{2,10},{3,11},{4,12},{5,13},{6,14},{7,15},{8,0},{9,1},... | collective-permute-start | bytes 393224 | tf_op jit(solution)/shard_map/ppermute | solution.py:42
  66.7 11.0 %copy-start.4 = (f32[128,2048]{1,0:T(8,128)S(1)}, f32[128,2048]{1,0:T(8,128)}, u32[]{:S(2)}) copy-start(f32[128,2048]{1,0:T(8,128)} %get-tuple-element.12) | copy-start | bytes 3145732
  66.8 8.7 %collective-permute-start.5 = (bf16[64,4096]{1,0:T(8,128)(2,1)S(1)}, bf16[64,4096]{1,0:T(8,128)(2,1)S(1)}, u32[]{:S(2)}, u32[]{:S(2)}) collective-permute-start(bf16[64,4096]{1,0:T(8,128)(2,1)S(1)} %pad_maximum_fusion.1), channel_id=1, source_target_pairs={{0,1},{1,0},{2,3},{3,2},{4,5},{5,4},{6,7},{7,6},{8,9},{9,8},{10,11... | collective-permute-start | bytes 1572872 | tf_op jit(solution)/shard_map/ppermute | solution.py:87
  72.6 4.6 %collective-permute-start.9 = (bf16[1,8,4096]{2,1,0:T(8,128)(2,1)S(1)}, bf16[1,8,4096]{2,1,0:T(8,128)(2,1)S(1)}, u32[]{:S(2)}, u32[]{:S(2)}) collective-permute-start(bf16[1,8,4096]{2,1,0:T(8,128)(2,1)S(1)} %fusion.8), channel_id=1, source_target_pairs={{0,16},{1,17},{2,18},{3,19},{4,20},{5,21},{6,22},{7,23},{8,24},{9,... | collective-permute-start | bytes 196616 | tf_op jit(solution)/shard_map/ppermute | solution.py:42
  76.2 2.7 %copy-start.3 = (f32[128,2048]{1,0:T(8,128)S(1)}, f32[128,2048]{1,0:T(8,128)}, u32[]{:S(2)}) copy-start(f32[128,2048]{1,0:T(8,128)} %get-tuple-element.14) | copy-start | bytes 3145732
  80.1 6.8 %copy-start.5 = (bf16[64,2048]{1,0:T(8,128)(2,1)S(1)}, bf16[64,2048]{1,0:T(8,128)(2,1)}, u32[]{:S(2)}) copy-start(bf16[64,2048]{1,0:T(8,128)(2,1)} %get-tuple-element.31) | copy-start | bytes 786436
  80.3 8.4 %collective-permute-start.10 = (bf16[64,4096]{1,0:T(8,128)(2,1)S(1)}, bf16[64,4096]{1,0:T(8,128)(2,1)S(1)}, u32[]{:S(2)}, u32[]{:S(2)}) collective-permute-start(bf16[64,4096]{1,0:T(8,128)(2,1)S(1)} %pad_maximum_fusion.2), channel_id=1, source_target_pairs={{0,1},{1,0},{2,3},{3,2},{4,5},{5,4},{6,7},{7,6},{8,9},{9,8},{10,11... | collective-permute-start | bytes 1572872 | tf_op jit(solution)/shard_map/ppermute | solution.py:87

commit v8 on v7

--- a/solution.py
+++ b/solution.py
@@ -34,12 +34,30 @@
     return bit
 
 
-def exchange(x, bit):
+def exchange(x, mask):
     size = group_size()
-    pairs = [
-        (g * 2 + c, (g ^ (1 << physical_bit(c, bit))) * 2 + c) for g in range(size) for c in range(2)
-    ]
+    pairs = []
+    for g in range(size):
+        for c in range(2):
+            phys = 0
+            for bit in range(group_bits()):
+                if (mask >> bit) & 1:
+                    phys |= 1 << physical_bit(c, bit)
+            pairs.append((g * 2 + c, (g ^ phys) * 2 + c))
     return lax.ppermute(x, ("seq", "hx", "hc"), pairs)
+
+
+def rounds():
+    bits = list(range(group_bits()))
+    return [tuple(bits[i:i + 2]) for i in range(0, len(bits), 2)]
+
+
+def round_index(me, bits):
+    return sum(((me >> b) & 1) << i for i, b in enumerate(bits))
+
+
+def round_mask(m, bits):
+    return sum(((m >> i) & 1) << b for i, b in enumerate(bits))
 
 
 def swap_low_bits(x, core):
@@ -61,10 +79,13 @@
 def gather_blocks(x, core):
     me = virtual_index(core)
     held = x[None]
-    for bit in reversed(range(group_bits())):
-        got = exchange(held, bit)
-        low = ((me >> bit) & 1) == 0
-        held = jnp.where(low, jnp.stack([held, got], 1), jnp.stack([got, held], 1))
+    for bits in reversed(rounds()):
+        width = 1 << len(bits)
+        t_me = round_index(me, bits)
+        got = jnp.stack([held] + [exchange(held, round_mask(m, bits)) for m in range(1, width)], 1)
+        held = jnp.stack(
+            [lax.dynamic_index_in_dim(got, t ^ t_me, 1, keepdims=False) for t in range(width)], 1
+        )
         held = held.reshape((-1,) + x.shape)
     held = swap_low_bits(held, core)
     return held.reshape((-1,) + x.shape[1:])
@@ -74,12 +95,16 @@
     me = virtual_index(core)
     size = group_size()
     held = swap_low_bits(x.reshape((size, -1) + x.shape[1:]), core)
-    for bit in range(group_bits()):
-        pairs = held.reshape((held.shape[0] // 2, 2) + held.shape[1:])
-        mine = (me >> bit) & 1
-        keep = jnp.where(mine == 0, pairs[:, 0], pairs[:, 1])
-        send = jnp.where(mine == 0, pairs[:, 1], pairs[:, 0])
-        held = keep + exchange(send.astype(jnp.bfloat16), bit).astype(jnp.float32)
+    for bits in rounds():
+        width = 1 << len(bits)
+        t_me = round_index(me, bits)
+        parts = held.reshape((held.shape[0] // width, width) + held.shape[1:])
+        total = lax.dynamic_index_in_dim(parts, t_me, 1, keepdims=False)
+        for m in range(1, width):
+            send = lax.dynamic_index_in_dim(parts, t_me ^ m, 1, keepdims=False)
+            got = exchange(send.astype(jnp.bfloat16), round_mask(m, bits))
+            total = total + got.astype(jnp.float32)
+        held = total
     return held.reshape(x.shape[0] // size, *x.shape[1:])
 
 

time: 91.4 us -> 83.5 us (0.914)
  starting transfers between devices: 27.6 us -> 16.5 us
  waiting for transfers between devices: 29.2 us -> 33.7 us
    ppermute x3, starting transfers between devices: 12.4 us -> 3.46 us  [swap_with_partner(): return lax.ppermute(x, 'hc', [(0, 1), (1, 0)])]
    ppermute x8 -> x12, waiting for transfers between devices: 27 us -> 31.4 us  [exchange(): return lax.ppermute(x, ('seq', 'hx', 'hc'), pairs)]
    ppermute x8 -> x12, starting transfers between devices: 15.2 us -> 13 us  [exchange(): return lax.ppermute(x, ('seq', 'hx', 'hc'), pairs)]
    add x3 -> x2, other arithmetic: 1.28 us -> 0.15 us  [reduce_blocks(): total = total + got.astype(jnp.float32)]
  transfers between devices with their start and end apart: 11 -> 15, of which waited for: 8 -> 11; matrix products, arithmetic and copies ran while one was open for 5% -> 10% of each run, Pallas kernels for 0% -> 0%
where the time goes in v8:
time: 83.5 us; the launch traced here: 83.3 us
  waiting for transfers between devices  33.7 us (40%)
  starting transfers between devices  16.5 us (20%)
  Pallas kernels  13.4 us (16%)
  other arithmetic  11.1 us (13%)
  local copies, waits for them, and re-layouts  7.63 us (9%)
  between operations  1.02 us (1%)
    ppermute x12, waiting for transfers between devices, exchange(): return lax.ppermute(x, ('seq', 'hx', 'hc'), pairs)  31.4 us
    pallas_call x1, Pallas kernels, attention(): pl.pallas_call(attention_kernel, grid=(heads // per_step, nb), in_specs=[...  13.4 us
    ppermute x12, starting transfers between devices, exchange(): return lax.ppermute(x, ('seq', 'hx', 'hc'), pairs)  13 us
    select_n x4, other arithmetic, to_token_layout(): jnp.where(core == 0, jnp.concatenate([m, r], 1), jnp.concatenate([r, m], 1))  3.66 us
    ppermute x3, starting transfers between devices, swap_with_partner(): return lax.ppermute(x, 'hc', [(0, 1), (1, 0)])  3.46 us
    ppermute x3, waiting for transfers between devices, swap_with_partner(): return lax.ppermute(x, 'hc', [(0, 1), (1, 0)])  2.22 us
    select_n x4, other arithmetic, to_block_layout(): jnp.where(core == 0, jnp.concatenate([m, r], 0), jnp.concatenate([r, m], 0))  2.01 us
    transpose x1, local copies, waits for them, and re-layouts, swap_low_bits(): jnp.swapaxes(x.reshape((size // 4, 2, 2) + x.shape[1:]), 1, 2)  1.89 us
  transfers between devices with their start and end apart: 15, of which 11 were waited for; matrix products, arithmetic and copies ran while one was open for 10% of the time, Pallas kernels for 0%

profile of v8, /device:TPU:1, one launch (start us, length us, event | category | flops | bytes accessed | tf_op | source)
XLA Modules:
  0.0 83.3 jit_solution(12661321826547102203)
XLA Ops:
  0.7 1.3 %constant_dynamic-slice_fusion.19 = (bf16[64,2048]{1,0:T(8,128)(2,1)S(1)}, bf16[64,2048]{1,0:T(8,128)(2,1)S(1)}, bf16[64,2048]{1,0:T(8,128)(2,1)S(1)}, bf16[64,2048]{1,0:T(8,128)(2,1)S(1)}) fusion(bf16[64,4096]{1,0:T(8,128)(2,1)} %param.8, s32[]{:T(128)S(6)} %select_n.153, s32[]{:T(128)S(6)} %select_n.154, bf16[64,4096]{1,0:T(8,128)(2,1)} %param.7), kind=kLoop, calls=%fused_computation.62 | loop fusion | bytes 2097160 | tf_op jit(solution)/shard_map/dynamic_slice | solution.py:118
  2.9 2.2 %collective-permute-done = bf16[64,8192]{1,0:T(8,128)(2,1)S(1)} collective-permute-done((bf16[64,8192]{1,0:T(8,128)(2,1)S(1)}, bf16[64,8192]{1,0:T(8,128)(2,1)S(1)}, u32[]{:S(2)}, u32[]{:S(2)}) %collective-permute-start) | collective-permute-done | bytes 1048608 | tf_op jit(solution)/shard_map/ppermute | solution.py:112
  6.7 4.5 %collective-permute-start.3 = (bf16[1,8,4096]{2,1,0:T(8,128)(2,1)S(1)}, bf16[1,8,4096]{2,1,0:T(8,128)(2,1)S(1)}, u32[]{:S(2)}, u32[]{:S(2)}) collective-permute-start(bf16[1,8,4096]{2,1,0:T(8,128)(2,1)S(1)} %bitcast.78), channel_id=1, source_target_pairs={{0,24},{1,25},{2,26},{3,27},{4,28},{5,29},{6,30},{7,31},{8,16},{9,... | collective-permute-start | bytes 196616 | tf_op jit(solution)/shard_map/ppermute | solution.py:47
  11.6 1.8 %collective-permute-done.3 = bf16[1,8,4096]{2,1,0:T(8,128)(2,1)S(1)} collective-permute-done((bf16[1,8,4096]{2,1,0:T(8,128)(2,1)S(1)}, bf16[1,8,4096]{2,1,0:T(8,128)(2,1)S(1)}, u32[]{:S(2)}, u32[]{:S(2)}) %collective-permute-start.3) | collective-permute-done | bytes 65568 | tf_op jit(solution)/shard_map/ppermute | solution.py:47
  13.4 3.5 %collective-permute-done.2 = bf16[1,8,4096]{2,1,0:T(8,128)(2,1)S(1)} collective-permute-done((bf16[1,8,4096]{2,1,0:T(8,128)(2,1)S(1)}, bf16[1,8,4096]{2,1,0:T(8,128)(2,1)S(1)}, u32[]{:S(2)}, u32[]{:S(2)}) %collective-permute-start.2) | collective-permute-done | bytes 65568 | tf_op jit(solution)/shard_map/ppermute | solution.py:47
  17.1 2.2 %collective-permute-start.6 = (bf16[4,8,4096]{2,1,0:T(8,128)(2,1)S(1)}, bf16[4,8,4096]{2,1,0:T(8,128)(2,1)S(1)}, u32[]{:S(2)}, u32[]{:S(2)}) collective-permute-start(bf16[4,8,4096]{2,1,0:T(8,128)(2,1)S(1)} %get-tuple-element.52), channel_id=1, source_target_pairs={{0,6},{1,7},{2,4},{3,5},{4,2},{5,3},{6,0},{7,1},{8,14},{9,15},{10,... | collective-permute-start | bytes 786440 | tf_op jit(solution)/shard_map/ppermute | solution.py:47
  21.6 3.5 %collective-permute-done.6 = bf16[4,8,4096]{2,1,0:T(8,128)(2,1)S(1)} collective-permute-done((bf16[4,8,4096]{2,1,0:T(8,128)(2,1)S(1)}, bf16[4,8,4096]{2,1,0:T(8,128)(2,1)S(1)}, u32[]{:S(2)}, u32[]{:S(2)}) %collective-permute-start.6) | collective-permute-done | bytes 262176 | tf_op jit(solution)/shard_map/ppermute | solution.py:47
  25.1 5.7 %collective-permute-done.5 = bf16[4,8,4096]{2,1,0:T(8,128)(2,1)S(1)} collective-permute-done((bf16[4,8,4096]{2,1,0:T(8,128)(2,1)S(1)}, bf16[4,8,4096]{2,1,0:T(8,128)(2,1)S(1)}, u32[]{:S(2)}, u32[]{:S(2)}) %collective-permute-start.5) | collective-permute-done | bytes 262176 | tf_op jit(solution)/shard_map/ppermute | solution.py:47
  30.7 1.1 %collective-permute-done.4 = bf16[4,8,4096]{2,1,0:T(8,128)(2,1)S(1)} collective-permute-done((bf16[4,8,4096]{2,1,0:T(8,128)(2,1)S(1)}, bf16[4,8,4096]{2,1,0:T(8,128)(2,1)S(1)}, u32[]{:S(2)}, u32[]{:S(2)}) %collective-permute-start.4) | collective-permute-done | bytes 262176 | tf_op jit(solution)/shard_map/ppermute | solution.py:47
  32.4 1.3 %bitcast_select_fusion.s_all = bf16[128,4096]{1,0:T(8,128)(2,1)} fusion(bf16[4,2,2,8,4096]{4,3,1,2,0:T(8,128)(2,1)S(1)} %copy.14, bf16[4,4,8,4096]{3,2,1,0:T(8,128)(2,1)S(1)} %pad_maximum_fusion.2, pred[]{:T(512)S(6)} %eq.5), kind=kLoop, calls=%fused_computation.7 | loop fusion | flops 524288 | bytes 3145729 | tf_op jit(solution)/shard_map/jit(_where)/select_n | solution.py:68
  34.2 13.4 %shard_map.84 = (bf16[128,2048]{1,0:T(8,128)(2,1)}, bf16[128,2048]{1,0:T(8,128)(2,1)}, f32[128,2048]{1,0:T(8,128)}, f32[128,2048]{1,0:T(8,128)}, f32[128,4096]{1,0:T(8,128)}) custom-call(bf16[128,2048]{1,0:T(8,128)(2,1)} %maximum_select_fusion.q_all, bf16[128,2048]{1,0:T(8,128)(2,1)} %copy-done.2, bf16[128,2048]{1,0:T(8,128)(2,1)} %copy-done.1, ...), custom_call_target="tpu_custom_call" | custom-call | flops 805306368 | bytes 7340032 | tf_op jit(solution)/shard_map/pallas_call | solution.py:212
  47.6 1.9 %copy.15 = f32[4,2,2,8,4096]{4,3,2,1,0:T(8,128)S(1)} copy(f32[4,2,2,8,4096]{4,3,1,2,0:T(8,128)} %bitcast.73) | data formatting | bytes 4194304 | tf_op jit(solution)/shard_map/transpose | solution.py:67
  50.2 1.3 %collective-permute-start.8 = (bf16[4,8,4096]{2,1,0:T(8,128)(2,1)S(1)}, bf16[4,8,4096]{2,1,0:T(8,128)(2,1)S(1)}, u32[]{:S(2)}, u32[]{:S(2)}) collective-permute-start(bf16[4,8,4096]{2,1,0:T(8,128)(2,1)S(1)} %get-tuple-element.17), channel_id=1, source_target_pairs={{0,2},{1,5},{2,0},{3,7},{4,6},{5,1},{6,4},{7,3},{8,10},{9,13},{10,... | collective-permute-start | bytes 786440 | tf_op jit(solution)/shard_map/ppermute | solution.py:47
  51.5 1.2 %collective-permute-start.10 = (bf16[4,8,4096]{2,1,0:T(8,128)(2,1)S(1)}, bf16[4,8,4096]{2,1,0:T(8,128)(2,1)S(1)}, u32[]{:S(2)}, u32[]{:S(2)}) collective-permute-start(bf16[4,8,4096]{2,1,0:T(8,128)(2,1)S(1)} %get-tuple-element.18), channel_id=1, source_target_pairs={{0,6},{1,7},{2,4},{3,5},{4,2},{5,3},{6,0},{7,1},{8,14},{9,15},{10,... | collective-permute-start | bytes 786440 | tf_op jit(solution)/shard_map/ppermute | solution.py:47
  53.0 4.3 %collective-permute-done.8 = bf16[4,8,4096]{2,1,0:T(8,128)(2,1)S(1)} collective-permute-done((bf16[4,8,4096]{2,1,0:T(8,128)(2,1)S(1)}, bf16[4,8,4096]{2,1,0:T(8,128)(2,1)S(1)}, u32[]{:S(2)}, u32[]{:S(2)}) %collective-permute-start.8) | collective-permute-done | bytes 262176 | tf_op jit(solution)/shard_map/ppermute | solution.py:47
  57.3 3.4 %collective-permute-done.10 = bf16[4,8,4096]{2,1,0:T(8,128)(2,1)S(1)} collective-permute-done((bf16[4,8,4096]{2,1,0:T(8,128)(2,1)S(1)}, bf16[4,8,4096]{2,1,0:T(8,128)(2,1)S(1)}, u32[]{:S(2)}, u32[]{:S(2)}) %collective-permute-start.10) | collective-permute-done | bytes 262176 | tf_op jit(solution)/shard_map/ppermute | solution.py:47
  60.7 4.5 %collective-permute-done.9 = bf16[4,8,4096]{2,1,0:T(8,128)(2,1)S(1)} collective-permute-done((bf16[4,8,4096]{2,1,0:T(8,128)(2,1)S(1)}, bf16[4,8,4096]{2,1,0:T(8,128)(2,1)S(1)}, u32[]{:S(2)}, u32[]{:S(2)}) %collective-permute-start.9) | collective-permute-done | bytes 262176 | tf_op jit(solution)/shard_map/ppermute | solution.py:47
  65.6 1.8 %collective-permute-start.13 = (bf16[1,8,4096]{2,1,0:T(8,128)(2,1)S(1)}, bf16[1,8,4096]{2,1,0:T(8,128)(2,1)S(1)}, u32[]{:S(2)}, u32[]{:S(2)}) collective-permute-start(bf16[1,8,4096]{2,1,0:T(8,128)(2,1)S(1)} %get-tuple-element.35), channel_id=1, source_target_pairs={{0,24},{1,25},{2,26},{3,27},{4,28},{5,29},{6,30},{7,31},{8,16},{9,... | collective-permute-start | bytes 196616 | tf_op jit(solution)/shard_map/ppermute | solution.py:47
  69.0 1.9 %collective-permute-start.7 = (bf16[64,4096]{1,0:T(8,128)(2,1)}, bf16[64,4096]{1,0:T(8,128)(2,1)}, u32[]{:S(2)}, u32[]{:S(2)}) collective-permute-start(bf16[64,4096]{1,0:T(8,128)(2,1)} %pad_maximum_fusion.3), channel_id=1, source_target_pairs={{0,1},{1,0},{2,3},{3,2},{4,5},{5,4},{6,7},{7,6},{8,9},{9,8},{10,11... | collective-permute-start | bytes 1572872 | tf_op jit(solution)/shard_map/ppermute | solution.py:112
  70.9 3.5 %collective-permute-done.12 = bf16[1,8,4096]{2,1,0:T(8,128)(2,1)S(1)} collective-permute-done((bf16[1,8,4096]{2,1,0:T(8,128)(2,1)S(1)}, bf16[1,8,4096]{2,1,0:T(8,128)(2,1)S(1)}, u32[]{:S(2)}, u32[]{:S(2)}) %collective-permute-start.12) | collective-permute-done | bytes 65568 | tf_op jit(solution)/shard_map/ppermute | solution.py:47
  74.5 1.1 %scatter_custom_fusion = f32[128,2048]{1,0:T(8,128)S(1)} fusion(f32[128,2048]{1,0:T(8,128)S(1)} %copy-done.4, s32[8]{0:T(128)S(1)} %fusion.9, f32[8,16,2,128]{3,0,2,1:T(8,128)S(1)} %bitcast.76), kind=kCustom, calls=%fused_computation.37 | custom fusion | flops 16384 | bytes 1114112 | tf_op jit(solution)/shard_map/scatter-add | solution.py:265
  75.7 1.1 %scatter_custom_fusion.1 = f32[128,2048]{1,0:T(8,128)S(1)} fusion(f32[128,2048]{1,0:T(8,128)S(1)} %copy-done.3, s32[8]{0:T(128)S(1)} %fusion.9, f32[8,16,2,128]{3,0,2,1:T(8,128)S(1)} %bitcast.77), kind=kCustom, calls=%fused_computation.35 | custom fusion | flops 16384 | bytes 1114112 | tf_op jit(solution)/shard_map/scatter-add | solution.py:266
  77.0 1.5 %collective-permute-start.14 = (bf16[64,4096]{1,0:T(8,128)(2,1)S(1)}, bf16[64,4096]{1,0:T(8,128)(2,1)S(1)}, u32[]{:S(2)}, u32[]{:S(2)}) collective-permute-start(bf16[64,4096]{1,0:T(8,128)(2,1)S(1)} %pad_maximum_fusion.4), channel_id=1, source_target_pairs={{0,1},{1,0},{2,3},{3,2},{4,5},{5,4},{6,7},{7,6},{8,9},{9,8},{10,11... | collective-permute-start | bytes 1572872 | tf_op jit(solution)/shard_map/ppermute | solution.py:112
  78.5 1.1 %fusion.12 = (bf16[64,2048]{1,0:T(8,128)(2,1)S(1)}, bf16[64,2048]{1,0:T(8,128)(2,1)S(1)}) fusion(bf16[64,4096]{1,0:T(8,128)(2,1)} %collective-permute-done.7), kind=kLoop, calls=%fused_computation.80 | loop fusion | bytes 1048576 | tf_op jit(solution)/shard_map/slice | solution.py:136
  (75 shorter events, 13.1 us)
Async XLA Ops:
  0.6 1.4 %copy-start.7 = (bf16[64,4096]{1,0:T(8,128)(2,1)S(1)}, bf16[64,4096]{1,0:T(8,128)(2,1)}, u32[]{:S(2)}) copy-start(bf16[64,4096]{1,0:T(8,128)(2,1)} %param.10) | copy-start | bytes 1572868
  0.6 1.5 %copy-start.8 = (bf16[64,4096]{1,0:T(8,128)(2,1)S(1)}, bf16[64,4096]{1,0:T(8,128)(2,1)}, u32[]{:S(2)}) copy-start(bf16[64,4096]{1,0:T(8,128)(2,1)} %param.9) | copy-start | bytes 1572868
  2.3 2.7 %collective-permute-start = (bf16[64,8192]{1,0:T(8,128)(2,1)S(1)}, bf16[64,8192]{1,0:T(8,128)(2,1)S(1)}, u32[]{:S(2)}, u32[]{:S(2)}) collective-permute-start(bf16[64,8192]{1,0:T(8,128)(2,1)S(1)} %pad_maximum_fusion), channel_id=1, source_target_pairs={{0,1},{1,0},{2,3},{3,2},{4,5},{5,4},{6,7},{7,6},{8,9},{9,8},{10,11... | collective-permute-start | bytes 3145736 | tf_op jit(solution)/shard_map/ppermute | solution.py:112
  5.3 15.4 %copy-start.1 = (bf16[128,2048]{1,0:T(8,128)(2,1)}, bf16[128,2048]{1,0:T(8,128)(2,1)S(1)}, u32[]{:S(2)}) copy-start(bf16[128,2048]{1,0:T(8,128)(2,1)S(1)} %maximum_select_fusion.2.v_all) | copy-start | bytes 1572868
  6.0 15.6 %copy-start.2 = (bf16[128,2048]{1,0:T(8,128)(2,1)}, bf16[128,2048]{1,0:T(8,128)(2,1)S(1)}, u32[]{:S(2)}) copy-start(bf16[128,2048]{1,0:T(8,128)(2,1)S(1)} %maximum_select_fusion.1.k_all) | copy-start | bytes 1572868
  6.7 6.7 %collective-permute-start.3 = (bf16[1,8,4096]{2,1,0:T(8,128)(2,1)S(1)}, bf16[1,8,4096]{2,1,0:T(8,128)(2,1)S(1)}, u32[]{:S(2)}, u32[]{:S(2)}) collective-permute-start(bf16[1,8,4096]{2,1,0:T(8,128)(2,1)S(1)} %bitcast.78), channel_id=1, source_target_pairs={{0,24},{1,25},{2,26},{3,27},{4,28},{5,29},{6,30},{7,31},{8,16},{9,... | collective-permute-start | bytes 196616 | tf_op jit(solution)/shard_map/ppermute | solution.py:47
  11.2 5.7 %collective-permute-start.2 = (bf16[1,8,4096]{2,1,0:T(8,128)(2,1)S(1)}, bf16[1,8,4096]{2,1,0:T(8,128)(2,1)S(1)}, u32[]{:S(2)}, u32[]{:S(2)}) collective-permute-start(bf16[1,8,4096]{2,1,0:T(8,128)(2,1)S(1)} %bitcast.79), channel_id=1, source_target_pairs={{0,16},{1,17},{2,18},{3,19},{4,20},{5,21},{6,22},{7,23},{8,24},{9,... | collective-permute-start | bytes 196616 | tf_op jit(solution)/shard_map/ppermute | solution.py:47
  11.2 5.7 %collective-permute-start.1 = (bf16[1,8,4096]{2,1,0:T(8,128)(2,1)S(1)}, bf16[1,8,4096]{2,1,0:T(8,128)(2,1)S(1)}, u32[]{:S(2)}, u32[]{:S(2)}) collective-permute-start(bf16[1,8,4096]{2,1,0:T(8,128)(2,1)S(1)} %bitcast.80), channel_id=1, source_target_pairs={{0,8},{1,9},{2,10},{3,11},{4,12},{5,13},{6,14},{7,15},{8,0},{9,1},... | collective-permute-start | bytes 196616 | tf_op jit(solution)/shard_map/ppermute | solution.py:47
  17.1 8.0 %collective-permute-start.6 = (bf16[4,8,4096]{2,1,0:T(8,128)(2,1)S(1)}, bf16[4,8,4096]{2,1,0:T(8,128)(2,1)S(1)}, u32[]{:S(2)}, u32[]{:S(2)}) collective-permute-start(bf16[4,8,4096]{2,1,0:T(8,128)(2,1)S(1)} %get-tuple-element.52), channel_id=1, source_target_pairs={{0,6},{1,7},{2,4},{3,5},{4,2},{5,3},{6,0},{7,1},{8,14},{9,15},{10,... | collective-permute-start | bytes 786440 | tf_op jit(solution)/shard_map/ppermute | solution.py:47
  19.3 11.4 %collective-permute-start.5 = (bf16[4,8,4096]{2,1,0:T(8,128)(2,1)S(1)}, bf16[4,8,4096]{2,1,0:T(8,128)(2,1)S(1)}, u32[]{:S(2)}, u32[]{:S(2)}) collective-permute-start(bf16[4,8,4096]{2,1,0:T(8,128)(2,1)S(1)} %get-tuple-element.52), channel_id=1, source_target_pairs={{0,4},{1,3},{2,6},{3,1},{4,0},{5,7},{6,2},{7,5},{8,12},{9,11},{10,... | collective-permute-start | bytes 786440 | tf_op jit(solution)/shard_map/ppermute | solution.py:47
  19.5 12.3 %collective-permute-start.4 = (bf16[4,8,4096]{2,1,0:T(8,128)(2,1)S(1)}, bf16[4,8,4096]{2,1,0:T(8,128)(2,1)S(1)}, u32[]{:S(2)}, u32[]{:S(2)}) collective-permute-start(bf16[4,8,4096]{2,1,0:T(8,128)(2,1)S(1)} %get-tuple-element.52), channel_id=1, source_target_pairs={{0,2},{1,5},{2,0},{3,7},{4,6},{5,1},{6,4},{7,3},{8,10},{9,13},{10,... | collective-permute-start | bytes 786440 | tf_op jit(solution)/shard_map/ppermute | solution.py:47
  47.6 2.2 %copy-start = (f32[128,4096]{1,0:T(8,128)S(1)}, f32[128,4096]{1,0:T(8,128)}, u32[]{:S(2)}) copy-start(f32[128,4096]{1,0:T(8,128)} %get-tuple-element.13) | copy-start | bytes 6291460
  49.8 3.1 %copy-start.6 = (bf16[128,2048]{1,0:T(8,128)(2,1)S(1)}, bf16[128,2048]{1,0:T(8,128)(2,1)}, u32[]{:S(2)}) copy-start(bf16[128,2048]{1,0:T(8,128)(2,1)} %get-tuple-element.10) | copy-start | bytes 1572868
  50.1 2.9 %copy-start.5 = (bf16[128,2048]{1,0:T(8,128)(2,1)S(1)}, bf16[128,2048]{1,0:T(8,128)(2,1)}, u32[]{:S(2)}) copy-start(bf16[128,2048]{1,0:T(8,128)(2,1)} %get-tuple-element.11) | copy-start | bytes 1572868
  50.2 7.1 %collective-permute-start.8 = (bf16[4,8,4096]{2,1,0:T(8,128)(2,1)S(1)}, bf16[4,8,4096]{2,1,0:T(8,128)(2,1)S(1)}, u32[]{:S(2)}, u32[]{:S(2)}) collective-permute-start(bf16[4,8,4096]{2,1,0:T(8,128)(2,1)S(1)} %get-tuple-element.17), channel_id=1, source_target_pairs={{0,2},{1,5},{2,0},{3,7},{4,6},{5,1},{6,4},{7,3},{8,10},{9,13},{10,... | collective-permute-start | bytes 786440 | tf_op jit(solution)/shard_map/ppermute | solution.py:47
  51.5 9.2 %collective-permute-start.10 = (bf16[4,8,4096]{2,1,0:T(8,128)(2,1)S(1)}, bf16[4,8,4096]{2,1,0:T(8,128)(2,1)S(1)}, u32[]{:S(2)}, u32[]{:S(2)}) collective-permute-start(bf16[4,8,4096]{2,1,0:T(8,128)(2,1)S(1)} %get-tuple-element.18), channel_id=1, source_target_pairs={{0,6},{1,7},{2,4},{3,5},{4,2},{5,3},{6,0},{7,1},{8,14},{9,15},{10,... | collective-permute-start | bytes 786440 | tf_op jit(solution)/shard_map/ppermute | solution.py:47
  52.7 12.5 %collective-permute-start.9 = (bf16[4,8,4096]{2,1,0:T(8,128)(2,1)S(1)}, bf16[4,8,4096]{2,1,0:T(8,128)(2,1)S(1)}, u32[]{:S(2)}, u32[]{:S(2)}) collective-permute-start(bf16[4,8,4096]{2,1,0:T(8,128)(2,1)S(1)} %get-tuple-element.19), channel_id=1, source_target_pairs={{0,4},{1,3},{2,6},{3,1},{4,0},{5,7},{6,2},{7,5},{8,12},{9,11},{10,... | collective-permute-start | bytes 786440 | tf_op jit(solution)/shard_map/ppermute | solution.py:47
  53.0 21.4 %copy-start.4 = (f32[128,2048]{1,0:T(8,128)S(1)}, f32[128,2048]{1,0:T(8,128)}, u32[]{:S(2)}) copy-start(f32[128,2048]{1,0:T(8,128)} %get-tuple-element.12) | copy-start | bytes 3145732
  65.4 5.4 %collective-permute-start.11 = (bf16[1,8,4096]{2,1,0:T(8,128)(2,1)S(1)}, bf16[1,8,4096]{2,1,0:T(8,128)(2,1)S(1)}, u32[]{:S(2)}, u32[]{:S(2)}) collective-permute-start(bf16[1,8,4096]{2,1,0:T(8,128)(2,1)S(1)} %get-tuple-element.34), channel_id=1, source_target_pairs={{0,8},{1,9},{2,10},{3,11},{4,12},{5,13},{6,14},{7,15},{8,0},{9,1},... | collective-permute-start | bytes 196616 | tf_op jit(solution)/shard_map/ppermute | solution.py:47
  65.6 5.3 %collective-permute-start.13 = (bf16[1,8,4096]{2,1,0:T(8,128)(2,1)S(1)}, bf16[1,8,4096]{2,1,0:T(8,128)(2,1)S(1)}, u32[]{:S(2)}, u32[]{:S(2)}) collective-permute-start(bf16[1,8,4096]{2,1,0:T(8,128)(2,1)S(1)} %get-tuple-element.35), channel_id=1, source_target_pairs={{0,24},{1,25},{2,26},{3,27},{4,28},{5,29},{6,30},{7,31},{8,16},{9,... | collective-permute-start | bytes 196616 | tf_op jit(solution)/shard_map/ppermute | solution.py:47
  67.4 7.0 %collective-permute-start.12 = (bf16[1,8,4096]{2,1,0:T(8,128)(2,1)S(1)}, bf16[1,8,4096]{2,1,0:T(8,128)(2,1)S(1)}, u32[]{:S(2)}, u32[]{:S(2)}) collective-permute-start(bf16[1,8,4096]{2,1,0:T(8,128)(2,1)S(1)} %get-tuple-element.36), channel_id=1, source_target_pairs={{0,16},{1,17},{2,18},{3,19},{4,20},{5,21},{6,22},{7,23},{8,24},{9,... | collective-permute-start | bytes 196616 | tf_op jit(solution)/shard_map/ppermute | solution.py:47
  68.1 7.5 %copy-start.3 = (f32[128,2048]{1,0:T(8,128)S(1)}, f32[128,2048]{1,0:T(8,128)}, u32[]{:S(2)}) copy-start(f32[128,2048]{1,0:T(8,128)} %get-tuple-element.14) | copy-start | bytes 3145732
  69.0 9.5 %collective-permute-start.7 = (bf16[64,4096]{1,0:T(8,128)(2,1)}, bf16[64,4096]{1,0:T(8,128)(2,1)}, u32[]{:S(2)}, u32[]{:S(2)}) collective-permute-start(bf16[64,4096]{1,0:T(8,128)(2,1)} %pad_maximum_fusion.3), channel_id=1, source_target_pairs={{0,1},{1,0},{2,3},{3,2},{4,5},{5,4},{6,7},{7,6},{8,9},{9,8},{10,11... | collective-permute-start | bytes 1572872 | tf_op jit(solution)/shard_map/ppermute | solution.py:112
  77.0 4.4 %collective-permute-start.14 = (bf16[64,4096]{1,0:T(8,128)(2,1)S(1)}, bf16[64,4096]{1,0:T(8,128)(2,1)S(1)}, u32[]{:S(2)}, u32[]{:S(2)}) collective-permute-start(bf16[64,4096]{1,0:T(8,128)(2,1)S(1)} %pad_maximum_fusion.4), channel_id=1, source_target_pairs={{0,1},{1,0},{2,3},{3,2},{4,5},{5,4},{6,7},{7,6},{8,9},{9,8},{10,11... | collective-permute-start | bytes 1572872 | tf_op jit(solution)/shard_map/ppermute | solution.py:112
  (1 other events, 0.7 us)

commit v9 on v8

--- a/solution.py
+++ b/solution.py
@@ -165,13 +165,18 @@
 
         sw = jnp.where(causal, mm(q, k, trans_b=True) * scale, MASKED_SCORE)
         ss = jnp.where(allowed, mm(q, sk, trans_b=True) * scale, MASKED_SCORE)
-        top = jnp.maximum(jnp.max(sw, axis=1, keepdims=True), jnp.max(ss, axis=1, keepdims=True))
-        total = jnp.sum(jnp.exp(sw - top), axis=1, keepdims=True) + jnp.sum(
-            jnp.exp(ss - top), axis=1, keepdims=True
-        )
-        log_norm = top + jnp.log(total)
-        pw = jnp.where(causal, jnp.exp(sw - log_norm), 0.0)
-        ps = jnp.where(allowed, jnp.exp(ss - log_norm), 0.0)
+        fold = sw
+        for c in range(ss.shape[1] // BLOCK):
+            fold = jnp.maximum(fold, ss[:, c * BLOCK:(c + 1) * BLOCK])
+        top = jnp.max(fold, axis=1, keepdims=True)
+        ew = jnp.exp(sw - top)
+        es = jnp.exp(ss - top)
+        fold = ew
+        for c in range(es.shape[1] // BLOCK):
+            fold = fold + es[:, c * BLOCK:(c + 1) * BLOCK]
+        inv = 1.0 / jnp.sum(fold, axis=1, keepdims=True)
+        pw = ew * inv
+        ps = es * inv
         pw_low = pw.astype(bf16)
         ps_low = ps.astype(bf16)
         att = (mm(pw_low, v) + mm(ps_low, sv)).astype(bf16)

time: 83.5 us -> 82.9 us (level)
  no operation moved by 1% of the time
where the time goes in v9:
time: 82.9 us; the launch traced here: 82.7 us
  waiting for transfers between devices  33.7 us (41%)
  starting transfers between devices  16.5 us (20%)
  Pallas kernels  12.8 us (15%)
  other arithmetic  11.1 us (13%)
  local copies, waits for them, and re-layouts  7.63 us (9%)
  between operations  1.02 us (1%)
    ppermute x12, waiting for transfers between devices, exchange(): return lax.ppermute(x, ('seq', 'hx', 'hc'), pairs)  31.4 us
    ppermute x12, starting transfers between devices, exchange(): return lax.ppermute(x, ('seq', 'hx', 'hc'), pairs)  13 us
    pallas_call x1, Pallas kernels, attention(): pl.pallas_call(attention_kernel, grid=(heads // per_step, nb), in_specs=[...  12.8 us
    select_n x4, other arithmetic, to_token_layout(): jnp.where(core == 0, jnp.concatenate([m, r], 1), jnp.concatenate([r, m], 1))  3.66 us
    ppermute x3, starting transfers between devices, swap_with_partner(): return lax.ppermute(x, 'hc', [(0, 1), (1, 0)])  3.46 us
    ppermute x3, waiting for transfers between devices, swap_with_partner(): return lax.ppermute(x, 'hc', [(0, 1), (1, 0)])  2.22 us
    select_n x4, other arithmetic, to_block_layout(): jnp.where(core == 0, jnp.concatenate([m, r], 0), jnp.concatenate([r, m], 0))  2.01 us
    transpose x1, local copies, waits for them, and re-layouts, swap_low_bits(): jnp.swapaxes(x.reshape((size // 4, 2, 2) + x.shape[1:]), 1, 2)  1.89 us
  transfers between devices with their start and end apart: 15, of which 11 were waited for; matrix products, arithmetic and copies ran while one was open for 10% of the time, Pallas kernels for 0%

profile of v9, /device:TPU:1, one launch (start us, length us, event | category | flops | bytes accessed | tf_op | source)
XLA Modules:
  0.0 82.7 jit_solution(5623121206873459566)
XLA Ops:
  0.7 1.3 %constant_dynamic-slice_fusion.19 = (bf16[64,2048]{1,0:T(8,128)(2,1)S(1)}, bf16[64,2048]{1,0:T(8,128)(2,1)S(1)}, bf16[64,2048]{1,0:T(8,128)(2,1)S(1)}, bf16[64,2048]{1,0:T(8,128)(2,1)S(1)}) fusion(bf16[64,4096]{1,0:T(8,128)(2,1)} %param.8, s32[]{:T(128)S(6)} %select_n.153, s32[]{:T(128)S(6)} %select_n.154, bf16[64,4096]{1,0:T(8,128)(2,1)} %param.7), kind=kLoop, calls=%fused_computation.62 | loop fusion | bytes 2097160 | tf_op jit(solution)/shard_map/dynamic_slice | solution.py:118
  2.9 2.2 %collective-permute-done = bf16[64,8192]{1,0:T(8,128)(2,1)S(1)} collective-permute-done((bf16[64,8192]{1,0:T(8,128)(2,1)S(1)}, bf16[64,8192]{1,0:T(8,128)(2,1)S(1)}, u32[]{:S(2)}, u32[]{:S(2)}) %collective-permute-start) | collective-permute-done | bytes 1048608 | tf_op jit(solution)/shard_map/ppermute | solution.py:112
  6.7 4.5 %collective-permute-start.3 = (bf16[1,8,4096]{2,1,0:T(8,128)(2,1)S(1)}, bf16[1,8,4096]{2,1,0:T(8,128)(2,1)S(1)}, u32[]{:S(2)}, u32[]{:S(2)}) collective-permute-start(bf16[1,8,4096]{2,1,0:T(8,128)(2,1)S(1)} %bitcast.78), channel_id=1, source_target_pairs={{0,24},{1,25},{2,26},{3,27},{4,28},{5,29},{6,30},{7,31},{8,16},{9,... | collective-permute-start | bytes 196616 | tf_op jit(solution)/shard_map/ppermute | solution.py:47
  11.6 1.8 %collective-permute-done.3 = bf16[1,8,4096]{2,1,0:T(8,128)(2,1)S(1)} collective-permute-done((bf16[1,8,4096]{2,1,0:T(8,128)(2,1)S(1)}, bf16[1,8,4096]{2,1,0:T(8,128)(2,1)S(1)}, u32[]{:S(2)}, u32[]{:S(2)}) %collective-permute-start.3) | collective-permute-done | bytes 65568 | tf_op jit(solution)/shard_map/ppermute | solution.py:47
  13.4 3.5 %collective-permute-done.2 = bf16[1,8,4096]{2,1,0:T(8,128)(2,1)S(1)} collective-permute-done((bf16[1,8,4096]{2,1,0:T(8,128)(2,1)S(1)}, bf16[1,8,4096]{2,1,0:T(8,128)(2,1)S(1)}, u32[]{:S(2)}, u32[]{:S(2)}) %collective-permute-start.2) | collective-permute-done | bytes 65568 | tf_op jit(solution)/shard_map/ppermute | solution.py:47
  17.1 2.2 %collective-permute-start.6 = (bf16[4,8,4096]{2,1,0:T(8,128)(2,1)S(1)}, bf16[4,8,4096]{2,1,0:T(8,128)(2,1)S(1)}, u32[]{:S(2)}, u32[]{:S(2)}) collective-permute-start(bf16[4,8,4096]{2,1,0:T(8,128)(2,1)S(1)} %get-tuple-element.52), channel_id=1, source_target_pairs={{0,6},{1,7},{2,4},{3,5},{4,2},{5,3},{6,0},{7,1},{8,14},{9,15},{10,... | collective-permute-start | bytes 786440 | tf_op jit(solution)/shard_map/ppermute | solution.py:47
  21.6 3.5 %collective-permute-done.6 = bf16[4,8,4096]{2,1,0:T(8,128)(2,1)S(1)} collective-permute-done((bf16[4,8,4096]{2,1,0:T(8,128)(2,1)S(1)}, bf16[4,8,4096]{2,1,0:T(8,128)(2,1)S(1)}, u32[]{:S(2)}, u32[]{:S(2)}) %collective-permute-start.6) | collective-permute-done | bytes 262176 | tf_op jit(solution)/shard_map/ppermute | solution.py:47
  25.1 5.7 %collective-permute-done.5 = bf16[4,8,4096]{2,1,0:T(8,128)(2,1)S(1)} collective-permute-done((bf16[4,8,4096]{2,1,0:T(8,128)(2,1)S(1)}, bf16[4,8,4096]{2,1,0:T(8,128)(2,1)S(1)}, u32[]{:S(2)}, u32[]{:S(2)}) %collective-permute-start.5) | collective-permute-done | bytes 262176 | tf_op jit(solution)/shard_map/ppermute | solution.py:47
  30.7 1.1 %collective-permute-done.4 = bf16[4,8,4096]{2,1,0:T(8,128)(2,1)S(1)} collective-permute-done((bf16[4,8,4096]{2,1,0:T(8,128)(2,1)S(1)}, bf16[4,8,4096]{2,1,0:T(8,128)(2,1)S(1)}, u32[]{:S(2)}, u32[]{:S(2)}) %collective-permute-start.4) | collective-permute-done | bytes 262176 | tf_op jit(solution)/shard_map/ppermute | solution.py:47
  32.4 1.3 %bitcast_select_fusion.s_all = bf16[128,4096]{1,0:T(8,128)(2,1)} fusion(bf16[4,2,2,8,4096]{4,3,1,2,0:T(8,128)(2,1)S(1)} %copy.14, bf16[4,4,8,4096]{3,2,1,0:T(8,128)(2,1)S(1)} %pad_maximum_fusion.2, pred[]{:T(512)S(6)} %eq.5), kind=kLoop, calls=%fused_computation.7 | loop fusion | flops 524288 | bytes 3145729 | tf_op jit(solution)/shard_map/jit(_where)/select_n | solution.py:68
  34.2 12.8 %shard_map.84 = (bf16[128,2048]{1,0:T(8,128)(2,1)}, bf16[128,2048]{1,0:T(8,128)(2,1)}, f32[128,2048]{1,0:T(8,128)}, f32[128,2048]{1,0:T(8,128)}, f32[128,4096]{1,0:T(8,128)}) custom-call(bf16[128,2048]{1,0:T(8,128)(2,1)} %maximum_select_fusion.q_all, bf16[128,2048]{1,0:T(8,128)(2,1)} %copy-done.2, bf16[128,2048]{1,0:T(8,128)(2,1)} %copy-done.1, ...), custom_call_target="tpu_custom_call" | custom-call | flops 805306368 | bytes 7340032 | tf_op jit(solution)/shard_map/pallas_call | solution.py:217
  47.0 1.9 %copy.15 = f32[4,2,2,8,4096]{4,3,2,1,0:T(8,128)S(1)} copy(f32[4,2,2,8,4096]{4,3,1,2,0:T(8,128)} %bitcast.73) | data formatting | bytes 4194304 | tf_op jit(solution)/shard_map/transpose | solution.py:67
  49.6 1.3 %collective-permute-start.8 = (bf16[4,8,4096]{2,1,0:T(8,128)(2,1)S(1)}, bf16[4,8,4096]{2,1,0:T(8,128)(2,1)S(1)}, u32[]{:S(2)}, u32[]{:S(2)}) collective-permute-start(bf16[4,8,4096]{2,1,0:T(8,128)(2,1)S(1)} %get-tuple-element.17), channel_id=1, source_target_pairs={{0,2},{1,5},{2,0},{3,7},{4,6},{5,1},{6,4},{7,3},{8,10},{9,13},{10,... | collective-permute-start | bytes 786440 | tf_op jit(solution)/shard_map/ppermute | solution.py:47
  50.9 1.2 %collective-permute-start.10 = (bf16[4,8,4096]{2,1,0:T(8,128)(2,1)S(1)}, bf16[4,8,4096]{2,1,0:T(8,128)(2,1)S(1)}, u32[]{:S(2)}, u32[]{:S(2)}) collective-permute-start(bf16[4,8,4096]{2,1,0:T(8,128)(2,1)S(1)} %get-tuple-element.18), channel_id=1, source_target_pairs={{0,6},{1,7},{2,4},{3,5},{4,2},{5,3},{6,0},{7,1},{8,14},{9,15},{10,... | collective-permute-start | bytes 786440 | tf_op jit(solution)/shard_map/ppermute | solution.py:47
  52.5 4.3 %collective-permute-done.8 = bf16[4,8,4096]{2,1,0:T(8,128)(2,1)S(1)} collective-permute-done((bf16[4,8,4096]{2,1,0:T(8,128)(2,1)S(1)}, bf16[4,8,4096]{2,1,0:T(8,128)(2,1)S(1)}, u32[]{:S(2)}, u32[]{:S(2)}) %collective-permute-start.8) | collective-permute-done | bytes 262176 | tf_op jit(solution)/shard_map/ppermute | solution.py:47
  56.8 3.4 %collective-permute-done.10 = bf16[4,8,4096]{2,1,0:T(8,128)(2,1)S(1)} collective-permute-done((bf16[4,8,4096]{2,1,0:T(8,128)(2,1)S(1)}, bf16[4,8,4096]{2,1,0:T(8,128)(2,1)S(1)}, u32[]{:S(2)}, u32[]{:S(2)}) %collective-permute-start.10) | collective-permute-done | bytes 262176 | tf_op jit(solution)/shard_map/ppermute | solution.py:47
  60.2 4.5 %collective-permute-done.9 = bf16[4,8,4096]{2,1,0:T(8,128)(2,1)S(1)} collective-permute-done((bf16[4,8,4096]{2,1,0:T(8,128)(2,1)S(1)}, bf16[4,8,4096]{2,1,0:T(8,128)(2,1)S(1)}, u32[]{:S(2)}, u32[]{:S(2)}) %collective-permute-start.9) | collective-permute-done | bytes 262176 | tf_op jit(solution)/shard_map/ppermute | solution.py:47
  65.1 1.8 %collective-permute-start.13 = (bf16[1,8,4096]{2,1,0:T(8,128)(2,1)S(1)}, bf16[1,8,4096]{2,1,0:T(8,128)(2,1)S(1)}, u32[]{:S(2)}, u32[]{:S(2)}) collective-permute-start(bf16[1,8,4096]{2,1,0:T(8,128)(2,1)S(1)} %get-tuple-element.35), channel_id=1, source_target_pairs={{0,24},{1,25},{2,26},{3,27},{4,28},{5,29},{6,30},{7,31},{8,16},{9,... | collective-permute-start | bytes 196616 | tf_op jit(solution)/shard_map/ppermute | solution.py:47
  68.4 1.9 %collective-permute-start.7 = (bf16[64,4096]{1,0:T(8,128)(2,1)}, bf16[64,4096]{1,0:T(8,128)(2,1)}, u32[]{:S(2)}, u32[]{:S(2)}) collective-permute-start(bf16[64,4096]{1,0:T(8,128)(2,1)} %pad_maximum_fusion.3), channel_id=1, source_target_pairs={{0,1},{1,0},{2,3},{3,2},{4,5},{5,4},{6,7},{7,6},{8,9},{9,8},{10,11... | collective-permute-start | bytes 1572872 | tf_op jit(solution)/shard_map/ppermute | solution.py:112
  70.4 3.5 %collective-permute-done.12 = bf16[1,8,4096]{2,1,0:T(8,128)(2,1)S(1)} collective-permute-done((bf16[1,8,4096]{2,1,0:T(8,128)(2,1)S(1)}, bf16[1,8,4096]{2,1,0:T(8,128)(2,1)S(1)}, u32[]{:S(2)}, u32[]{:S(2)}) %collective-permute-start.12) | collective-permute-done | bytes 65568 | tf_op jit(solution)/shard_map/ppermute | solution.py:47
  73.9 1.1 %scatter_custom_fusion = f32[128,2048]{1,0:T(8,128)S(1)} fusion(f32[128,2048]{1,0:T(8,128)S(1)} %copy-done.4, s32[8]{0:T(128)S(1)} %fusion.9, f32[8,16,2,128]{3,0,2,1:T(8,128)S(1)} %bitcast.76), kind=kCustom, calls=%fused_computation.37 | custom fusion | flops 16384 | bytes 1114112 | tf_op jit(solution)/shard_map/scatter-add | solution.py:270
  75.1 1.1 %scatter_custom_fusion.1 = f32[128,2048]{1,0:T(8,128)S(1)} fusion(f32[128,2048]{1,0:T(8,128)S(1)} %copy-done.3, s32[8]{0:T(128)S(1)} %fusion.9, f32[8,16,2,128]{3,0,2,1:T(8,128)S(1)} %bitcast.77), kind=kCustom, calls=%fused_computation.35 | custom fusion | flops 16384 | bytes 1114112 | tf_op jit(solution)/shard_map/scatter-add | solution.py:271
  76.4 1.5 %collective-permute-start.14 = (bf16[64,4096]{1,0:T(8,128)(2,1)S(1)}, bf16[64,4096]{1,0:T(8,128)(2,1)S(1)}, u32[]{:S(2)}, u32[]{:S(2)}) collective-permute-start(bf16[64,4096]{1,0:T(8,128)(2,1)S(1)} %pad_maximum_fusion.4), channel_id=1, source_target_pairs={{0,1},{1,0},{2,3},{3,2},{4,5},{5,4},{6,7},{7,6},{8,9},{9,8},{10,11... | collective-permute-start | bytes 1572872 | tf_op jit(solution)/shard_map/ppermute | solution.py:112
  77.9 1.1 %fusion.12 = (bf16[64,2048]{1,0:T(8,128)(2,1)S(1)}, bf16[64,2048]{1,0:T(8,128)(2,1)S(1)}) fusion(bf16[64,4096]{1,0:T(8,128)(2,1)} %collective-permute-done.7), kind=kLoop, calls=%fused_computation.80 | loop fusion | bytes 1048576 | tf_op jit(solution)/shard_map/slice | solution.py:136
  (75 shorter events, 13.1 us)
Async XLA Ops:
  0.6 1.4 %copy-start.7 = (bf16[64,4096]{1,0:T(8,128)(2,1)S(1)}, bf16[64,4096]{1,0:T(8,128)(2,1)}, u32[]{:S(2)}) copy-start(bf16[64,4096]{1,0:T(8,128)(2,1)} %param.10) | copy-start | bytes 1572868
  0.6 1.5 %copy-start.8 = (bf16[64,4096]{1,0:T(8,128)(2,1)S(1)}, bf16[64,4096]{1,0:T(8,128)(2,1)}, u32[]{:S(2)}) copy-start(bf16[64,4096]{1,0:T(8,128)(2,1)} %param.9) | copy-start | bytes 1572868
  2.3 2.7 %collective-permute-start = (bf16[64,8192]{1,0:T(8,128)(2,1)S(1)}, bf16[64,8192]{1,0:T(8,128)(2,1)S(1)}, u32[]{:S(2)}, u32[]{:S(2)}) collective-permute-start(bf16[64,8192]{1,0:T(8,128)(2,1)S(1)} %pad_maximum_fusion), channel_id=1, source_target_pairs={{0,1},{1,0},{2,3},{3,2},{4,5},{5,4},{6,7},{7,6},{8,9},{9,8},{10,11... | collective-permute-start | bytes 3145736 | tf_op jit(solution)/shard_map/ppermute | solution.py:112
  5.3 15.4 %copy-start.1 = (bf16[128,2048]{1,0:T(8,128)(2,1)}, bf16[128,2048]{1,0:T(8,128)(2,1)S(1)}, u32[]{:S(2)}) copy-start(bf16[128,2048]{1,0:T(8,128)(2,1)S(1)} %maximum_select_fusion.2.v_all) | copy-start | bytes 1572868
  6.0 15.6 %copy-start.2 = (bf16[128,2048]{1,0:T(8,128)(2,1)}, bf16[128,2048]{1,0:T(8,128)(2,1)S(1)}, u32[]{:S(2)}) copy-start(bf16[128,2048]{1,0:T(8,128)(2,1)S(1)} %maximum_select_fusion.1.k_all) | copy-start | bytes 1572868
  6.7 6.7 %collective-permute-start.3 = (bf16[1,8,4096]{2,1,0:T(8,128)(2,1)S(1)}, bf16[1,8,4096]{2,1,0:T(8,128)(2,1)S(1)}, u32[]{:S(2)}, u32[]{:S(2)}) collective-permute-start(bf16[1,8,4096]{2,1,0:T(8,128)(2,1)S(1)} %bitcast.78), channel_id=1, source_target_pairs={{0,24},{1,25},{2,26},{3,27},{4,28},{5,29},{6,30},{7,31},{8,16},{9,... | collective-permute-start | bytes 196616 | tf_op jit(solution)/shard_map/ppermute | solution.py:47
  11.2 5.7 %collective-permute-start.2 = (bf16[1,8,4096]{2,1,0:T(8,128)(2,1)S(1)}, bf16[1,8,4096]{2,1,0:T(8,128)(2,1)S(1)}, u32[]{:S(2)}, u32[]{:S(2)}) collective-permute-start(bf16[1,8,4096]{2,1,0:T(8,128)(2,1)S(1)} %bitcast.79), channel_id=1, source_target_pairs={{0,16},{1,17},{2,18},{3,19},{4,20},{5,21},{6,22},{7,23},{8,24},{9,... | collective-permute-start | bytes 196616 | tf_op jit(solution)/shard_map/ppermute | solution.py:47
  11.2 5.7 %collective-permute-start.1 = (bf16[1,8,4096]{2,1,0:T(8,128)(2,1)S(1)}, bf16[1,8,4096]{2,1,0:T(8,128)(2,1)S(1)}, u32[]{:S(2)}, u32[]{:S(2)}) collective-permute-start(bf16[1,8,4096]{2,1,0:T(8,128)(2,1)S(1)} %bitcast.80), channel_id=1, source_target_pairs={{0,8},{1,9},{2,10},{3,11},{4,12},{5,13},{6,14},{7,15},{8,0},{9,1},... | collective-permute-start | bytes 196616 | tf_op jit(solution)/shard_map/ppermute | solution.py:47
  17.1 8.0 %collective-permute-start.6 = (bf16[4,8,4096]{2,1,0:T(8,128)(2,1)S(1)}, bf16[4,8,4096]{2,1,0:T(8,128)(2,1)S(1)}, u32[]{:S(2)}, u32[]{:S(2)}) collective-permute-start(bf16[4,8,4096]{2,1,0:T(8,128)(2,1)S(1)} %get-tuple-element.52), channel_id=1, source_target_pairs={{0,6},{1,7},{2,4},{3,5},{4,2},{5,3},{6,0},{7,1},{8,14},{9,15},{10,... | collective-permute-start | bytes 786440 | tf_op jit(solution)/shard_map/ppermute | solution.py:47
  19.3 11.4 %collective-permute-start.5 = (bf16[4,8,4096]{2,1,0:T(8,128)(2,1)S(1)}, bf16[4,8,4096]{2,1,0:T(8,128)(2,1)S(1)}, u32[]{:S(2)}, u32[]{:S(2)}) collective-permute-start(bf16[4,8,4096]{2,1,0:T(8,128)(2,1)S(1)} %get-tuple-element.52), channel_id=1, source_target_pairs={{0,4},{1,3},{2,6},{3,1},{4,0},{5,7},{6,2},{7,5},{8,12},{9,11},{10,... | collective-permute-start | bytes 786440 | tf_op jit(solution)/shard_map/ppermute | solution.py:47
  19.5 12.3 %collective-permute-start.4 = (bf16[4,8,4096]{2,1,0:T(8,128)(2,1)S(1)}, bf16[4,8,4096]{2,1,0:T(8,128)(2,1)S(1)}, u32[]{:S(2)}, u32[]{:S(2)}) collective-permute-start(bf16[4,8,4096]{2,1,0:T(8,128)(2,1)S(1)} %get-tuple-element.52), channel_id=1, source_target_pairs={{0,2},{1,5},{2,0},{3,7},{4,6},{5,1},{6,4},{7,3},{8,10},{9,13},{10,... | collective-permute-start | bytes 786440 | tf_op jit(solution)/shard_map/ppermute | solution.py:47
  47.0 2.2 %copy-start = (f32[128,4096]{1,0:T(8,128)S(1)}, f32[128,4096]{1,0:T(8,128)}, u32[]{:S(2)}) copy-start(f32[128,4096]{1,0:T(8,128)} %get-tuple-element.13) | copy-start | bytes 6291460
  49.3 3.1 %copy-start.6 = (bf16[128,2048]{1,0:T(8,128)(2,1)S(1)}, bf16[128,2048]{1,0:T(8,128)(2,1)}, u32[]{:S(2)}) copy-start(bf16[128,2048]{1,0:T(8,128)(2,1)} %get-tuple-element.10) | copy-start | bytes 1572868
  49.5 2.9 %copy-start.5 = (bf16[128,2048]{1,0:T(8,128)(2,1)S(1)}, bf16[128,2048]{1,0:T(8,128)(2,1)}, u32[]{:S(2)}) copy-start(bf16[128,2048]{1,0:T(8,128)(2,1)} %get-tuple-element.11) | copy-start | bytes 1572868
  49.6 7.1 %collective-permute-start.8 = (bf16[4,8,4096]{2,1,0:T(8,128)(2,1)S(1)}, bf16[4,8,4096]{2,1,0:T(8,128)(2,1)S(1)}, u32[]{:S(2)}, u32[]{:S(2)}) collective-permute-start(bf16[4,8,4096]{2,1,0:T(8,128)(2,1)S(1)} %get-tuple-element.17), channel_id=1, source_target_pairs={{0,2},{1,5},{2,0},{3,7},{4,6},{5,1},{6,4},{7,3},{8,10},{9,13},{10,... | collective-permute-start | bytes 786440 | tf_op jit(solution)/shard_map/ppermute | solution.py:47
  50.9 9.2 %collective-permute-start.10 = (bf16[4,8,4096]{2,1,0:T(8,128)(2,1)S(1)}, bf16[4,8,4096]{2,1,0:T(8,128)(2,1)S(1)}, u32[]{:S(2)}, u32[]{:S(2)}) collective-permute-start(bf16[4,8,4096]{2,1,0:T(8,128)(2,1)S(1)} %get-tuple-element.18), channel_id=1, source_target_pairs={{0,6},{1,7},{2,4},{3,5},{4,2},{5,3},{6,0},{7,1},{8,14},{9,15},{10,... | collective-permute-start | bytes 786440 | tf_op jit(solution)/shard_map/ppermute | solution.py:47
  52.2 12.5 %collective-permute-start.9 = (bf16[4,8,4096]{2,1,0:T(8,128)(2,1)S(1)}, bf16[4,8,4096]{2,1,0:T(8,128)(2,1)S(1)}, u32[]{:S(2)}, u32[]{:S(2)}) collective-permute-start(bf16[4,8,4096]{2,1,0:T(8,128)(2,1)S(1)} %get-tuple-element.19), channel_id=1, source_target_pairs={{0,4},{1,3},{2,6},{3,1},{4,0},{5,7},{6,2},{7,5},{8,12},{9,11},{10,... | collective-permute-start | bytes 786440 | tf_op jit(solution)/shard_map/ppermute | solution.py:47
  52.5 21.4 %copy-start.4 = (f32[128,2048]{1,0:T(8,128)S(1)}, f32[128,2048]{1,0:T(8,128)}, u32[]{:S(2)}) copy-start(f32[128,2048]{1,0:T(8,128)} %get-tuple-element.12) | copy-start | bytes 3145732
  64.9 5.4 %collective-permute-start.11 = (bf16[1,8,4096]{2,1,0:T(8,128)(2,1)S(1)}, bf16[1,8,4096]{2,1,0:T(8,128)(2,1)S(1)}, u32[]{:S(2)}, u32[]{:S(2)}) collective-permute-start(bf16[1,8,4096]{2,1,0:T(8,128)(2,1)S(1)} %get-tuple-element.34), channel_id=1, source_target_pairs={{0,8},{1,9},{2,10},{3,11},{4,12},{5,13},{6,14},{7,15},{8,0},{9,1},... | collective-permute-start | bytes 196616 | tf_op jit(solution)/shard_map/ppermute | solution.py:47
  65.1 5.3 %collective-permute-start.13 = (bf16[1,8,4096]{2,1,0:T(8,128)(2,1)S(1)}, bf16[1,8,4096]{2,1,0:T(8,128)(2,1)S(1)}, u32[]{:S(2)}, u32[]{:S(2)}) collective-permute-start(bf16[1,8,4096]{2,1,0:T(8,128)(2,1)S(1)} %get-tuple-element.35), channel_id=1, source_target_pairs={{0,24},{1,25},{2,26},{3,27},{4,28},{5,29},{6,30},{7,31},{8,16},{9,... | collective-permute-start | bytes 196616 | tf_op jit(solution)/shard_map/ppermute | solution.py:47
  66.9 7.0 %collective-permute-start.12 = (bf16[1,8,4096]{2,1,0:T(8,128)(2,1)S(1)}, bf16[1,8,4096]{2,1,0:T(8,128)(2,1)S(1)}, u32[]{:S(2)}, u32[]{:S(2)}) collective-permute-start(bf16[1,8,4096]{2,1,0:T(8,128)(2,1)S(1)} %get-tuple-element.36), channel_id=1, source_target_pairs={{0,16},{1,17},{2,18},{3,19},{4,20},{5,21},{6,22},{7,23},{8,24},{9,... | collective-permute-start | bytes 196616 | tf_op jit(solution)/shard_map/ppermute | solution.py:47
  67.6 7.5 %copy-start.3 = (f32[128,2048]{1,0:T(8,128)S(1)}, f32[128,2048]{1,0:T(8,128)}, u32[]{:S(2)}) copy-start(f32[128,2048]{1,0:T(8,128)} %get-tuple-element.14) | copy-start | bytes 3145732
  68.4 9.5 %collective-permute-start.7 = (bf16[64,4096]{1,0:T(8,128)(2,1)}, bf16[64,4096]{1,0:T(8,128)(2,1)}, u32[]{:S(2)}, u32[]{:S(2)}) collective-permute-start(bf16[64,4096]{1,0:T(8,128)(2,1)} %pad_maximum_fusion.3), channel_id=1, source_target_pairs={{0,1},{1,0},{2,3},{3,2},{4,5},{5,4},{6,7},{7,6},{8,9},{9,8},{10,11... | collective-permute-start | bytes 1572872 | tf_op jit(solution)/shard_map/ppermute | solution.py:112
  76.4 4.4 %collective-permute-start.14 = (bf16[64,4096]{1,0:T(8,128)(2,1)S(1)}, bf16[64,4096]{1,0:T(8,128)(2,1)S(1)}, u32[]{:S(2)}, u32[]{:S(2)}) collective-permute-start(bf16[64,4096]{1,0:T(8,128)(2,1)S(1)} %pad_maximum_fusion.4), channel_id=1, source_target_pairs={{0,1},{1,0},{2,3},{3,2},{4,5},{5,4},{6,7},{7,6},{8,9},{9,8},{10,11... | collective-permute-start | bytes 1572872 | tf_op jit(solution)/shard_map/ppermute | solution.py:112
  (1 other events, 0.7 us)

commit v10 on v9

--- a/solution.py
+++ b/solution.py
@@ -60,20 +60,15 @@
     return sum(((m >> i) & 1) << b for i, b in enumerate(bits))
 
 
-def swap_low_bits(x, core):
-    if group_bits() < 2:
-        return x
-    size = x.shape[0]
-    swapped = jnp.swapaxes(x.reshape((size // 4, 2, 2) + x.shape[1:]), 1, 2).reshape(x.shape)
-    return jnp.where(core == 1, swapped, x)
+def swap_low_bits(index):
+    return (index & ~3) | ((index & 1) << 1) | ((index >> 1) & 1)
 
 
 def virtual_index(core):
     g = lax.axis_index("seq") * lax.axis_size("hx") + lax.axis_index("hx")
     if group_bits() < 2:
         return g
-    swapped = (g & ~3) | ((g & 1) << 1) | ((g >> 1) & 1)
-    return jnp.where(core == 1, swapped, g)
+    return jnp.where(core == 1, swap_low_bits(g), g)
 
 
 def gather_blocks(x, core):
@@ -87,14 +82,13 @@
             [lax.dynamic_index_in_dim(got, t ^ t_me, 1, keepdims=False) for t in range(width)], 1
         )
         held = held.reshape((-1,) + x.shape)
-    held = swap_low_bits(held, core)
     return held.reshape((-1,) + x.shape[1:])
 
 
 def reduce_blocks(x, core):
     me = virtual_index(core)
     size = group_size()
-    held = swap_low_bits(x.reshape((size, -1) + x.shape[1:]), core)
+    held = x.reshape((size, -1) + x.shape[1:])
     for bits in rounds():
         width = 1 << len(bits)
         t_me = round_index(me, bits)
@@ -258,7 +252,11 @@
     ).reshape(-1, 2 * half)
     all_sum = gather_blocks(own_sum, core)
     sum_count = all_sum.shape[0]
-    key_block = jnp.arange(sum_count, dtype=jnp.int32) // SUMMARY
+    slot = jnp.arange(sum_count, dtype=jnp.int32) // SUMMARY
+    member = slot // nb
+    if group_bits() >= 2:
+        member = jnp.where(core == 1, swap_low_bits(member), member)
+    key_block = member * nb + slot % nb
     query_block = first_block + jnp.arange(nb, dtype=jnp.int32)
     mask = (key_block[None, :] < query_block[:, None]).astype(jnp.int32)
     mask = jnp.repeat(mask, 8, axis=0)

time: 82.9 us -> 82.5 us (level)
  waiting for transfers between devices: 33.7 us -> 32.6 us
    transpose x1 -> x0, local copies, waits for them, and re-layouts: 1.89 us -> none  [swap_low_bits(): jnp.swapaxes(x.reshape((size // 4, 2, 2) + x.shape[1:]), 1, 2)]
    select_n x2 -> x0, other arithmetic: 1.53 us -> none  [swap_low_bits(): return jnp.where(core == 1, swapped, x)]
    convert_element_type x2, local copies, waits for them, and re-layouts: 0.13 us -> 1.54 us  [reduce_blocks(): got = exchange(send.astype(jnp.bfloat16), round_mask(m, bits))]
    another operation x1, other arithmetic: 0.13 us -> 1.17 us  [gather_blocks(): jnp.stack([lax.dynamic_index_in_dim(got, t ^ t_me, 1, keepdims=False) for...]
    dynamic_slice x4, local copies, waits for them, and re-layouts: 0.18 us -> 1.2 us  [to_token_layout(): mine = [lax.dynamic_slice_in_dim(a, core * rows, rows, 0) for a in arrays]]
    add x2, other arithmetic: 0.15 us -> 1.18 us  [reduce_blocks(): total = total + got.astype(jnp.float32)]
    ppermute x12, waiting for transfers between devices: 31.4 us -> 30.4 us  [exchange(): return lax.ppermute(x, ('seq', 'hx', 'hc'), pairs)]
  transfers between devices with their start and end apart: 15 -> 15, of which waited for: 11 -> 11; matrix products, arithmetic and copies ran while one was open for 10% -> 11% of each run, Pallas kernels for 0% -> 0%
where the time goes in v10:
time: 82.5 us; the launch traced here: 82.2 us
  waiting for transfers between devices  32.6 us (40%)
  starting transfers between devices  16.5 us (20%)
  Pallas kernels  12.8 us (16%)
  other arithmetic  11.6 us (14%)
  local copies, waits for them, and re-layouts  7.78 us (9%)
  between operations  0.97 us (1%)
    ppermute x12, waiting for transfers between devices, exchange(): return lax.ppermute(x, ('seq', 'hx', 'hc'), pairs)  30.4 us
    ppermute x12, starting transfers between devices, exchange(): return lax.ppermute(x, ('seq', 'hx', 'hc'), pairs)  13 us
    pallas_call x1, Pallas kernels, attention(): pl.pallas_call(attention_kernel, grid=(heads // per_step, nb), in_specs=[...  12.8 us
    select_n x4, other arithmetic, to_token_layout(): jnp.where(core == 0, jnp.concatenate([m, r], 1), jnp.concatenate([r, m], 1))  3.66 us
    ppermute x3, starting transfers between devices, swap_with_partner(): return lax.ppermute(x, 'hc', [(0, 1), (1, 0)])  3.45 us
    ppermute x3, waiting for transfers between devices, swap_with_partner(): return lax.ppermute(x, 'hc', [(0, 1), (1, 0)])  2.22 us
    select_n x4, other arithmetic, to_block_layout(): jnp.where(core == 0, jnp.concatenate([m, r], 0), jnp.concatenate([r, m], 0))  2.01 us
  transfers between devices with their start and end apart: 15, of which 11 were waited for; matrix products, arithmetic and copies ran while one was open for 11% of the time, Pallas kernels for 0%

profile of v10, /device:TPU:1, one launch (start us, length us, event | category | flops | bytes accessed | tf_op | source)
XLA Modules:
  0.0 82.2 jit_solution(15881945510104191306)
XLA Ops:
  0.7 1.3 %constant_dynamic-slice_fusion.19 = (bf16[64,2048]{1,0:T(8,128)(2,1)S(1)}, bf16[64,2048]{1,0:T(8,128)(2,1)S(1)}, bf16[64,2048]{1,0:T(8,128)(2,1)S(1)}, bf16[64,2048]{1,0:T(8,128)(2,1)S(1)}) fusion(bf16[64,4096]{1,0:T(8,128)(2,1)} %param.8, s32[]{:T(128)S(6)} %select_n.157, s32[]{:T(128)S(6)} %select_n.158, bf16[64,4096]{1,0:T(8,128)(2,1)} %param.7), kind=kLoop, calls=%fused_computation.60 | loop fusion | bytes 2097160 | tf_op jit(solution)/shard_map/dynamic_slice | solution.py:112
  2.9 2.2 %collective-permute-done = bf16[64,8192]{1,0:T(8,128)(2,1)S(1)} collective-permute-done((bf16[64,8192]{1,0:T(8,128)(2,1)S(1)}, bf16[64,8192]{1,0:T(8,128)(2,1)S(1)}, u32[]{:S(2)}, u32[]{:S(2)}) %collective-permute-start) | collective-permute-done | bytes 1048608 | tf_op jit(solution)/shard_map/ppermute | solution.py:106
  6.7 4.5 %collective-permute-start.3 = (bf16[1,8,4096]{2,1,0:T(8,128)(2,1)S(1)}, bf16[1,8,4096]{2,1,0:T(8,128)(2,1)S(1)}, u32[]{:S(2)}, u32[]{:S(2)}) collective-permute-start(bf16[1,8,4096]{2,1,0:T(8,128)(2,1)S(1)} %bitcast.67), channel_id=1, source_target_pairs={{0,24},{1,25},{2,26},{3,27},{4,28},{5,29},{6,30},{7,31},{8,16},{9,... | collective-permute-start | bytes 196616 | tf_op jit(solution)/shard_map/ppermute | solution.py:47
  11.6 1.8 %collective-permute-done.3 = bf16[1,8,4096]{2,1,0:T(8,128)(2,1)S(1)} collective-permute-done((bf16[1,8,4096]{2,1,0:T(8,128)(2,1)S(1)}, bf16[1,8,4096]{2,1,0:T(8,128)(2,1)S(1)}, u32[]{:S(2)}, u32[]{:S(2)}) %collective-permute-start.3) | collective-permute-done | bytes 65568 | tf_op jit(solution)/shard_map/ppermute | solution.py:47
  13.4 3.5 %collective-permute-done.2 = bf16[1,8,4096]{2,1,0:T(8,128)(2,1)S(1)} collective-permute-done((bf16[1,8,4096]{2,1,0:T(8,128)(2,1)S(1)}, bf16[1,8,4096]{2,1,0:T(8,128)(2,1)S(1)}, u32[]{:S(2)}, u32[]{:S(2)}) %collective-permute-start.2) | collective-permute-done | bytes 65568 | tf_op jit(solution)/shard_map/ppermute | solution.py:47
  17.1 2.2 %collective-permute-start.6 = (bf16[4,8,4096]{2,1,0:T(8,128)(2,1)S(1)}, bf16[4,8,4096]{2,1,0:T(8,128)(2,1)S(1)}, u32[]{:S(2)}, u32[]{:S(2)}) collective-permute-start(bf16[4,8,4096]{2,1,0:T(8,128)(2,1)S(1)} %get-tuple-element.52), channel_id=1, source_target_pairs={{0,6},{1,7},{2,4},{3,5},{4,2},{5,3},{6,0},{7,1},{8,14},{9,15},{10,... | collective-permute-start | bytes 786440 | tf_op jit(solution)/shard_map/ppermute | solution.py:47
  21.6 3.5 %collective-permute-done.6 = bf16[4,8,4096]{2,1,0:T(8,128)(2,1)S(1)} collective-permute-done((bf16[4,8,4096]{2,1,0:T(8,128)(2,1)S(1)}, bf16[4,8,4096]{2,1,0:T(8,128)(2,1)S(1)}, u32[]{:S(2)}, u32[]{:S(2)}) %collective-permute-start.6) | collective-permute-done | bytes 262176 | tf_op jit(solution)/shard_map/ppermute | solution.py:47
  25.1 5.7 %collective-permute-done.5 = bf16[4,8,4096]{2,1,0:T(8,128)(2,1)S(1)} collective-permute-done((bf16[4,8,4096]{2,1,0:T(8,128)(2,1)S(1)}, bf16[4,8,4096]{2,1,0:T(8,128)(2,1)S(1)}, u32[]{:S(2)}, u32[]{:S(2)}) %collective-permute-start.5) | collective-permute-done | bytes 262176 | tf_op jit(solution)/shard_map/ppermute | solution.py:47
  30.7 1.1 %collective-permute-done.4 = bf16[4,8,4096]{2,1,0:T(8,128)(2,1)S(1)} collective-permute-done((bf16[4,8,4096]{2,1,0:T(8,128)(2,1)S(1)}, bf16[4,8,4096]{2,1,0:T(8,128)(2,1)S(1)}, u32[]{:S(2)}, u32[]{:S(2)}) %collective-permute-start.4) | collective-permute-done | bytes 262176 | tf_op jit(solution)/shard_map/ppermute | solution.py:47
  32.1 1.2 %pad_maximum_fusion.2 = bf16[4,4,8,4096]{3,2,1,0:T(8,128)(2,1)} fusion(bf16[4,1,8,4096]{3,2,1,0:T(8,128)(2,1)S(1)} %get-tuple-element.21, bf16[4,1,8,4096]{3,2,1,0:T(8,128)(2,1)S(1)} %get-tuple-element.22, bf16[4,1,8,4096]{3,2,1,0:T(8,128)(2,1)S(1)} %get-tuple-element.23, bf16[4,1,8,4096]{3,2,1,0:T(8,128)(2,1)S(1)} %get-tuple-element.20), kind=kLoop, calls=%fused_computation.6 | loop fusion | flops 1572864 | bytes 2097152 | tf_op jit(solution)/shard_map/stack | solution.py:81
  33.9 12.8 %shard_map.84 = (bf16[128,2048]{1,0:T(8,128)(2,1)}, bf16[128,2048]{1,0:T(8,128)(2,1)}, f32[128,2048]{1,0:T(8,128)}, f32[128,2048]{1,0:T(8,128)}, f32[128,4096]{1,0:T(8,128)}) custom-call(bf16[128,2048]{1,0:T(8,128)(2,1)} %maximum_select_fusion.q_all, bf16[128,2048]{1,0:T(8,128)(2,1)} %copy-done.1, bf16[128,2048]{1,0:T(8,128)(2,1)} %copy-done, ...), custom_call_target="tpu_custom_call" | custom-call | flops 805306368 | bytes 7340032 | tf_op jit(solution)/shard_map/pallas_call | solution.py:211
  46.6 1.5 %fusion.3 = (bf16[4,8,4096]{2,1,0:T(8,128)(2,1)S(1)}, bf16[4,8,4096]{2,1,0:T(8,128)(2,1)S(1)}, bf16[4,8,4096]{2,1,0:T(8,128)(2,1)S(1)}) fusion(f32[4,4,8,4096]{3,2,1,0:T(8,128)} %bitcast.63, s32[]{:T(128)S(6)} %select_n.170, s32[]{:T(128)S(6)} %select_n.172, s32[]{:T(128)S(6)} %select_n.171), kind=kLoop, calls=%fused_computation.24 | loop fusion | bytes 1572876 | tf_op jit(solution)/shard_map/convert_element_type | solution.py:99
  48.2 1.3 %collective-permute-start.8 = (bf16[4,8,4096]{2,1,0:T(8,128)(2,1)S(1)}, bf16[4,8,4096]{2,1,0:T(8,128)(2,1)S(1)}, u32[]{:S(2)}, u32[]{:S(2)}) collective-permute-start(bf16[4,8,4096]{2,1,0:T(8,128)(2,1)S(1)} %get-tuple-element.17), channel_id=1, source_target_pairs={{0,2},{1,5},{2,0},{3,7},{4,6},{5,1},{6,4},{7,3},{8,10},{9,13},{10,... | collective-permute-start | bytes 786440 | tf_op jit(solution)/shard_map/ppermute | solution.py:47
  49.5 1.2 %collective-permute-start.10 = (bf16[4,8,4096]{2,1,0:T(8,128)(2,1)S(1)}, bf16[4,8,4096]{2,1,0:T(8,128)(2,1)S(1)}, u32[]{:S(2)}, u32[]{:S(2)}) collective-permute-start(bf16[4,8,4096]{2,1,0:T(8,128)(2,1)S(1)} %get-tuple-element.18), channel_id=1, source_target_pairs={{0,6},{1,7},{2,4},{3,5},{4,2},{5,3},{6,0},{7,1},{8,14},{9,15},{10,... | collective-permute-start | bytes 786440 | tf_op jit(solution)/shard_map/ppermute | solution.py:47
  52.0 3.3 %collective-permute-done.8 = bf16[4,8,4096]{2,1,0:T(8,128)(2,1)S(1)} collective-permute-done((bf16[4,8,4096]{2,1,0:T(8,128)(2,1)S(1)}, bf16[4,8,4096]{2,1,0:T(8,128)(2,1)S(1)}, u32[]{:S(2)}, u32[]{:S(2)}) %collective-permute-start.8) | collective-permute-done | bytes 262176 | tf_op jit(solution)/shard_map/ppermute | solution.py:47
  55.3 3.4 %collective-permute-done.10 = bf16[4,8,4096]{2,1,0:T(8,128)(2,1)S(1)} collective-permute-done((bf16[4,8,4096]{2,1,0:T(8,128)(2,1)S(1)}, bf16[4,8,4096]{2,1,0:T(8,128)(2,1)S(1)}, u32[]{:S(2)}, u32[]{:S(2)}) %collective-permute-start.10) | collective-permute-done | bytes 262176 | tf_op jit(solution)/shard_map/ppermute | solution.py:47
  58.7 4.5 %collective-permute-done.9 = bf16[4,8,4096]{2,1,0:T(8,128)(2,1)S(1)} collective-permute-done((bf16[4,8,4096]{2,1,0:T(8,128)(2,1)S(1)}, bf16[4,8,4096]{2,1,0:T(8,128)(2,1)S(1)}, u32[]{:S(2)}, u32[]{:S(2)}) %collective-permute-start.9) | collective-permute-done | bytes 262176 | tf_op jit(solution)/shard_map/ppermute | solution.py:47
  63.2 1.1 %fusion.1 = f32[4,8,4096]{2,1,0:T(8,128)S(1)} fusion(bf16[4,8,4096]{2,1,0:T(8,128)(2,1)S(1)} %collective-permute-done.10, bf16[4,8,4096]{2,1,0:T(8,128)(2,1)S(1)} %collective-permute-done.9, bf16[4,8,4096]{2,1,0:T(8,128)(2,1)S(1)} %collective-permute-done.8, f32[4,4,8,4096]{3,2,1,0:T(8,128)} %bitcast.64, s32[]{:T(128)S(6)} %select_n.169), kind=kLoop, calls=%fused_computation.21 | loop fusion | flops 786432 | bytes 1835012 | tf_op jit(solution)/shard_map/add | solution.py:100
  64.6 1.8 %collective-permute-start.13 = (bf16[1,8,4096]{2,1,0:T(8,128)(2,1)S(1)}, bf16[1,8,4096]{2,1,0:T(8,128)(2,1)S(1)}, u32[]{:S(2)}, u32[]{:S(2)}) collective-permute-start(bf16[1,8,4096]{2,1,0:T(8,128)(2,1)S(1)} %get-tuple-element.35), channel_id=1, source_target_pairs={{0,24},{1,25},{2,26},{3,27},{4,28},{5,29},{6,30},{7,31},{8,16},{9,... | collective-permute-start | bytes 196616 | tf_op jit(solution)/shard_map/ppermute | solution.py:47
  68.0 1.9 %collective-permute-start.7 = (bf16[64,4096]{1,0:T(8,128)(2,1)}, bf16[64,4096]{1,0:T(8,128)(2,1)}, u32[]{:S(2)}, u32[]{:S(2)}) collective-permute-start(bf16[64,4096]{1,0:T(8,128)(2,1)} %pad_maximum_fusion.3), channel_id=1, source_target_pairs={{0,1},{1,0},{2,3},{3,2},{4,5},{5,4},{6,7},{7,6},{8,9},{9,8},{10,11... | collective-permute-start | bytes 1572872 | tf_op jit(solution)/shard_map/ppermute | solution.py:106
  69.9 3.5 %collective-permute-done.12 = bf16[1,8,4096]{2,1,0:T(8,128)(2,1)S(1)} collective-permute-done((bf16[1,8,4096]{2,1,0:T(8,128)(2,1)S(1)}, bf16[1,8,4096]{2,1,0:T(8,128)(2,1)S(1)}, u32[]{:S(2)}, u32[]{:S(2)}) %collective-permute-start.12) | collective-permute-done | bytes 65568 | tf_op jit(solution)/shard_map/ppermute | solution.py:47
  73.5 1.1 %scatter_custom_fusion = f32[128,2048]{1,0:T(8,128)S(1)} fusion(f32[128,2048]{1,0:T(8,128)S(1)} %copy-done.3, s32[8]{0:T(128)S(1)} %fusion.9, f32[8,16,2,128]{3,0,2,1:T(8,128)S(1)} %bitcast.65), kind=kCustom, calls=%fused_computation.35 | custom fusion | flops 16384 | bytes 1114112 | tf_op jit(solution)/shard_map/scatter-add | solution.py:268
  74.7 1.1 %scatter_custom_fusion.1 = f32[128,2048]{1,0:T(8,128)S(1)} fusion(f32[128,2048]{1,0:T(8,128)S(1)} %copy-done.2, s32[8]{0:T(128)S(1)} %fusion.9, f32[8,16,2,128]{3,0,2,1:T(8,128)S(1)} %bitcast.66), kind=kCustom, calls=%fused_computation.33 | custom fusion | flops 16384 | bytes 1114112 | tf_op jit(solution)/shard_map/scatter-add | solution.py:269
  76.0 1.5 %collective-permute-start.14 = (bf16[64,4096]{1,0:T(8,128)(2,1)S(1)}, bf16[64,4096]{1,0:T(8,128)(2,1)S(1)}, u32[]{:S(2)}, u32[]{:S(2)}) collective-permute-start(bf16[64,4096]{1,0:T(8,128)(2,1)S(1)} %pad_maximum_fusion.4), channel_id=1, source_target_pairs={{0,1},{1,0},{2,3},{3,2},{4,5},{5,4},{6,7},{7,6},{8,9},{9,8},{10,11... | collective-permute-start | bytes 1572872 | tf_op jit(solution)/shard_map/ppermute | solution.py:106
  (67 shorter events, 14.2 us)
Async XLA Ops:
  0.6 1.4 %copy-start.5 = (bf16[64,4096]{1,0:T(8,128)(2,1)S(1)}, bf16[64,4096]{1,0:T(8,128)(2,1)}, u32[]{:S(2)}) copy-start(bf16[64,4096]{1,0:T(8,128)(2,1)} %param.10) | copy-start | bytes 1572868
  0.6 1.5 %copy-start.6 = (bf16[64,4096]{1,0:T(8,128)(2,1)S(1)}, bf16[64,4096]{1,0:T(8,128)(2,1)}, u32[]{:S(2)}) copy-start(bf16[64,4096]{1,0:T(8,128)(2,1)} %param.9) | copy-start | bytes 1572868
  2.1 0.7 copy-start.7
  2.3 2.7 %collective-permute-start = (bf16[64,8192]{1,0:T(8,128)(2,1)S(1)}, bf16[64,8192]{1,0:T(8,128)(2,1)S(1)}, u32[]{:S(2)}, u32[]{:S(2)}) collective-permute-start(bf16[64,8192]{1,0:T(8,128)(2,1)S(1)} %pad_maximum_fusion), channel_id=1, source_target_pairs={{0,1},{1,0},{2,3},{3,2},{4,5},{5,4},{6,7},{7,6},{8,9},{9,8},{10,11... | collective-permute-start | bytes 3145736 | tf_op jit(solution)/shard_map/ppermute | solution.py:106
  5.3 15.4 %copy-start = (bf16[128,2048]{1,0:T(8,128)(2,1)}, bf16[128,2048]{1,0:T(8,128)(2,1)S(1)}, u32[]{:S(2)}) copy-start(bf16[128,2048]{1,0:T(8,128)(2,1)S(1)} %maximum_select_fusion.2.v_all) | copy-start | bytes 1572868
  6.0 15.6 %copy-start.1 = (bf16[128,2048]{1,0:T(8,128)(2,1)}, bf16[128,2048]{1,0:T(8,128)(2,1)S(1)}, u32[]{:S(2)}) copy-start(bf16[128,2048]{1,0:T(8,128)(2,1)S(1)} %maximum_select_fusion.1.k_all) | copy-start | bytes 1572868
  6.7 6.7 %collective-permute-start.3 = (bf16[1,8,4096]{2,1,0:T(8,128)(2,1)S(1)}, bf16[1,8,4096]{2,1,0:T(8,128)(2,1)S(1)}, u32[]{:S(2)}, u32[]{:S(2)}) collective-permute-start(bf16[1,8,4096]{2,1,0:T(8,128)(2,1)S(1)} %bitcast.67), channel_id=1, source_target_pairs={{0,24},{1,25},{2,26},{3,27},{4,28},{5,29},{6,30},{7,31},{8,16},{9,... | collective-permute-start | bytes 196616 | tf_op jit(solution)/shard_map/ppermute | solution.py:47
  11.2 5.7 %collective-permute-start.2 = (bf16[1,8,4096]{2,1,0:T(8,128)(2,1)S(1)}, bf16[1,8,4096]{2,1,0:T(8,128)(2,1)S(1)}, u32[]{:S(2)}, u32[]{:S(2)}) collective-permute-start(bf16[1,8,4096]{2,1,0:T(8,128)(2,1)S(1)} %bitcast.68), channel_id=1, source_target_pairs={{0,16},{1,17},{2,18},{3,19},{4,20},{5,21},{6,22},{7,23},{8,24},{9,... | collective-permute-start | bytes 196616 | tf_op jit(solution)/shard_map/ppermute | solution.py:47
  11.2 5.7 %collective-permute-start.1 = (bf16[1,8,4096]{2,1,0:T(8,128)(2,1)S(1)}, bf16[1,8,4096]{2,1,0:T(8,128)(2,1)S(1)}, u32[]{:S(2)}, u32[]{:S(2)}) collective-permute-start(bf16[1,8,4096]{2,1,0:T(8,128)(2,1)S(1)} %bitcast.69), channel_id=1, source_target_pairs={{0,8},{1,9},{2,10},{3,11},{4,12},{5,13},{6,14},{7,15},{8,0},{9,1},... | collective-permute-start | bytes 196616 | tf_op jit(solution)/shard_map/ppermute | solution.py:47
  17.1 8.0 %collective-permute-start.6 = (bf16[4,8,4096]{2,1,0:T(8,128)(2,1)S(1)}, bf16[4,8,4096]{2,1,0:T(8,128)(2,1)S(1)}, u32[]{:S(2)}, u32[]{:S(2)}) collective-permute-start(bf16[4,8,4096]{2,1,0:T(8,128)(2,1)S(1)} %get-tuple-element.52), channel_id=1, source_target_pairs={{0,6},{1,7},{2,4},{3,5},{4,2},{5,3},{6,0},{7,1},{8,14},{9,15},{10,... | collective-permute-start | bytes 786440 | tf_op jit(solution)/shard_map/ppermute | solution.py:47
  19.3 11.4 %collective-permute-start.5 = (bf16[4,8,4096]{2,1,0:T(8,128)(2,1)S(1)}, bf16[4,8,4096]{2,1,0:T(8,128)(2,1)S(1)}, u32[]{:S(2)}, u32[]{:S(2)}) collective-permute-start(bf16[4,8,4096]{2,1,0:T(8,128)(2,1)S(1)} %get-tuple-element.52), channel_id=1, source_target_pairs={{0,4},{1,3},{2,6},{3,1},{4,0},{5,7},{6,2},{7,5},{8,12},{9,11},{10,... | collective-permute-start | bytes 786440 | tf_op jit(solution)/shard_map/ppermute | solution.py:47
  19.5 12.3 %collective-permute-start.4 = (bf16[4,8,4096]{2,1,0:T(8,128)(2,1)S(1)}, bf16[4,8,4096]{2,1,0:T(8,128)(2,1)S(1)}, u32[]{:S(2)}, u32[]{:S(2)}) collective-permute-start(bf16[4,8,4096]{2,1,0:T(8,128)(2,1)S(1)} %get-tuple-element.52), channel_id=1, source_target_pairs={{0,2},{1,5},{2,0},{3,7},{4,6},{5,1},{6,4},{7,3},{8,10},{9,13},{10,... | collective-permute-start | bytes 786440 | tf_op jit(solution)/shard_map/ppermute | solution.py:47
  46.6 5.3 %copy-start.4 = (bf16[128,2048]{1,0:T(8,128)(2,1)S(1)}, bf16[128,2048]{1,0:T(8,128)(2,1)}, u32[]{:S(2)}) copy-start(bf16[128,2048]{1,0:T(8,128)(2,1)} %get-tuple-element.11) | copy-start | bytes 1572868
  48.2 7.1 %collective-permute-start.8 = (bf16[4,8,4096]{2,1,0:T(8,128)(2,1)S(1)}, bf16[4,8,4096]{2,1,0:T(8,128)(2,1)S(1)}, u32[]{:S(2)}, u32[]{:S(2)}) collective-permute-start(bf16[4,8,4096]{2,1,0:T(8,128)(2,1)S(1)} %get-tuple-element.17), channel_id=1, source_target_pairs={{0,2},{1,5},{2,0},{3,7},{4,6},{5,1},{6,4},{7,3},{8,10},{9,13},{10,... | collective-permute-start | bytes 786440 | tf_op jit(solution)/shard_map/ppermute | solution.py:47
  49.5 9.2 %collective-permute-start.10 = (bf16[4,8,4096]{2,1,0:T(8,128)(2,1)S(1)}, bf16[4,8,4096]{2,1,0:T(8,128)(2,1)S(1)}, u32[]{:S(2)}, u32[]{:S(2)}) collective-permute-start(bf16[4,8,4096]{2,1,0:T(8,128)(2,1)S(1)} %get-tuple-element.18), channel_id=1, source_target_pairs={{0,6},{1,7},{2,4},{3,5},{4,2},{5,3},{6,0},{7,1},{8,14},{9,15},{10,... | collective-permute-start | bytes 786440 | tf_op jit(solution)/shard_map/ppermute | solution.py:47
  50.7 12.5 %collective-permute-start.9 = (bf16[4,8,4096]{2,1,0:T(8,128)(2,1)S(1)}, bf16[4,8,4096]{2,1,0:T(8,128)(2,1)S(1)}, u32[]{:S(2)}, u32[]{:S(2)}) collective-permute-start(bf16[4,8,4096]{2,1,0:T(8,128)(2,1)S(1)} %get-tuple-element.19), channel_id=1, source_target_pairs={{0,4},{1,3},{2,6},{3,1},{4,0},{5,7},{6,2},{7,5},{8,12},{9,11},{10,... | collective-permute-start | bytes 786440 | tf_op jit(solution)/shard_map/ppermute | solution.py:47
  52.0 21.4 %copy-start.3 = (f32[128,2048]{1,0:T(8,128)S(1)}, f32[128,2048]{1,0:T(8,128)}, u32[]{:S(2)}) copy-start(f32[128,2048]{1,0:T(8,128)} %get-tuple-element.12) | copy-start | bytes 3145732
  64.4 5.4 %collective-permute-start.11 = (bf16[1,8,4096]{2,1,0:T(8,128)(2,1)S(1)}, bf16[1,8,4096]{2,1,0:T(8,128)(2,1)S(1)}, u32[]{:S(2)}, u32[]{:S(2)}) collective-permute-start(bf16[1,8,4096]{2,1,0:T(8,128)(2,1)S(1)} %get-tuple-element.34), channel_id=1, source_target_pairs={{0,8},{1,9},{2,10},{3,11},{4,12},{5,13},{6,14},{7,15},{8,0},{9,1},... | collective-permute-start | bytes 196616 | tf_op jit(solution)/shard_map/ppermute | solution.py:47
  64.6 5.3 %collective-permute-start.13 = (bf16[1,8,4096]{2,1,0:T(8,128)(2,1)S(1)}, bf16[1,8,4096]{2,1,0:T(8,128)(2,1)S(1)}, u32[]{:S(2)}, u32[]{:S(2)}) collective-permute-start(bf16[1,8,4096]{2,1,0:T(8,128)(2,1)S(1)} %get-tuple-element.35), channel_id=1, source_target_pairs={{0,24},{1,25},{2,26},{3,27},{4,28},{5,29},{6,30},{7,31},{8,16},{9,... | collective-permute-start | bytes 196616 | tf_op jit(solution)/shard_map/ppermute | solution.py:47
  66.4 7.0 %collective-permute-start.12 = (bf16[1,8,4096]{2,1,0:T(8,128)(2,1)S(1)}, bf16[1,8,4096]{2,1,0:T(8,128)(2,1)S(1)}, u32[]{:S(2)}, u32[]{:S(2)}) collective-permute-start(bf16[1,8,4096]{2,1,0:T(8,128)(2,1)S(1)} %get-tuple-element.36), channel_id=1, source_target_pairs={{0,16},{1,17},{2,18},{3,19},{4,20},{5,21},{6,22},{7,23},{8,24},{9,... | collective-permute-start | bytes 196616 | tf_op jit(solution)/shard_map/ppermute | solution.py:47
  67.1 7.5 %copy-start.2 = (f32[128,2048]{1,0:T(8,128)S(1)}, f32[128,2048]{1,0:T(8,128)}, u32[]{:S(2)}) copy-start(f32[128,2048]{1,0:T(8,128)} %get-tuple-element.14) | copy-start | bytes 3145732
  68.0 9.5 %collective-permute-start.7 = (bf16[64,4096]{1,0:T(8,128)(2,1)}, bf16[64,4096]{1,0:T(8,128)(2,1)}, u32[]{:S(2)}, u32[]{:S(2)}) collective-permute-start(bf16[64,4096]{1,0:T(8,128)(2,1)} %pad_maximum_fusion.3), channel_id=1, source_target_pairs={{0,1},{1,0},{2,3},{3,2},{4,5},{5,4},{6,7},{7,6},{8,9},{9,8},{10,11... | collective-permute-start | bytes 1572872 | tf_op jit(solution)/shard_map/ppermute | solution.py:106
  76.0 4.4 %collective-permute-start.14 = (bf16[64,4096]{1,0:T(8,128)(2,1)S(1)}, bf16[64,4096]{1,0:T(8,128)(2,1)S(1)}, u32[]{:S(2)}, u32[]{:S(2)}) collective-permute-start(bf16[64,4096]{1,0:T(8,128)(2,1)S(1)} %pad_maximum_fusion.4), channel_id=1, source_target_pairs={{0,1},{1,0},{2,3},{3,2},{4,5},{5,4},{6,7},{7,6},{8,9},{9,8},{10,11... | collective-permute-start | bytes 1572872 | tf_op jit(solution)/shard_map/ppermute | solution.py:106

commit v11 on v10

--- a/solution.py
+++ b/solution.py
@@ -72,31 +72,23 @@
 
 
 def gather_blocks(x, core):
-    me = virtual_index(core)
     held = x[None]
     for bits in reversed(rounds()):
         width = 1 << len(bits)
-        t_me = round_index(me, bits)
-        got = jnp.stack([held] + [exchange(held, round_mask(m, bits)) for m in range(1, width)], 1)
-        held = jnp.stack(
-            [lax.dynamic_index_in_dim(got, t ^ t_me, 1, keepdims=False) for t in range(width)], 1
-        )
-        held = held.reshape((-1,) + x.shape)
+        got = [held] + [exchange(held, round_mask(m, bits)) for m in range(1, width)]
+        held = jnp.stack(got, 1).reshape((-1,) + x.shape)
     return held.reshape((-1,) + x.shape[1:])
 
 
 def reduce_blocks(x, core):
-    me = virtual_index(core)
     size = group_size()
     held = x.reshape((size, -1) + x.shape[1:])
     for bits in rounds():
         width = 1 << len(bits)
-        t_me = round_index(me, bits)
         parts = held.reshape((held.shape[0] // width, width) + held.shape[1:])
-        total = lax.dynamic_index_in_dim(parts, t_me, 1, keepdims=False)
+        total = parts[:, 0]
         for m in range(1, width):
-            send = lax.dynamic_index_in_dim(parts, t_me ^ m, 1, keepdims=False)
-            got = exchange(send.astype(jnp.bfloat16), round_mask(m, bits))
+            got = exchange(parts[:, m].astype(jnp.bfloat16), round_mask(m, bits))
             total = total + got.astype(jnp.float32)
         held = total
     return held.reshape(x.shape[0] // size, *x.shape[1:])
@@ -253,7 +245,7 @@
     all_sum = gather_blocks(own_sum, core)
     sum_count = all_sum.shape[0]
     slot = jnp.arange(sum_count, dtype=jnp.int32) // SUMMARY
-    member = slot // nb
+    member = (slot // nb) ^ virtual_index(core)
     if group_bits() >= 2:
         member = jnp.where(core == 1, swap_low_bits(member), member)
     key_block = member * nb + slot % nb

time: 82.5 us -> 82.5 us (level)
  local copies, waits for them, and re-layouts: 7.78 us -> 5.18 us
  other arithmetic: 11.6 us -> 13.2 us
  waiting for transfers between devices: 32.6 us -> 33.6 us
    another operation x4, other arithmetic: 1.39 us -> 4.14 us  [the longest x1 1.17 us: gather_blocks(): jnp.stack([lax.dynamic_index_in_dim(got, t ^ t_me, 1, keepdims=False) for...]
    convert_element_type x2, local copies, waits for them, and re-layouts: 1.54 us -> 0.07 us  [reduce_blocks(): got = exchange(parts[:, m].astype(jnp.bfloat16), round_mask(m, bits))]
    add x2 -> x1, other arithmetic: 1.18 us -> 0.03 us  [reduce_blocks(): total = total + got.astype(jnp.float32)]
    dynamic_slice x4, local copies, waits for them, and re-layouts: 1.2 us -> 0.18 us  [to_token_layout(): mine = [lax.dynamic_slice_in_dim(a, core * rows, rows, 0) for a in arrays]]
    ppermute x12, waiting for transfers between devices: 30.4 us -> 31.4 us  [exchange(): return lax.ppermute(x, ('seq', 'hx', 'hc'), pairs)]
  transfers between devices with their start and end apart: 15 -> 15, of which waited for: 11 -> 11; matrix products, arithmetic and copies ran while one was open for 11% -> 10% of each run, Pallas kernels for 0% -> 0%
where the time goes in v11:
time: 82.5 us; the launch traced here: 82.2 us
  waiting for transfers between devices  33.6 us (41%)
  starting transfers between devices  16.5 us (20%)
  other arithmetic  13.2 us (16%)
  Pallas kernels  12.8 us (16%)
  local copies, waits for them, and re-layouts  5.18 us (6%)
  between operations  0.94 us (1%)
    ppermute x12, waiting for transfers between devices, exchange(): return lax.ppermute(x, ('seq', 'hx', 'hc'), pairs)  31.4 us
    ppermute x12, starting transfers between devices, exchange(): return lax.ppermute(x, ('seq', 'hx', 'hc'), pairs)  13 us
    pallas_call x1, Pallas kernels, attention(): pl.pallas_call(attention_kernel, grid=(heads // per_step, nb), in_specs=[...  12.8 us
    select_n x4, other arithmetic, to_token_layout(): jnp.where(core == 0, jnp.concatenate([m, r], 1), jnp.concatenate([r, m], 1))  3.66 us
    ppermute x3, starting transfers between devices, swap_with_partner(): return lax.ppermute(x, 'hc', [(0, 1), (1, 0)])  3.46 us
    another operation x2, other arithmetic  2.92 us
    ppermute x3, waiting for transfers between devices, swap_with_partner(): return lax.ppermute(x, 'hc', [(0, 1), (1, 0)])  2.21 us
    select_n x4, other arithmetic, to_block_layout(): jnp.where(core == 0, jnp.concatenate([m, r], 0), jnp.concatenate([r, m], 0))  2.01 us
  transfers between devices with their start and end apart: 15, of which 11 were waited for; matrix products, arithmetic and copies ran while one was open for 10% of the time, Pallas kernels for 0%

profile of v11, /device:TPU:1, one launch (start us, length us, event | category | flops | bytes accessed | tf_op | source)
XLA Modules:
  0.0 82.2 jit_solution(11959084384312187283)
XLA Ops:
  0.7 1.3 %constant_dynamic-slice_fusion.11 = (bf16[64,2048]{1,0:T(8,128)(2,1)S(1)}, bf16[64,2048]{1,0:T(8,128)(2,1)S(1)}, bf16[64,2048]{1,0:T(8,128)(2,1)S(1)}, bf16[64,2048]{1,0:T(8,128)(2,1)S(1)}) fusion(bf16[64,4096]{1,0:T(8,128)(2,1)} %param.8, s32[]{:T(128)S(6)} %select_n.118, s32[]{:T(128)S(6)} %select_n.119, bf16[64,4096]{1,0:T(8,128)(2,1)} %param.7), kind=kLoop, calls=%fused_computation.52 | loop fusion | bytes 2097160 | tf_op jit(solution)/shard_map/dynamic_slice | solution.py:104
  2.9 2.2 %collective-permute-done = bf16[64,8192]{1,0:T(8,128)(2,1)S(1)} collective-permute-done((bf16[64,8192]{1,0:T(8,128)(2,1)S(1)}, bf16[64,8192]{1,0:T(8,128)(2,1)S(1)}, u32[]{:S(2)}, u32[]{:S(2)}) %collective-permute-start) | collective-permute-done | bytes 1048608 | tf_op jit(solution)/shard_map/ppermute | solution.py:98
  6.7 4.5 %collective-permute-start.3 = (bf16[1,8,4096]{2,1,0:T(8,128)(2,1)S(1)}, bf16[1,8,4096]{2,1,0:T(8,128)(2,1)S(1)}, u32[]{:S(2)}, u32[]{:S(2)}) collective-permute-start(bf16[1,8,4096]{2,1,0:T(8,128)(2,1)S(1)} %bitcast.87), channel_id=1, source_target_pairs={{0,24},{1,25},{2,26},{3,27},{4,28},{5,29},{6,30},{7,31},{8,16},{9,... | collective-permute-start | bytes 196616 | tf_op jit(solution)/shard_map/ppermute | solution.py:47
  11.6 1.8 %collective-permute-done.3 = bf16[1,8,4096]{2,1,0:T(8,128)(2,1)S(1)} collective-permute-done((bf16[1,8,4096]{2,1,0:T(8,128)(2,1)S(1)}, bf16[1,8,4096]{2,1,0:T(8,128)(2,1)S(1)}, u32[]{:S(2)}, u32[]{:S(2)}) %collective-permute-start.3) | collective-permute-done | bytes 65568 | tf_op jit(solution)/shard_map/ppermute | solution.py:47
  13.4 3.5 %collective-permute-done.2 = bf16[1,8,4096]{2,1,0:T(8,128)(2,1)S(1)} collective-permute-done((bf16[1,8,4096]{2,1,0:T(8,128)(2,1)S(1)}, bf16[1,8,4096]{2,1,0:T(8,128)(2,1)S(1)}, u32[]{:S(2)}, u32[]{:S(2)}) %collective-permute-start.2) | collective-permute-done | bytes 65568 | tf_op jit(solution)/shard_map/ppermute | solution.py:47
  17.0 2.2 %collective-permute-start.6 = (bf16[4,8,4096]{2,1,0:T(8,128)(2,1)S(1)}, bf16[4,8,4096]{2,1,0:T(8,128)(2,1)S(1)}, u32[]{:S(2)}, u32[]{:S(2)}) collective-permute-start(bf16[4,8,4096]{2,1,0:T(8,128)(2,1)S(1)} %get-tuple-element.50), channel_id=1, source_target_pairs={{0,6},{1,7},{2,4},{3,5},{4,2},{5,3},{6,0},{7,1},{8,14},{9,15},{10,... | collective-permute-start | bytes 786440 | tf_op jit(solution)/shard_map/ppermute | solution.py:47
  21.5 3.5 %collective-permute-done.6 = bf16[4,8,4096]{2,1,0:T(8,128)(2,1)S(1)} collective-permute-done((bf16[4,8,4096]{2,1,0:T(8,128)(2,1)S(1)}, bf16[4,8,4096]{2,1,0:T(8,128)(2,1)S(1)}, u32[]{:S(2)}, u32[]{:S(2)}) %collective-permute-start.6) | collective-permute-done | bytes 262176 | tf_op jit(solution)/shard_map/ppermute | solution.py:47
  25.0 5.7 %collective-permute-done.5 = bf16[4,8,4096]{2,1,0:T(8,128)(2,1)S(1)} collective-permute-done((bf16[4,8,4096]{2,1,0:T(8,128)(2,1)S(1)}, bf16[4,8,4096]{2,1,0:T(8,128)(2,1)S(1)}, u32[]{:S(2)}, u32[]{:S(2)}) %collective-permute-start.5) | collective-permute-done | bytes 262176 | tf_op jit(solution)/shard_map/ppermute | solution.py:47
  30.7 1.1 %collective-permute-done.4 = bf16[4,8,4096]{2,1,0:T(8,128)(2,1)S(1)} collective-permute-done((bf16[4,8,4096]{2,1,0:T(8,128)(2,1)S(1)}, bf16[4,8,4096]{2,1,0:T(8,128)(2,1)S(1)}, u32[]{:S(2)}, u32[]{:S(2)}) %collective-permute-start.4) | collective-permute-done | bytes 262176 | tf_op jit(solution)/shard_map/ppermute | solution.py:47
  31.8 1.2 %pad_maximum_fusion.1 = bf16[4,4,8,4096]{3,2,1,0:T(8,128)(2,1)} fusion(bf16[4,1,8,4096]{3,2,1,0:T(8,128)(2,1)S(1)} %bitcast.91, bf16[4,1,8,4096]{3,2,1,0:T(8,128)(2,1)S(1)} %bitcast.92, bf16[4,1,8,4096]{3,2,1,0:T(8,128)(2,1)S(1)} %bitcast.93, bf16[4,1,8,4096]{3,2,1,0:T(8,128)(2,1)S(1)} %get-tuple-element.49), kind=kLoop, calls=%fused_computation.5 | loop fusion | flops 1572864 | bytes 2097152 | tf_op jit(solution)/shard_map/stack | solution.py:79
  33.6 12.8 %shard_map.84 = (bf16[128,2048]{1,0:T(8,128)(2,1)}, bf16[128,2048]{1,0:T(8,128)(2,1)}, f32[128,2048]{1,0:T(8,128)}, f32[128,2048]{1,0:T(8,128)}, f32[128,4096]{1,0:T(8,128)}) custom-call(bf16[128,2048]{1,0:T(8,128)(2,1)} %maximum_select_fusion.q_all, bf16[128,2048]{1,0:T(8,128)(2,1)} %copy-done.1, bf16[128,2048]{1,0:T(8,128)(2,1)} %copy-done, ...), custom_call_target="tpu_custom_call" | custom-call | flops 805306368 | bytes 7340032 | tf_op jit(solution)/shard_map/pallas_call | solution.py:203
  46.3 1.8 %convert.10 = bf16[4,4,8,4096]{3,2,1,0:T(8,128)(2,1)S(1)} convert(f32[4,4,8,4096]{3,2,1,0:T(8,128)} %bitcast.83) | non-fusion elementwise | flops 524288 | bytes 3145728 | tf_op jit(solution)/shard_map/convert.5
  48.2 1.3 %collective-permute-start.8 = (bf16[4,8,4096]{2,1,0:T(8,128)(2,1)S(1)}, bf16[4,8,4096]{2,1,0:T(8,128)(2,1)S(1)}, u32[]{:S(2)}, u32[]{:S(2)}) collective-permute-start(bf16[4,8,4096]{2,1,0:T(8,128)(2,1)S(1)} %get-tuple-element.19), channel_id=1, source_target_pairs={{0,2},{1,5},{2,0},{3,7},{4,6},{5,1},{6,4},{7,3},{8,10},{9,13},{10,... | collective-permute-start | bytes 786440 | tf_op jit(solution)/shard_map/ppermute | solution.py:47
  49.5 1.2 %collective-permute-start.10 = (bf16[4,8,4096]{2,1,0:T(8,128)(2,1)S(1)}, bf16[4,8,4096]{2,1,0:T(8,128)(2,1)S(1)}, u32[]{:S(2)}, u32[]{:S(2)}) collective-permute-start(bf16[4,8,4096]{2,1,0:T(8,128)(2,1)S(1)} %get-tuple-element.20), channel_id=1, source_target_pairs={{0,6},{1,7},{2,4},{3,5},{4,2},{5,3},{6,0},{7,1},{8,14},{9,15},{10,... | collective-permute-start | bytes 786440 | tf_op jit(solution)/shard_map/ppermute | solution.py:47
  51.0 4.3 %collective-permute-done.8 = bf16[4,8,4096]{2,1,0:T(8,128)(2,1)S(1)} collective-permute-done((bf16[4,8,4096]{2,1,0:T(8,128)(2,1)S(1)}, bf16[4,8,4096]{2,1,0:T(8,128)(2,1)S(1)}, u32[]{:S(2)}, u32[]{:S(2)}) %collective-permute-start.8) | collective-permute-done | bytes 262176 | tf_op jit(solution)/shard_map/ppermute | solution.py:47
  55.3 3.4 %collective-permute-done.10 = bf16[4,8,4096]{2,1,0:T(8,128)(2,1)S(1)} collective-permute-done((bf16[4,8,4096]{2,1,0:T(8,128)(2,1)S(1)}, bf16[4,8,4096]{2,1,0:T(8,128)(2,1)S(1)}, u32[]{:S(2)}, u32[]{:S(2)}) %collective-permute-start.10) | collective-permute-done | bytes 262176 | tf_op jit(solution)/shard_map/ppermute | solution.py:47
  58.7 4.5 %collective-permute-done.9 = bf16[4,8,4096]{2,1,0:T(8,128)(2,1)S(1)} collective-permute-done((bf16[4,8,4096]{2,1,0:T(8,128)(2,1)S(1)}, bf16[4,8,4096]{2,1,0:T(8,128)(2,1)S(1)}, u32[]{:S(2)}, u32[]{:S(2)}) %collective-permute-start.9) | collective-permute-done | bytes 262176 | tf_op jit(solution)/shard_map/ppermute | solution.py:47
  63.2 1.2 %fusion.13 = (bf16[1,4,8,4096]{3,2,1,0:T(8,128)(2,1)S(1)}, f32[1,4,8,4096]{3,2,1,0:T(8,128)S(1)}) fusion(bf16[4,8,4096]{2,1,0:T(8,128)(2,1)S(1)} %collective-permute-done.10, bf16[4,8,4096]{2,1,0:T(8,128)(2,1)S(1)} %collective-permute-done.9, bf16[4,8,4096]{2,1,0:T(8,128)(2,1)S(1)} %collective-permute-done.8, f32[4,4,8,4096]{3,2,1,0:T(8,128)} %bitcast.84), kind=kLoop, calls=%fused_computation.70 | loop fusion | flops 917504 | bytes 2097152 | tf_op jit(solution)/shard_map/convert.2
  64.6 1.8 %collective-permute-start.13 = (bf16[1,8,4096]{2,1,0:T(8,128)(2,1)S(1)}, bf16[1,8,4096]{2,1,0:T(8,128)(2,1)S(1)}, u32[]{:S(2)}, u32[]{:S(2)}) collective-permute-start(bf16[1,8,4096]{2,1,0:T(8,128)(2,1)S(1)} %get-tuple-element.47), channel_id=1, source_target_pairs={{0,24},{1,25},{2,26},{3,27},{4,28},{5,29},{6,30},{7,31},{8,16},{9,... | collective-permute-start | bytes 196616 | tf_op jit(solution)/shard_map/ppermute | solution.py:47
  68.0 1.9 %collective-permute-start.7 = (bf16[64,4096]{1,0:T(8,128)(2,1)}, bf16[64,4096]{1,0:T(8,128)(2,1)}, u32[]{:S(2)}, u32[]{:S(2)}) collective-permute-start(bf16[64,4096]{1,0:T(8,128)(2,1)} %pad_maximum_fusion.2), channel_id=1, source_target_pairs={{0,1},{1,0},{2,3},{3,2},{4,5},{5,4},{6,7},{7,6},{8,9},{9,8},{10,11... | collective-permute-start | bytes 1572872 | tf_op jit(solution)/shard_map/ppermute | solution.py:98
  69.9 3.5 %collective-permute-done.12 = bf16[1,8,4096]{2,1,0:T(8,128)(2,1)S(1)} collective-permute-done((bf16[1,8,4096]{2,1,0:T(8,128)(2,1)S(1)}, bf16[1,8,4096]{2,1,0:T(8,128)(2,1)S(1)}, u32[]{:S(2)}, u32[]{:S(2)}) %collective-permute-start.12) | collective-permute-done | bytes 65568 | tf_op jit(solution)/shard_map/ppermute | solution.py:47
  73.5 1.1 %scatter_custom_fusion = f32[128,2048]{1,0:T(8,128)S(1)} fusion(f32[128,2048]{1,0:T(8,128)S(1)} %copy-done.3, s32[8]{0:T(128)S(1)} %fusion.12, f32[8,16,2,128]{3,0,2,1:T(8,128)S(1)} %bitcast.85), kind=kCustom, calls=%fused_computation.32 | custom fusion | flops 16384 | bytes 1114112 | tf_op jit(solution)/shard_map/scatter-add | solution.py:260
  74.7 1.1 %scatter_custom_fusion.1 = f32[128,2048]{1,0:T(8,128)S(1)} fusion(f32[128,2048]{1,0:T(8,128)S(1)} %copy-done.2, s32[8]{0:T(128)S(1)} %fusion.12, f32[8,16,2,128]{3,0,2,1:T(8,128)S(1)} %bitcast.86), kind=kCustom, calls=%fused_computation.30 | custom fusion | flops 16384 | bytes 1114112 | tf_op jit(solution)/shard_map/scatter-add | solution.py:261
  76.0 1.5 %collective-permute-start.14 = (bf16[64,4096]{1,0:T(8,128)(2,1)S(1)}, bf16[64,4096]{1,0:T(8,128)(2,1)S(1)}, u32[]{:S(2)}, u32[]{:S(2)}) collective-permute-start(bf16[64,4096]{1,0:T(8,128)(2,1)S(1)} %pad_maximum_fusion.3), channel_id=1, source_target_pairs={{0,1},{1,0},{2,3},{3,2},{4,5},{5,4},{6,7},{7,6},{8,9},{9,8},{10,11... | collective-permute-start | bytes 1572872 | tf_op jit(solution)/shard_map/ppermute | solution.py:98
  (66 shorter events, 13.0 us)
Async XLA Ops:
  0.6 1.4 %copy-start.6 = (bf16[64,4096]{1,0:T(8,128)(2,1)S(1)}, bf16[64,4096]{1,0:T(8,128)(2,1)}, u32[]{:S(2)}) copy-start(bf16[64,4096]{1,0:T(8,128)(2,1)} %param.10) | copy-start | bytes 1572868
  0.6 1.5 %copy-start.7 = (bf16[64,4096]{1,0:T(8,128)(2,1)S(1)}, bf16[64,4096]{1,0:T(8,128)(2,1)}, u32[]{:S(2)}) copy-start(bf16[64,4096]{1,0:T(8,128)(2,1)} %param.9) | copy-start | bytes 1572868
  2.1 0.7 copy-start.8
  2.3 2.7 %collective-permute-start = (bf16[64,8192]{1,0:T(8,128)(2,1)S(1)}, bf16[64,8192]{1,0:T(8,128)(2,1)S(1)}, u32[]{:S(2)}, u32[]{:S(2)}) collective-permute-start(bf16[64,8192]{1,0:T(8,128)(2,1)S(1)} %pad_maximum_fusion), channel_id=1, source_target_pairs={{0,1},{1,0},{2,3},{3,2},{4,5},{5,4},{6,7},{7,6},{8,9},{9,8},{10,11... | collective-permute-start | bytes 3145736 | tf_op jit(solution)/shard_map/ppermute | solution.py:98
  5.3 16.2 %copy-start = (bf16[128,2048]{1,0:T(8,128)(2,1)}, bf16[128,2048]{1,0:T(8,128)(2,1)S(1)}, u32[]{:S(2)}) copy-start(bf16[128,2048]{1,0:T(8,128)(2,1)S(1)} %maximum_select_fusion.2.v_all) | copy-start | bytes 1572868
  6.0 27.0 %copy-start.1 = (bf16[128,2048]{1,0:T(8,128)(2,1)}, bf16[128,2048]{1,0:T(8,128)(2,1)S(1)}, u32[]{:S(2)}) copy-start(bf16[128,2048]{1,0:T(8,128)(2,1)S(1)} %maximum_select_fusion.1.k_all) | copy-start | bytes 1572868
  6.7 6.7 %collective-permute-start.3 = (bf16[1,8,4096]{2,1,0:T(8,128)(2,1)S(1)}, bf16[1,8,4096]{2,1,0:T(8,128)(2,1)S(1)}, u32[]{:S(2)}, u32[]{:S(2)}) collective-permute-start(bf16[1,8,4096]{2,1,0:T(8,128)(2,1)S(1)} %bitcast.87), channel_id=1, source_target_pairs={{0,24},{1,25},{2,26},{3,27},{4,28},{5,29},{6,30},{7,31},{8,16},{9,... | collective-permute-start | bytes 196616 | tf_op jit(solution)/shard_map/ppermute | solution.py:47
  11.2 5.7 %collective-permute-start.2 = (bf16[1,8,4096]{2,1,0:T(8,128)(2,1)S(1)}, bf16[1,8,4096]{2,1,0:T(8,128)(2,1)S(1)}, u32[]{:S(2)}, u32[]{:S(2)}) collective-permute-start(bf16[1,8,4096]{2,1,0:T(8,128)(2,1)S(1)} %bitcast.88), channel_id=1, source_target_pairs={{0,16},{1,17},{2,18},{3,19},{4,20},{5,21},{6,22},{7,23},{8,24},{9,... | collective-permute-start | bytes 196616 | tf_op jit(solution)/shard_map/ppermute | solution.py:47
  11.2 5.7 %collective-permute-start.1 = (bf16[1,8,4096]{2,1,0:T(8,128)(2,1)S(1)}, bf16[1,8,4096]{2,1,0:T(8,128)(2,1)S(1)}, u32[]{:S(2)}, u32[]{:S(2)}) collective-permute-start(bf16[1,8,4096]{2,1,0:T(8,128)(2,1)S(1)} %bitcast.89), channel_id=1, source_target_pairs={{0,8},{1,9},{2,10},{3,11},{4,12},{5,13},{6,14},{7,15},{8,0},{9,1},... | collective-permute-start | bytes 196616 | tf_op jit(solution)/shard_map/ppermute | solution.py:47
  17.0 8.0 %collective-permute-start.6 = (bf16[4,8,4096]{2,1,0:T(8,128)(2,1)S(1)}, bf16[4,8,4096]{2,1,0:T(8,128)(2,1)S(1)}, u32[]{:S(2)}, u32[]{:S(2)}) collective-permute-start(bf16[4,8,4096]{2,1,0:T(8,128)(2,1)S(1)} %get-tuple-element.50), channel_id=1, source_target_pairs={{0,6},{1,7},{2,4},{3,5},{4,2},{5,3},{6,0},{7,1},{8,14},{9,15},{10,... | collective-permute-start | bytes 786440 | tf_op jit(solution)/shard_map/ppermute | solution.py:47
  19.2 11.4 %collective-permute-start.5 = (bf16[4,8,4096]{2,1,0:T(8,128)(2,1)S(1)}, bf16[4,8,4096]{2,1,0:T(8,128)(2,1)S(1)}, u32[]{:S(2)}, u32[]{:S(2)}) collective-permute-start(bf16[4,8,4096]{2,1,0:T(8,128)(2,1)S(1)} %get-tuple-element.50), channel_id=1, source_target_pairs={{0,4},{1,3},{2,6},{3,1},{4,0},{5,7},{6,2},{7,5},{8,12},{9,11},{10,... | collective-permute-start | bytes 786440 | tf_op jit(solution)/shard_map/ppermute | solution.py:47
  19.5 12.3 %collective-permute-start.4 = (bf16[4,8,4096]{2,1,0:T(8,128)(2,1)S(1)}, bf16[4,8,4096]{2,1,0:T(8,128)(2,1)S(1)}, u32[]{:S(2)}, u32[]{:S(2)}) collective-permute-start(bf16[4,8,4096]{2,1,0:T(8,128)(2,1)S(1)} %get-tuple-element.50), channel_id=1, source_target_pairs={{0,2},{1,5},{2,0},{3,7},{4,6},{5,1},{6,4},{7,3},{8,10},{9,13},{10,... | collective-permute-start | bytes 786440 | tf_op jit(solution)/shard_map/ppermute | solution.py:47
  46.3 4.6 %copy-start.5 = (bf16[128,2048]{1,0:T(8,128)(2,1)S(1)}, bf16[128,2048]{1,0:T(8,128)(2,1)}, u32[]{:S(2)}) copy-start(bf16[128,2048]{1,0:T(8,128)(2,1)} %get-tuple-element.10) | copy-start | bytes 1572868
  48.1 2.8 %copy-start.4 = (bf16[128,2048]{1,0:T(8,128)(2,1)S(1)}, bf16[128,2048]{1,0:T(8,128)(2,1)}, u32[]{:S(2)}) copy-start(bf16[128,2048]{1,0:T(8,128)(2,1)} %get-tuple-element.11) | copy-start | bytes 1572868
  48.2 7.1 %collective-permute-start.8 = (bf16[4,8,4096]{2,1,0:T(8,128)(2,1)S(1)}, bf16[4,8,4096]{2,1,0:T(8,128)(2,1)S(1)}, u32[]{:S(2)}, u32[]{:S(2)}) collective-permute-start(bf16[4,8,4096]{2,1,0:T(8,128)(2,1)S(1)} %get-tuple-element.19), channel_id=1, source_target_pairs={{0,2},{1,5},{2,0},{3,7},{4,6},{5,1},{6,4},{7,3},{8,10},{9,13},{10,... | collective-permute-start | bytes 786440 | tf_op jit(solution)/shard_map/ppermute | solution.py:47
  49.5 9.2 %collective-permute-start.10 = (bf16[4,8,4096]{2,1,0:T(8,128)(2,1)S(1)}, bf16[4,8,4096]{2,1,0:T(8,128)(2,1)S(1)}, u32[]{:S(2)}, u32[]{:S(2)}) collective-permute-start(bf16[4,8,4096]{2,1,0:T(8,128)(2,1)S(1)} %get-tuple-element.20), channel_id=1, source_target_pairs={{0,6},{1,7},{2,4},{3,5},{4,2},{5,3},{6,0},{7,1},{8,14},{9,15},{10,... | collective-permute-start | bytes 786440 | tf_op jit(solution)/shard_map/ppermute | solution.py:47
  50.7 12.5 %collective-permute-start.9 = (bf16[4,8,4096]{2,1,0:T(8,128)(2,1)S(1)}, bf16[4,8,4096]{2,1,0:T(8,128)(2,1)S(1)}, u32[]{:S(2)}, u32[]{:S(2)}) collective-permute-start(bf16[4,8,4096]{2,1,0:T(8,128)(2,1)S(1)} %get-tuple-element.21), channel_id=1, source_target_pairs={{0,4},{1,3},{2,6},{3,1},{4,0},{5,7},{6,2},{7,5},{8,12},{9,11},{10,... | collective-permute-start | bytes 786440 | tf_op jit(solution)/shard_map/ppermute | solution.py:47
  51.0 22.5 %copy-start.3 = (f32[128,2048]{1,0:T(8,128)S(1)}, f32[128,2048]{1,0:T(8,128)}, u32[]{:S(2)}) copy-start(f32[128,2048]{1,0:T(8,128)} %get-tuple-element.12) | copy-start | bytes 3145732
  64.4 5.4 %collective-permute-start.11 = (bf16[1,8,4096]{2,1,0:T(8,128)(2,1)S(1)}, bf16[1,8,4096]{2,1,0:T(8,128)(2,1)S(1)}, u32[]{:S(2)}, u32[]{:S(2)}) collective-permute-start(bf16[1,8,4096]{2,1,0:T(8,128)(2,1)S(1)} %get-tuple-element.46), channel_id=1, source_target_pairs={{0,8},{1,9},{2,10},{3,11},{4,12},{5,13},{6,14},{7,15},{8,0},{9,1},... | collective-permute-start | bytes 196616 | tf_op jit(solution)/shard_map/ppermute | solution.py:47
  64.6 5.3 %collective-permute-start.13 = (bf16[1,8,4096]{2,1,0:T(8,128)(2,1)S(1)}, bf16[1,8,4096]{2,1,0:T(8,128)(2,1)S(1)}, u32[]{:S(2)}, u32[]{:S(2)}) collective-permute-start(bf16[1,8,4096]{2,1,0:T(8,128)(2,1)S(1)} %get-tuple-element.47), channel_id=1, source_target_pairs={{0,24},{1,25},{2,26},{3,27},{4,28},{5,29},{6,30},{7,31},{8,16},{9,... | collective-permute-start | bytes 196616 | tf_op jit(solution)/shard_map/ppermute | solution.py:47
  66.4 7.0 %collective-permute-start.12 = (bf16[1,8,4096]{2,1,0:T(8,128)(2,1)S(1)}, bf16[1,8,4096]{2,1,0:T(8,128)(2,1)S(1)}, u32[]{:S(2)}, u32[]{:S(2)}) collective-permute-start(bf16[1,8,4096]{2,1,0:T(8,128)(2,1)S(1)} %get-tuple-element.48), channel_id=1, source_target_pairs={{0,16},{1,17},{2,18},{3,19},{4,20},{5,21},{6,22},{7,23},{8,24},{9,... | collective-permute-start | bytes 196616 | tf_op jit(solution)/shard_map/ppermute | solution.py:47
  67.1 7.5 %copy-start.2 = (f32[128,2048]{1,0:T(8,128)S(1)}, f32[128,2048]{1,0:T(8,128)}, u32[]{:S(2)}) copy-start(f32[128,2048]{1,0:T(8,128)} %get-tuple-element.14) | copy-start | bytes 3145732
  68.0 9.5 %collective-permute-start.7 = (bf16[64,4096]{1,0:T(8,128)(2,1)}, bf16[64,4096]{1,0:T(8,128)(2,1)}, u32[]{:S(2)}, u32[]{:S(2)}) collective-permute-start(bf16[64,4096]{1,0:T(8,128)(2,1)} %pad_maximum_fusion.2), channel_id=1, source_target_pairs={{0,1},{1,0},{2,3},{3,2},{4,5},{5,4},{6,7},{7,6},{8,9},{9,8},{10,11... | collective-permute-start | bytes 1572872 | tf_op jit(solution)/shard_map/ppermute | solution.py:98
  76.0 4.4 %collective-permute-start.14 = (bf16[64,4096]{1,0:T(8,128)(2,1)S(1)}, bf16[64,4096]{1,0:T(8,128)(2,1)S(1)}, u32[]{:S(2)}, u32[]{:S(2)}) collective-permute-start(bf16[64,4096]{1,0:T(8,128)(2,1)S(1)} %pad_maximum_fusion.3), channel_id=1, source_target_pairs={{0,1},{1,0},{2,3},{3,2},{4,5},{5,4},{6,7},{7,6},{8,9},{9,8},{10,11... | collective-permute-start | bytes 1572872 | tf_op jit(solution)/shard_map/ppermute | solution.py:98

commit v12 on v11

--- a/solution.py
+++ b/solution.py
@@ -86,7 +86,7 @@
     for bits in rounds():
         width = 1 << len(bits)
         parts = held.reshape((held.shape[0] // width, width) + held.shape[1:])
-        total = parts[:, 0]
+        total = parts[:, 0].astype(jnp.float32)
         for m in range(1, width):
             got = exchange(parts[:, m].astype(jnp.bfloat16), round_mask(m, bits))
             total = total + got.astype(jnp.float32)
@@ -130,7 +130,7 @@
 
 
 def attention_kernel(
-    q_all, k_all, v_all, g_all, s_all, mask_ref, att_all, dq_all, dkw_all, dvw_all, ds_all
+    q_all, k_all, v_all, g_all, s_all, mask_ref, att_all, dq_all, dkw_all, dvw_all, ds_out, ds_all
 ):
     j = pl.program_id(1)
     scale = 1.0 / math.sqrt(HEAD_DIM)
@@ -188,6 +188,10 @@
             ds_all[:, kcols] += dks
             ds_all[:, vcols] += dvs
 
+    @pl.when(j == pl.num_programs(1) - 1)
+    def _():
+        ds_out[...] = ds_all[...].astype(ds_out.dtype)
+
 
 def attention(q, k, v, g, summary, mask):
     rows, half = q.shape
@@ -210,8 +214,9 @@
             jax.ShapeDtypeStruct((rows, half), bf16),
             jax.ShapeDtypeStruct((rows, half), f32),
             jax.ShapeDtypeStruct((rows, half), f32),
-            jax.ShapeDtypeStruct((count, 2 * half), f32),
+            jax.ShapeDtypeStruct((count, 2 * half), bf16),
         ],
+        scratch_shapes=[pltpu.VMEM((count, 2 * per_step * HEAD_DIM), f32)],
         cost_estimate=pl.CostEstimate(
             flops=flops, transcendentals=rows * heads * (BLOCK + count) * 2,
             bytes_accessed=rows * half * 2 * 8 + count * half * 2 * 6,

time: 82.5 us -> 82.9 us (level)
  local copies, waits for them, and re-layouts: 5.18 us -> 7.6 us
  other arithmetic: 13.2 us -> 11.3 us
    another operation x2 -> x1, other arithmetic: 2.92 us -> 1.08 us
    unnamed x18, local copies, waits for them, and re-layouts: 0.52 us -> 1.78 us
    squeeze x0 -> x1, local copies, waits for them, and re-layouts: none -> 1.25 us  [reduce_blocks(): got = exchange(parts[:, m].astype(jnp.bfloat16), round_mask(m, bits))]
where the time goes in v12:
time: 82.9 us; the launch traced here: 82.6 us
  waiting for transfers between devices  33.6 us (41%)
  starting transfers between devices  16.5 us (20%)
  Pallas kernels  12.7 us (15%)
  other arithmetic  11.3 us (14%)
  local copies, waits for them, and re-layouts  7.6 us (9%)
  between operations  0.94 us (1%)
    ppermute x12, waiting for transfers between devices, exchange(): return lax.ppermute(x, ('seq', 'hx', 'hc'), pairs)  31.5 us
    ppermute x12, starting transfers between devices, exchange(): return lax.ppermute(x, ('seq', 'hx', 'hc'), pairs)  13 us
    pallas_call x1, Pallas kernels, attention(): pl.pallas_call(attention_kernel, grid=(heads // per_step, nb), in_specs=[...  12.7 us
    select_n x4, other arithmetic, to_token_layout(): jnp.where(core == 0, jnp.concatenate([m, r], 1), jnp.concatenate([r, m], 1))  3.66 us
    ppermute x3, starting transfers between devices, swap_with_partner(): return lax.ppermute(x, 'hc', [(0, 1), (1, 0)])  3.46 us
    ppermute x3, waiting for transfers between devices, swap_with_partner(): return lax.ppermute(x, 'hc', [(0, 1), (1, 0)])  2.11 us
    select_n x4, other arithmetic, to_block_layout(): jnp.where(core == 0, jnp.concatenate([m, r], 0), jnp.concatenate([r, m], 0))  2.01 us
    unnamed x18, local copies, waits for them, and re-layouts  1.78 us
  transfers between devices with their start and end apart: 15, of which 11 were waited for; matrix products, arithmetic and copies ran while one was open for 10% of the time, Pallas kernels for 0%

profile of v12, /device:TPU:1, one launch (start us, length us, event | category | flops | bytes accessed | tf_op | source)
XLA Modules:
  0.0 82.6 jit_solution(6915281163076727837)
XLA Ops:
  0.7 1.4 %constant_dynamic-slice_fusion.11 = (bf16[64,2048]{1,0:T(8,128)(2,1)S(1)}, bf16[64,2048]{1,0:T(8,128)(2,1)S(1)}, bf16[64,2048]{1,0:T(8,128)(2,1)S(1)}, bf16[64,2048]{1,0:T(8,128)(2,1)S(1)}) fusion(bf16[64,4096]{1,0:T(8,128)(2,1)} %param.8, s32[]{:T(128)S(6)} %select_n.118, s32[]{:T(128)S(6)} %select_n.119, bf16[64,4096]{1,0:T(8,128)(2,1)} %param.7), kind=kLoop, calls=%fused_computation.52 | loop fusion | bytes 2097160 | tf_op jit(solution)/shard_map/dynamic_slice | solution.py:104
  2.9 2.1 %collective-permute-done = bf16[64,8192]{1,0:T(8,128)(2,1)S(1)} collective-permute-done((bf16[64,8192]{1,0:T(8,128)(2,1)S(1)}, bf16[64,8192]{1,0:T(8,128)(2,1)S(1)}, u32[]{:S(2)}, u32[]{:S(2)}) %collective-permute-start) | collective-permute-done | bytes 1048608 | tf_op jit(solution)/shard_map/ppermute | solution.py:98
  6.7 4.5 %collective-permute-start.3 = (bf16[1,8,4096]{2,1,0:T(8,128)(2,1)S(1)}, bf16[1,8,4096]{2,1,0:T(8,128)(2,1)S(1)}, u32[]{:S(2)}, u32[]{:S(2)}) collective-permute-start(bf16[1,8,4096]{2,1,0:T(8,128)(2,1)S(1)} %bitcast.82), channel_id=1, source_target_pairs={{0,24},{1,25},{2,26},{3,27},{4,28},{5,29},{6,30},{7,31},{8,16},{9,... | collective-permute-start | bytes 196616 | tf_op jit(solution)/shard_map/ppermute | solution.py:47
  11.6 1.8 %collective-permute-done.3 = bf16[1,8,4096]{2,1,0:T(8,128)(2,1)S(1)} collective-permute-done((bf16[1,8,4096]{2,1,0:T(8,128)(2,1)S(1)}, bf16[1,8,4096]{2,1,0:T(8,128)(2,1)S(1)}, u32[]{:S(2)}, u32[]{:S(2)}) %collective-permute-start.3) | collective-permute-done | bytes 65568 | tf_op jit(solution)/shard_map/ppermute | solution.py:47
  13.4 3.5 %collective-permute-done.2 = bf16[1,8,4096]{2,1,0:T(8,128)(2,1)S(1)} collective-permute-done((bf16[1,8,4096]{2,1,0:T(8,128)(2,1)S(1)}, bf16[1,8,4096]{2,1,0:T(8,128)(2,1)S(1)}, u32[]{:S(2)}, u32[]{:S(2)}) %collective-permute-start.2) | collective-permute-done | bytes 65568 | tf_op jit(solution)/shard_map/ppermute | solution.py:47
  17.0 2.2 %collective-permute-start.6 = (bf16[4,8,4096]{2,1,0:T(8,128)(2,1)S(1)}, bf16[4,8,4096]{2,1,0:T(8,128)(2,1)S(1)}, u32[]{:S(2)}, u32[]{:S(2)}) collective-permute-start(bf16[4,8,4096]{2,1,0:T(8,128)(2,1)S(1)} %get-tuple-element.50), channel_id=1, source_target_pairs={{0,6},{1,7},{2,4},{3,5},{4,2},{5,3},{6,0},{7,1},{8,14},{9,15},{10,... | collective-permute-start | bytes 786440 | tf_op jit(solution)/shard_map/ppermute | solution.py:47
  21.5 3.5 %collective-permute-done.6 = bf16[4,8,4096]{2,1,0:T(8,128)(2,1)S(1)} collective-permute-done((bf16[4,8,4096]{2,1,0:T(8,128)(2,1)S(1)}, bf16[4,8,4096]{2,1,0:T(8,128)(2,1)S(1)}, u32[]{:S(2)}, u32[]{:S(2)}) %collective-permute-start.6) | collective-permute-done | bytes 262176 | tf_op jit(solution)/shard_map/ppermute | solution.py:47
  25.0 5.7 %collective-permute-done.5 = bf16[4,8,4096]{2,1,0:T(8,128)(2,1)S(1)} collective-permute-done((bf16[4,8,4096]{2,1,0:T(8,128)(2,1)S(1)}, bf16[4,8,4096]{2,1,0:T(8,128)(2,1)S(1)}, u32[]{:S(2)}, u32[]{:S(2)}) %collective-permute-start.5) | collective-permute-done | bytes 262176 | tf_op jit(solution)/shard_map/ppermute | solution.py:47
  30.6 1.1 %collective-permute-done.4 = bf16[4,8,4096]{2,1,0:T(8,128)(2,1)S(1)} collective-permute-done((bf16[4,8,4096]{2,1,0:T(8,128)(2,1)S(1)}, bf16[4,8,4096]{2,1,0:T(8,128)(2,1)S(1)}, u32[]{:S(2)}, u32[]{:S(2)}) %collective-permute-start.4) | collective-permute-done | bytes 262176 | tf_op jit(solution)/shard_map/ppermute | solution.py:47
  31.8 1.1 %pad_maximum_fusion.1 = bf16[4,4,8,4096]{3,2,1,0:T(8,128)(2,1)} fusion(bf16[4,1,8,4096]{3,2,1,0:T(8,128)(2,1)S(1)} %bitcast.86, bf16[4,1,8,4096]{3,2,1,0:T(8,128)(2,1)S(1)} %bitcast.87, bf16[4,1,8,4096]{3,2,1,0:T(8,128)(2,1)S(1)} %bitcast.88, bf16[4,1,8,4096]{3,2,1,0:T(8,128)(2,1)S(1)} %get-tuple-element.49), kind=kLoop, calls=%fused_computation.5 | loop fusion | flops 1572864 | bytes 2097152 | tf_op jit(solution)/shard_map/stack | solution.py:79
  33.5 12.7 %shard_map.84 = (bf16[128,2048]{1,0:T(8,128)(2,1)}, bf16[128,2048]{1,0:T(8,128)(2,1)}, f32[128,2048]{1,0:T(8,128)}, f32[128,2048]{1,0:T(8,128)}, bf16[128,4096]{1,0:T(8,128)(2,1)}) custom-call(bf16[128,2048]{1,0:T(8,128)(2,1)} %maximum_select_fusion.q_all, bf16[128,2048]{1,0:T(8,128)(2,1)} %copy-done.1, bf16[128,2048]{1,0:T(8,128)(2,1)} %copy-done, ...), custom_call_target="tpu_custom_call" | custom-call | flops 805306368 | bytes 7340032 | tf_op jit(solution)/shard_map/pallas_call | solution.py:207
  46.2 1.2 %slice_bitcast_fusion.2 = (bf16[4,8,4096]{2,1,0:T(8,128)(2,1)S(1)}, bf16[4,8,4096]{2,1,0:T(8,128)(2,1)S(1)}, bf16[4,8,4096]{2,1,0:T(8,128)(2,1)S(1)}) fusion(bf16[4,4,8,4096]{3,2,1,0:T(8,128)(2,1)} %bitcast.78), kind=kLoop, calls=%fused_computation.22 | loop fusion | bytes 1572864 | tf_op jit(solution)/shard_map/squeeze | solution.py:91
  47.4 1.3 %collective-permute-start.8 = (bf16[4,8,4096]{2,1,0:T(8,128)(2,1)S(1)}, bf16[4,8,4096]{2,1,0:T(8,128)(2,1)S(1)}, u32[]{:S(2)}, u32[]{:S(2)}) collective-permute-start(bf16[4,8,4096]{2,1,0:T(8,128)(2,1)S(1)} %get-tuple-element.19), channel_id=1, source_target_pairs={{0,2},{1,5},{2,0},{3,7},{4,6},{5,1},{6,4},{7,3},{8,10},{9,13},{10,... | collective-permute-start | bytes 786440 | tf_op jit(solution)/shard_map/ppermute | solution.py:47
  48.7 1.2 %collective-permute-start.10 = (bf16[4,8,4096]{2,1,0:T(8,128)(2,1)S(1)}, bf16[4,8,4096]{2,1,0:T(8,128)(2,1)S(1)}, u32[]{:S(2)}, u32[]{:S(2)}) collective-permute-start(bf16[4,8,4096]{2,1,0:T(8,128)(2,1)S(1)} %get-tuple-element.20), channel_id=1, source_target_pairs={{0,6},{1,7},{2,4},{3,5},{4,2},{5,3},{6,0},{7,1},{8,14},{9,15},{10,... | collective-permute-start | bytes 786440 | tf_op jit(solution)/shard_map/ppermute | solution.py:47
  50.3 4.3 %collective-permute-done.8 = bf16[4,8,4096]{2,1,0:T(8,128)(2,1)S(1)} collective-permute-done((bf16[4,8,4096]{2,1,0:T(8,128)(2,1)S(1)}, bf16[4,8,4096]{2,1,0:T(8,128)(2,1)S(1)}, u32[]{:S(2)}, u32[]{:S(2)}) %collective-permute-start.8) | collective-permute-done | bytes 262176 | tf_op jit(solution)/shard_map/ppermute | solution.py:47
  54.6 3.4 %collective-permute-done.10 = bf16[4,8,4096]{2,1,0:T(8,128)(2,1)S(1)} collective-permute-done((bf16[4,8,4096]{2,1,0:T(8,128)(2,1)S(1)}, bf16[4,8,4096]{2,1,0:T(8,128)(2,1)S(1)}, u32[]{:S(2)}, u32[]{:S(2)}) %collective-permute-start.10) | collective-permute-done | bytes 262176 | tf_op jit(solution)/shard_map/ppermute | solution.py:47
  58.0 4.5 %collective-permute-done.9 = bf16[4,8,4096]{2,1,0:T(8,128)(2,1)S(1)} collective-permute-done((bf16[4,8,4096]{2,1,0:T(8,128)(2,1)S(1)}, bf16[4,8,4096]{2,1,0:T(8,128)(2,1)S(1)}, u32[]{:S(2)}, u32[]{:S(2)}) %collective-permute-start.9) | collective-permute-done | bytes 262176 | tf_op jit(solution)/shard_map/ppermute | solution.py:47
  63.8 1.8 %collective-permute-start.13 = (bf16[1,8,4096]{2,1,0:T(8,128)(2,1)S(1)}, bf16[1,8,4096]{2,1,0:T(8,128)(2,1)S(1)}, u32[]{:S(2)}, u32[]{:S(2)}) collective-permute-start(bf16[1,8,4096]{2,1,0:T(8,128)(2,1)S(1)} %get-tuple-element.47), channel_id=1, source_target_pairs={{0,24},{1,25},{2,26},{3,27},{4,28},{5,29},{6,30},{7,31},{8,16},{9,... | collective-permute-start | bytes 196616 | tf_op jit(solution)/shard_map/ppermute | solution.py:47
  67.2 1.9 %collective-permute-start.7 = (bf16[64,4096]{1,0:T(8,128)(2,1)}, bf16[64,4096]{1,0:T(8,128)(2,1)}, u32[]{:S(2)}, u32[]{:S(2)}) collective-permute-start(bf16[64,4096]{1,0:T(8,128)(2,1)} %pad_maximum_fusion.2), channel_id=1, source_target_pairs={{0,1},{1,0},{2,3},{3,2},{4,5},{5,4},{6,7},{7,6},{8,9},{9,8},{10,11... | collective-permute-start | bytes 1572872 | tf_op jit(solution)/shard_map/ppermute | solution.py:98
  69.1 3.5 %collective-permute-done.12 = bf16[1,8,4096]{2,1,0:T(8,128)(2,1)S(1)} collective-permute-done((bf16[1,8,4096]{2,1,0:T(8,128)(2,1)S(1)}, bf16[1,8,4096]{2,1,0:T(8,128)(2,1)S(1)}, u32[]{:S(2)}, u32[]{:S(2)}) %collective-permute-start.12) | collective-permute-done | bytes 65568 | tf_op jit(solution)/shard_map/ppermute | solution.py:47
  72.7 1.1 %scatter_custom_fusion = f32[128,2048]{1,0:T(8,128)S(1)} fusion(f32[128,2048]{1,0:T(8,128)S(1)} %copy-done.3, s32[8]{0:T(128)S(1)} %fusion.11, f32[8,16,2,128]{3,0,2,1:T(8,128)S(1)} %bitcast.80), kind=kCustom, calls=%fused_computation.32 | custom fusion | flops 16384 | bytes 1114112 | tf_op jit(solution)/shard_map/scatter-add | solution.py:265
  73.8 1.1 %copy-done.2 = f32[128,2048]{1,0:T(8,128)S(1)} copy-done((f32[128,2048]{1,0:T(8,128)S(1)}, f32[128,2048]{1,0:T(8,128)}, u32[]{:S(2)}) %copy-start.2) | copy-done | bytes 1048600
  75.0 1.1 %scatter_custom_fusion.1 = f32[128,2048]{1,0:T(8,128)S(1)} fusion(f32[128,2048]{1,0:T(8,128)S(1)} %copy-done.2, s32[8]{0:T(128)S(1)} %fusion.11, f32[8,16,2,128]{3,0,2,1:T(8,128)S(1)} %bitcast.81), kind=kCustom, calls=%fused_computation.30 | custom fusion | flops 16384 | bytes 1114112 | tf_op jit(solution)/shard_map/scatter-add | solution.py:266
  76.3 1.5 %collective-permute-start.14 = (bf16[64,4096]{1,0:T(8,128)(2,1)S(1)}, bf16[64,4096]{1,0:T(8,128)(2,1)S(1)}, u32[]{:S(2)}, u32[]{:S(2)}) collective-permute-start(bf16[64,4096]{1,0:T(8,128)(2,1)S(1)} %pad_maximum_fusion.3), channel_id=1, source_target_pairs={{0,1},{1,0},{2,3},{3,2},{4,5},{5,4},{6,7},{7,6},{8,9},{9,8},{10,11... | collective-permute-start | bytes 1572872 | tf_op jit(solution)/shard_map/ppermute | solution.py:98
  (65 shorter events, 14.1 us)
Async XLA Ops:
  0.6 1.4 %copy-start.6 = (bf16[64,4096]{1,0:T(8,128)(2,1)S(1)}, bf16[64,4096]{1,0:T(8,128)(2,1)}, u32[]{:S(2)}) copy-start(bf16[64,4096]{1,0:T(8,128)(2,1)} %param.10) | copy-start | bytes 1572868
  0.6 1.5 %copy-start.7 = (bf16[64,4096]{1,0:T(8,128)(2,1)S(1)}, bf16[64,4096]{1,0:T(8,128)(2,1)}, u32[]{:S(2)}) copy-start(bf16[64,4096]{1,0:T(8,128)(2,1)} %param.9) | copy-start | bytes 1572868
  2.2 0.7 copy-start.8
  2.3 2.7 %collective-permute-start = (bf16[64,8192]{1,0:T(8,128)(2,1)S(1)}, bf16[64,8192]{1,0:T(8,128)(2,1)S(1)}, u32[]{:S(2)}, u32[]{:S(2)}) collective-permute-start(bf16[64,8192]{1,0:T(8,128)(2,1)S(1)} %pad_maximum_fusion), channel_id=1, source_target_pairs={{0,1},{1,0},{2,3},{3,2},{4,5},{5,4},{6,7},{7,6},{8,9},{9,8},{10,11... | collective-permute-start | bytes 3145736 | tf_op jit(solution)/shard_map/ppermute | solution.py:98
  5.3 11.7 %copy-start = (bf16[128,2048]{1,0:T(8,128)(2,1)}, bf16[128,2048]{1,0:T(8,128)(2,1)S(1)}, u32[]{:S(2)}) copy-start(bf16[128,2048]{1,0:T(8,128)(2,1)S(1)} %maximum_select_fusion.2.v_all) | copy-start | bytes 1572868
  6.0 14.6 %copy-start.1 = (bf16[128,2048]{1,0:T(8,128)(2,1)}, bf16[128,2048]{1,0:T(8,128)(2,1)S(1)}, u32[]{:S(2)}) copy-start(bf16[128,2048]{1,0:T(8,128)(2,1)S(1)} %maximum_select_fusion.1.k_all) | copy-start | bytes 1572868
  6.7 6.7 %collective-permute-start.3 = (bf16[1,8,4096]{2,1,0:T(8,128)(2,1)S(1)}, bf16[1,8,4096]{2,1,0:T(8,128)(2,1)S(1)}, u32[]{:S(2)}, u32[]{:S(2)}) collective-permute-start(bf16[1,8,4096]{2,1,0:T(8,128)(2,1)S(1)} %bitcast.82), channel_id=1, source_target_pairs={{0,24},{1,25},{2,26},{3,27},{4,28},{5,29},{6,30},{7,31},{8,16},{9,... | collective-permute-start | bytes 196616 | tf_op jit(solution)/shard_map/ppermute | solution.py:47
  11.2 5.7 %collective-permute-start.2 = (bf16[1,8,4096]{2,1,0:T(8,128)(2,1)S(1)}, bf16[1,8,4096]{2,1,0:T(8,128)(2,1)S(1)}, u32[]{:S(2)}, u32[]{:S(2)}) collective-permute-start(bf16[1,8,4096]{2,1,0:T(8,128)(2,1)S(1)} %bitcast.83), channel_id=1, source_target_pairs={{0,16},{1,17},{2,18},{3,19},{4,20},{5,21},{6,22},{7,23},{8,24},{9,... | collective-permute-start | bytes 196616 | tf_op jit(solution)/shard_map/ppermute | solution.py:47
  11.2 5.7 %collective-permute-start.1 = (bf16[1,8,4096]{2,1,0:T(8,128)(2,1)S(1)}, bf16[1,8,4096]{2,1,0:T(8,128)(2,1)S(1)}, u32[]{:S(2)}, u32[]{:S(2)}) collective-permute-start(bf16[1,8,4096]{2,1,0:T(8,128)(2,1)S(1)} %bitcast.84), channel_id=1, source_target_pairs={{0,8},{1,9},{2,10},{3,11},{4,12},{5,13},{6,14},{7,15},{8,0},{9,1},... | collective-permute-start | bytes 196616 | tf_op jit(solution)/shard_map/ppermute | solution.py:47
  17.0 8.0 %collective-permute-start.6 = (bf16[4,8,4096]{2,1,0:T(8,128)(2,1)S(1)}, bf16[4,8,4096]{2,1,0:T(8,128)(2,1)S(1)}, u32[]{:S(2)}, u32[]{:S(2)}) collective-permute-start(bf16[4,8,4096]{2,1,0:T(8,128)(2,1)S(1)} %get-tuple-element.50), channel_id=1, source_target_pairs={{0,6},{1,7},{2,4},{3,5},{4,2},{5,3},{6,0},{7,1},{8,14},{9,15},{10,... | collective-permute-start | bytes 786440 | tf_op jit(solution)/shard_map/ppermute | solution.py:47
  19.2 11.4 %collective-permute-start.5 = (bf16[4,8,4096]{2,1,0:T(8,128)(2,1)S(1)}, bf16[4,8,4096]{2,1,0:T(8,128)(2,1)S(1)}, u32[]{:S(2)}, u32[]{:S(2)}) collective-permute-start(bf16[4,8,4096]{2,1,0:T(8,128)(2,1)S(1)} %get-tuple-element.50), channel_id=1, source_target_pairs={{0,4},{1,3},{2,6},{3,1},{4,0},{5,7},{6,2},{7,5},{8,12},{9,11},{10,... | collective-permute-start | bytes 786440 | tf_op jit(solution)/shard_map/ppermute | solution.py:47
  19.5 12.3 %collective-permute-start.4 = (bf16[4,8,4096]{2,1,0:T(8,128)(2,1)S(1)}, bf16[4,8,4096]{2,1,0:T(8,128)(2,1)S(1)}, u32[]{:S(2)}, u32[]{:S(2)}) collective-permute-start(bf16[4,8,4096]{2,1,0:T(8,128)(2,1)S(1)} %get-tuple-element.50), channel_id=1, source_target_pairs={{0,2},{1,5},{2,0},{3,7},{4,6},{5,1},{6,4},{7,3},{8,10},{9,13},{10,... | collective-permute-start | bytes 786440 | tf_op jit(solution)/shard_map/ppermute | solution.py:47
  46.2 4.0 %copy-start.5 = (bf16[128,2048]{1,0:T(8,128)(2,1)S(1)}, bf16[128,2048]{1,0:T(8,128)(2,1)}, u32[]{:S(2)}) copy-start(bf16[128,2048]{1,0:T(8,128)(2,1)} %get-tuple-element.10) | copy-start | bytes 1572868
  46.2 4.0 %copy-start.4 = (bf16[128,2048]{1,0:T(8,128)(2,1)S(1)}, bf16[128,2048]{1,0:T(8,128)(2,1)}, u32[]{:S(2)}) copy-start(bf16[128,2048]{1,0:T(8,128)(2,1)} %get-tuple-element.11) | copy-start | bytes 1572868
  47.4 7.1 %collective-permute-start.8 = (bf16[4,8,4096]{2,1,0:T(8,128)(2,1)S(1)}, bf16[4,8,4096]{2,1,0:T(8,128)(2,1)S(1)}, u32[]{:S(2)}, u32[]{:S(2)}) collective-permute-start(bf16[4,8,4096]{2,1,0:T(8,128)(2,1)S(1)} %get-tuple-element.19), channel_id=1, source_target_pairs={{0,2},{1,5},{2,0},{3,7},{4,6},{5,1},{6,4},{7,3},{8,10},{9,13},{10,... | collective-permute-start | bytes 786440 | tf_op jit(solution)/shard_map/ppermute | solution.py:47
  48.7 9.2 %collective-permute-start.10 = (bf16[4,8,4096]{2,1,0:T(8,128)(2,1)S(1)}, bf16[4,8,4096]{2,1,0:T(8,128)(2,1)S(1)}, u32[]{:S(2)}, u32[]{:S(2)}) collective-permute-start(bf16[4,8,4096]{2,1,0:T(8,128)(2,1)S(1)} %get-tuple-element.20), channel_id=1, source_target_pairs={{0,6},{1,7},{2,4},{3,5},{4,2},{5,3},{6,0},{7,1},{8,14},{9,15},{10,... | collective-permute-start | bytes 786440 | tf_op jit(solution)/shard_map/ppermute | solution.py:47
  50.0 12.5 %collective-permute-start.9 = (bf16[4,8,4096]{2,1,0:T(8,128)(2,1)S(1)}, bf16[4,8,4096]{2,1,0:T(8,128)(2,1)S(1)}, u32[]{:S(2)}, u32[]{:S(2)}) collective-permute-start(bf16[4,8,4096]{2,1,0:T(8,128)(2,1)S(1)} %get-tuple-element.21), channel_id=1, source_target_pairs={{0,4},{1,3},{2,6},{3,1},{4,0},{5,7},{6,2},{7,5},{8,12},{9,11},{10,... | collective-permute-start | bytes 786440 | tf_op jit(solution)/shard_map/ppermute | solution.py:47
  63.6 9.1 %copy-start.3 = (f32[128,2048]{1,0:T(8,128)S(1)}, f32[128,2048]{1,0:T(8,128)}, u32[]{:S(2)}) copy-start(f32[128,2048]{1,0:T(8,128)} %get-tuple-element.12) | copy-start | bytes 3145732
  63.6 5.4 %collective-permute-start.11 = (bf16[1,8,4096]{2,1,0:T(8,128)(2,1)S(1)}, bf16[1,8,4096]{2,1,0:T(8,128)(2,1)S(1)}, u32[]{:S(2)}, u32[]{:S(2)}) collective-permute-start(bf16[1,8,4096]{2,1,0:T(8,128)(2,1)S(1)} %get-tuple-element.46), channel_id=1, source_target_pairs={{0,8},{1,9},{2,10},{3,11},{4,12},{5,13},{6,14},{7,15},{8,0},{9,1},... | collective-permute-start | bytes 196616 | tf_op jit(solution)/shard_map/ppermute | solution.py:47
  63.8 5.3 %collective-permute-start.13 = (bf16[1,8,4096]{2,1,0:T(8,128)(2,1)S(1)}, bf16[1,8,4096]{2,1,0:T(8,128)(2,1)S(1)}, u32[]{:S(2)}, u32[]{:S(2)}) collective-permute-start(bf16[1,8,4096]{2,1,0:T(8,128)(2,1)S(1)} %get-tuple-element.47), channel_id=1, source_target_pairs={{0,24},{1,25},{2,26},{3,27},{4,28},{5,29},{6,30},{7,31},{8,16},{9,... | collective-permute-start | bytes 196616 | tf_op jit(solution)/shard_map/ppermute | solution.py:47
  65.6 7.0 %collective-permute-start.12 = (bf16[1,8,4096]{2,1,0:T(8,128)(2,1)S(1)}, bf16[1,8,4096]{2,1,0:T(8,128)(2,1)S(1)}, u32[]{:S(2)}, u32[]{:S(2)}) collective-permute-start(bf16[1,8,4096]{2,1,0:T(8,128)(2,1)S(1)} %get-tuple-element.48), channel_id=1, source_target_pairs={{0,16},{1,17},{2,18},{3,19},{4,20},{5,21},{6,22},{7,23},{8,24},{9,... | collective-permute-start | bytes 196616 | tf_op jit(solution)/shard_map/ppermute | solution.py:47
  67.2 10.6 %collective-permute-start.7 = (bf16[64,4096]{1,0:T(8,128)(2,1)}, bf16[64,4096]{1,0:T(8,128)(2,1)}, u32[]{:S(2)}, u32[]{:S(2)}) collective-permute-start(bf16[64,4096]{1,0:T(8,128)(2,1)} %pad_maximum_fusion.2), channel_id=1, source_target_pairs={{0,1},{1,0},{2,3},{3,2},{4,5},{5,4},{6,7},{7,6},{8,9},{9,8},{10,11... | collective-permute-start | bytes 1572872 | tf_op jit(solution)/shard_map/ppermute | solution.py:98
  73.8 1.2 %copy-start.2 = (f32[128,2048]{1,0:T(8,128)S(1)}, f32[128,2048]{1,0:T(8,128)}, u32[]{:S(2)}) copy-start(f32[128,2048]{1,0:T(8,128)} %get-tuple-element.14) | copy-start | bytes 3145732
  76.3 4.4 %collective-permute-start.14 = (bf16[64,4096]{1,0:T(8,128)(2,1)S(1)}, bf16[64,4096]{1,0:T(8,128)(2,1)S(1)}, u32[]{:S(2)}, u32[]{:S(2)}) collective-permute-start(bf16[64,4096]{1,0:T(8,128)(2,1)S(1)} %pad_maximum_fusion.3), channel_id=1, source_target_pairs={{0,1},{1,0},{2,3},{3,2},{4,5},{5,4},{6,7},{7,6},{8,9},{9,8},{10,11... | collective-permute-start | bytes 1572872 | tf_op jit(solution)/shard_map/ppermute | solution.py:98

commit v13 on v12

--- a/solution.py
+++ b/solution.py
@@ -56,6 +56,16 @@
     return sum(((me >> b) & 1) << i for i, b in enumerate(bits))
 
 
+def exchange_member(index):
+    out = 0
+    rest = index
+    for bits in reversed(rounds()):
+        width = 1 << len(bits)
+        out = out + (rest % width) * (1 << bits[0])
+        rest = rest // width
+    return out
+
+
 def round_mask(m, bits):
     return sum(((m >> i) & 1) << b for i, b in enumerate(bits))
 
@@ -76,7 +86,7 @@
     for bits in reversed(rounds()):
         width = 1 << len(bits)
         got = [held] + [exchange(held, round_mask(m, bits)) for m in range(1, width)]
-        held = jnp.stack(got, 1).reshape((-1,) + x.shape)
+        held = jnp.concatenate(got, 0)
     return held.reshape((-1,) + x.shape[1:])
 
 
@@ -85,10 +95,10 @@
     held = x.reshape((size, -1) + x.shape[1:])
     for bits in rounds():
         width = 1 << len(bits)
-        parts = held.reshape((held.shape[0] // width, width) + held.shape[1:])
-        total = parts[:, 0].astype(jnp.float32)
+        parts = held.reshape((width, held.shape[0] // width) + held.shape[1:])
+        total = parts[0].astype(jnp.float32)
         for m in range(1, width):
-            got = exchange(parts[:, m].astype(jnp.bfloat16), round_mask(m, bits))
+            got = exchange(parts[m].astype(jnp.bfloat16), round_mask(m, bits))
             total = total + got.astype(jnp.float32)
         held = total
     return held.reshape(x.shape[0] // size, *x.shape[1:])
@@ -250,7 +260,7 @@
     all_sum = gather_blocks(own_sum, core)
     sum_count = all_sum.shape[0]
     slot = jnp.arange(sum_count, dtype=jnp.int32) // SUMMARY
-    member = (slot // nb) ^ virtual_index(core)
+    member = exchange_member(slot // nb) ^ virtual_index(core)
     if group_bits() >= 2:
         member = jnp.where(core == 1, swap_low_bits(member), member)
     key_block = member * nb + slot % nb

time: 82.9 us -> 82.9 us (level)
  local copies, waits for them, and re-layouts: 7.6 us -> 8.75 us
  other arithmetic: 11.3 us -> 10.2 us
    another operation x3 -> x1, other arithmetic: 2.26 us -> 1.08 us  [the longest x2 1.18 us: gather_blocks(): held = jnp.stack(got, 1).reshape((-1,) + x.shape)]
    unnamed x18 -> x28, local copies, waits for them, and re-layouts: 1.78 us -> 2.17 us
  transfers between devices with their start and end apart: 15 -> 15, of which waited for: 11 -> 8; matrix products, arithmetic and copies ran while one was open for 10% -> 10% of each run, Pallas kernels for 0% -> 0%
where the time goes in v13:
time: 82.9 us; the launch traced here: 82.6 us
  waiting for transfers between devices  33.5 us (40%)
  starting transfers between devices  16.4 us (20%)
  Pallas kernels  12.7 us (15%)
  other arithmetic  10.2 us (12%)
  local copies, waits for them, and re-layouts  8.75 us (11%)
  between operations  1 us (1%)
    ppermute x12, waiting for transfers between devices, exchange(): return lax.ppermute(x, ('seq', 'hx', 'hc'), pairs)  31.4 us
    ppermute x12, starting transfers between devices, exchange(): return lax.ppermute(x, ('seq', 'hx', 'hc'), pairs)  13 us
    pallas_call x1, Pallas kernels, attention(): pl.pallas_call(attention_kernel, grid=(heads // per_step, nb), in_specs=[...  12.7 us
    select_n x4, other arithmetic, to_token_layout(): jnp.where(core == 0, jnp.concatenate([m, r], 1), jnp.concatenate([r, m], 1))  3.66 us
    ppermute x3, starting transfers between devices, swap_with_partner(): return lax.ppermute(x, 'hc', [(0, 1), (1, 0)])  3.37 us
    unnamed x28, local copies, waits for them, and re-layouts  2.17 us
    ppermute x3, waiting for transfers between devices, swap_with_partner(): return lax.ppermute(x, 'hc', [(0, 1), (1, 0)])  2.11 us
    select_n x4, other arithmetic, to_block_layout(): jnp.where(core == 0, jnp.concatenate([m, r], 0), jnp.concatenate([r, m], 0))  2.01 us
  transfers between devices with their start and end apart: 15, of which 8 were waited for; matrix products, arithmetic and copies ran while one was open for 10% of the time, Pallas kernels for 0%

profile of v13, /device:TPU:1, one launch (start us, length us, event | category | flops | bytes accessed | tf_op | source)
XLA Modules:
  0.0 82.6 jit_solution(3996169564981127341)
XLA Ops:
  0.7 1.4 %constant_dynamic-slice_fusion.11 = (bf16[64,2048]{1,0:T(8,128)(2,1)S(1)}, bf16[64,2048]{1,0:T(8,128)(2,1)S(1)}, bf16[64,2048]{1,0:T(8,128)(2,1)S(1)}, bf16[64,2048]{1,0:T(8,128)(2,1)S(1)}) fusion(bf16[64,4096]{1,0:T(8,128)(2,1)} %param.8, s32[]{:T(128)S(6)} %select_n.135, s32[]{:T(128)S(6)} %select_n.136, bf16[64,4096]{1,0:T(8,128)(2,1)} %param.7), kind=kLoop, calls=%fused_computation.50 | loop fusion | bytes 2097160 | tf_op jit(solution)/shard_map/dynamic_slice | solution.py:114
  2.9 2.1 %collective-permute-done = bf16[64,8192]{1,0:T(8,128)(2,1)S(1)} collective-permute-done((bf16[64,8192]{1,0:T(8,128)(2,1)S(1)}, bf16[64,8192]{1,0:T(8,128)(2,1)S(1)}, u32[]{:S(2)}, u32[]{:S(2)}) %collective-permute-start) | collective-permute-done | bytes 1048608 | tf_op jit(solution)/shard_map/ppermute | solution.py:108
  7.4 4.5 %collective-permute-start.3 = (bf16[1,8,4096]{2,1,0:T(8,128)(2,1)S(1)}, bf16[1,8,4096]{2,1,0:T(8,128)(2,1)S(1)}, u32[]{:S(2)}, u32[]{:S(2)}) collective-permute-start(bf16[1,8,4096]{2,1,0:T(8,128)(2,1)S(1)} %bitcast.35), channel_id=1, source_target_pairs={{0,24},{1,25},{2,26},{3,27},{4,28},{5,29},{6,30},{7,31},{8,16},{9,... | collective-permute-start | bytes 196616 | tf_op jit(solution)/shard_map/ppermute | solution.py:47
  14.1 3.5 %collective-permute-done.2 = bf16[1,8,4096]{2,1,0:T(8,128)(2,1)S(1)} collective-permute-done((bf16[1,8,4096]{2,1,0:T(8,128)(2,1)S(1)}, bf16[1,8,4096]{2,1,0:T(8,128)(2,1)S(1)}, u32[]{:S(2)}, u32[]{:S(2)}) %collective-permute-start.2) | collective-permute-done | bytes 65568 | tf_op jit(solution)/shard_map/ppermute | solution.py:47
  17.7 2.2 %collective-permute-start.6 = (bf16[4,8,4096]{2,1,0:T(8,128)(2,1)S(1)}, bf16[4,8,4096]{2,1,0:T(8,128)(2,1)S(1)}, u32[]{:S(2)}, u32[]{:S(2)}) collective-permute-start(bf16[4,8,4096]{2,1,0:T(8,128)(2,1)S(1)} %pad_maximum_fusion.3), channel_id=1, source_target_pairs={{0,6},{1,7},{2,4},{3,5},{4,2},{5,3},{6,0},{7,1},{8,14},{9,15},{10,... | collective-permute-start | bytes 786440 | tf_op jit(solution)/shard_map/ppermute | solution.py:47
  20.4 12.1 %collective-permute-done.4 = bf16[4,8,4096]{2,1,0:T(8,128)(2,1)S(1)} collective-permute-done((bf16[4,8,4096]{2,1,0:T(8,128)(2,1)S(1)}, bf16[4,8,4096]{2,1,0:T(8,128)(2,1)S(1)}, u32[]{:S(2)}, u32[]{:S(2)}) %collective-permute-start.4) | collective-permute-done | bytes 262176 | tf_op jit(solution)/shard_map/ppermute | solution.py:47
  33.6 12.7 %shard_map.84 = (bf16[128,2048]{1,0:T(8,128)(2,1)}, bf16[128,2048]{1,0:T(8,128)(2,1)}, f32[128,2048]{1,0:T(8,128)}, f32[128,2048]{1,0:T(8,128)}, bf16[128,4096]{1,0:T(8,128)(2,1)}) custom-call(bf16[128,2048]{1,0:T(8,128)(2,1)} %maximum_select_fusion.q_all, bf16[128,2048]{1,0:T(8,128)(2,1)} %copy-done.1, bf16[128,2048]{1,0:T(8,128)(2,1)} %copy-done, ...), custom_call_target="tpu_custom_call" | custom-call | flops 805306368 | bytes 7340032 | tf_op jit(solution)/shard_map/pallas_call | solution.py:217
  46.3 1.2 %slice_bitcast_fusion.2 = (bf16[4,8,4096]{2,1,0:T(8,128)(2,1)S(1)}, bf16[4,8,4096]{2,1,0:T(8,128)(2,1)S(1)}, bf16[4,8,4096]{2,1,0:T(8,128)(2,1)S(1)}) fusion(bf16[128,4096]{1,0:T(8,128)(2,1)} %get-tuple-element.13), kind=kLoop, calls=%fused_computation.21 | loop fusion | bytes 1572864 | tf_op jit(solution)/shard_map/squeeze | solution.py:101
  47.5 1.3 %collective-permute-start.8 = (bf16[4,8,4096]{2,1,0:T(8,128)(2,1)S(1)}, bf16[4,8,4096]{2,1,0:T(8,128)(2,1)S(1)}, u32[]{:S(2)}, u32[]{:S(2)}) collective-permute-start(bf16[4,8,4096]{2,1,0:T(8,128)(2,1)S(1)} %get-tuple-element.19), channel_id=1, source_target_pairs={{0,2},{1,5},{2,0},{3,7},{4,6},{5,1},{6,4},{7,3},{8,10},{9,13},{10,... | collective-permute-start | bytes 786440 | tf_op jit(solution)/shard_map/ppermute | solution.py:47
  48.8 1.2 %collective-permute-start.10 = (bf16[4,8,4096]{2,1,0:T(8,128)(2,1)S(1)}, bf16[4,8,4096]{2,1,0:T(8,128)(2,1)S(1)}, u32[]{:S(2)}, u32[]{:S(2)}) collective-permute-start(bf16[4,8,4096]{2,1,0:T(8,128)(2,1)S(1)} %get-tuple-element.20), channel_id=1, source_target_pairs={{0,6},{1,7},{2,4},{3,5},{4,2},{5,3},{6,0},{7,1},{8,14},{9,15},{10,... | collective-permute-start | bytes 786440 | tf_op jit(solution)/shard_map/ppermute | solution.py:47
  50.3 4.3 %collective-permute-done.8 = bf16[4,8,4096]{2,1,0:T(8,128)(2,1)S(1)} collective-permute-done((bf16[4,8,4096]{2,1,0:T(8,128)(2,1)S(1)}, bf16[4,8,4096]{2,1,0:T(8,128)(2,1)S(1)}, u32[]{:S(2)}, u32[]{:S(2)}) %collective-permute-start.8) | collective-permute-done | bytes 262176 | tf_op jit(solution)/shard_map/ppermute | solution.py:47
  54.7 3.4 %collective-permute-done.10 = bf16[4,8,4096]{2,1,0:T(8,128)(2,1)S(1)} collective-permute-done((bf16[4,8,4096]{2,1,0:T(8,128)(2,1)S(1)}, bf16[4,8,4096]{2,1,0:T(8,128)(2,1)S(1)}, u32[]{:S(2)}, u32[]{:S(2)}) %collective-permute-start.10) | collective-permute-done | bytes 262176 | tf_op jit(solution)/shard_map/ppermute | solution.py:47
  58.0 4.5 %collective-permute-done.9 = bf16[4,8,4096]{2,1,0:T(8,128)(2,1)S(1)} collective-permute-done((bf16[4,8,4096]{2,1,0:T(8,128)(2,1)S(1)}, bf16[4,8,4096]{2,1,0:T(8,128)(2,1)S(1)}, u32[]{:S(2)}, u32[]{:S(2)}) %collective-permute-start.9) | collective-permute-done | bytes 262176 | tf_op jit(solution)/shard_map/ppermute | solution.py:47
  62.6 1.1 %fusion.10 = (bf16[4,8,4096]{2,1,0:T(8,128)(2,1)S(1)}, f32[4,8,4096]{2,1,0:T(8,128)S(1)}) fusion(bf16[4,8,4096]{2,1,0:T(8,128)(2,1)S(1)} %collective-permute-done.10, bf16[4,8,4096]{2,1,0:T(8,128)(2,1)S(1)} %collective-permute-done.9, bf16[4,8,4096]{2,1,0:T(8,128)(2,1)S(1)} %collective-permute-done.8, bf16[128,4096]{1,0:T(8,128)(2,1)} %get-tuple-element.13), kind=kLoop, calls=%fused_computation.78 | loop fusion | flops 1048576 | bytes 1835008 | tf_op jit(solution)/shard_map/convert.3
  63.9 1.8 %collective-permute-start.13 = (bf16[1,8,4096]{2,1,0:T(8,128)(2,1)S(1)}, bf16[1,8,4096]{2,1,0:T(8,128)(2,1)S(1)}, u32[]{:S(2)}, u32[]{:S(2)}) collective-permute-start(bf16[1,8,4096]{2,1,0:T(8,128)(2,1)S(1)} %get-tuple-element.47), channel_id=1, source_target_pairs={{0,24},{1,25},{2,26},{3,27},{4,28},{5,29},{6,30},{7,31},{8,16},{9,... | collective-permute-start | bytes 196616 | tf_op jit(solution)/shard_map/ppermute | solution.py:47
  67.2 1.8 %collective-permute-start.7 = (bf16[64,4096]{1,0:T(8,128)(2,1)}, bf16[64,4096]{1,0:T(8,128)(2,1)}, u32[]{:S(2)}, u32[]{:S(2)}) collective-permute-start(bf16[64,4096]{1,0:T(8,128)(2,1)} %pad_maximum_fusion.1), channel_id=1, source_target_pairs={{0,1},{1,0},{2,3},{3,2},{4,5},{5,4},{6,7},{7,6},{8,9},{9,8},{10,11... | collective-permute-start | bytes 1572872 | tf_op jit(solution)/shard_map/ppermute | solution.py:108
  69.1 3.5 %collective-permute-done.12 = bf16[1,8,4096]{2,1,0:T(8,128)(2,1)S(1)} collective-permute-done((bf16[1,8,4096]{2,1,0:T(8,128)(2,1)S(1)}, bf16[1,8,4096]{2,1,0:T(8,128)(2,1)S(1)}, u32[]{:S(2)}, u32[]{:S(2)}) %collective-permute-start.12) | collective-permute-done | bytes 65568 | tf_op jit(solution)/shard_map/ppermute | solution.py:47
  72.7 1.1 %scatter_custom_fusion = f32[128,2048]{1,0:T(8,128)S(1)} fusion(f32[128,2048]{1,0:T(8,128)S(1)} %copy-done.4, s32[8]{0:T(128)S(1)} %fusion.9, f32[8,16,2,128]{3,0,2,1:T(8,128)S(1)} %bitcast.40), kind=kCustom, calls=%fused_computation.28 | custom fusion | flops 16384 | bytes 1114112 | tf_op jit(solution)/shard_map/scatter-add | solution.py:275
  73.8 1.1 %copy-done.3 = f32[128,2048]{1,0:T(8,128)S(1)} copy-done((f32[128,2048]{1,0:T(8,128)S(1)}, f32[128,2048]{1,0:T(8,128)}, u32[]{:S(2)}) %copy-start.3) | copy-done | bytes 1048600
  75.0 1.1 %scatter_custom_fusion.1 = f32[128,2048]{1,0:T(8,128)S(1)} fusion(f32[128,2048]{1,0:T(8,128)S(1)} %copy-done.3, s32[8]{0:T(128)S(1)} %fusion.9, f32[8,16,2,128]{3,0,2,1:T(8,128)S(1)} %bitcast.41), kind=kCustom, calls=%fused_computation.26 | custom fusion | flops 16384 | bytes 1114112 | tf_op jit(solution)/shard_map/scatter-add | solution.py:276
  76.3 1.5 %collective-permute-start.14 = (bf16[64,4096]{1,0:T(8,128)(2,1)S(1)}, bf16[64,4096]{1,0:T(8,128)(2,1)S(1)}, u32[]{:S(2)}, u32[]{:S(2)}) collective-permute-start(bf16[64,4096]{1,0:T(8,128)(2,1)S(1)} %pad_maximum_fusion.2), channel_id=1, source_target_pairs={{0,1},{1,0},{2,3},{3,2},{4,5},{5,4},{6,7},{7,6},{8,9},{9,8},{10,11... | collective-permute-start | bytes 1572872 | tf_op jit(solution)/shard_map/ppermute | solution.py:108
  77.8 1.1 %fusion.14 = (bf16[64,2048]{1,0:T(8,128)(2,1)S(1)}, bf16[64,2048]{1,0:T(8,128)(2,1)S(1)}) fusion(bf16[64,4096]{1,0:T(8,128)(2,1)} %collective-permute-done.7), kind=kLoop, calls=%fused_computation.81 | loop fusion | bytes 1048576 | tf_op jit(solution)/shard_map/slice | solution.py:132
  78.8 0.9 %maximum_select_fusion.5 = bf16[64,4096]{1,0:T(8,128)(2,1)} fusion(bf16[64,2048]{1,0:T(8,128)(2,1)S(1)} %get-tuple-element.34, bf16[64,2048]{1,0:T(8,128)(2,1)S(1)} %get-tuple-element.32, pred[]{:T(512)S(6)} %eq.8), kind=kLoop, calls=%fused_computation.11 | loop fusion | flops 2359296 | bytes 1048577 | tf_op jit(solution)/shard_map/jit(_where)/select_n | solution.py:133
  80.7 0.9 %maximum_select_fusion.7 = bf16[64,4096]{1,0:T(8,128)(2,1)} fusion(bf16[64,2048]{1,0:T(8,128)(2,1)S(1)} %get-tuple-element.28, bf16[64,2048]{1,0:T(8,128)(2,1)S(1)} %get-tuple-element.26, pred[]{:T(512)S(6)} %eq.8), kind=kLoop, calls=%fused_computation.14 | loop fusion | flops 2359296 | bytes 1048577 | tf_op jit(solution)/shard_map/jit(_where)/select_n | solution.py:133
  (75 shorter events, 11.2 us)
Async XLA Ops:
  0.6 1.4 %copy-start.8 = (bf16[64,4096]{1,0:T(8,128)(2,1)S(1)}, bf16[64,4096]{1,0:T(8,128)(2,1)}, u32[]{:S(2)}) copy-start(bf16[64,4096]{1,0:T(8,128)(2,1)} %param.10) | copy-start | bytes 1572868
  0.6 1.5 %copy-start.9 = (bf16[64,4096]{1,0:T(8,128)(2,1)S(1)}, bf16[64,4096]{1,0:T(8,128)(2,1)}, u32[]{:S(2)}) copy-start(bf16[64,4096]{1,0:T(8,128)(2,1)} %param.9) | copy-start | bytes 1572868
  2.3 2.7 %collective-permute-start = (bf16[64,8192]{1,0:T(8,128)(2,1)S(1)}, bf16[64,8192]{1,0:T(8,128)(2,1)S(1)}, u32[]{:S(2)}, u32[]{:S(2)}) collective-permute-start(bf16[64,8192]{1,0:T(8,128)(2,1)S(1)} %pad_maximum_fusion), channel_id=1, source_target_pairs={{0,1},{1,0},{2,3},{3,2},{4,5},{5,4},{6,7},{7,6},{8,9},{9,8},{10,11... | collective-permute-start | bytes 3145736 | tf_op jit(solution)/shard_map/ppermute | solution.py:108
  6.0 6.3 %copy-start = (bf16[128,2048]{1,0:T(8,128)(2,1)}, bf16[128,2048]{1,0:T(8,128)(2,1)S(1)}, u32[]{:S(2)}) copy-start(bf16[128,2048]{1,0:T(8,128)(2,1)S(1)} %maximum_select_fusion.2.v_all) | copy-start | bytes 1572868
  6.0 6.3 %copy-start.5 = (bf16[64,2048]{1,0:T(8,128)(2,1)S(1)}, bf16[64,2048]{1,0:T(8,128)(2,1)}, u32[]{:S(2)}) copy-start(bf16[64,2048]{1,0:T(8,128)(2,1)} %get-tuple-element.22) | copy-start | bytes 786436
  6.7 7.4 %copy-start.1 = (bf16[128,2048]{1,0:T(8,128)(2,1)}, bf16[128,2048]{1,0:T(8,128)(2,1)S(1)}, u32[]{:S(2)}) copy-start(bf16[128,2048]{1,0:T(8,128)(2,1)S(1)} %maximum_select_fusion.1.k_all) | copy-start | bytes 1572868
  7.4 6.7 %collective-permute-start.3 = (bf16[1,8,4096]{2,1,0:T(8,128)(2,1)S(1)}, bf16[1,8,4096]{2,1,0:T(8,128)(2,1)S(1)}, u32[]{:S(2)}, u32[]{:S(2)}) collective-permute-start(bf16[1,8,4096]{2,1,0:T(8,128)(2,1)S(1)} %bitcast.35), channel_id=1, source_target_pairs={{0,24},{1,25},{2,26},{3,27},{4,28},{5,29},{6,30},{7,31},{8,16},{9,... | collective-permute-start | bytes 196616 | tf_op jit(solution)/shard_map/ppermute | solution.py:47
  11.9 5.7 %collective-permute-start.2 = (bf16[1,8,4096]{2,1,0:T(8,128)(2,1)S(1)}, bf16[1,8,4096]{2,1,0:T(8,128)(2,1)S(1)}, u32[]{:S(2)}, u32[]{:S(2)}) collective-permute-start(bf16[1,8,4096]{2,1,0:T(8,128)(2,1)S(1)} %bitcast.36), channel_id=1, source_target_pairs={{0,16},{1,17},{2,18},{3,19},{4,20},{5,21},{6,22},{7,23},{8,24},{9,... | collective-permute-start | bytes 196616 | tf_op jit(solution)/shard_map/ppermute | solution.py:47
  11.9 5.7 %collective-permute-start.1 = (bf16[1,8,4096]{2,1,0:T(8,128)(2,1)S(1)}, bf16[1,8,4096]{2,1,0:T(8,128)(2,1)S(1)}, u32[]{:S(2)}, u32[]{:S(2)}) collective-permute-start(bf16[1,8,4096]{2,1,0:T(8,128)(2,1)S(1)} %bitcast.37), channel_id=1, source_target_pairs={{0,8},{1,9},{2,10},{3,11},{4,12},{5,13},{6,14},{7,15},{8,0},{9,1},... | collective-permute-start | bytes 196616 | tf_op jit(solution)/shard_map/ppermute | solution.py:47
  17.7 14.9 %collective-permute-start.6 = (bf16[4,8,4096]{2,1,0:T(8,128)(2,1)S(1)}, bf16[4,8,4096]{2,1,0:T(8,128)(2,1)S(1)}, u32[]{:S(2)}, u32[]{:S(2)}) collective-permute-start(bf16[4,8,4096]{2,1,0:T(8,128)(2,1)S(1)} %pad_maximum_fusion.3), channel_id=1, source_target_pairs={{0,6},{1,7},{2,4},{3,5},{4,2},{5,3},{6,0},{7,1},{8,14},{9,15},{10,... | collective-permute-start | bytes 786440 | tf_op jit(solution)/shard_map/ppermute | solution.py:47
  19.9 12.6 %collective-permute-start.5 = (bf16[4,8,4096]{2,1,0:T(8,128)(2,1)S(1)}, bf16[4,8,4096]{2,1,0:T(8,128)(2,1)S(1)}, u32[]{:S(2)}, u32[]{:S(2)}) collective-permute-start(bf16[4,8,4096]{2,1,0:T(8,128)(2,1)S(1)} %pad_maximum_fusion.3), channel_id=1, source_target_pairs={{0,4},{1,3},{2,6},{3,1},{4,0},{5,7},{6,2},{7,5},{8,12},{9,11},{10,... | collective-permute-start | bytes 786440 | tf_op jit(solution)/shard_map/ppermute | solution.py:47
  20.1 12.3 %collective-permute-start.4 = (bf16[4,8,4096]{2,1,0:T(8,128)(2,1)S(1)}, bf16[4,8,4096]{2,1,0:T(8,128)(2,1)S(1)}, u32[]{:S(2)}, u32[]{:S(2)}) collective-permute-start(bf16[4,8,4096]{2,1,0:T(8,128)(2,1)S(1)} %pad_maximum_fusion.3), channel_id=1, source_target_pairs={{0,2},{1,5},{2,0},{3,7},{4,6},{5,1},{6,4},{7,3},{8,10},{9,13},{10,... | collective-permute-start | bytes 786440 | tf_op jit(solution)/shard_map/ppermute | solution.py:47
  46.2 4.0 %copy-start.7 = (bf16[128,2048]{1,0:T(8,128)(2,1)S(1)}, bf16[128,2048]{1,0:T(8,128)(2,1)}, u32[]{:S(2)}) copy-start(bf16[128,2048]{1,0:T(8,128)(2,1)} %get-tuple-element.10) | copy-start | bytes 1572868
  46.2 4.0 %copy-start.6 = (bf16[128,2048]{1,0:T(8,128)(2,1)S(1)}, bf16[128,2048]{1,0:T(8,128)(2,1)}, u32[]{:S(2)}) copy-start(bf16[128,2048]{1,0:T(8,128)(2,1)} %get-tuple-element.11) | copy-start | bytes 1572868
  47.5 7.2 %collective-permute-start.8 = (bf16[4,8,4096]{2,1,0:T(8,128)(2,1)S(1)}, bf16[4,8,4096]{2,1,0:T(8,128)(2,1)S(1)}, u32[]{:S(2)}, u32[]{:S(2)}) collective-permute-start(bf16[4,8,4096]{2,1,0:T(8,128)(2,1)S(1)} %get-tuple-element.19), channel_id=1, source_target_pairs={{0,2},{1,5},{2,0},{3,7},{4,6},{5,1},{6,4},{7,3},{8,10},{9,13},{10,... | collective-permute-start | bytes 786440 | tf_op jit(solution)/shard_map/ppermute | solution.py:47
  48.8 9.2 %collective-permute-start.10 = (bf16[4,8,4096]{2,1,0:T(8,128)(2,1)S(1)}, bf16[4,8,4096]{2,1,0:T(8,128)(2,1)S(1)}, u32[]{:S(2)}, u32[]{:S(2)}) collective-permute-start(bf16[4,8,4096]{2,1,0:T(8,128)(2,1)S(1)} %get-tuple-element.20), channel_id=1, source_target_pairs={{0,6},{1,7},{2,4},{3,5},{4,2},{5,3},{6,0},{7,1},{8,14},{9,15},{10,... | collective-permute-start | bytes 786440 | tf_op jit(solution)/shard_map/ppermute | solution.py:47
  50.0 12.5 %collective-permute-start.9 = (bf16[4,8,4096]{2,1,0:T(8,128)(2,1)S(1)}, bf16[4,8,4096]{2,1,0:T(8,128)(2,1)S(1)}, u32[]{:S(2)}, u32[]{:S(2)}) collective-permute-start(bf16[4,8,4096]{2,1,0:T(8,128)(2,1)S(1)} %get-tuple-element.21), channel_id=1, source_target_pairs={{0,4},{1,3},{2,6},{3,1},{4,0},{5,7},{6,2},{7,5},{8,12},{9,11},{10,... | collective-permute-start | bytes 786440 | tf_op jit(solution)/shard_map/ppermute | solution.py:47
  63.7 9.0 %copy-start.4 = (f32[128,2048]{1,0:T(8,128)S(1)}, f32[128,2048]{1,0:T(8,128)}, u32[]{:S(2)}) copy-start(f32[128,2048]{1,0:T(8,128)} %get-tuple-element.12) | copy-start | bytes 3145732
  63.7 5.3 %collective-permute-start.11 = (bf16[1,8,4096]{2,1,0:T(8,128)(2,1)S(1)}, bf16[1,8,4096]{2,1,0:T(8,128)(2,1)S(1)}, u32[]{:S(2)}, u32[]{:S(2)}) collective-permute-start(bf16[1,8,4096]{2,1,0:T(8,128)(2,1)S(1)} %get-tuple-element.46), channel_id=1, source_target_pairs={{0,8},{1,9},{2,10},{3,11},{4,12},{5,13},{6,14},{7,15},{8,0},{9,1},... | collective-permute-start | bytes 196616 | tf_op jit(solution)/shard_map/ppermute | solution.py:47
  63.9 5.2 %collective-permute-start.13 = (bf16[1,8,4096]{2,1,0:T(8,128)(2,1)S(1)}, bf16[1,8,4096]{2,1,0:T(8,128)(2,1)S(1)}, u32[]{:S(2)}, u32[]{:S(2)}) collective-permute-start(bf16[1,8,4096]{2,1,0:T(8,128)(2,1)S(1)} %get-tuple-element.47), channel_id=1, source_target_pairs={{0,24},{1,25},{2,26},{3,27},{4,28},{5,29},{6,30},{7,31},{8,16},{9,... | collective-permute-start | bytes 196616 | tf_op jit(solution)/shard_map/ppermute | solution.py:47
  65.7 6.9 %collective-permute-start.12 = (bf16[1,8,4096]{2,1,0:T(8,128)(2,1)S(1)}, bf16[1,8,4096]{2,1,0:T(8,128)(2,1)S(1)}, u32[]{:S(2)}, u32[]{:S(2)}) collective-permute-start(bf16[1,8,4096]{2,1,0:T(8,128)(2,1)S(1)} %get-tuple-element.48), channel_id=1, source_target_pairs={{0,16},{1,17},{2,18},{3,19},{4,20},{5,21},{6,22},{7,23},{8,24},{9,... | collective-permute-start | bytes 196616 | tf_op jit(solution)/shard_map/ppermute | solution.py:47
  67.2 10.5 %collective-permute-start.7 = (bf16[64,4096]{1,0:T(8,128)(2,1)}, bf16[64,4096]{1,0:T(8,128)(2,1)}, u32[]{:S(2)}, u32[]{:S(2)}) collective-permute-start(bf16[64,4096]{1,0:T(8,128)(2,1)} %pad_maximum_fusion.1), channel_id=1, source_target_pairs={{0,1},{1,0},{2,3},{3,2},{4,5},{5,4},{6,7},{7,6},{8,9},{9,8},{10,11... | collective-permute-start | bytes 1572872 | tf_op jit(solution)/shard_map/ppermute | solution.py:108
  73.8 1.2 %copy-start.3 = (f32[128,2048]{1,0:T(8,128)S(1)}, f32[128,2048]{1,0:T(8,128)}, u32[]{:S(2)}) copy-start(f32[128,2048]{1,0:T(8,128)} %get-tuple-element.14) | copy-start | bytes 3145732
  76.3 4.4 %collective-permute-start.14 = (bf16[64,4096]{1,0:T(8,128)(2,1)S(1)}, bf16[64,4096]{1,0:T(8,128)(2,1)S(1)}, u32[]{:S(2)}, u32[]{:S(2)}) collective-permute-start(bf16[64,4096]{1,0:T(8,128)(2,1)S(1)} %pad_maximum_fusion.2), channel_id=1, source_target_pairs={{0,1},{1,0},{2,3},{3,2},{4,5},{5,4},{6,7},{7,6},{8,9},{9,8},{10,11... | collective-permute-start | bytes 1572872 | tf_op jit(solution)/shard_map/ppermute | solution.py:108
  (2 other events, 1.7 us)

commit v14 on v11

--- a/solution.py
+++ b/solution.py
@@ -226,7 +226,8 @@
     score_scale = 1.0 / math.sqrt(HEAD_DIM)
     f32 = jnp.float32
 
-    qb, kb, vb, gb = to_block_layout([queries, key_rows, value_rows, out_grad], core)
+    kb, vb = to_block_layout([key_rows, value_rows], core)
+    qb, gb = to_block_layout([queries, out_grad], core)
     rows, half = qb.shape
     heads = half // HEAD_DIM
     nb = rows // BLOCK

time: 82.5 us -> 82.6 us (level)
    ppermute x3 -> x4, waiting for transfers between devices: 2.21 us -> 1.45 us  [swap_with_partner(): return lax.ppermute(x, 'hc', [(0, 1), (1, 0)])]
    ppermute x3 -> x4, starting transfers between devices: 3.46 us -> 3.91 us  [swap_with_partner(): return lax.ppermute(x, 'hc', [(0, 1), (1, 0)])]
  transfers between devices with their start and end apart: 15 -> 16, of which waited for: 11 -> 11; matrix products, arithmetic and copies ran while one was open for 10% -> 12% of each run, Pallas kernels for 0% -> 0%
where the time goes in v14:
time: 82.6 us; the launch traced here: 82.3 us
  waiting for transfers between devices  32.8 us (40%)
  starting transfers between devices  16.9 us (20%)
  other arithmetic  14 us (17%)
  Pallas kernels  12.8 us (15%)
  local copies, waits for them, and re-layouts  4.78 us (6%)
  between operations  0.95 us (1%)
    ppermute x12, waiting for transfers between devices, exchange(): return lax.ppermute(x, ('seq', 'hx', 'hc'), pairs)  31.4 us
    ppermute x12, starting transfers between devices, exchange(): return lax.ppermute(x, ('seq', 'hx', 'hc'), pairs)  13 us
    pallas_call x1, Pallas kernels, attention(): pl.pallas_call(attention_kernel, grid=(heads // per_step, nb), in_specs=[...  12.8 us
    ppermute x4, starting transfers between devices, swap_with_partner(): return lax.ppermute(x, 'hc', [(0, 1), (1, 0)])  3.91 us
    select_n x4, other arithmetic, to_token_layout(): jnp.where(core == 0, jnp.concatenate([m, r], 1), jnp.concatenate([r, m], 1))  3.66 us
    another operation x2, other arithmetic  2.92 us
    select_n x4, other arithmetic, to_block_layout(): jnp.where(core == 0, jnp.concatenate([m, r], 0), jnp.concatenate([r, m], 0))  2.01 us
  transfers between devices with their start and end apart: 16, of which 11 were waited for; matrix products, arithmetic and copies ran while one was open for 12% of the time, Pallas kernels for 0%

profile of v14, /device:TPU:1, one launch (start us, length us, event | category | flops | bytes accessed | tf_op | source)
XLA Modules:
  0.0 82.3 jit_solution(5235274142997578025)
XLA Ops:
  0.7 1.4 %constant_dynamic-slice_fusion.13 = (bf16[64,2048]{1,0:T(8,128)(2,1)S(1)}, bf16[64,2048]{1,0:T(8,128)(2,1)S(1)}, bf16[64,2048]{1,0:T(8,128)(2,1)S(1)}, bf16[64,2048]{1,0:T(8,128)(2,1)S(1)}) fusion(bf16[64,4096]{1,0:T(8,128)(2,1)} %param.8, s32[]{:T(128)S(6)} %select_n.118, s32[]{:T(128)S(6)} %select_n.119, bf16[64,4096]{1,0:T(8,128)(2,1)} %param.7), kind=kLoop, calls=%fused_computation.55 | loop fusion | bytes 2097160 | tf_op jit(solution)/shard_map/dynamic_slice | solution.py:104
  3.8 1.4 %collective-permute-done.1 = bf16[64,4096]{1,0:T(8,128)(2,1)S(1)} collective-permute-done((bf16[64,4096]{1,0:T(8,128)(2,1)}, bf16[64,4096]{1,0:T(8,128)(2,1)S(1)}, u32[]{:S(2)}, u32[]{:S(2)}) %collective-permute-start.1) | collective-permute-done | bytes 524320 | tf_op jit(solution)/shard_map/ppermute | solution.py:98
  6.8 4.5 %collective-permute-start.4 = (bf16[1,8,4096]{2,1,0:T(8,128)(2,1)S(1)}, bf16[1,8,4096]{2,1,0:T(8,128)(2,1)S(1)}, u32[]{:S(2)}, u32[]{:S(2)}) collective-permute-start(bf16[1,8,4096]{2,1,0:T(8,128)(2,1)S(1)} %bitcast.87), channel_id=1, source_target_pairs={{0,24},{1,25},{2,26},{3,27},{4,28},{5,29},{6,30},{7,31},{8,16},{9,... | collective-permute-start | bytes 196616 | tf_op jit(solution)/shard_map/ppermute | solution.py:47
  11.7 1.7 %collective-permute-done.4 = bf16[1,8,4096]{2,1,0:T(8,128)(2,1)S(1)} collective-permute-done((bf16[1,8,4096]{2,1,0:T(8,128)(2,1)S(1)}, bf16[1,8,4096]{2,1,0:T(8,128)(2,1)S(1)}, u32[]{:S(2)}, u32[]{:S(2)}) %collective-permute-start.4) | collective-permute-done | bytes 65568 | tf_op jit(solution)/shard_map/ppermute | solution.py:47
  13.4 3.5 %collective-permute-done.3 = bf16[1,8,4096]{2,1,0:T(8,128)(2,1)S(1)} collective-permute-done((bf16[1,8,4096]{2,1,0:T(8,128)(2,1)S(1)}, bf16[1,8,4096]{2,1,0:T(8,128)(2,1)S(1)}, u32[]{:S(2)}, u32[]{:S(2)}) %collective-permute-start.3) | collective-permute-done | bytes 65568 | tf_op jit(solution)/shard_map/ppermute | solution.py:47
  17.0 2.2 %collective-permute-start.7 = (bf16[4,8,4096]{2,1,0:T(8,128)(2,1)S(1)}, bf16[4,8,4096]{2,1,0:T(8,128)(2,1)S(1)}, u32[]{:S(2)}, u32[]{:S(2)}) collective-permute-start(bf16[4,8,4096]{2,1,0:T(8,128)(2,1)S(1)} %get-tuple-element.50), channel_id=1, source_target_pairs={{0,6},{1,7},{2,4},{3,5},{4,2},{5,3},{6,0},{7,1},{8,14},{9,15},{10,... | collective-permute-start | bytes 786440 | tf_op jit(solution)/shard_map/ppermute | solution.py:47
  21.6 3.5 %collective-permute-done.7 = bf16[4,8,4096]{2,1,0:T(8,128)(2,1)S(1)} collective-permute-done((bf16[4,8,4096]{2,1,0:T(8,128)(2,1)S(1)}, bf16[4,8,4096]{2,1,0:T(8,128)(2,1)S(1)}, u32[]{:S(2)}, u32[]{:S(2)}) %collective-permute-start.7) | collective-permute-done | bytes 262176 | tf_op jit(solution)/shard_map/ppermute | solution.py:47
  25.0 5.7 %collective-permute-done.6 = bf16[4,8,4096]{2,1,0:T(8,128)(2,1)S(1)} collective-permute-done((bf16[4,8,4096]{2,1,0:T(8,128)(2,1)S(1)}, bf16[4,8,4096]{2,1,0:T(8,128)(2,1)S(1)}, u32[]{:S(2)}, u32[]{:S(2)}) %collective-permute-start.6) | collective-permute-done | bytes 262176 | tf_op jit(solution)/shard_map/ppermute | solution.py:47
  30.7 1.1 %collective-permute-done.5 = bf16[4,8,4096]{2,1,0:T(8,128)(2,1)S(1)} collective-permute-done((bf16[4,8,4096]{2,1,0:T(8,128)(2,1)S(1)}, bf16[4,8,4096]{2,1,0:T(8,128)(2,1)S(1)}, u32[]{:S(2)}, u32[]{:S(2)}) %collective-permute-start.5) | collective-permute-done | bytes 262176 | tf_op jit(solution)/shard_map/ppermute | solution.py:47
  31.9 1.2 %pad_maximum_fusion = bf16[4,4,8,4096]{3,2,1,0:T(8,128)(2,1)} fusion(bf16[4,1,8,4096]{3,2,1,0:T(8,128)(2,1)S(1)} %bitcast.91, bf16[4,1,8,4096]{3,2,1,0:T(8,128)(2,1)S(1)} %bitcast.92, bf16[4,1,8,4096]{3,2,1,0:T(8,128)(2,1)S(1)} %bitcast.93, bf16[4,1,8,4096]{3,2,1,0:T(8,128)(2,1)S(1)} %get-tuple-element.49), kind=kLoop, calls=%fused_computation.4 | loop fusion | flops 1572864 | bytes 2097152 | tf_op jit(solution)/shard_map/stack | solution.py:79
  33.6 12.8 %shard_map.84 = (bf16[128,2048]{1,0:T(8,128)(2,1)}, bf16[128,2048]{1,0:T(8,128)(2,1)}, f32[128,2048]{1,0:T(8,128)}, f32[128,2048]{1,0:T(8,128)}, f32[128,4096]{1,0:T(8,128)}) custom-call(bf16[128,2048]{1,0:T(8,128)(2,1)} %maximum_select_fusion.q_all, bf16[128,2048]{1,0:T(8,128)(2,1)} %copy-done.1, bf16[128,2048]{1,0:T(8,128)(2,1)} %copy-done, ...), custom_call_target="tpu_custom_call" | custom-call | flops 805306368 | bytes 7340032 | tf_op jit(solution)/shard_map/pallas_call | solution.py:203
  46.4 1.8 %convert.10 = bf16[4,4,8,4096]{3,2,1,0:T(8,128)(2,1)S(1)} convert(f32[4,4,8,4096]{3,2,1,0:T(8,128)} %bitcast.83) | non-fusion elementwise | flops 524288 | bytes 3145728 | tf_op jit(solution)/shard_map/convert.5
  48.3 1.3 %collective-permute-start.9 = (bf16[4,8,4096]{2,1,0:T(8,128)(2,1)S(1)}, bf16[4,8,4096]{2,1,0:T(8,128)(2,1)S(1)}, u32[]{:S(2)}, u32[]{:S(2)}) collective-permute-start(bf16[4,8,4096]{2,1,0:T(8,128)(2,1)S(1)} %get-tuple-element.19), channel_id=1, source_target_pairs={{0,2},{1,5},{2,0},{3,7},{4,6},{5,1},{6,4},{7,3},{8,10},{9,13},{10,... | collective-permute-start | bytes 786440 | tf_op jit(solution)/shard_map/ppermute | solution.py:47
  49.6 1.2 %collective-permute-start.11 = (bf16[4,8,4096]{2,1,0:T(8,128)(2,1)S(1)}, bf16[4,8,4096]{2,1,0:T(8,128)(2,1)S(1)}, u32[]{:S(2)}, u32[]{:S(2)}) collective-permute-start(bf16[4,8,4096]{2,1,0:T(8,128)(2,1)S(1)} %get-tuple-element.20), channel_id=1, source_target_pairs={{0,6},{1,7},{2,4},{3,5},{4,2},{5,3},{6,0},{7,1},{8,14},{9,15},{10,... | collective-permute-start | bytes 786440 | tf_op jit(solution)/shard_map/ppermute | solution.py:47
  51.1 4.3 %collective-permute-done.9 = bf16[4,8,4096]{2,1,0:T(8,128)(2,1)S(1)} collective-permute-done((bf16[4,8,4096]{2,1,0:T(8,128)(2,1)S(1)}, bf16[4,8,4096]{2,1,0:T(8,128)(2,1)S(1)}, u32[]{:S(2)}, u32[]{:S(2)}) %collective-permute-start.9) | collective-permute-done | bytes 262176 | tf_op jit(solution)/shard_map/ppermute | solution.py:47
  55.4 3.4 %collective-permute-done.11 = bf16[4,8,4096]{2,1,0:T(8,128)(2,1)S(1)} collective-permute-done((bf16[4,8,4096]{2,1,0:T(8,128)(2,1)S(1)}, bf16[4,8,4096]{2,1,0:T(8,128)(2,1)S(1)}, u32[]{:S(2)}, u32[]{:S(2)}) %collective-permute-start.11) | collective-permute-done | bytes 262176 | tf_op jit(solution)/shard_map/ppermute | solution.py:47
  58.8 4.5 %collective-permute-done.10 = bf16[4,8,4096]{2,1,0:T(8,128)(2,1)S(1)} collective-permute-done((bf16[4,8,4096]{2,1,0:T(8,128)(2,1)S(1)}, bf16[4,8,4096]{2,1,0:T(8,128)(2,1)S(1)}, u32[]{:S(2)}, u32[]{:S(2)}) %collective-permute-start.10) | collective-permute-done | bytes 262176 | tf_op jit(solution)/shard_map/ppermute | solution.py:47
  63.3 1.2 %fusion.13 = (bf16[1,4,8,4096]{3,2,1,0:T(8,128)(2,1)S(1)}, f32[1,4,8,4096]{3,2,1,0:T(8,128)S(1)}) fusion(bf16[4,8,4096]{2,1,0:T(8,128)(2,1)S(1)} %collective-permute-done.11, bf16[4,8,4096]{2,1,0:T(8,128)(2,1)S(1)} %collective-permute-done.10, bf16[4,8,4096]{2,1,0:T(8,128)(2,1)S(1)} %collective-permute-done.9, f32[4,4,8,4096]{3,2,1,0:T(8,128)} %bitcast.84), kind=kLoop, calls=%fused_computation.71 | loop fusion | flops 917504 | bytes 2097152 | tf_op jit(solution)/shard_map/convert.2
  64.7 1.8 %collective-permute-start.14 = (bf16[1,8,4096]{2,1,0:T(8,128)(2,1)S(1)}, bf16[1,8,4096]{2,1,0:T(8,128)(2,1)S(1)}, u32[]{:S(2)}, u32[]{:S(2)}) collective-permute-start(bf16[1,8,4096]{2,1,0:T(8,128)(2,1)S(1)} %get-tuple-element.47), channel_id=1, source_target_pairs={{0,24},{1,25},{2,26},{3,27},{4,28},{5,29},{6,30},{7,31},{8,16},{9,... | collective-permute-start | bytes 196616 | tf_op jit(solution)/shard_map/ppermute | solution.py:47
  68.1 1.9 %collective-permute-start.8 = (bf16[64,4096]{1,0:T(8,128)(2,1)}, bf16[64,4096]{1,0:T(8,128)(2,1)}, u32[]{:S(2)}, u32[]{:S(2)}) collective-permute-start(bf16[64,4096]{1,0:T(8,128)(2,1)} %pad_maximum_fusion.3), channel_id=1, source_target_pairs={{0,1},{1,0},{2,3},{3,2},{4,5},{5,4},{6,7},{7,6},{8,9},{9,8},{10,11... | collective-permute-start | bytes 1572872 | tf_op jit(solution)/shard_map/ppermute | solution.py:98
  70.0 3.5 %collective-permute-done.13 = bf16[1,8,4096]{2,1,0:T(8,128)(2,1)S(1)} collective-permute-done((bf16[1,8,4096]{2,1,0:T(8,128)(2,1)S(1)}, bf16[1,8,4096]{2,1,0:T(8,128)(2,1)S(1)}, u32[]{:S(2)}, u32[]{:S(2)}) %collective-permute-start.13) | collective-permute-done | bytes 65568 | tf_op jit(solution)/shard_map/ppermute | solution.py:47
  73.6 1.1 %scatter_custom_fusion = f32[128,2048]{1,0:T(8,128)S(1)} fusion(f32[128,2048]{1,0:T(8,128)S(1)} %copy-done.3, s32[8]{0:T(128)S(1)} %fusion.12, f32[8,16,2,128]{3,0,2,1:T(8,128)S(1)} %bitcast.85), kind=kCustom, calls=%fused_computation.33 | custom fusion | flops 16384 | bytes 1114112 | tf_op jit(solution)/shard_map/scatter-add | solution.py:261
  74.7 1.1 %scatter_custom_fusion.1 = f32[128,2048]{1,0:T(8,128)S(1)} fusion(f32[128,2048]{1,0:T(8,128)S(1)} %copy-done.2, s32[8]{0:T(128)S(1)} %fusion.12, f32[8,16,2,128]{3,0,2,1:T(8,128)S(1)} %bitcast.86), kind=kCustom, calls=%fused_computation.31 | custom fusion | flops 16384 | bytes 1114112 | tf_op jit(solution)/shard_map/scatter-add | solution.py:262
  76.1 1.5 %collective-permute-start.15 = (bf16[64,4096]{1,0:T(8,128)(2,1)S(1)}, bf16[64,4096]{1,0:T(8,128)(2,1)S(1)}, u32[]{:S(2)}, u32[]{:S(2)}) collective-permute-start(bf16[64,4096]{1,0:T(8,128)(2,1)S(1)} %pad_maximum_fusion.4), channel_id=1, source_target_pairs={{0,1},{1,0},{2,3},{3,2},{4,5},{5,4},{6,7},{7,6},{8,9},{9,8},{10,11... | collective-permute-start | bytes 1572872 | tf_op jit(solution)/shard_map/ppermute | solution.py:98
  (70 shorter events, 13.8 us)
Async XLA Ops:
  0.6 1.5 %copy-start.7 = (bf16[64,4096]{1,0:T(8,128)(2,1)S(1)}, bf16[64,4096]{1,0:T(8,128)(2,1)}, u32[]{:S(2)}) copy-start(bf16[64,4096]{1,0:T(8,128)(2,1)} %param.9) | copy-start | bytes 1572868
  2.1 1.6 %copy-start.8 = (s32[2,8]{1,0:T(2,128)S(1)}, s32[2,8]{1,0:T(2,128)}, u32[]{:S(2)}) copy-start(s32[2,8]{1,0:T(2,128)} %param.11) | copy-start | bytes 196
  3.1 2.1 %collective-permute-start.1 = (bf16[64,4096]{1,0:T(8,128)(2,1)}, bf16[64,4096]{1,0:T(8,128)(2,1)S(1)}, u32[]{:S(2)}, u32[]{:S(2)}) collective-permute-start(bf16[64,4096]{1,0:T(8,128)(2,1)} %pad_maximum_fusion.2), channel_id=1, source_target_pairs={{0,1},{1,0},{2,3},{3,2},{4,5},{5,4},{6,7},{7,6},{8,9},{9,8},{10,11... | collective-permute-start | bytes 1572872 | tf_op jit(solution)/shard_map/ppermute | solution.py:98
  3.2 8.5 %collective-permute-start = (bf16[64,4096]{1,0:T(8,128)(2,1)S(1)}, bf16[64,4096]{1,0:T(8,128)(2,1)S(1)}, u32[]{:S(2)}, u32[]{:S(2)}) collective-permute-start(bf16[64,4096]{1,0:T(8,128)(2,1)S(1)} %pad_maximum_fusion.1), channel_id=1, source_target_pairs={{0,1},{1,0},{2,3},{3,2},{4,5},{5,4},{6,7},{7,6},{8,9},{9,8},{10,11... | collective-permute-start | bytes 1572872 | tf_op jit(solution)/shard_map/ppermute | solution.py:98
  5.4 15.3 %copy-start = (bf16[128,2048]{1,0:T(8,128)(2,1)}, bf16[128,2048]{1,0:T(8,128)(2,1)S(1)}, u32[]{:S(2)}) copy-start(bf16[128,2048]{1,0:T(8,128)(2,1)S(1)} %maximum_select_fusion.2.v_all) | copy-start | bytes 1572868
  6.1 15.5 %copy-start.1 = (bf16[128,2048]{1,0:T(8,128)(2,1)}, bf16[128,2048]{1,0:T(8,128)(2,1)S(1)}, u32[]{:S(2)}) copy-start(bf16[128,2048]{1,0:T(8,128)(2,1)S(1)} %maximum_select_fusion.1.k_all) | copy-start | bytes 1572868
  6.8 6.7 %collective-permute-start.4 = (bf16[1,8,4096]{2,1,0:T(8,128)(2,1)S(1)}, bf16[1,8,4096]{2,1,0:T(8,128)(2,1)S(1)}, u32[]{:S(2)}, u32[]{:S(2)}) collective-permute-start(bf16[1,8,4096]{2,1,0:T(8,128)(2,1)S(1)} %bitcast.87), channel_id=1, source_target_pairs={{0,24},{1,25},{2,26},{3,27},{4,28},{5,29},{6,30},{7,31},{8,16},{9,... | collective-permute-start | bytes 196616 | tf_op jit(solution)/shard_map/ppermute | solution.py:47
  11.3 5.7 %collective-permute-start.3 = (bf16[1,8,4096]{2,1,0:T(8,128)(2,1)S(1)}, bf16[1,8,4096]{2,1,0:T(8,128)(2,1)S(1)}, u32[]{:S(2)}, u32[]{:S(2)}) collective-permute-start(bf16[1,8,4096]{2,1,0:T(8,128)(2,1)S(1)} %bitcast.88), channel_id=1, source_target_pairs={{0,16},{1,17},{2,18},{3,19},{4,20},{5,21},{6,22},{7,23},{8,24},{9,... | collective-permute-start | bytes 196616 | tf_op jit(solution)/shard_map/ppermute | solution.py:47
  11.3 5.7 %collective-permute-start.2 = (bf16[1,8,4096]{2,1,0:T(8,128)(2,1)S(1)}, bf16[1,8,4096]{2,1,0:T(8,128)(2,1)S(1)}, u32[]{:S(2)}, u32[]{:S(2)}) collective-permute-start(bf16[1,8,4096]{2,1,0:T(8,128)(2,1)S(1)} %bitcast.89), channel_id=1, source_target_pairs={{0,8},{1,9},{2,10},{3,11},{4,12},{5,13},{6,14},{7,15},{8,0},{9,1},... | collective-permute-start | bytes 196616 | tf_op jit(solution)/shard_map/ppermute | solution.py:47
  17.0 8.0 %collective-permute-start.7 = (bf16[4,8,4096]{2,1,0:T(8,128)(2,1)S(1)}, bf16[4,8,4096]{2,1,0:T(8,128)(2,1)S(1)}, u32[]{:S(2)}, u32[]{:S(2)}) collective-permute-start(bf16[4,8,4096]{2,1,0:T(8,128)(2,1)S(1)} %get-tuple-element.50), channel_id=1, source_target_pairs={{0,6},{1,7},{2,4},{3,5},{4,2},{5,3},{6,0},{7,1},{8,14},{9,15},{10,... | collective-permute-start | bytes 786440 | tf_op jit(solution)/shard_map/ppermute | solution.py:47
  19.3 11.4 %collective-permute-start.6 = (bf16[4,8,4096]{2,1,0:T(8,128)(2,1)S(1)}, bf16[4,8,4096]{2,1,0:T(8,128)(2,1)S(1)}, u32[]{:S(2)}, u32[]{:S(2)}) collective-permute-start(bf16[4,8,4096]{2,1,0:T(8,128)(2,1)S(1)} %get-tuple-element.50), channel_id=1, source_target_pairs={{0,4},{1,3},{2,6},{3,1},{4,0},{5,7},{6,2},{7,5},{8,12},{9,11},{10,... | collective-permute-start | bytes 786440 | tf_op jit(solution)/shard_map/ppermute | solution.py:47
  19.5 12.3 %collective-permute-start.5 = (bf16[4,8,4096]{2,1,0:T(8,128)(2,1)S(1)}, bf16[4,8,4096]{2,1,0:T(8,128)(2,1)S(1)}, u32[]{:S(2)}, u32[]{:S(2)}) collective-permute-start(bf16[4,8,4096]{2,1,0:T(8,128)(2,1)S(1)} %get-tuple-element.50), channel_id=1, source_target_pairs={{0,2},{1,5},{2,0},{3,7},{4,6},{5,1},{6,4},{7,3},{8,10},{9,13},{10,... | collective-permute-start | bytes 786440 | tf_op jit(solution)/shard_map/ppermute | solution.py:47
  46.4 4.6 %copy-start.5 = (bf16[128,2048]{1,0:T(8,128)(2,1)S(1)}, bf16[128,2048]{1,0:T(8,128)(2,1)}, u32[]{:S(2)}) copy-start(bf16[128,2048]{1,0:T(8,128)(2,1)} %get-tuple-element.10) | copy-start | bytes 1572868
  48.2 2.8 %copy-start.4 = (bf16[128,2048]{1,0:T(8,128)(2,1)S(1)}, bf16[128,2048]{1,0:T(8,128)(2,1)}, u32[]{:S(2)}) copy-start(bf16[128,2048]{1,0:T(8,128)(2,1)} %get-tuple-element.11) | copy-start | bytes 1572868
  48.3 7.1 %collective-permute-start.9 = (bf16[4,8,4096]{2,1,0:T(8,128)(2,1)S(1)}, bf16[4,8,4096]{2,1,0:T(8,128)(2,1)S(1)}, u32[]{:S(2)}, u32[]{:S(2)}) collective-permute-start(bf16[4,8,4096]{2,1,0:T(8,128)(2,1)S(1)} %get-tuple-element.19), channel_id=1, source_target_pairs={{0,2},{1,5},{2,0},{3,7},{4,6},{5,1},{6,4},{7,3},{8,10},{9,13},{10,... | collective-permute-start | bytes 786440 | tf_op jit(solution)/shard_map/ppermute | solution.py:47
  49.6 9.2 %collective-permute-start.11 = (bf16[4,8,4096]{2,1,0:T(8,128)(2,1)S(1)}, bf16[4,8,4096]{2,1,0:T(8,128)(2,1)S(1)}, u32[]{:S(2)}, u32[]{:S(2)}) collective-permute-start(bf16[4,8,4096]{2,1,0:T(8,128)(2,1)S(1)} %get-tuple-element.20), channel_id=1, source_target_pairs={{0,6},{1,7},{2,4},{3,5},{4,2},{5,3},{6,0},{7,1},{8,14},{9,15},{10,... | collective-permute-start | bytes 786440 | tf_op jit(solution)/shard_map/ppermute | solution.py:47
  50.8 12.5 %collective-permute-start.10 = (bf16[4,8,4096]{2,1,0:T(8,128)(2,1)S(1)}, bf16[4,8,4096]{2,1,0:T(8,128)(2,1)S(1)}, u32[]{:S(2)}, u32[]{:S(2)}) collective-permute-start(bf16[4,8,4096]{2,1,0:T(8,128)(2,1)S(1)} %get-tuple-element.21), channel_id=1, source_target_pairs={{0,4},{1,3},{2,6},{3,1},{4,0},{5,7},{6,2},{7,5},{8,12},{9,11},{10,... | collective-permute-start | bytes 786440 | tf_op jit(solution)/shard_map/ppermute | solution.py:47
  51.1 22.5 %copy-start.3 = (f32[128,2048]{1,0:T(8,128)S(1)}, f32[128,2048]{1,0:T(8,128)}, u32[]{:S(2)}) copy-start(f32[128,2048]{1,0:T(8,128)} %get-tuple-element.12) | copy-start | bytes 3145732
  64.5 5.4 %collective-permute-start.12 = (bf16[1,8,4096]{2,1,0:T(8,128)(2,1)S(1)}, bf16[1,8,4096]{2,1,0:T(8,128)(2,1)S(1)}, u32[]{:S(2)}, u32[]{:S(2)}) collective-permute-start(bf16[1,8,4096]{2,1,0:T(8,128)(2,1)S(1)} %get-tuple-element.46), channel_id=1, source_target_pairs={{0,8},{1,9},{2,10},{3,11},{4,12},{5,13},{6,14},{7,15},{8,0},{9,1},... | collective-permute-start | bytes 196616 | tf_op jit(solution)/shard_map/ppermute | solution.py:47
  64.7 5.3 %collective-permute-start.14 = (bf16[1,8,4096]{2,1,0:T(8,128)(2,1)S(1)}, bf16[1,8,4096]{2,1,0:T(8,128)(2,1)S(1)}, u32[]{:S(2)}, u32[]{:S(2)}) collective-permute-start(bf16[1,8,4096]{2,1,0:T(8,128)(2,1)S(1)} %get-tuple-element.47), channel_id=1, source_target_pairs={{0,24},{1,25},{2,26},{3,27},{4,28},{5,29},{6,30},{7,31},{8,16},{9,... | collective-permute-start | bytes 196616 | tf_op jit(solution)/shard_map/ppermute | solution.py:47
  66.5 7.0 %collective-permute-start.13 = (bf16[1,8,4096]{2,1,0:T(8,128)(2,1)S(1)}, bf16[1,8,4096]{2,1,0:T(8,128)(2,1)S(1)}, u32[]{:S(2)}, u32[]{:S(2)}) collective-permute-start(bf16[1,8,4096]{2,1,0:T(8,128)(2,1)S(1)} %get-tuple-element.48), channel_id=1, source_target_pairs={{0,16},{1,17},{2,18},{3,19},{4,20},{5,21},{6,22},{7,23},{8,24},{9,... | collective-permute-start | bytes 196616 | tf_op jit(solution)/shard_map/ppermute | solution.py:47
  67.2 7.5 %copy-start.2 = (f32[128,2048]{1,0:T(8,128)S(1)}, f32[128,2048]{1,0:T(8,128)}, u32[]{:S(2)}) copy-start(f32[128,2048]{1,0:T(8,128)} %get-tuple-element.14) | copy-start | bytes 3145732
  68.1 9.5 %collective-permute-start.8 = (bf16[64,4096]{1,0:T(8,128)(2,1)}, bf16[64,4096]{1,0:T(8,128)(2,1)}, u32[]{:S(2)}, u32[]{:S(2)}) collective-permute-start(bf16[64,4096]{1,0:T(8,128)(2,1)} %pad_maximum_fusion.3), channel_id=1, source_target_pairs={{0,1},{1,0},{2,3},{3,2},{4,5},{5,4},{6,7},{7,6},{8,9},{9,8},{10,11... | collective-permute-start | bytes 1572872 | tf_op jit(solution)/shard_map/ppermute | solution.py:98
  76.1 4.4 %collective-permute-start.15 = (bf16[64,4096]{1,0:T(8,128)(2,1)S(1)}, bf16[64,4096]{1,0:T(8,128)(2,1)S(1)}, u32[]{:S(2)}, u32[]{:S(2)}) collective-permute-start(bf16[64,4096]{1,0:T(8,128)(2,1)S(1)} %pad_maximum_fusion.4), channel_id=1, source_target_pairs={{0,1},{1,0},{2,3},{3,2},{4,5},{5,4},{6,7},{7,6},{8,9},{9,8},{10,11... | collective-permute-start | bytes 1572872 | tf_op jit(solution)/shard_map/ppermute | solution.py:98
  (1 other events, 1.4 us)

commit v15 on v11

--- a/solution.py
+++ b/solution.py
@@ -257,8 +257,10 @@
     att_tok, dq_tok = to_token_layout([attended, dq], core)
 
     own_grad = reduce_blocks(parts, core).reshape(-1, heads, 2, HEAD_DIM)
-    dk = dkw.at[positions].add(own_grad[:, :, 0].reshape(-1, half))
-    dv = dvw.at[positions].add(own_grad[:, :, 1].reshape(-1, half))
+    place = (jnp.arange(rows, dtype=jnp.int32)[:, None] == positions[None, :]).astype(jnp.float32)
+    exact = lax.Precision.HIGHEST
+    dk = dkw + jnp.dot(place, own_grad[:, :, 0].reshape(-1, half), precision=exact)
+    dv = dvw + jnp.dot(place, own_grad[:, :, 1].reshape(-1, half), precision=exact)
     dk_tok, dv_tok = to_token_layout([dk.astype(jnp.bfloat16), dv.astype(jnp.bfloat16)], core)
     return att_tok, dq_tok, dk_tok, dv_tok
 

time: 82.5 us -> 80.2 us (0.972)
  other arithmetic: 13.2 us -> 10 us
  matrix products: 0 us -> 1.11 us
  local copies, waits for them, and re-layouts: 5.18 us -> 4.14 us
    scatter-add x2 -> x0, other arithmetic: 2.21 us -> none  [the longest x1 1.1 us: body(): dk = dkw.at[positions].add(own_grad[:, :, 0].reshape(-1, half))]
    dot_general x0 -> x2, matrix products: none -> 1.11 us  [the longest x1 0.56 us: body(): jnp.dot(place, own_grad[:, :, 1].reshape(-1, half), precision=exact)]
    slice x2, local copies, waits for them, and re-layouts: 1.11 us -> 0.08 us  [to_token_layout(): r = got[:, i * half:(i + 1) * half]]
  transfers between devices with their start and end apart: 15 -> 15, of which waited for: 11 -> 11; matrix products, arithmetic and copies ran while one was open for 10% -> 6% of each run, Pallas kernels for 0% -> 0%
where the time goes in v15:
time: 80.2 us; the launch traced here: 79.9 us
  waiting for transfers between devices  34.4 us (43%)
  starting transfers between devices  16.6 us (21%)
  Pallas kernels  12.8 us (16%)
  other arithmetic  10 us (12%)
  local copies, waits for them, and re-layouts  4.14 us (5%)
  matrix products  1.11 us (1%)
  between operations  0.94 us (1%)
    ppermute x12, waiting for transfers between devices, exchange(): return lax.ppermute(x, ('seq', 'hx', 'hc'), pairs)  32.2 us
    ppermute x12, starting transfers between devices, exchange(): return lax.ppermute(x, ('seq', 'hx', 'hc'), pairs)  13 us
    pallas_call x1, Pallas kernels, attention(): pl.pallas_call(attention_kernel, grid=(heads // per_step, nb), in_specs=[...  12.8 us
    select_n x4, other arithmetic, to_token_layout(): jnp.where(core == 0, jnp.concatenate([m, r], 1), jnp.concatenate([r, m], 1))  3.66 us
    ppermute x3, starting transfers between devices, swap_with_partner(): return lax.ppermute(x, 'hc', [(0, 1), (1, 0)])  3.54 us
    another operation x2, other arithmetic  2.92 us
    ppermute x3, waiting for transfers between devices, swap_with_partner(): return lax.ppermute(x, 'hc', [(0, 1), (1, 0)])  2.21 us
    select_n x4, other arithmetic, to_block_layout(): jnp.where(core == 0, jnp.concatenate([m, r], 0), jnp.concatenate([r, m], 0))  2.01 us
  transfers between devices with their start and end apart: 15, of which 11 were waited for; matrix products, arithmetic and copies ran while one was open for 6% of the time, Pallas kernels for 0%

profile of v15, /device:TPU:1, one launch (start us, length us, event | category | flops | bytes accessed | tf_op | source)
XLA Modules:
  0.0 79.9 jit_solution(17537420248182142861)
XLA Ops:
  0.7 1.3 %constant_dynamic-slice_fusion.11 = (bf16[64,2048]{1,0:T(8,128)(2,1)S(1)}, bf16[64,2048]{1,0:T(8,128)(2,1)S(1)}, bf16[64,2048]{1,0:T(8,128)(2,1)S(1)}, bf16[64,2048]{1,0:T(8,128)(2,1)S(1)}) fusion(bf16[64,4096]{1,0:T(8,128)(2,1)} %param.8, s32[]{:T(128)S(6)} %select_n.107, s32[]{:T(128)S(6)} %select_n.108, bf16[64,4096]{1,0:T(8,128)(2,1)} %param.7), kind=kLoop, calls=%fused_computation.55 | loop fusion | bytes 2097160 | tf_op jit(solution)/shard_map/dynamic_slice | solution.py:104
  2.9 2.2 %collective-permute-done = bf16[64,8192]{1,0:T(8,128)(2,1)S(1)} collective-permute-done((bf16[64,8192]{1,0:T(8,128)(2,1)S(1)}, bf16[64,8192]{1,0:T(8,128)(2,1)S(1)}, u32[]{:S(2)}, u32[]{:S(2)}) %collective-permute-start) | collective-permute-done | bytes 1048608 | tf_op jit(solution)/shard_map/ppermute | solution.py:98
  6.7 4.5 %collective-permute-start.3 = (bf16[1,8,4096]{2,1,0:T(8,128)(2,1)S(1)}, bf16[1,8,4096]{2,1,0:T(8,128)(2,1)S(1)}, u32[]{:S(2)}, u32[]{:S(2)}) collective-permute-start(bf16[1,8,4096]{2,1,0:T(8,128)(2,1)S(1)} %bitcast.79), channel_id=1, source_target_pairs={{0,24},{1,25},{2,26},{3,27},{4,28},{5,29},{6,30},{7,31},{8,16},{9,... | collective-permute-start | bytes 196616 | tf_op jit(solution)/shard_map/ppermute | solution.py:47
  11.6 1.8 %collective-permute-done.3 = bf16[1,8,4096]{2,1,0:T(8,128)(2,1)S(1)} collective-permute-done((bf16[1,8,4096]{2,1,0:T(8,128)(2,1)S(1)}, bf16[1,8,4096]{2,1,0:T(8,128)(2,1)S(1)}, u32[]{:S(2)}, u32[]{:S(2)}) %collective-permute-start.3) | collective-permute-done | bytes 65568 | tf_op jit(solution)/shard_map/ppermute | solution.py:47
  13.4 3.5 %collective-permute-done.2 = bf16[1,8,4096]{2,1,0:T(8,128)(2,1)S(1)} collective-permute-done((bf16[1,8,4096]{2,1,0:T(8,128)(2,1)S(1)}, bf16[1,8,4096]{2,1,0:T(8,128)(2,1)S(1)}, u32[]{:S(2)}, u32[]{:S(2)}) %collective-permute-start.2) | collective-permute-done | bytes 65568 | tf_op jit(solution)/shard_map/ppermute | solution.py:47
  17.0 2.2 %collective-permute-start.6 = (bf16[4,8,4096]{2,1,0:T(8,128)(2,1)S(1)}, bf16[4,8,4096]{2,1,0:T(8,128)(2,1)S(1)}, u32[]{:S(2)}, u32[]{:S(2)}) collective-permute-start(bf16[4,8,4096]{2,1,0:T(8,128)(2,1)S(1)} %get-tuple-element.50), channel_id=1, source_target_pairs={{0,6},{1,7},{2,4},{3,5},{4,2},{5,3},{6,0},{7,1},{8,14},{9,15},{10,... | collective-permute-start | bytes 786440 | tf_op jit(solution)/shard_map/ppermute | solution.py:47
  21.5 3.5 %collective-permute-done.6 = bf16[4,8,4096]{2,1,0:T(8,128)(2,1)S(1)} collective-permute-done((bf16[4,8,4096]{2,1,0:T(8,128)(2,1)S(1)}, bf16[4,8,4096]{2,1,0:T(8,128)(2,1)S(1)}, u32[]{:S(2)}, u32[]{:S(2)}) %collective-permute-start.6) | collective-permute-done | bytes 262176 | tf_op jit(solution)/shard_map/ppermute | solution.py:47
  25.0 5.7 %collective-permute-done.5 = bf16[4,8,4096]{2,1,0:T(8,128)(2,1)S(1)} collective-permute-done((bf16[4,8,4096]{2,1,0:T(8,128)(2,1)S(1)}, bf16[4,8,4096]{2,1,0:T(8,128)(2,1)S(1)}, u32[]{:S(2)}, u32[]{:S(2)}) %collective-permute-start.5) | collective-permute-done | bytes 262176 | tf_op jit(solution)/shard_map/ppermute | solution.py:47
  30.7 1.1 %collective-permute-done.4 = bf16[4,8,4096]{2,1,0:T(8,128)(2,1)S(1)} collective-permute-done((bf16[4,8,4096]{2,1,0:T(8,128)(2,1)S(1)}, bf16[4,8,4096]{2,1,0:T(8,128)(2,1)S(1)}, u32[]{:S(2)}, u32[]{:S(2)}) %collective-permute-start.4) | collective-permute-done | bytes 262176 | tf_op jit(solution)/shard_map/ppermute | solution.py:47
  31.8 1.1 %pad_maximum_fusion.1 = bf16[4,4,8,4096]{3,2,1,0:T(8,128)(2,1)} fusion(bf16[4,1,8,4096]{3,2,1,0:T(8,128)(2,1)S(1)} %bitcast.83, bf16[4,1,8,4096]{3,2,1,0:T(8,128)(2,1)S(1)} %bitcast.84, bf16[4,1,8,4096]{3,2,1,0:T(8,128)(2,1)S(1)} %bitcast.85, bf16[4,1,8,4096]{3,2,1,0:T(8,128)(2,1)S(1)} %get-tuple-element.49), kind=kLoop, calls=%fused_computation.7 | loop fusion | flops 1572864 | bytes 2097152 | tf_op jit(solution)/shard_map/stack | solution.py:79
  33.5 12.8 %shard_map.84 = (bf16[128,2048]{1,0:T(8,128)(2,1)}, bf16[128,2048]{1,0:T(8,128)(2,1)}, f32[128,2048]{1,0:T(8,128)}, f32[128,2048]{1,0:T(8,128)}, f32[128,4096]{1,0:T(8,128)}) custom-call(bf16[128,2048]{1,0:T(8,128)(2,1)} %maximum_select_fusion.q_all, bf16[128,2048]{1,0:T(8,128)(2,1)} %copy-done.1, bf16[128,2048]{1,0:T(8,128)(2,1)} %copy-done, ...), custom_call_target="tpu_custom_call" | custom-call | flops 805306368 | bytes 7340032 | tf_op jit(solution)/shard_map/pallas_call | solution.py:203
  46.3 1.8 %convert.10 = bf16[4,4,8,4096]{3,2,1,0:T(8,128)(2,1)S(1)} convert(f32[4,4,8,4096]{3,2,1,0:T(8,128)} %bitcast.75) | non-fusion elementwise | flops 524288 | bytes 3145728 | tf_op jit(solution)/shard_map/convert.5
  48.1 1.3 %collective-permute-start.8 = (bf16[4,8,4096]{2,1,0:T(8,128)(2,1)S(1)}, bf16[4,8,4096]{2,1,0:T(8,128)(2,1)S(1)}, u32[]{:S(2)}, u32[]{:S(2)}) collective-permute-start(bf16[4,8,4096]{2,1,0:T(8,128)(2,1)S(1)} %get-tuple-element.19), channel_id=1, source_target_pairs={{0,2},{1,5},{2,0},{3,7},{4,6},{5,1},{6,4},{7,3},{8,10},{9,13},{10,... | collective-permute-start | bytes 786440 | tf_op jit(solution)/shard_map/ppermute | solution.py:47
  49.4 1.2 %collective-permute-start.10 = (bf16[4,8,4096]{2,1,0:T(8,128)(2,1)S(1)}, bf16[4,8,4096]{2,1,0:T(8,128)(2,1)S(1)}, u32[]{:S(2)}, u32[]{:S(2)}) collective-permute-start(bf16[4,8,4096]{2,1,0:T(8,128)(2,1)S(1)} %get-tuple-element.20), channel_id=1, source_target_pairs={{0,6},{1,7},{2,4},{3,5},{4,2},{5,3},{6,0},{7,1},{8,14},{9,15},{10,... | collective-permute-start | bytes 786440 | tf_op jit(solution)/shard_map/ppermute | solution.py:47
  50.9 4.3 %collective-permute-done.8 = bf16[4,8,4096]{2,1,0:T(8,128)(2,1)S(1)} collective-permute-done((bf16[4,8,4096]{2,1,0:T(8,128)(2,1)S(1)}, bf16[4,8,4096]{2,1,0:T(8,128)(2,1)S(1)}, u32[]{:S(2)}, u32[]{:S(2)}) %collective-permute-start.8) | collective-permute-done | bytes 262176 | tf_op jit(solution)/shard_map/ppermute | solution.py:47
  55.2 3.4 %collective-permute-done.10 = bf16[4,8,4096]{2,1,0:T(8,128)(2,1)S(1)} collective-permute-done((bf16[4,8,4096]{2,1,0:T(8,128)(2,1)S(1)}, bf16[4,8,4096]{2,1,0:T(8,128)(2,1)S(1)}, u32[]{:S(2)}, u32[]{:S(2)}) %collective-permute-start.10) | collective-permute-done | bytes 262176 | tf_op jit(solution)/shard_map/ppermute | solution.py:47
  58.6 4.5 %collective-permute-done.9 = bf16[4,8,4096]{2,1,0:T(8,128)(2,1)S(1)} collective-permute-done((bf16[4,8,4096]{2,1,0:T(8,128)(2,1)S(1)}, bf16[4,8,4096]{2,1,0:T(8,128)(2,1)S(1)}, u32[]{:S(2)}, u32[]{:S(2)}) %collective-permute-start.9) | collective-permute-done | bytes 262176 | tf_op jit(solution)/shard_map/ppermute | solution.py:47
  63.2 1.2 %fusion.15 = (bf16[1,4,8,4096]{3,2,1,0:T(8,128)(2,1)S(1)}, f32[1,4,8,4096]{3,2,1,0:T(8,128)S(1)}) fusion(bf16[4,8,4096]{2,1,0:T(8,128)(2,1)S(1)} %collective-permute-done.10, bf16[4,8,4096]{2,1,0:T(8,128)(2,1)S(1)} %collective-permute-done.9, bf16[4,8,4096]{2,1,0:T(8,128)(2,1)S(1)} %collective-permute-done.8, f32[4,4,8,4096]{3,2,1,0:T(8,128)} %bitcast.76), kind=kLoop, calls=%fused_computation.72 | loop fusion | flops 917504 | bytes 2097152 | tf_op jit(solution)/shard_map/convert.2
  64.6 1.8 %collective-permute-start.13 = (bf16[1,8,4096]{2,1,0:T(8,128)(2,1)S(1)}, bf16[1,8,4096]{2,1,0:T(8,128)(2,1)S(1)}, u32[]{:S(2)}, u32[]{:S(2)}) collective-permute-start(bf16[1,8,4096]{2,1,0:T(8,128)(2,1)S(1)} %get-tuple-element.47), channel_id=1, source_target_pairs={{0,24},{1,25},{2,26},{3,27},{4,28},{5,29},{6,30},{7,31},{8,16},{9,... | collective-permute-start | bytes 196616 | tf_op jit(solution)/shard_map/ppermute | solution.py:47
  67.1 1.9 %collective-permute-start.7 = (bf16[64,4096]{1,0:T(8,128)(2,1)S(1)}, bf16[64,4096]{1,0:T(8,128)(2,1)S(1)}, u32[]{:S(2)}, u32[]{:S(2)}) collective-permute-start(bf16[64,4096]{1,0:T(8,128)(2,1)S(1)} %pad_maximum_fusion.2), channel_id=1, source_target_pairs={{0,1},{1,0},{2,3},{3,2},{4,5},{5,4},{6,7},{7,6},{8,9},{9,8},{10,11... | collective-permute-start | bytes 1572872 | tf_op jit(solution)/shard_map/ppermute | solution.py:98
  69.9 3.5 %collective-permute-done.12 = bf16[1,8,4096]{2,1,0:T(8,128)(2,1)S(1)} collective-permute-done((bf16[1,8,4096]{2,1,0:T(8,128)(2,1)S(1)}, bf16[1,8,4096]{2,1,0:T(8,128)(2,1)S(1)}, u32[]{:S(2)}, u32[]{:S(2)}) %collective-permute-start.12) | collective-permute-done | bytes 65568 | tf_op jit(solution)/shard_map/ppermute | solution.py:47
  74.7 1.5 %collective-permute-start.14 = (bf16[64,4096]{1,0:T(8,128)(2,1)S(1)}, bf16[64,4096]{1,0:T(8,128)(2,1)S(1)}, u32[]{:S(2)}, u32[]{:S(2)}) collective-permute-start(bf16[64,4096]{1,0:T(8,128)(2,1)S(1)} %pad_maximum_fusion.3), channel_id=1, source_target_pairs={{0,1},{1,0},{2,3},{3,2},{4,5},{5,4},{6,7},{7,6},{8,9},{9,8},{10,11... | collective-permute-start | bytes 1572872 | tf_op jit(solution)/shard_map/ppermute | solution.py:98
  76.2 0.9 %maximum_select_fusion.5 = bf16[64,4096]{1,0:T(8,128)(2,1)} fusion(bf16[64,2048]{1,0:T(8,128)(2,1)S(1)} %get-tuple-element.34, bf16[64,2048]{1,0:T(8,128)(2,1)S(1)} %get-tuple-element.32, pred[]{:T(512)S(6)} %eq.12), kind=kLoop, calls=%fused_computation.19 | loop fusion | flops 2359296 | bytes 1048577 | tf_op jit(solution)/shard_map/jit(_where)/select_n | solution.py:123
  78.1 0.9 %maximum_select_fusion.7 = bf16[64,4096]{1,0:T(8,128)(2,1)} fusion(bf16[64,2048]{1,0:T(8,128)(2,1)S(1)} %get-tuple-element.28, bf16[64,2048]{1,0:T(8,128)(2,1)S(1)} %get-tuple-element.26, pred[]{:T(512)S(6)} %eq.12), kind=kLoop, calls=%fused_computation.22 | loop fusion | flops 2359296 | bytes 1048577 | tf_op jit(solution)/shard_map/jit(_where)/select_n | solution.py:123
  (64 shorter events, 11.0 us)
Async XLA Ops:
  0.6 1.4 %copy-start.6 = (bf16[64,4096]{1,0:T(8,128)(2,1)S(1)}, bf16[64,4096]{1,0:T(8,128)(2,1)}, u32[]{:S(2)}) copy-start(bf16[64,4096]{1,0:T(8,128)(2,1)} %param.10) | copy-start | bytes 1572868
  0.6 1.5 %copy-start.7 = (bf16[64,4096]{1,0:T(8,128)(2,1)S(1)}, bf16[64,4096]{1,0:T(8,128)(2,1)}, u32[]{:S(2)}) copy-start(bf16[64,4096]{1,0:T(8,128)(2,1)} %param.9) | copy-start | bytes 1572868
  2.1 0.7 copy-start.8
  2.3 2.7 %collective-permute-start = (bf16[64,8192]{1,0:T(8,128)(2,1)S(1)}, bf16[64,8192]{1,0:T(8,128)(2,1)S(1)}, u32[]{:S(2)}, u32[]{:S(2)}) collective-permute-start(bf16[64,8192]{1,0:T(8,128)(2,1)S(1)} %pad_maximum_fusion), channel_id=1, source_target_pairs={{0,1},{1,0},{2,3},{3,2},{4,5},{5,4},{6,7},{7,6},{8,9},{9,8},{10,11... | collective-permute-start | bytes 3145736 | tf_op jit(solution)/shard_map/ppermute | solution.py:98
  5.3 16.2 %copy-start = (bf16[128,2048]{1,0:T(8,128)(2,1)}, bf16[128,2048]{1,0:T(8,128)(2,1)S(1)}, u32[]{:S(2)}) copy-start(bf16[128,2048]{1,0:T(8,128)(2,1)S(1)} %maximum_select_fusion.2.v_all) | copy-start | bytes 1572868
  6.0 26.9 %copy-start.1 = (bf16[128,2048]{1,0:T(8,128)(2,1)}, bf16[128,2048]{1,0:T(8,128)(2,1)S(1)}, u32[]{:S(2)}) copy-start(bf16[128,2048]{1,0:T(8,128)(2,1)S(1)} %maximum_select_fusion.1.k_all) | copy-start | bytes 1572868
  6.7 6.7 %collective-permute-start.3 = (bf16[1,8,4096]{2,1,0:T(8,128)(2,1)S(1)}, bf16[1,8,4096]{2,1,0:T(8,128)(2,1)S(1)}, u32[]{:S(2)}, u32[]{:S(2)}) collective-permute-start(bf16[1,8,4096]{2,1,0:T(8,128)(2,1)S(1)} %bitcast.79), channel_id=1, source_target_pairs={{0,24},{1,25},{2,26},{3,27},{4,28},{5,29},{6,30},{7,31},{8,16},{9,... | collective-permute-start | bytes 196616 | tf_op jit(solution)/shard_map/ppermute | solution.py:47
  11.2 5.7 %collective-permute-start.2 = (bf16[1,8,4096]{2,1,0:T(8,128)(2,1)S(1)}, bf16[1,8,4096]{2,1,0:T(8,128)(2,1)S(1)}, u32[]{:S(2)}, u32[]{:S(2)}) collective-permute-start(bf16[1,8,4096]{2,1,0:T(8,128)(2,1)S(1)} %bitcast.80), channel_id=1, source_target_pairs={{0,16},{1,17},{2,18},{3,19},{4,20},{5,21},{6,22},{7,23},{8,24},{9,... | collective-permute-start | bytes 196616 | tf_op jit(solution)/shard_map/ppermute | solution.py:47
  11.2 5.7 %collective-permute-start.1 = (bf16[1,8,4096]{2,1,0:T(8,128)(2,1)S(1)}, bf16[1,8,4096]{2,1,0:T(8,128)(2,1)S(1)}, u32[]{:S(2)}, u32[]{:S(2)}) collective-permute-start(bf16[1,8,4096]{2,1,0:T(8,128)(2,1)S(1)} %bitcast.81), channel_id=1, source_target_pairs={{0,8},{1,9},{2,10},{3,11},{4,12},{5,13},{6,14},{7,15},{8,0},{9,1},... | collective-permute-start | bytes 196616 | tf_op jit(solution)/shard_map/ppermute | solution.py:47
  17.0 8.0 %collective-permute-start.6 = (bf16[4,8,4096]{2,1,0:T(8,128)(2,1)S(1)}, bf16[4,8,4096]{2,1,0:T(8,128)(2,1)S(1)}, u32[]{:S(2)}, u32[]{:S(2)}) collective-permute-start(bf16[4,8,4096]{2,1,0:T(8,128)(2,1)S(1)} %get-tuple-element.50), channel_id=1, source_target_pairs={{0,6},{1,7},{2,4},{3,5},{4,2},{5,3},{6,0},{7,1},{8,14},{9,15},{10,... | collective-permute-start | bytes 786440 | tf_op jit(solution)/shard_map/ppermute | solution.py:47
  19.2 11.4 %collective-permute-start.5 = (bf16[4,8,4096]{2,1,0:T(8,128)(2,1)S(1)}, bf16[4,8,4096]{2,1,0:T(8,128)(2,1)S(1)}, u32[]{:S(2)}, u32[]{:S(2)}) collective-permute-start(bf16[4,8,4096]{2,1,0:T(8,128)(2,1)S(1)} %get-tuple-element.50), channel_id=1, source_target_pairs={{0,4},{1,3},{2,6},{3,1},{4,0},{5,7},{6,2},{7,5},{8,12},{9,11},{10,... | collective-permute-start | bytes 786440 | tf_op jit(solution)/shard_map/ppermute | solution.py:47
  19.5 12.3 %collective-permute-start.4 = (bf16[4,8,4096]{2,1,0:T(8,128)(2,1)S(1)}, bf16[4,8,4096]{2,1,0:T(8,128)(2,1)S(1)}, u32[]{:S(2)}, u32[]{:S(2)}) collective-permute-start(bf16[4,8,4096]{2,1,0:T(8,128)(2,1)S(1)} %get-tuple-element.50), channel_id=1, source_target_pairs={{0,2},{1,5},{2,0},{3,7},{4,6},{5,1},{6,4},{7,3},{8,10},{9,13},{10,... | collective-permute-start | bytes 786440 | tf_op jit(solution)/shard_map/ppermute | solution.py:47
  46.3 4.6 %copy-start.5 = (bf16[128,2048]{1,0:T(8,128)(2,1)S(1)}, bf16[128,2048]{1,0:T(8,128)(2,1)}, u32[]{:S(2)}) copy-start(bf16[128,2048]{1,0:T(8,128)(2,1)} %get-tuple-element.10) | copy-start | bytes 1572868
  48.0 2.8 %copy-start.4 = (bf16[128,2048]{1,0:T(8,128)(2,1)S(1)}, bf16[128,2048]{1,0:T(8,128)(2,1)}, u32[]{:S(2)}) copy-start(bf16[128,2048]{1,0:T(8,128)(2,1)} %get-tuple-element.11) | copy-start | bytes 1572868
  48.1 7.1 %collective-permute-start.8 = (bf16[4,8,4096]{2,1,0:T(8,128)(2,1)S(1)}, bf16[4,8,4096]{2,1,0:T(8,128)(2,1)S(1)}, u32[]{:S(2)}, u32[]{:S(2)}) collective-permute-start(bf16[4,8,4096]{2,1,0:T(8,128)(2,1)S(1)} %get-tuple-element.19), channel_id=1, source_target_pairs={{0,2},{1,5},{2,0},{3,7},{4,6},{5,1},{6,4},{7,3},{8,10},{9,13},{10,... | collective-permute-start | bytes 786440 | tf_op jit(solution)/shard_map/ppermute | solution.py:47
  49.4 9.2 %collective-permute-start.10 = (bf16[4,8,4096]{2,1,0:T(8,128)(2,1)S(1)}, bf16[4,8,4096]{2,1,0:T(8,128)(2,1)S(1)}, u32[]{:S(2)}, u32[]{:S(2)}) collective-permute-start(bf16[4,8,4096]{2,1,0:T(8,128)(2,1)S(1)} %get-tuple-element.20), channel_id=1, source_target_pairs={{0,6},{1,7},{2,4},{3,5},{4,2},{5,3},{6,0},{7,1},{8,14},{9,15},{10,... | collective-permute-start | bytes 786440 | tf_op jit(solution)/shard_map/ppermute | solution.py:47
  50.6 12.5 %collective-permute-start.9 = (bf16[4,8,4096]{2,1,0:T(8,128)(2,1)S(1)}, bf16[4,8,4096]{2,1,0:T(8,128)(2,1)S(1)}, u32[]{:S(2)}, u32[]{:S(2)}) collective-permute-start(bf16[4,8,4096]{2,1,0:T(8,128)(2,1)S(1)} %get-tuple-element.21), channel_id=1, source_target_pairs={{0,4},{1,3},{2,6},{3,1},{4,0},{5,7},{6,2},{7,5},{8,12},{9,11},{10,... | collective-permute-start | bytes 786440 | tf_op jit(solution)/shard_map/ppermute | solution.py:47
  50.9 22.5 %copy-start.3 = (f32[128,2048]{1,0:T(8,128)S(1)}, f32[128,2048]{1,0:T(8,128)}, u32[]{:S(2)}) copy-start(f32[128,2048]{1,0:T(8,128)} %get-tuple-element.14) | copy-start | bytes 3145732
  64.3 9.6 %copy-start.2 = (f32[128,2048]{1,0:T(8,128)S(1)}, f32[128,2048]{1,0:T(8,128)}, u32[]{:S(2)}) copy-start(f32[128,2048]{1,0:T(8,128)} %get-tuple-element.12) | copy-start | bytes 3145732
  64.4 4.7 %collective-permute-start.11 = (bf16[1,8,4096]{2,1,0:T(8,128)(2,1)S(1)}, bf16[1,8,4096]{2,1,0:T(8,128)(2,1)S(1)}, u32[]{:S(2)}, u32[]{:S(2)}) collective-permute-start(bf16[1,8,4096]{2,1,0:T(8,128)(2,1)S(1)} %get-tuple-element.46), channel_id=1, source_target_pairs={{0,8},{1,9},{2,10},{3,11},{4,12},{5,13},{6,14},{7,15},{8,0},{9,1},... | collective-permute-start | bytes 196616 | tf_op jit(solution)/shard_map/ppermute | solution.py:47
  64.6 5.3 %collective-permute-start.13 = (bf16[1,8,4096]{2,1,0:T(8,128)(2,1)S(1)}, bf16[1,8,4096]{2,1,0:T(8,128)(2,1)S(1)}, u32[]{:S(2)}, u32[]{:S(2)}) collective-permute-start(bf16[1,8,4096]{2,1,0:T(8,128)(2,1)S(1)} %get-tuple-element.47), channel_id=1, source_target_pairs={{0,24},{1,25},{2,26},{3,27},{4,28},{5,29},{6,30},{7,31},{8,16},{9,... | collective-permute-start | bytes 196616 | tf_op jit(solution)/shard_map/ppermute | solution.py:47
  66.4 7.0 %collective-permute-start.12 = (bf16[1,8,4096]{2,1,0:T(8,128)(2,1)S(1)}, bf16[1,8,4096]{2,1,0:T(8,128)(2,1)S(1)}, u32[]{:S(2)}, u32[]{:S(2)}) collective-permute-start(bf16[1,8,4096]{2,1,0:T(8,128)(2,1)S(1)} %get-tuple-element.48), channel_id=1, source_target_pairs={{0,16},{1,17},{2,18},{3,19},{4,20},{5,21},{6,22},{7,23},{8,24},{9,... | collective-permute-start | bytes 196616 | tf_op jit(solution)/shard_map/ppermute | solution.py:47
  67.1 9.0 %collective-permute-start.7 = (bf16[64,4096]{1,0:T(8,128)(2,1)S(1)}, bf16[64,4096]{1,0:T(8,128)(2,1)S(1)}, u32[]{:S(2)}, u32[]{:S(2)}) collective-permute-start(bf16[64,4096]{1,0:T(8,128)(2,1)S(1)} %pad_maximum_fusion.2), channel_id=1, source_target_pairs={{0,1},{1,0},{2,3},{3,2},{4,5},{5,4},{6,7},{7,6},{8,9},{9,8},{10,11... | collective-permute-start | bytes 1572872 | tf_op jit(solution)/shard_map/ppermute | solution.py:98
  74.7 3.4 %collective-permute-start.14 = (bf16[64,4096]{1,0:T(8,128)(2,1)S(1)}, bf16[64,4096]{1,0:T(8,128)(2,1)S(1)}, u32[]{:S(2)}, u32[]{:S(2)}) collective-permute-start(bf16[64,4096]{1,0:T(8,128)(2,1)S(1)} %pad_maximum_fusion.3), channel_id=1, source_target_pairs={{0,1},{1,0},{2,3},{3,2},{4,5},{5,4},{6,7},{7,6},{8,9},{9,8},{10,11... | collective-permute-start | bytes 1572872 | tf_op jit(solution)/shard_map/ppermute | solution.py:98

commit v16 on v15

--- a/solution.py
+++ b/solution.py
@@ -107,15 +107,15 @@
     out = []
     for i, m in enumerate(mine):
         r = got[:, i * half:(i + 1) * half]
-        out.append(jnp.where(core == 0, jnp.concatenate([m, r], 0), jnp.concatenate([r, m], 0)))
+        out.append(jnp.concatenate([m, r], 0))
     return out
 
 
 def to_token_layout(arrays, core):
     rows2, half = arrays[0].shape
     rows = rows2 // 2
-    mine = [lax.dynamic_slice_in_dim(a, core * rows, rows, 0) for a in arrays]
-    theirs = [lax.dynamic_slice_in_dim(a, (1 - core) * rows, rows, 0) for a in arrays]
+    mine = [a[:rows] for a in arrays]
+    theirs = [a[rows:] for a in arrays]
     got = swap_with_partner(jnp.concatenate(theirs, axis=1))
     out = []
     for i, m in enumerate(mine):
@@ -130,16 +130,14 @@
 
 
 def attention_kernel(
-    q_all, k_all, v_all, g_all, s_all, mask_ref, att_all, dq_all, dkw_all, dvw_all, ds_all
+    q_all, k_all, v_all, g_all, s_all, mask_ref, row_ref, col_ref, att_all, dq_all, dkw_all, dvw_all, ds_all
 ):
     j = pl.program_id(1)
     scale = 1.0 / math.sqrt(HEAD_DIM)
     f32 = jnp.float32
     bf16 = jnp.bfloat16
     allowed = mask_ref[0:1, :] > 0
-    row = lax.broadcasted_iota(jnp.int32, (BLOCK, BLOCK), 0)
-    col = lax.broadcasted_iota(jnp.int32, (BLOCK, BLOCK), 1)
-    causal = row >= col
+    causal = row_ref[:, 0:1] >= col_ref[0:1, :]
     for hh in range(q_all.shape[1] // HEAD_DIM):
         cols = pl.ds(hh * HEAD_DIM, HEAD_DIM)
         q = q_all[:, cols]
@@ -189,7 +187,7 @@
             ds_all[:, vcols] += dvs
 
 
-def attention(q, k, v, g, summary, mask):
+def attention(q, k, v, g, summary, mask, row_offset, col_offset):
     rows, half = q.shape
     heads = half // HEAD_DIM
     nb = rows // BLOCK
@@ -203,7 +201,12 @@
     return pl.pallas_call(
         attention_kernel,
         grid=(heads // per_step, nb),
-        in_specs=[tile, tile, tile, tile, pair, pl.BlockSpec((8, count), lambda h, j: (j, 0))],
+        in_specs=[
+            tile, tile, tile, tile, pair,
+            pl.BlockSpec((8, count), lambda h, j: (j, 0)),
+            pl.BlockSpec((BLOCK, BLOCK), lambda h, j: (j, 0)),
+            pl.BlockSpec((8, BLOCK), lambda h, j: (j, 0)),
+        ],
         out_specs=[tile, tile, tile, tile, pair],
         out_shape=[
             jax.ShapeDtypeStruct((rows, half), bf16),
@@ -216,7 +219,7 @@
             flops=flops, transcendentals=rows * heads * (BLOCK + count) * 2,
             bytes_accessed=rows * half * 2 * 8 + count * half * 2 * 6,
         ),
-    )(q, k, v, g, summary, mask)
+    )(q, k, v, g, summary, mask, row_offset, col_offset)
 
 
 def body(queries, key_rows, value_rows, out_grad, summary_columns):
@@ -233,7 +236,13 @@
     pair_count = summary_columns.shape[0] // nb
     first_block = (shard * pair_count + hx) * nb
     cols = lax.dynamic_slice_in_dim(summary_columns, hx * nb, nb, 0)
-    positions = (jnp.arange(nb, dtype=jnp.int32)[:, None] * BLOCK + cols).reshape(-1)
+    true_positions = (jnp.arange(nb, dtype=jnp.int32)[:, None] * BLOCK + cols).reshape(-1)
+    own_rows = queries.shape[0]
+    positions = (true_positions - core * own_rows) % rows
+    true_row = (jnp.arange(rows, dtype=jnp.int32) + core * own_rows) % rows
+    in_block = true_row % BLOCK
+    row_offset = jnp.broadcast_to(in_block[:, None], (rows, BLOCK))
+    col_offset = jnp.repeat(in_block.reshape(nb, BLOCK), 8, axis=0)
 
     own_sum = jnp.stack(
         [
@@ -249,11 +258,11 @@
     if group_bits() >= 2:
         member = jnp.where(core == 1, swap_low_bits(member), member)
     key_block = member * nb + slot % nb
-    query_block = first_block + jnp.arange(nb, dtype=jnp.int32)
+    query_block = first_block + true_row.reshape(nb, BLOCK)[:, 0] // BLOCK
     mask = (key_block[None, :] < query_block[:, None]).astype(jnp.int32)
     mask = jnp.repeat(mask, 8, axis=0)
 
-    attended, dq, dkw, dvw, parts = attention(qb, kb, vb, gb, all_sum, mask)
+    attended, dq, dkw, dvw, parts = attention(qb, kb, vb, gb, all_sum, mask, row_offset, col_offset)
     att_tok, dq_tok = to_token_layout([attended, dq], core)
 
     own_grad = reduce_blocks(parts, core).reshape(-1, heads, 2, HEAD_DIM)

time: 80.2 us -> 83.8 us (1.045)
  local copies, waits for them, and re-layouts: 4.14 us -> 7.29 us
    select_n x5 -> x2, other arithmetic: 2.01 us -> 0.03 us  [the longest x1 0.02 us: body(): in_block = true_row % BLOCK]
    concatenate x0 -> x4, other arithmetic: none -> 1.74 us  [to_block_layout(): out.append(jnp.concatenate([m, r], 0))]
    slice x0 -> x4, local copies, waits for them, and re-layouts: none -> 1.18 us  [to_token_layout(): mine = [a[:rows] for a in arrays]]
where the time goes in v16:
time: 83.8 us; the launch traced here: 83.5 us
  waiting for transfers between devices  34.6 us (41%)
  starting transfers between devices  16.5 us (20%)
  Pallas kernels  12.8 us (15%)
  other arithmetic  10.1 us (12%)
  local copies, waits for them, and re-layouts  7.29 us (9%)
  matrix products  1.11 us (1%)
  between operations  1.11 us (1%)
    ppermute x12, waiting for transfers between devices, exchange(): return lax.ppermute(x, ('seq', 'hx', 'hc'), pairs)  32.4 us
    ppermute x12, starting transfers between devices, exchange(): return lax.ppermute(x, ('seq', 'hx', 'hc'), pairs)  13 us
    pallas_call x1, Pallas kernels, attention(): pl.pallas_call(attention_kernel, grid=(heads // per_step, nb), in_specs=[...  12.8 us
    select_n x4, other arithmetic, to_token_layout(): jnp.where(core == 0, jnp.concatenate([m, r], 1), jnp.concatenate([r, m], 1))  3.66 us
    ppermute x3, starting transfers between devices, swap_with_partner(): return lax.ppermute(x, 'hc', [(0, 1), (1, 0)])  3.51 us
    another operation x2, other arithmetic  2.92 us
    ppermute x3, waiting for transfers between devices, swap_with_partner(): return lax.ppermute(x, 'hc', [(0, 1), (1, 0)])  2.19 us
    concatenate x4, other arithmetic, to_block_layout(): out.append(jnp.concatenate([m, r], 0))  1.74 us
  transfers between devices with their start and end apart: 15, of which 11 were waited for; matrix products, arithmetic and copies ran while one was open for 6% of the time, Pallas kernels for 0%

profile of v16, /device:TPU:1, one launch (start us, length us, event | category | flops | bytes accessed | tf_op | source)
XLA Modules:
  0.0 83.5 jit_solution(13494113962823039775)
XLA Ops:
  0.7 1.3 %constant_dynamic-slice_fusion.3 = (bf16[64,2048]{1,0:T(8,128)(2,1)S(1)}, bf16[64,2048]{1,0:T(8,128)(2,1)S(1)}, bf16[64,2048]{1,0:T(8,128)(2,1)S(1)}, bf16[64,2048]{1,0:T(8,128)(2,1)S(1)}) fusion(bf16[64,4096]{1,0:T(8,128)(2,1)} %param.8, s32[]{:T(128)S(6)} %select_n.113, s32[]{:T(128)S(6)} %select_n.114, bf16[64,4096]{1,0:T(8,128)(2,1)} %param.7), kind=kLoop, calls=%fused_computation.49 | loop fusion | bytes 2097160 | tf_op jit(solution)/shard_map/dynamic_slice | solution.py:104
  2.9 2.2 %collective-permute-done = bf16[64,8192]{1,0:T(8,128)(2,1)S(1)} collective-permute-done((bf16[64,8192]{1,0:T(8,128)(2,1)S(1)}, bf16[64,8192]{1,0:T(8,128)(2,1)S(1)}, u32[]{:S(2)}, u32[]{:S(2)}) %collective-permute-start) | collective-permute-done | bytes 1048608 | tf_op jit(solution)/shard_map/ppermute | solution.py:98
  6.6 4.5 %collective-permute-start.3 = (bf16[1,8,4096]{2,1,0:T(8,128)(2,1)S(1)}, bf16[1,8,4096]{2,1,0:T(8,128)(2,1)S(1)}, u32[]{:S(2)}, u32[]{:S(2)}) collective-permute-start(bf16[1,8,4096]{2,1,0:T(8,128)(2,1)S(1)} %bitcast.85), channel_id=1, source_target_pairs={{0,24},{1,25},{2,26},{3,27},{4,28},{5,29},{6,30},{7,31},{8,16},{9,... | collective-permute-start | bytes 196616 | tf_op jit(solution)/shard_map/ppermute | solution.py:47
  11.5 1.8 %collective-permute-done.3 = bf16[1,8,4096]{2,1,0:T(8,128)(2,1)S(1)} collective-permute-done((bf16[1,8,4096]{2,1,0:T(8,128)(2,1)S(1)}, bf16[1,8,4096]{2,1,0:T(8,128)(2,1)S(1)}, u32[]{:S(2)}, u32[]{:S(2)}) %collective-permute-start.3) | collective-permute-done | bytes 65568 | tf_op jit(solution)/shard_map/ppermute | solution.py:47
  13.3 3.5 %collective-permute-done.2 = bf16[1,8,4096]{2,1,0:T(8,128)(2,1)S(1)} collective-permute-done((bf16[1,8,4096]{2,1,0:T(8,128)(2,1)S(1)}, bf16[1,8,4096]{2,1,0:T(8,128)(2,1)S(1)}, u32[]{:S(2)}, u32[]{:S(2)}) %collective-permute-start.2) | collective-permute-done | bytes 65568 | tf_op jit(solution)/shard_map/ppermute | solution.py:47
  16.9 2.2 %collective-permute-start.6 = (bf16[4,8,4096]{2,1,0:T(8,128)(2,1)S(1)}, bf16[4,8,4096]{2,1,0:T(8,128)(2,1)S(1)}, u32[]{:S(2)}, u32[]{:S(2)}) collective-permute-start(bf16[4,8,4096]{2,1,0:T(8,128)(2,1)S(1)} %get-tuple-element.50), channel_id=1, source_target_pairs={{0,6},{1,7},{2,4},{3,5},{4,2},{5,3},{6,0},{7,1},{8,14},{9,15},{10,... | collective-permute-start | bytes 786440 | tf_op jit(solution)/shard_map/ppermute | solution.py:47
  21.2 3.6 %collective-permute-done.6 = bf16[4,8,4096]{2,1,0:T(8,128)(2,1)S(1)} collective-permute-done((bf16[4,8,4096]{2,1,0:T(8,128)(2,1)S(1)}, bf16[4,8,4096]{2,1,0:T(8,128)(2,1)S(1)}, u32[]{:S(2)}, u32[]{:S(2)}) %collective-permute-start.6) | collective-permute-done | bytes 262176 | tf_op jit(solution)/shard_map/ppermute | solution.py:47
  24.9 5.7 %collective-permute-done.5 = bf16[4,8,4096]{2,1,0:T(8,128)(2,1)S(1)} collective-permute-done((bf16[4,8,4096]{2,1,0:T(8,128)(2,1)S(1)}, bf16[4,8,4096]{2,1,0:T(8,128)(2,1)S(1)}, u32[]{:S(2)}, u32[]{:S(2)}) %collective-permute-start.5) | collective-permute-done | bytes 262176 | tf_op jit(solution)/shard_map/ppermute | solution.py:47
  30.5 1.1 %collective-permute-done.4 = bf16[4,8,4096]{2,1,0:T(8,128)(2,1)S(1)} collective-permute-done((bf16[4,8,4096]{2,1,0:T(8,128)(2,1)S(1)}, bf16[4,8,4096]{2,1,0:T(8,128)(2,1)S(1)}, u32[]{:S(2)}, u32[]{:S(2)}) %collective-permute-start.4) | collective-permute-done | bytes 262176 | tf_op jit(solution)/shard_map/ppermute | solution.py:47
  31.7 1.1 %pad_maximum_fusion.1 = bf16[4,4,8,4096]{3,2,1,0:T(8,128)(2,1)} fusion(bf16[4,1,8,4096]{3,2,1,0:T(8,128)(2,1)S(1)} %bitcast.89, bf16[4,1,8,4096]{3,2,1,0:T(8,128)(2,1)S(1)} %bitcast.90, bf16[4,1,8,4096]{3,2,1,0:T(8,128)(2,1)S(1)} %bitcast.91, bf16[4,1,8,4096]{3,2,1,0:T(8,128)(2,1)S(1)} %get-tuple-element.49), kind=kLoop, calls=%fused_computation.3 | loop fusion | flops 1572864 | bytes 2097152 | tf_op jit(solution)/shard_map/stack | solution.py:79
  34.7 12.8 %shard_map.84 = (bf16[128,2048]{1,0:T(8,128)(2,1)}, bf16[128,2048]{1,0:T(8,128)(2,1)}, f32[128,2048]{1,0:T(8,128)}, f32[128,2048]{1,0:T(8,128)}, f32[128,4096]{1,0:T(8,128)}) custom-call(bf16[128,2048]{1,0:T(8,128)(2,1)} %pad_maximum_fusion.2.q_all, bf16[128,2048]{1,0:T(8,128)(2,1)} %copy-done.1, bf16[128,2048]{1,0:T(8,128)(2,1)} %copy-done, ...), custom_call_target="tpu_custom_call" | custom-call | flops 805306368 | bytes 7340032 | tf_op jit(solution)/shard_map/pallas_call | solution.py:201
  47.5 1.1 %fusion.29 = (bf16[64,2048]{1,0:T(8,128)(2,1)S(1)}, bf16[64,2048]{1,0:T(8,128)(2,1)S(1)}) fusion(bf16[128,2048]{1,0:T(8,128)(2,1)} %get-tuple-element.10), kind=kLoop, calls=%fused_computation.92 | loop fusion | bytes 1048576 | tf_op jit(solution)/shard_map/slice | solution.py:117
  48.6 1.8 %convert.10 = bf16[4,4,8,4096]{3,2,1,0:T(8,128)(2,1)S(1)} convert(f32[4,4,8,4096]{3,2,1,0:T(8,128)} %bitcast.81) | non-fusion elementwise | flops 524288 | bytes 3145728 | tf_op jit(solution)/shard_map/convert.5
  50.4 1.3 %collective-permute-start.8 = (bf16[4,8,4096]{2,1,0:T(8,128)(2,1)S(1)}, bf16[4,8,4096]{2,1,0:T(8,128)(2,1)S(1)}, u32[]{:S(2)}, u32[]{:S(2)}) collective-permute-start(bf16[4,8,4096]{2,1,0:T(8,128)(2,1)S(1)} %get-tuple-element.19), channel_id=1, source_target_pairs={{0,2},{1,5},{2,0},{3,7},{4,6},{5,1},{6,4},{7,3},{8,10},{9,13},{10,... | collective-permute-start | bytes 786440 | tf_op jit(solution)/shard_map/ppermute | solution.py:47
  51.7 1.2 %collective-permute-start.10 = (bf16[4,8,4096]{2,1,0:T(8,128)(2,1)S(1)}, bf16[4,8,4096]{2,1,0:T(8,128)(2,1)S(1)}, u32[]{:S(2)}, u32[]{:S(2)}) collective-permute-start(bf16[4,8,4096]{2,1,0:T(8,128)(2,1)S(1)} %get-tuple-element.20), channel_id=1, source_target_pairs={{0,6},{1,7},{2,4},{3,5},{4,2},{5,3},{6,0},{7,1},{8,14},{9,15},{10,... | collective-permute-start | bytes 786440 | tf_op jit(solution)/shard_map/ppermute | solution.py:47
  53.2 4.4 %collective-permute-done.8 = bf16[4,8,4096]{2,1,0:T(8,128)(2,1)S(1)} collective-permute-done((bf16[4,8,4096]{2,1,0:T(8,128)(2,1)S(1)}, bf16[4,8,4096]{2,1,0:T(8,128)(2,1)S(1)}, u32[]{:S(2)}, u32[]{:S(2)}) %collective-permute-start.8) | collective-permute-done | bytes 262176 | tf_op jit(solution)/shard_map/ppermute | solution.py:47
  57.5 3.4 %collective-permute-done.10 = bf16[4,8,4096]{2,1,0:T(8,128)(2,1)S(1)} collective-permute-done((bf16[4,8,4096]{2,1,0:T(8,128)(2,1)S(1)}, bf16[4,8,4096]{2,1,0:T(8,128)(2,1)S(1)}, u32[]{:S(2)}, u32[]{:S(2)}) %collective-permute-start.10) | collective-permute-done | bytes 262176 | tf_op jit(solution)/shard_map/ppermute | solution.py:47
  60.9 4.5 %collective-permute-done.9 = bf16[4,8,4096]{2,1,0:T(8,128)(2,1)S(1)} collective-permute-done((bf16[4,8,4096]{2,1,0:T(8,128)(2,1)S(1)}, bf16[4,8,4096]{2,1,0:T(8,128)(2,1)S(1)}, u32[]{:S(2)}, u32[]{:S(2)}) %collective-permute-start.9) | collective-permute-done | bytes 262176 | tf_op jit(solution)/shard_map/ppermute | solution.py:47
  65.5 1.2 %fusion.21 = (bf16[1,4,8,4096]{3,2,1,0:T(8,128)(2,1)S(1)}, f32[1,4,8,4096]{3,2,1,0:T(8,128)S(1)}) fusion(bf16[4,8,4096]{2,1,0:T(8,128)(2,1)S(1)} %collective-permute-done.10, bf16[4,8,4096]{2,1,0:T(8,128)(2,1)S(1)} %collective-permute-done.9, bf16[4,8,4096]{2,1,0:T(8,128)(2,1)S(1)} %collective-permute-done.8, f32[4,4,8,4096]{3,2,1,0:T(8,128)} %bitcast.82), kind=kLoop, calls=%fused_computation.85 | loop fusion | flops 917504 | bytes 2097152 | tf_op jit(solution)/shard_map/convert.2
  66.9 1.8 %collective-permute-start.13 = (bf16[1,8,4096]{2,1,0:T(8,128)(2,1)S(1)}, bf16[1,8,4096]{2,1,0:T(8,128)(2,1)S(1)}, u32[]{:S(2)}, u32[]{:S(2)}) collective-permute-start(bf16[1,8,4096]{2,1,0:T(8,128)(2,1)S(1)} %get-tuple-element.47), channel_id=1, source_target_pairs={{0,24},{1,25},{2,26},{3,27},{4,28},{5,29},{6,30},{7,31},{8,16},{9,... | collective-permute-start | bytes 196616 | tf_op jit(solution)/shard_map/ppermute | solution.py:47
  69.4 1.9 %collective-permute-start.7 = (bf16[64,4096]{1,0:T(8,128)(2,1)S(1)}, bf16[64,4096]{1,0:T(8,128)(2,1)S(1)}, u32[]{:S(2)}, u32[]{:S(2)}) collective-permute-start(bf16[64,4096]{1,0:T(8,128)(2,1)S(1)} %pad_maximum_fusion.6), channel_id=1, source_target_pairs={{0,1},{1,0},{2,3},{3,2},{4,5},{5,4},{6,7},{7,6},{8,9},{9,8},{10,11... | collective-permute-start | bytes 1572872 | tf_op jit(solution)/shard_map/ppermute | solution.py:98
  72.2 3.5 %collective-permute-done.12 = bf16[1,8,4096]{2,1,0:T(8,128)(2,1)S(1)} collective-permute-done((bf16[1,8,4096]{2,1,0:T(8,128)(2,1)S(1)}, bf16[1,8,4096]{2,1,0:T(8,128)(2,1)S(1)}, u32[]{:S(2)}, u32[]{:S(2)}) %collective-permute-start.12) | collective-permute-done | bytes 65568 | tf_op jit(solution)/shard_map/ppermute | solution.py:47
  77.0 1.0 %copy-done.2 = f32[128,2048]{1,0:T(8,128)S(1)} copy-done((f32[128,2048]{1,0:T(8,128)S(1)}, f32[128,2048]{1,0:T(8,128)}, u32[]{:S(2)}) %copy-start.2) | copy-done | bytes 1048600
  78.2 1.5 %collective-permute-start.14 = (bf16[64,4096]{1,0:T(8,128)(2,1)S(1)}, bf16[64,4096]{1,0:T(8,128)(2,1)S(1)}, u32[]{:S(2)}, u32[]{:S(2)}) collective-permute-start(bf16[64,4096]{1,0:T(8,128)(2,1)S(1)} %pad_maximum_fusion.7), channel_id=1, source_target_pairs={{0,1},{1,0},{2,3},{3,2},{4,5},{5,4},{6,7},{7,6},{8,9},{9,8},{10,11... | collective-permute-start | bytes 1572872 | tf_op jit(solution)/shard_map/ppermute | solution.py:98
  (68 shorter events, 13.9 us)
Async XLA Ops:
  0.6 1.4 %copy-start.5 = (bf16[64,4096]{1,0:T(8,128)(2,1)S(1)}, bf16[64,4096]{1,0:T(8,128)(2,1)}, u32[]{:S(2)}) copy-start(bf16[64,4096]{1,0:T(8,128)(2,1)} %param.10) | copy-start | bytes 1572868
  0.6 1.5 %copy-start.6 = (bf16[64,4096]{1,0:T(8,128)(2,1)S(1)}, bf16[64,4096]{1,0:T(8,128)(2,1)}, u32[]{:S(2)}) copy-start(bf16[64,4096]{1,0:T(8,128)(2,1)} %param.9) | copy-start | bytes 1572868
  2.1 0.7 copy-start.7
  2.3 2.7 %collective-permute-start = (bf16[64,8192]{1,0:T(8,128)(2,1)S(1)}, bf16[64,8192]{1,0:T(8,128)(2,1)S(1)}, u32[]{:S(2)}, u32[]{:S(2)}) collective-permute-start(bf16[64,8192]{1,0:T(8,128)(2,1)S(1)} %pad_maximum_fusion), channel_id=1, source_target_pairs={{0,1},{1,0},{2,3},{3,2},{4,5},{5,4},{6,7},{7,6},{8,9},{9,8},{10,11... | collective-permute-start | bytes 3145736 | tf_op jit(solution)/shard_map/ppermute | solution.py:98
  5.2 16.0 %copy-start = (bf16[128,2048]{1,0:T(8,128)(2,1)}, bf16[128,2048]{1,0:T(8,128)(2,1)S(1)}, u32[]{:S(2)}) copy-start(bf16[128,2048]{1,0:T(8,128)(2,1)S(1)} %pad_maximum_fusion.4.v_all) | copy-start | bytes 1572868
  5.9 26.9 %copy-start.1 = (bf16[128,2048]{1,0:T(8,128)(2,1)}, bf16[128,2048]{1,0:T(8,128)(2,1)S(1)}, u32[]{:S(2)}) copy-start(bf16[128,2048]{1,0:T(8,128)(2,1)S(1)} %pad_maximum_fusion.3.k_all) | copy-start | bytes 1572868
  6.6 6.7 %collective-permute-start.3 = (bf16[1,8,4096]{2,1,0:T(8,128)(2,1)S(1)}, bf16[1,8,4096]{2,1,0:T(8,128)(2,1)S(1)}, u32[]{:S(2)}, u32[]{:S(2)}) collective-permute-start(bf16[1,8,4096]{2,1,0:T(8,128)(2,1)S(1)} %bitcast.85), channel_id=1, source_target_pairs={{0,24},{1,25},{2,26},{3,27},{4,28},{5,29},{6,30},{7,31},{8,16},{9,... | collective-permute-start | bytes 196616 | tf_op jit(solution)/shard_map/ppermute | solution.py:47
  11.1 5.7 %collective-permute-start.2 = (bf16[1,8,4096]{2,1,0:T(8,128)(2,1)S(1)}, bf16[1,8,4096]{2,1,0:T(8,128)(2,1)S(1)}, u32[]{:S(2)}, u32[]{:S(2)}) collective-permute-start(bf16[1,8,4096]{2,1,0:T(8,128)(2,1)S(1)} %bitcast.86), channel_id=1, source_target_pairs={{0,16},{1,17},{2,18},{3,19},{4,20},{5,21},{6,22},{7,23},{8,24},{9,... | collective-permute-start | bytes 196616 | tf_op jit(solution)/shard_map/ppermute | solution.py:47
  11.1 5.7 %collective-permute-start.1 = (bf16[1,8,4096]{2,1,0:T(8,128)(2,1)S(1)}, bf16[1,8,4096]{2,1,0:T(8,128)(2,1)S(1)}, u32[]{:S(2)}, u32[]{:S(2)}) collective-permute-start(bf16[1,8,4096]{2,1,0:T(8,128)(2,1)S(1)} %bitcast.87), channel_id=1, source_target_pairs={{0,8},{1,9},{2,10},{3,11},{4,12},{5,13},{6,14},{7,15},{8,0},{9,1},... | collective-permute-start | bytes 196616 | tf_op jit(solution)/shard_map/ppermute | solution.py:47
  16.9 8.0 %collective-permute-start.6 = (bf16[4,8,4096]{2,1,0:T(8,128)(2,1)S(1)}, bf16[4,8,4096]{2,1,0:T(8,128)(2,1)S(1)}, u32[]{:S(2)}, u32[]{:S(2)}) collective-permute-start(bf16[4,8,4096]{2,1,0:T(8,128)(2,1)S(1)} %get-tuple-element.50), channel_id=1, source_target_pairs={{0,6},{1,7},{2,4},{3,5},{4,2},{5,3},{6,0},{7,1},{8,14},{9,15},{10,... | collective-permute-start | bytes 786440 | tf_op jit(solution)/shard_map/ppermute | solution.py:47
  19.1 11.4 %collective-permute-start.5 = (bf16[4,8,4096]{2,1,0:T(8,128)(2,1)S(1)}, bf16[4,8,4096]{2,1,0:T(8,128)(2,1)S(1)}, u32[]{:S(2)}, u32[]{:S(2)}) collective-permute-start(bf16[4,8,4096]{2,1,0:T(8,128)(2,1)S(1)} %get-tuple-element.50), channel_id=1, source_target_pairs={{0,4},{1,3},{2,6},{3,1},{4,0},{5,7},{6,2},{7,5},{8,12},{9,11},{10,... | collective-permute-start | bytes 786440 | tf_op jit(solution)/shard_map/ppermute | solution.py:47
  19.3 12.3 %collective-permute-start.4 = (bf16[4,8,4096]{2,1,0:T(8,128)(2,1)S(1)}, bf16[4,8,4096]{2,1,0:T(8,128)(2,1)S(1)}, u32[]{:S(2)}, u32[]{:S(2)}) collective-permute-start(bf16[4,8,4096]{2,1,0:T(8,128)(2,1)S(1)} %get-tuple-element.50), channel_id=1, source_target_pairs={{0,2},{1,5},{2,0},{3,7},{4,6},{5,1},{6,4},{7,3},{8,10},{9,13},{10,... | collective-permute-start | bytes 786440 | tf_op jit(solution)/shard_map/ppermute | solution.py:47
  48.5 4.6 %copy-start.4 = (bf16[128,2048]{1,0:T(8,128)(2,1)S(1)}, bf16[128,2048]{1,0:T(8,128)(2,1)}, u32[]{:S(2)}) copy-start(bf16[128,2048]{1,0:T(8,128)(2,1)} %get-tuple-element.11) | copy-start | bytes 1572868
  50.4 7.1 %collective-permute-start.8 = (bf16[4,8,4096]{2,1,0:T(8,128)(2,1)S(1)}, bf16[4,8,4096]{2,1,0:T(8,128)(2,1)S(1)}, u32[]{:S(2)}, u32[]{:S(2)}) collective-permute-start(bf16[4,8,4096]{2,1,0:T(8,128)(2,1)S(1)} %get-tuple-element.19), channel_id=1, source_target_pairs={{0,2},{1,5},{2,0},{3,7},{4,6},{5,1},{6,4},{7,3},{8,10},{9,13},{10,... | collective-permute-start | bytes 786440 | tf_op jit(solution)/shard_map/ppermute | solution.py:47
  51.7 9.2 %collective-permute-start.10 = (bf16[4,8,4096]{2,1,0:T(8,128)(2,1)S(1)}, bf16[4,8,4096]{2,1,0:T(8,128)(2,1)S(1)}, u32[]{:S(2)}, u32[]{:S(2)}) collective-permute-start(bf16[4,8,4096]{2,1,0:T(8,128)(2,1)S(1)} %get-tuple-element.20), channel_id=1, source_target_pairs={{0,6},{1,7},{2,4},{3,5},{4,2},{5,3},{6,0},{7,1},{8,14},{9,15},{10,... | collective-permute-start | bytes 786440 | tf_op jit(solution)/shard_map/ppermute | solution.py:47
  52.9 12.5 %collective-permute-start.9 = (bf16[4,8,4096]{2,1,0:T(8,128)(2,1)S(1)}, bf16[4,8,4096]{2,1,0:T(8,128)(2,1)S(1)}, u32[]{:S(2)}, u32[]{:S(2)}) collective-permute-start(bf16[4,8,4096]{2,1,0:T(8,128)(2,1)S(1)} %get-tuple-element.21), channel_id=1, source_target_pairs={{0,4},{1,3},{2,6},{3,1},{4,0},{5,7},{6,2},{7,5},{8,12},{9,11},{10,... | collective-permute-start | bytes 786440 | tf_op jit(solution)/shard_map/ppermute | solution.py:47
  66.6 10.2 %copy-start.3 = (f32[128,2048]{1,0:T(8,128)S(1)}, f32[128,2048]{1,0:T(8,128)}, u32[]{:S(2)}) copy-start(f32[128,2048]{1,0:T(8,128)} %get-tuple-element.14) | copy-start | bytes 3145732
  66.7 4.7 %collective-permute-start.11 = (bf16[1,8,4096]{2,1,0:T(8,128)(2,1)S(1)}, bf16[1,8,4096]{2,1,0:T(8,128)(2,1)S(1)}, u32[]{:S(2)}, u32[]{:S(2)}) collective-permute-start(bf16[1,8,4096]{2,1,0:T(8,128)(2,1)S(1)} %get-tuple-element.46), channel_id=1, source_target_pairs={{0,8},{1,9},{2,10},{3,11},{4,12},{5,13},{6,14},{7,15},{8,0},{9,1},... | collective-permute-start | bytes 196616 | tf_op jit(solution)/shard_map/ppermute | solution.py:47
  66.9 5.3 %collective-permute-start.13 = (bf16[1,8,4096]{2,1,0:T(8,128)(2,1)S(1)}, bf16[1,8,4096]{2,1,0:T(8,128)(2,1)S(1)}, u32[]{:S(2)}, u32[]{:S(2)}) collective-permute-start(bf16[1,8,4096]{2,1,0:T(8,128)(2,1)S(1)} %get-tuple-element.47), channel_id=1, source_target_pairs={{0,24},{1,25},{2,26},{3,27},{4,28},{5,29},{6,30},{7,31},{8,16},{9,... | collective-permute-start | bytes 196616 | tf_op jit(solution)/shard_map/ppermute | solution.py:47
  68.7 7.0 %collective-permute-start.12 = (bf16[1,8,4096]{2,1,0:T(8,128)(2,1)S(1)}, bf16[1,8,4096]{2,1,0:T(8,128)(2,1)S(1)}, u32[]{:S(2)}, u32[]{:S(2)}) collective-permute-start(bf16[1,8,4096]{2,1,0:T(8,128)(2,1)S(1)} %get-tuple-element.48), channel_id=1, source_target_pairs={{0,16},{1,17},{2,18},{3,19},{4,20},{5,21},{6,22},{7,23},{8,24},{9,... | collective-permute-start | bytes 196616 | tf_op jit(solution)/shard_map/ppermute | solution.py:47
  69.4 10.3 %collective-permute-start.7 = (bf16[64,4096]{1,0:T(8,128)(2,1)S(1)}, bf16[64,4096]{1,0:T(8,128)(2,1)S(1)}, u32[]{:S(2)}, u32[]{:S(2)}) collective-permute-start(bf16[64,4096]{1,0:T(8,128)(2,1)S(1)} %pad_maximum_fusion.6), channel_id=1, source_target_pairs={{0,1},{1,0},{2,3},{3,2},{4,5},{5,4},{6,7},{7,6},{8,9},{9,8},{10,11... | collective-permute-start | bytes 1572872 | tf_op jit(solution)/shard_map/ppermute | solution.py:98
  76.8 1.2 %copy-start.2 = (f32[128,2048]{1,0:T(8,128)S(1)}, f32[128,2048]{1,0:T(8,128)}, u32[]{:S(2)}) copy-start(f32[128,2048]{1,0:T(8,128)} %get-tuple-element.12) | copy-start | bytes 3145732
  78.2 3.3 %collective-permute-start.14 = (bf16[64,4096]{1,0:T(8,128)(2,1)S(1)}, bf16[64,4096]{1,0:T(8,128)(2,1)S(1)}, u32[]{:S(2)}, u32[]{:S(2)}) collective-permute-start(bf16[64,4096]{1,0:T(8,128)(2,1)S(1)} %pad_maximum_fusion.7), channel_id=1, source_target_pairs={{0,1},{1,0},{2,3},{3,2},{4,5},{5,4},{6,7},{7,6},{8,9},{9,8},{10,11... | collective-permute-start | bytes 1572872 | tf_op jit(solution)/shard_map/ppermute | solution.py:98

commit v17 on v15

--- a/solution.py
+++ b/solution.py
@@ -235,10 +235,15 @@
     cols = lax.dynamic_slice_in_dim(summary_columns, hx * nb, nb, 0)
     positions = (jnp.arange(nb, dtype=jnp.int32)[:, None] * BLOCK + cols).reshape(-1)
 
+    chosen = (positions[:, None] == jnp.arange(rows, dtype=jnp.int32)[None, :]).astype(jnp.bfloat16)
+
+    def pick(x):
+        return jnp.dot(chosen, x, preferred_element_type=jnp.float32).astype(jnp.bfloat16)
+
     own_sum = jnp.stack(
         [
-            jnp.take(kb, positions, axis=0).reshape(-1, heads, HEAD_DIM),
-            jnp.take(vb, positions, axis=0).reshape(-1, heads, HEAD_DIM),
+            pick(kb).reshape(-1, heads, HEAD_DIM),
+            pick(vb).reshape(-1, heads, HEAD_DIM),
         ],
         axis=2,
     ).reshape(-1, 2 * half)

time: 80.2 us -> 79.5 us (level)
  local copies, waits for them, and re-layouts: 4.14 us -> 2.65 us
    gather x2 -> x0, local copies, waits for them, and re-layouts: 1.15 us -> none  [the longest x1 0.58 us: body(): jnp.take(vb, positions, axis=0).reshape(-1, heads, HEAD_DIM)]
    another operation x4 -> x3, other arithmetic: 3.01 us -> 2.94 us
where the time goes in v17:
time: 79.5 us; the launch traced here: 79.2 us
  waiting for transfers between devices  34.8 us (44%)
  starting transfers between devices  16.5 us (21%)
  Pallas kernels  12.8 us (16%)
  other arithmetic  9.97 us (13%)
  local copies, waits for them, and re-layouts  2.65 us (3%)
  matrix products  1.56 us (2%)
  between operations  0.92 us (1%)
    ppermute x12, waiting for transfers between devices, exchange(): return lax.ppermute(x, ('seq', 'hx', 'hc'), pairs)  32.2 us
    ppermute x12, starting transfers between devices, exchange(): return lax.ppermute(x, ('seq', 'hx', 'hc'), pairs)  13 us
    pallas_call x1, Pallas kernels, attention(): pl.pallas_call(attention_kernel, grid=(heads // per_step, nb), in_specs=[...  12.8 us
    select_n x4, other arithmetic, to_token_layout(): jnp.where(core == 0, jnp.concatenate([m, r], 1), jnp.concatenate([r, m], 1))  3.66 us
    ppermute x3, starting transfers between devices, swap_with_partner(): return lax.ppermute(x, 'hc', [(0, 1), (1, 0)])  3.51 us
    another operation x2, other arithmetic  2.92 us
    ppermute x3, waiting for transfers between devices, swap_with_partner(): return lax.ppermute(x, 'hc', [(0, 1), (1, 0)])  2.6 us
    select_n x4, other arithmetic, to_block_layout(): jnp.where(core == 0, jnp.concatenate([m, r], 0), jnp.concatenate([r, m], 0))  2.02 us
  transfers between devices with their start and end apart: 15, of which 11 were waited for; matrix products, arithmetic and copies ran while one was open for 6% of the time, Pallas kernels for 0%

profile of v17, /device:TPU:1, one launch (start us, length us, event | category | flops | bytes accessed | tf_op | source)
XLA Modules:
  0.0 79.2 jit_solution(3798000576234912995)
XLA Ops:
  0.7 1.3 %constant_dynamic-slice_fusion.11 = (bf16[64,2048]{1,0:T(8,128)(2,1)S(1)}, bf16[64,2048]{1,0:T(8,128)(2,1)S(1)}, bf16[64,2048]{1,0:T(8,128)(2,1)S(1)}, bf16[64,2048]{1,0:T(8,128)(2,1)S(1)}) fusion(bf16[64,4096]{1,0:T(8,128)(2,1)} %param.6, s32[]{:T(128)S(6)} %select_n.100, s32[]{:T(128)S(6)} %select_n.101, bf16[64,4096]{1,0:T(8,128)(2,1)} %param.5), kind=kLoop, calls=%fused_computation.55 | loop fusion | bytes 2097160 | tf_op jit(solution)/shard_map/dynamic_slice | solution.py:104
  2.5 2.6 %collective-permute-done = bf16[64,8192]{1,0:T(8,128)(2,1)S(1)} collective-permute-done((bf16[64,8192]{1,0:T(8,128)(2,1)S(1)}, bf16[64,8192]{1,0:T(8,128)(2,1)S(1)}, u32[]{:S(2)}, u32[]{:S(2)}) %collective-permute-start) | collective-permute-done | bytes 1048608 | tf_op jit(solution)/shard_map/ppermute | solution.py:98
  5.9 4.5 %collective-permute-start.3 = (bf16[1,8,4096]{2,1,0:T(8,128)(2,1)S(1)}, bf16[1,8,4096]{2,1,0:T(8,128)(2,1)S(1)}, u32[]{:S(2)}, u32[]{:S(2)}) collective-permute-start(bf16[1,8,4096]{2,1,0:T(8,128)(2,1)S(1)} %bitcast.80), channel_id=1, source_target_pairs={{0,24},{1,25},{2,26},{3,27},{4,28},{5,29},{6,30},{7,31},{8,16},{9,... | collective-permute-start | bytes 196616 | tf_op jit(solution)/shard_map/ppermute | solution.py:47
  10.8 1.8 %collective-permute-done.3 = bf16[1,8,4096]{2,1,0:T(8,128)(2,1)S(1)} collective-permute-done((bf16[1,8,4096]{2,1,0:T(8,128)(2,1)S(1)}, bf16[1,8,4096]{2,1,0:T(8,128)(2,1)S(1)}, u32[]{:S(2)}, u32[]{:S(2)}) %collective-permute-start.3) | collective-permute-done | bytes 65568 | tf_op jit(solution)/shard_map/ppermute | solution.py:47
  12.6 3.5 %collective-permute-done.2 = bf16[1,8,4096]{2,1,0:T(8,128)(2,1)S(1)} collective-permute-done((bf16[1,8,4096]{2,1,0:T(8,128)(2,1)S(1)}, bf16[1,8,4096]{2,1,0:T(8,128)(2,1)S(1)}, u32[]{:S(2)}, u32[]{:S(2)}) %collective-permute-start.2) | collective-permute-done | bytes 65568 | tf_op jit(solution)/shard_map/ppermute | solution.py:47
  16.2 2.2 %collective-permute-start.6 = (bf16[4,8,4096]{2,1,0:T(8,128)(2,1)S(1)}, bf16[4,8,4096]{2,1,0:T(8,128)(2,1)S(1)}, u32[]{:S(2)}, u32[]{:S(2)}) collective-permute-start(bf16[4,8,4096]{2,1,0:T(8,128)(2,1)S(1)} %get-tuple-element.47), channel_id=1, source_target_pairs={{0,6},{1,7},{2,4},{3,5},{4,2},{5,3},{6,0},{7,1},{8,14},{9,15},{10,... | collective-permute-start | bytes 786440 | tf_op jit(solution)/shard_map/ppermute | solution.py:47
  20.7 3.5 %collective-permute-done.6 = bf16[4,8,4096]{2,1,0:T(8,128)(2,1)S(1)} collective-permute-done((bf16[4,8,4096]{2,1,0:T(8,128)(2,1)S(1)}, bf16[4,8,4096]{2,1,0:T(8,128)(2,1)S(1)}, u32[]{:S(2)}, u32[]{:S(2)}) %collective-permute-start.6) | collective-permute-done | bytes 262176 | tf_op jit(solution)/shard_map/ppermute | solution.py:47
  24.2 5.7 %collective-permute-done.5 = bf16[4,8,4096]{2,1,0:T(8,128)(2,1)S(1)} collective-permute-done((bf16[4,8,4096]{2,1,0:T(8,128)(2,1)S(1)}, bf16[4,8,4096]{2,1,0:T(8,128)(2,1)S(1)}, u32[]{:S(2)}, u32[]{:S(2)}) %collective-permute-start.5) | collective-permute-done | bytes 262176 | tf_op jit(solution)/shard_map/ppermute | solution.py:47
  29.9 1.1 %collective-permute-done.4 = bf16[4,8,4096]{2,1,0:T(8,128)(2,1)S(1)} collective-permute-done((bf16[4,8,4096]{2,1,0:T(8,128)(2,1)S(1)}, bf16[4,8,4096]{2,1,0:T(8,128)(2,1)S(1)}, u32[]{:S(2)}, u32[]{:S(2)}) %collective-permute-start.4) | collective-permute-done | bytes 262176 | tf_op jit(solution)/shard_map/ppermute | solution.py:47
  31.0 1.1 %pad_maximum_fusion.1 = bf16[4,4,8,4096]{3,2,1,0:T(8,128)(2,1)} fusion(bf16[4,1,8,4096]{3,2,1,0:T(8,128)(2,1)S(1)} %bitcast.84, bf16[4,1,8,4096]{3,2,1,0:T(8,128)(2,1)S(1)} %bitcast.85, bf16[4,1,8,4096]{3,2,1,0:T(8,128)(2,1)S(1)} %bitcast.86, bf16[4,1,8,4096]{3,2,1,0:T(8,128)(2,1)S(1)} %get-tuple-element.46), kind=kLoop, calls=%fused_computation.9 | loop fusion | flops 1572864 | bytes 2097152 | tf_op jit(solution)/shard_map/stack | solution.py:79
  32.8 12.8 %shard_map.84 = (bf16[128,2048]{1,0:T(8,128)(2,1)}, bf16[128,2048]{1,0:T(8,128)(2,1)}, f32[128,2048]{1,0:T(8,128)}, f32[128,2048]{1,0:T(8,128)}, f32[128,4096]{1,0:T(8,128)}) custom-call(bf16[128,2048]{1,0:T(8,128)(2,1)} %maximum_select_fusion.q_all, bf16[128,2048]{1,0:T(8,128)(2,1)} %copy-done.2, bf16[128,2048]{1,0:T(8,128)(2,1)} %copy-done.1, ...), custom_call_target="tpu_custom_call" | custom-call | flops 805306368 | bytes 7340032 | tf_op jit(solution)/shard_map/pallas_call | solution.py:203
  45.6 1.8 %convert.10 = bf16[4,4,8,4096]{3,2,1,0:T(8,128)(2,1)S(1)} convert(f32[4,4,8,4096]{3,2,1,0:T(8,128)} %bitcast.76) | non-fusion elementwise | flops 524288 | bytes 3145728 | tf_op jit(solution)/shard_map/convert.5
  47.4 1.3 %collective-permute-start.8 = (bf16[4,8,4096]{2,1,0:T(8,128)(2,1)S(1)}, bf16[4,8,4096]{2,1,0:T(8,128)(2,1)S(1)}, u32[]{:S(2)}, u32[]{:S(2)}) collective-permute-start(bf16[4,8,4096]{2,1,0:T(8,128)(2,1)S(1)} %get-tuple-element.16), channel_id=1, source_target_pairs={{0,2},{1,5},{2,0},{3,7},{4,6},{5,1},{6,4},{7,3},{8,10},{9,13},{10,... | collective-permute-start | bytes 786440 | tf_op jit(solution)/shard_map/ppermute | solution.py:47
  48.7 1.2 %collective-permute-start.10 = (bf16[4,8,4096]{2,1,0:T(8,128)(2,1)S(1)}, bf16[4,8,4096]{2,1,0:T(8,128)(2,1)S(1)}, u32[]{:S(2)}, u32[]{:S(2)}) collective-permute-start(bf16[4,8,4096]{2,1,0:T(8,128)(2,1)S(1)} %get-tuple-element.17), channel_id=1, source_target_pairs={{0,6},{1,7},{2,4},{3,5},{4,2},{5,3},{6,0},{7,1},{8,14},{9,15},{10,... | collective-permute-start | bytes 786440 | tf_op jit(solution)/shard_map/ppermute | solution.py:47
  50.3 4.3 %collective-permute-done.8 = bf16[4,8,4096]{2,1,0:T(8,128)(2,1)S(1)} collective-permute-done((bf16[4,8,4096]{2,1,0:T(8,128)(2,1)S(1)}, bf16[4,8,4096]{2,1,0:T(8,128)(2,1)S(1)}, u32[]{:S(2)}, u32[]{:S(2)}) %collective-permute-start.8) | collective-permute-done | bytes 262176 | tf_op jit(solution)/shard_map/ppermute | solution.py:47
  54.6 3.4 %collective-permute-done.10 = bf16[4,8,4096]{2,1,0:T(8,128)(2,1)S(1)} collective-permute-done((bf16[4,8,4096]{2,1,0:T(8,128)(2,1)S(1)}, bf16[4,8,4096]{2,1,0:T(8,128)(2,1)S(1)}, u32[]{:S(2)}, u32[]{:S(2)}) %collective-permute-start.10) | collective-permute-done | bytes 262176 | tf_op jit(solution)/shard_map/ppermute | solution.py:47
  58.0 4.5 %collective-permute-done.9 = bf16[4,8,4096]{2,1,0:T(8,128)(2,1)S(1)} collective-permute-done((bf16[4,8,4096]{2,1,0:T(8,128)(2,1)S(1)}, bf16[4,8,4096]{2,1,0:T(8,128)(2,1)S(1)}, u32[]{:S(2)}, u32[]{:S(2)}) %collective-permute-start.9) | collective-permute-done | bytes 262176 | tf_op jit(solution)/shard_map/ppermute | solution.py:47
  62.5 1.2 %fusion.19 = (bf16[1,4,8,4096]{3,2,1,0:T(8,128)(2,1)S(1)}, f32[1,4,8,4096]{3,2,1,0:T(8,128)S(1)}) fusion(bf16[4,8,4096]{2,1,0:T(8,128)(2,1)S(1)} %collective-permute-done.10, bf16[4,8,4096]{2,1,0:T(8,128)(2,1)S(1)} %collective-permute-done.9, bf16[4,8,4096]{2,1,0:T(8,128)(2,1)S(1)} %collective-permute-done.8, f32[4,4,8,4096]{3,2,1,0:T(8,128)} %bitcast.77), kind=kLoop, calls=%fused_computation.72 | loop fusion | flops 917504 | bytes 2097152 | tf_op jit(solution)/shard_map/convert.2
  63.9 1.8 %collective-permute-start.13 = (bf16[1,8,4096]{2,1,0:T(8,128)(2,1)S(1)}, bf16[1,8,4096]{2,1,0:T(8,128)(2,1)S(1)}, u32[]{:S(2)}, u32[]{:S(2)}) collective-permute-start(bf16[1,8,4096]{2,1,0:T(8,128)(2,1)S(1)} %get-tuple-element.44), channel_id=1, source_target_pairs={{0,24},{1,25},{2,26},{3,27},{4,28},{5,29},{6,30},{7,31},{8,16},{9,... | collective-permute-start | bytes 196616 | tf_op jit(solution)/shard_map/ppermute | solution.py:47
  66.4 1.9 %collective-permute-start.7 = (bf16[64,4096]{1,0:T(8,128)(2,1)S(1)}, bf16[64,4096]{1,0:T(8,128)(2,1)S(1)}, u32[]{:S(2)}, u32[]{:S(2)}) collective-permute-start(bf16[64,4096]{1,0:T(8,128)(2,1)S(1)} %pad_maximum_fusion.2), channel_id=1, source_target_pairs={{0,1},{1,0},{2,3},{3,2},{4,5},{5,4},{6,7},{7,6},{8,9},{9,8},{10,11... | collective-permute-start | bytes 1572872 | tf_op jit(solution)/shard_map/ppermute | solution.py:98
  69.2 3.5 %collective-permute-done.12 = bf16[1,8,4096]{2,1,0:T(8,128)(2,1)S(1)} collective-permute-done((bf16[1,8,4096]{2,1,0:T(8,128)(2,1)S(1)}, bf16[1,8,4096]{2,1,0:T(8,128)(2,1)S(1)}, u32[]{:S(2)}, u32[]{:S(2)}) %collective-permute-start.12) | collective-permute-done | bytes 65568 | tf_op jit(solution)/shard_map/ppermute | solution.py:47
  74.0 1.5 %collective-permute-start.14 = (bf16[64,4096]{1,0:T(8,128)(2,1)S(1)}, bf16[64,4096]{1,0:T(8,128)(2,1)S(1)}, u32[]{:S(2)}, u32[]{:S(2)}) collective-permute-start(bf16[64,4096]{1,0:T(8,128)(2,1)S(1)} %pad_maximum_fusion.3), channel_id=1, source_target_pairs={{0,1},{1,0},{2,3},{3,2},{4,5},{5,4},{6,7},{7,6},{8,9},{9,8},{10,11... | collective-permute-start | bytes 1572872 | tf_op jit(solution)/shard_map/ppermute | solution.py:98
  75.5 0.9 %maximum_select_fusion.5 = bf16[64,4096]{1,0:T(8,128)(2,1)} fusion(bf16[64,2048]{1,0:T(8,128)(2,1)S(1)} %get-tuple-element.31, bf16[64,2048]{1,0:T(8,128)(2,1)S(1)} %get-tuple-element.29, pred[]{:T(512)S(6)} %eq.20), kind=kLoop, calls=%fused_computation.21 | loop fusion | flops 2359296 | bytes 1048577 | tf_op jit(solution)/shard_map/jit(_where)/select_n | solution.py:123
  77.4 0.9 %maximum_select_fusion.7 = bf16[64,4096]{1,0:T(8,128)(2,1)} fusion(bf16[64,2048]{1,0:T(8,128)(2,1)S(1)} %get-tuple-element.25, bf16[64,2048]{1,0:T(8,128)(2,1)S(1)} %get-tuple-element.23, pred[]{:T(512)S(6)} %eq.20), kind=kLoop, calls=%fused_computation.24 | loop fusion | flops 2359296 | bytes 1048577 | tf_op jit(solution)/shard_map/jit(_where)/select_n | solution.py:123
  (61 shorter events, 9.9 us)
Async XLA Ops:
  0.6 1.8 %copy-start = (s32[2,8]{1,0:T(2,128)S(1)}, s32[2,8]{1,0:T(2,128)}, u32[]{:S(2)}) copy-start(s32[2,8]{1,0:T(2,128)} %param.9) | copy-start | bytes 196
  0.6 1.4 %copy-start.7 = (bf16[64,4096]{1,0:T(8,128)(2,1)S(1)}, bf16[64,4096]{1,0:T(8,128)(2,1)}, u32[]{:S(2)}) copy-start(bf16[64,4096]{1,0:T(8,128)(2,1)} %param.8) | copy-start | bytes 1572868
  0.7 1.5 %copy-start.8 = (bf16[64,4096]{1,0:T(8,128)(2,1)S(1)}, bf16[64,4096]{1,0:T(8,128)(2,1)}, u32[]{:S(2)}) copy-start(bf16[64,4096]{1,0:T(8,128)(2,1)} %param.7) | copy-start | bytes 1572868
  2.4 2.7 %collective-permute-start = (bf16[64,8192]{1,0:T(8,128)(2,1)S(1)}, bf16[64,8192]{1,0:T(8,128)(2,1)S(1)}, u32[]{:S(2)}, u32[]{:S(2)}) collective-permute-start(bf16[64,8192]{1,0:T(8,128)(2,1)S(1)} %pad_maximum_fusion), channel_id=1, source_target_pairs={{0,1},{1,0},{2,3},{3,2},{4,5},{5,4},{6,7},{7,6},{8,9},{9,8},{10,11... | collective-permute-start | bytes 3145736 | tf_op jit(solution)/shard_map/ppermute | solution.py:98
  5.3 14.5 %copy-start.1 = (bf16[128,2048]{1,0:T(8,128)(2,1)}, bf16[128,2048]{1,0:T(8,128)(2,1)S(1)}, u32[]{:S(2)}) copy-start(bf16[128,2048]{1,0:T(8,128)(2,1)S(1)} %maximum_select_fusion.2.v_all) | copy-start | bytes 1572868
  5.7 26.5 %copy-start.2 = (bf16[128,2048]{1,0:T(8,128)(2,1)}, bf16[128,2048]{1,0:T(8,128)(2,1)S(1)}, u32[]{:S(2)}) copy-start(bf16[128,2048]{1,0:T(8,128)(2,1)S(1)} %maximum_select_fusion.1.k_all) | copy-start | bytes 1572868
  5.9 6.7 %collective-permute-start.3 = (bf16[1,8,4096]{2,1,0:T(8,128)(2,1)S(1)}, bf16[1,8,4096]{2,1,0:T(8,128)(2,1)S(1)}, u32[]{:S(2)}, u32[]{:S(2)}) collective-permute-start(bf16[1,8,4096]{2,1,0:T(8,128)(2,1)S(1)} %bitcast.80), channel_id=1, source_target_pairs={{0,24},{1,25},{2,26},{3,27},{4,28},{5,29},{6,30},{7,31},{8,16},{9,... | collective-permute-start | bytes 196616 | tf_op jit(solution)/shard_map/ppermute | solution.py:47
  10.5 5.7 %collective-permute-start.2 = (bf16[1,8,4096]{2,1,0:T(8,128)(2,1)S(1)}, bf16[1,8,4096]{2,1,0:T(8,128)(2,1)S(1)}, u32[]{:S(2)}, u32[]{:S(2)}) collective-permute-start(bf16[1,8,4096]{2,1,0:T(8,128)(2,1)S(1)} %bitcast.81), channel_id=1, source_target_pairs={{0,16},{1,17},{2,18},{3,19},{4,20},{5,21},{6,22},{7,23},{8,24},{9,... | collective-permute-start | bytes 196616 | tf_op jit(solution)/shard_map/ppermute | solution.py:47
  10.5 5.7 %collective-permute-start.1 = (bf16[1,8,4096]{2,1,0:T(8,128)(2,1)S(1)}, bf16[1,8,4096]{2,1,0:T(8,128)(2,1)S(1)}, u32[]{:S(2)}, u32[]{:S(2)}) collective-permute-start(bf16[1,8,4096]{2,1,0:T(8,128)(2,1)S(1)} %bitcast.82), channel_id=1, source_target_pairs={{0,8},{1,9},{2,10},{3,11},{4,12},{5,13},{6,14},{7,15},{8,0},{9,1},... | collective-permute-start | bytes 196616 | tf_op jit(solution)/shard_map/ppermute | solution.py:47
  16.2 8.0 %collective-permute-start.6 = (bf16[4,8,4096]{2,1,0:T(8,128)(2,1)S(1)}, bf16[4,8,4096]{2,1,0:T(8,128)(2,1)S(1)}, u32[]{:S(2)}, u32[]{:S(2)}) collective-permute-start(bf16[4,8,4096]{2,1,0:T(8,128)(2,1)S(1)} %get-tuple-element.47), channel_id=1, source_target_pairs={{0,6},{1,7},{2,4},{3,5},{4,2},{5,3},{6,0},{7,1},{8,14},{9,15},{10,... | collective-permute-start | bytes 786440 | tf_op jit(solution)/shard_map/ppermute | solution.py:47
  18.5 11.4 %collective-permute-start.5 = (bf16[4,8,4096]{2,1,0:T(8,128)(2,1)S(1)}, bf16[4,8,4096]{2,1,0:T(8,128)(2,1)S(1)}, u32[]{:S(2)}, u32[]{:S(2)}) collective-permute-start(bf16[4,8,4096]{2,1,0:T(8,128)(2,1)S(1)} %get-tuple-element.47), channel_id=1, source_target_pairs={{0,4},{1,3},{2,6},{3,1},{4,0},{5,7},{6,2},{7,5},{8,12},{9,11},{10,... | collective-permute-start | bytes 786440 | tf_op jit(solution)/shard_map/ppermute | solution.py:47
  18.7 12.3 %collective-permute-start.4 = (bf16[4,8,4096]{2,1,0:T(8,128)(2,1)S(1)}, bf16[4,8,4096]{2,1,0:T(8,128)(2,1)S(1)}, u32[]{:S(2)}, u32[]{:S(2)}) collective-permute-start(bf16[4,8,4096]{2,1,0:T(8,128)(2,1)S(1)} %get-tuple-element.47), channel_id=1, source_target_pairs={{0,2},{1,5},{2,0},{3,7},{4,6},{5,1},{6,4},{7,3},{8,10},{9,13},{10,... | collective-permute-start | bytes 786440 | tf_op jit(solution)/shard_map/ppermute | solution.py:47
  45.6 4.6 %copy-start.6 = (bf16[128,2048]{1,0:T(8,128)(2,1)S(1)}, bf16[128,2048]{1,0:T(8,128)(2,1)}, u32[]{:S(2)}) copy-start(bf16[128,2048]{1,0:T(8,128)(2,1)} %get-tuple-element.9) | copy-start | bytes 1572868
  47.4 2.8 %copy-start.5 = (bf16[128,2048]{1,0:T(8,128)(2,1)S(1)}, bf16[128,2048]{1,0:T(8,128)(2,1)}, u32[]{:S(2)}) copy-start(bf16[128,2048]{1,0:T(8,128)(2,1)} %get-tuple-element.10) | copy-start | bytes 1572868
  47.4 7.1 %collective-permute-start.8 = (bf16[4,8,4096]{2,1,0:T(8,128)(2,1)S(1)}, bf16[4,8,4096]{2,1,0:T(8,128)(2,1)S(1)}, u32[]{:S(2)}, u32[]{:S(2)}) collective-permute-start(bf16[4,8,4096]{2,1,0:T(8,128)(2,1)S(1)} %get-tuple-element.16), channel_id=1, source_target_pairs={{0,2},{1,5},{2,0},{3,7},{4,6},{5,1},{6,4},{7,3},{8,10},{9,13},{10,... | collective-permute-start | bytes 786440 | tf_op jit(solution)/shard_map/ppermute | solution.py:47
  48.7 9.2 %collective-permute-start.10 = (bf16[4,8,4096]{2,1,0:T(8,128)(2,1)S(1)}, bf16[4,8,4096]{2,1,0:T(8,128)(2,1)S(1)}, u32[]{:S(2)}, u32[]{:S(2)}) collective-permute-start(bf16[4,8,4096]{2,1,0:T(8,128)(2,1)S(1)} %get-tuple-element.17), channel_id=1, source_target_pairs={{0,6},{1,7},{2,4},{3,5},{4,2},{5,3},{6,0},{7,1},{8,14},{9,15},{10,... | collective-permute-start | bytes 786440 | tf_op jit(solution)/shard_map/ppermute | solution.py:47
  49.9 12.5 %collective-permute-start.9 = (bf16[4,8,4096]{2,1,0:T(8,128)(2,1)S(1)}, bf16[4,8,4096]{2,1,0:T(8,128)(2,1)S(1)}, u32[]{:S(2)}, u32[]{:S(2)}) collective-permute-start(bf16[4,8,4096]{2,1,0:T(8,128)(2,1)S(1)} %get-tuple-element.18), channel_id=1, source_target_pairs={{0,4},{1,3},{2,6},{3,1},{4,0},{5,7},{6,2},{7,5},{8,12},{9,11},{10,... | collective-permute-start | bytes 786440 | tf_op jit(solution)/shard_map/ppermute | solution.py:47
  50.2 22.5 %copy-start.4 = (f32[128,2048]{1,0:T(8,128)S(1)}, f32[128,2048]{1,0:T(8,128)}, u32[]{:S(2)}) copy-start(f32[128,2048]{1,0:T(8,128)} %get-tuple-element.13) | copy-start | bytes 3145732
  63.6 9.6 %copy-start.3 = (f32[128,2048]{1,0:T(8,128)S(1)}, f32[128,2048]{1,0:T(8,128)}, u32[]{:S(2)}) copy-start(f32[128,2048]{1,0:T(8,128)} %get-tuple-element.11) | copy-start | bytes 3145732
  63.7 4.7 %collective-permute-start.11 = (bf16[1,8,4096]{2,1,0:T(8,128)(2,1)S(1)}, bf16[1,8,4096]{2,1,0:T(8,128)(2,1)S(1)}, u32[]{:S(2)}, u32[]{:S(2)}) collective-permute-start(bf16[1,8,4096]{2,1,0:T(8,128)(2,1)S(1)} %get-tuple-element.43), channel_id=1, source_target_pairs={{0,8},{1,9},{2,10},{3,11},{4,12},{5,13},{6,14},{7,15},{8,0},{9,1},... | collective-permute-start | bytes 196616 | tf_op jit(solution)/shard_map/ppermute | solution.py:47
  63.9 5.3 %collective-permute-start.13 = (bf16[1,8,4096]{2,1,0:T(8,128)(2,1)S(1)}, bf16[1,8,4096]{2,1,0:T(8,128)(2,1)S(1)}, u32[]{:S(2)}, u32[]{:S(2)}) collective-permute-start(bf16[1,8,4096]{2,1,0:T(8,128)(2,1)S(1)} %get-tuple-element.44), channel_id=1, source_target_pairs={{0,24},{1,25},{2,26},{3,27},{4,28},{5,29},{6,30},{7,31},{8,16},{9,... | collective-permute-start | bytes 196616 | tf_op jit(solution)/shard_map/ppermute | solution.py:47
  65.7 7.0 %collective-permute-start.12 = (bf16[1,8,4096]{2,1,0:T(8,128)(2,1)S(1)}, bf16[1,8,4096]{2,1,0:T(8,128)(2,1)S(1)}, u32[]{:S(2)}, u32[]{:S(2)}) collective-permute-start(bf16[1,8,4096]{2,1,0:T(8,128)(2,1)S(1)} %get-tuple-element.45), channel_id=1, source_target_pairs={{0,16},{1,17},{2,18},{3,19},{4,20},{5,21},{6,22},{7,23},{8,24},{9,... | collective-permute-start | bytes 196616 | tf_op jit(solution)/shard_map/ppermute | solution.py:47
  66.4 9.0 %collective-permute-start.7 = (bf16[64,4096]{1,0:T(8,128)(2,1)S(1)}, bf16[64,4096]{1,0:T(8,128)(2,1)S(1)}, u32[]{:S(2)}, u32[]{:S(2)}) collective-permute-start(bf16[64,4096]{1,0:T(8,128)(2,1)S(1)} %pad_maximum_fusion.2), channel_id=1, source_target_pairs={{0,1},{1,0},{2,3},{3,2},{4,5},{5,4},{6,7},{7,6},{8,9},{9,8},{10,11... | collective-permute-start | bytes 1572872 | tf_op jit(solution)/shard_map/ppermute | solution.py:98
  74.0 3.4 %collective-permute-start.14 = (bf16[64,4096]{1,0:T(8,128)(2,1)S(1)}, bf16[64,4096]{1,0:T(8,128)(2,1)S(1)}, u32[]{:S(2)}, u32[]{:S(2)}) collective-permute-start(bf16[64,4096]{1,0:T(8,128)(2,1)S(1)} %pad_maximum_fusion.3), channel_id=1, source_target_pairs={{0,1},{1,0},{2,3},{3,2},{4,5},{5,4},{6,7},{7,6},{8,9},{9,8},{10,11... | collective-permute-start | bytes 1572872 | tf_op jit(solution)/shard_map/ppermute | solution.py:98
